TPU v7x, 512 devices: a whole 4x4x16 slice. The times are simulated.
512 devices in a mesh: seq: 64 (over z, y), tensor: 8 (over x, core).
Axes of the slice: x: 4, y: 4, z: 16, core: 2. Of those that a mesh axis runs over, the one named last changes fastest.
Arguments:
- hidden: bfloat16 [8192, 4096], P('seq', 'tensor')
- norm_gain: bfloat16 [4096], replicated, may hold values from 0.5 to 1.5
- w_query: bfloat16 [4096, 4096], P('seq', 'tensor')
- key_value_weight: bfloat16 [4096, 1024], P('seq')
- w_out: bfloat16 [4096, 4096], P('tensor', 'seq'), may hold values from -0.09375 to 0.09375
- prefix_key_cache: bfloat16 [64, 1024, 1024], P('seq')
- prefix_owner: int32 [64], replicated, may hold values from 0 to 63, each once
- token_counts: int32 [64, 64], P('seq'), may hold values from 0 to 4, as said below
Outputs:
- attn_out: bfloat16 [8192, 4096], P('seq', 'tensor')
- suffix_key_cache: bfloat16 [8192, 1024], P('seq', 'tensor')
Inputs may be any that keep to these rules, and one draw needn't show every extreme that they name: `token_counts`: each row sums to 128; one prefix receives exactly 4 tokens from every sequence index.
All inputs are finite; a program needn't handle non-finite values.
Results may differ from a plain program's by a relative error of at most 0.035.
Values may be sent and summed in bfloat16 or wider, within the bound.
No kernel may reach another device: no remote copies, remote signals or barrier semaphores. Data moves between devices by JAX's collectives and lax.ppermute only.
A program may use at most 64 MiB of HBM per device.

v0:
```python
import jax
import jax.numpy as jnp
from jax import lax
from jax.sharding import PartitionSpec as P

HEAD_DIM = 128
PREFIX_LENGTH = 1024


eps = 1e-06
theta = 5000000.0


def rotate(values, positions):
    half = values.shape[-1] // 2
    frequency = theta ** (-jnp.arange(half, dtype=jnp.float32) * 2.0 / values.shape[-1])
    angle = positions.astype(jnp.float32)[:, None] * frequency[None, :]
    cosine = jnp.cos(angle)[:, None, :]
    sine = jnp.sin(angle)[:, None, :]
    first = values[..., :half]
    second = values[..., half:]
    return jnp.concatenate(
        [first * cosine - second * sine, second * cosine + first * sine], axis=-1
    )


def layout(counts_row, length):
    ends = jnp.cumsum(counts_row)
    starts = ends - counts_row
    places = jnp.arange(length, dtype=jnp.int32)
    member = (places[:, None] >= starts[None, :]) & (places[:, None] < ends[None, :])
    labels = jnp.arange(counts_row.shape[0], dtype=jnp.int32)
    prefix_group = jnp.sum(jnp.where(member, labels[None, :], 0), axis=1)
    offset = places - jnp.sum(jnp.where(member, starts[None, :], 0), axis=1)
    return (starts, prefix_group, offset)


def attend(query_vectors, keys, values, allowed):
    scores = lax.dot_general(
        query_vectors, keys, (((1,), (1,)), ((), ())), preferred_element_type=jnp.float32
    )
    scores = scores * (1.0 / query_vectors.shape[-1] ** 0.5)
    if allowed is not None:
        scores = jnp.where(allowed, scores, -1e30)
    top = jnp.max(scores, axis=1, keepdims=True)
    expo = jnp.exp(scores - top)
    total = jnp.sum(expo, axis=1, keepdims=True)
    weights = (expo / total).astype(jnp.bfloat16)
    result = jnp.dot(weights, values, preferred_element_type=jnp.float32)
    return (result, top[:, 0] + jnp.log(total[:, 0]))


def shards(
    hidden,
    norm_gain,
    w_query,
    key_value_weight,
    w_out,
    prefix_key_cache,
    prefix_owner,
    token_counts,
):
    tensor_index = lax.axis_index("tensor")
    tensor_count = lax.axis_size("tensor")
    seq_count = lax.axis_size("seq")
    length = hidden.shape[0]
    head_size = HEAD_DIM
    whole = lax.all_gather(hidden, "tensor", axis=1, tiled=True)
    wide = whole.astype(jnp.float32)
    normalized_input = (
        wide
        * lax.rsqrt(jnp.mean(wide * wide, axis=1, keepdims=True) + eps)
        * norm_gain.astype(jnp.float32)
    ).astype(jnp.bfloat16)
    width_query = w_query.shape[1]
    full_width = key_value_weight.shape[1]
    heads_dev = width_query // head_size
    kv_heads = full_width // (2 * head_size)

    def contract(piece):
        return jnp.dot(normalized_input, piece, preferred_element_type=jnp.float32)

    query_vectors = contract(lax.all_gather(w_query, "seq", axis=0, tiled=True))
    key_value_pair = contract(lax.all_gather(key_value_weight, "seq", axis=0, tiled=True))
    counts = token_counts[0]
    num_groups = counts.shape[0]
    starts, prefix_group, offset = layout(counts, length)
    positions = PREFIX_LENGTH + offset
    query_vectors = rotate(query_vectors.reshape(length, heads_dev, head_size), positions).astype(
        jnp.bfloat16
    )
    pair_blocks = key_value_pair.reshape(length, kv_heads, 2, head_size)
    rotated_keys = rotate(pair_blocks[:, :, 0], positions)
    pair_all = jnp.stack([rotated_keys, pair_blocks[:, :, 1]], axis=2).astype(jnp.bfloat16)
    suffix_full = pair_all.reshape(length, full_width)
    share = full_width // tensor_count
    suffix_part = lax.dynamic_slice_in_dim(suffix_full, tensor_index * share, share, 1)
    group_full = heads_dev * tensor_count // kv_heads
    kv_local = max(1, heads_dev // group_full)
    kv_start = tensor_index * heads_dev // group_full
    suffix_mine = lax.dynamic_slice_in_dim(pair_all, kv_start, kv_local, 1)
    suffix_keys = suffix_mine[:, :, 0]
    suffix_values = suffix_mine[:, :, 1]
    cache_all = prefix_key_cache[0].reshape(-1, kv_heads, 2, head_size)
    cache_mine = lax.dynamic_slice_in_dim(cache_all, kv_start, kv_local, 1)
    cache_keys = cache_mine[:, :, 0]
    cache_values = cache_mine[:, :, 1]
    group_width = heads_dev // kv_local
    capacity = 2 * length // seq_count
    labels = jnp.arange(num_groups, dtype=jnp.int32)
    owner_match = prefix_owner[None, :] == jnp.arange(seq_count, dtype=jnp.int32)[:, None]
    owner_start = jnp.sum(jnp.where(owner_match, starts[None, :], 0), axis=1)
    owner_count = jnp.sum(jnp.where(owner_match, counts[None, :], 0), axis=1)
    slots = jnp.arange(capacity, dtype=jnp.int32)
    valid = slots[None, :] < owner_count[:, None]
    source_rows = jnp.where(valid, owner_start[:, None] + slots[None, :], 0)
    flat_query = query_vectors.reshape(length, width_query)
    outgoing = jnp.where(valid[:, :, None], flat_query[source_rows], jnp.zeros((), jnp.bfloat16))
    arrived = lax.all_to_all(outgoing, "seq", split_axis=0, concat_axis=0, tiled=True)
    items = arrived.shape[1]
    rows_in = arrived.reshape(seq_count * items, heads_dev, head_size)
    outs = []
    logs = []
    for serve_head in range(heads_dev):
        serve_result, serve_logsum = attend(
            rows_in[:, serve_head],
            cache_keys[:, serve_head // group_width],
            cache_values[:, serve_head // group_width],
            None,
        )
        outs.append(serve_result)
        logs.append(serve_logsum)
    out_block = jnp.stack(outs, axis=1).astype(jnp.bfloat16).reshape(seq_count, items, width_query)
    log_block = jnp.stack(logs, axis=1).reshape(seq_count, items, heads_dev)
    prefix_out = lax.all_to_all(out_block, "seq", split_axis=0, concat_axis=0, tiled=True)
    prefix_log = lax.all_to_all(
        log_block.astype(jnp.bfloat16), "seq", split_axis=0, concat_axis=0, tiled=True
    ).astype(log_block.dtype)
    owner_of_token = jnp.sum(
        jnp.where(prefix_group[:, None] == labels[None, :], prefix_owner[None, :], 0), axis=1
    )
    back_rows = owner_of_token * capacity + offset
    prefix_rows = prefix_out.reshape(seq_count * capacity, heads_dev, head_size)[back_rows]
    prefix_logsum = prefix_log.reshape(seq_count * capacity, heads_dev)[back_rows]
    places = jnp.arange(length, dtype=jnp.int32)
    allowed = (prefix_group[:, None] == prefix_group[None, :]) & (
        places[None, :] <= places[:, None]
    )
    outs = []
    logs = []
    for head in range(heads_dev):
        result, logsum = attend(
            query_vectors[:, head],
            suffix_keys[:, head // group_width],
            suffix_values[:, head // group_width],
            allowed,
        )
        outs.append(result)
        logs.append(logsum)
    suffix_attn = jnp.stack(outs, axis=1)
    suffix_logsum = jnp.stack(logs, axis=1)
    upper = jnp.maximum(prefix_logsum, suffix_logsum)
    left = jnp.exp(prefix_logsum - upper)[..., None]
    right = jnp.exp(suffix_logsum - upper)[..., None]
    context = (
        (left * prefix_rows.astype(jnp.float32) + right * suffix_attn) / (left + right)
    ).astype(jnp.bfloat16)
    context = context.reshape(length, width_query)
    partial_out = jnp.dot(
        context,
        lax.all_gather(w_out, "seq", axis=1, tiled=True),
        preferred_element_type=jnp.float32,
    )
    attn_out = lax.psum_scatter(
        partial_out.astype(jnp.bfloat16), "tensor", scatter_dimension=1, tiled=True
    )
    return (attn_out, suffix_part)


def solution(mesh):
    in_specs = (
        P("seq", "tensor"),
        P(),
        P("seq", "tensor"),
        P("seq", None),
        P("tensor", "seq"),
        P("seq", None, None),
        P(),
        P("seq", None),
    )
    out_specs = (P("seq", "tensor"), P("seq", "tensor"))
    return jax.shard_map(shards, mesh=mesh, in_specs=in_specs, out_specs=out_specs, check_vma=False)
```

profile of v0, /device:TPU:1, one launch (start us, length us, event | category | flops | bytes accessed | tf_op | source)
XLA Modules:
  0.0 540.5 jit_solution(3711993992200430537)
XLA Ops:
  12.4 2.9 copy.123
  16.5 1.0 multiply_cosine_fusion
  17.4 29.7 %all-gather.5.cloned.1.call-done = bf16[128,4096]{1,0:T(8,128)(2,1)} async-done(((bf16[128,512]{1,0:T(8,128)(2,1)}), bf16[128,4096]{1,0:T(8,128)(2,1)}) %all-gather.5.cloned.1.call-update) | async-done | bytes 1048592 | tf_op jit(solution)/shard_map/all_gather | solution.py:68
  47.1 1.5 fusion
  48.6 139.3 %all-gather.7.cloned.1.call-done = bf16[4096,512]{1,0:T(8,128)(2,1)} async-done(((bf16[64,512]{1,0:T(8,128)(2,1)}), bf16[4096,512]{1,0:T(8,128)(2,1)}) %all-gather.7.cloned.1.call-update) | async-done | bytes 4194320 | tf_op jit(solution)/shard_map/all_gather | solution.py:83
  187.9 4.0 fusion.17
  191.9 1.0 reshape.549
  192.9 0.9 fusion.69
  193.9 149.0 %all-gather.9.cloned.1.call-done = bf16[4096,1024]{1,0:T(8,128)(2,1)} async-done(((bf16[64,1024]{1,0:T(8,128)(2,1)}), bf16[4096,1024]{1,0:T(8,128)(2,1)}) %all-gather.9.cloned.1.call-update) | async-done | bytes 8388624 | tf_op jit(solution)/shard_map/all_gather | solution.py:84
  342.8 5.5 %fusion.15 = f32[128,1024]{1,0:T(8,128)} fusion(bf16[4096,1024]{1,0:T(8,128)(2,1)} %all-gather.9.cloned.1.call-done, bf16[128,4096]{1,0:T(8,128)(2,1)S(1)} %copy-done, f32[4096]{0:T(1024)S(1)} %convert_element_type.73, f32[128]{0:T(128)S(1)} %add_rsqrt_fusion), kind=kOutput, calls=%fused_computation.46 | convolution fusion | flops 1075838976 | bytes 9978368 | tf_op jit(solution)/shard_map/dot_general | solution.py:81
  348.3 1.5 reshape.555
  350.4 1.1 multiply_subtract_fusion
  351.7 1.2 gather_fusion
  352.9 0.9 broadcast_select_fusion
  353.8 8.7 %all-to-all-start = ((bf16[64,4,512]{2,1,0:T(4,128)(2,1)}), bf16[64,4,512]{2,1,0:T(4,128)(2,1)S(1)}, u32[]{:S(2)}, u32[]{:S(2)}) async-start(bf16[64,4,512]{2,1,0:T(4,128)(2,1)} %broadcast_select_fusion), calls=%async_computation | async-start | bytes 524288 | tf_op jit(solution)/shard_map/all_to_all | solution.py:119
  366.7 13.3 %all-to-all-done = bf16[64,4,512]{2,1,0:T(4,128)(2,1)S(1)} async-done(((bf16[64,4,512]{2,1,0:T(4,128)(2,1)}), bf16[64,4,512]{2,1,0:T(4,128)(2,1)S(1)}, u32[]{:S(2)}, u32[]{:S(2)}) %all-to-all-start) | async-done | bytes 262176 | tf_op jit(solution)/shard_map/all_to_all | solution.py:119
  380.1 1.1 fusion.68
  383.9 1.3 fusion.75
  385.2 1.0 copy-done.1
  387.5 1.4 add.237
  388.9 1.3 fusion.76
  390.2 1.0 copy-done.3
  392.7 1.4 add.235
  394.5 1.0 copy-done.5
  397.3 5.1 all-to-all-start.1
  402.4 1.1 fusion.6
  407.7 8.9 %all-to-all-done.1 = bf16[64,4,4]{1,2,0:T(4,128)(2,1)S(1)} async-done(((bf16[64,4,4]{1,2,0:T(4,128)(2,1)}), bf16[64,4,4]{1,2,0:T(4,128)(2,1)S(1)}, u32[]{:S(2)}, u32[]{:S(2)}) %all-to-all-start.1) | async-done | bytes 2080 | tf_op jit(solution)/shard_map/all_to_all | solution.py:136
  416.6 5.5 %all-to-all-start.2 = ((bf16[64,4,512]{2,1,0:T(4,128)(2,1)}), bf16[64,4,512]{2,1,0:T(4,128)(2,1)S(1)}, u32[]{:S(2)}, u32[]{:S(2)}) async-start(bf16[64,4,512]{2,1,0:T(4,128)(2,1)} %convert_element_type.83), calls=%async_computation.2 | async-start | bytes 524288 | tf_op jit(solution)/shard_map/all_to_all | solution.py:135
  424.0 15.6 %all-to-all-done.2 = bf16[64,4,512]{2,1,0:T(4,128)(2,1)S(1)} async-done(((bf16[64,4,512]{2,1,0:T(4,128)(2,1)}), bf16[64,4,512]{2,1,0:T(4,128)(2,1)S(1)}, u32[]{:S(2)}, u32[]{:S(2)}) %all-to-all-start.2) | async-done | bytes 262176 | tf_op jit(solution)/shard_map/all_to_all | solution.py:135
  440.8 47.6 %all-gather.11.cloned.1.call-done = bf16[512,4096]{0,1:T(8,128)(2,1)} async-done(((bf16[512,64]{0,1:T(8,128)(2,1)}), bf16[512,4096]{0,1:T(8,128)(2,1)}) %all-gather.11.cloned.1.call-update) | async-done | bytes 4194320 | tf_op jit(solution)/shard_map/all_gather | solution.py:171
  488.3 4.7 convolution_convert_fusion
  493.9 40.0 %reduce-scatter.2.cloned.1.call-done = bf16[128,512]{1,0:T(8,128)(2,1)} async-done(((bf16[128,4096]{1,0:T(8,128)(2,1)}), bf16[128,512]{1,0:T(8,128)(2,1)}) %reduce-scatter.2.cloned.1.call-update) | async-done | bytes 131088 | tf_op jit(solution)/shard_map/reduce_scatter | solution.py:174
  (166 shorter events, 26.9 us)
Async XLA Ops:
  7.2 39.9 %all-gather.5.cloned.1.call-start = ((), (), s32[]{:S(2)}) async-start(), calls=%async_computation.4 | async-start | bytes 1179648 | tf_op jit(solution)/shard_map/all_gather | solution.py:68
  7.9 180.0 %all-gather.7.cloned.1.call-start = ((), (), s32[]{:S(2)}) async-start(), calls=%async_computation.5 | async-start | bytes 4259840 | tf_op jit(solution)/shard_map/all_gather | solution.py:83
  8.6 334.2 %all-gather.9.cloned.1.call-start = ((), (), s32[]{:S(2)}) async-start(), calls=%async_computation.6 | async-start | bytes 8519680 | tf_op jit(solution)/shard_map/all_gather | solution.py:84
  9.4 478.9 %all-gather.11.cloned.1.call-start = ((), (), s32[]{:S(2)}) async-start(), calls=%async_computation.7 | async-start | bytes 4259840 | tf_op jit(solution)/shard_map/all_gather | solution.py:171
  12.4 2.9 copy-start.28
  12.4 2.9 copy-start.42
  48.6 294.2 %copy-start = (bf16[128,4096]{1,0:T(8,128)(2,1)S(1)}, bf16[128,4096]{1,0:T(8,128)(2,1)}, u32[]{:S(2)}) copy-start(bf16[128,4096]{1,0:T(8,128)(2,1)} %all-gather.5.cloned.1.call-done) | copy-start | bytes 3145732
  348.3 2.1 copy-start.7
  348.3 2.1 copy-start.8
  353.8 26.2 %all-to-all-start = ((bf16[64,4,512]{2,1,0:T(4,128)(2,1)}), bf16[64,4,512]{2,1,0:T(4,128)(2,1)S(1)}, u32[]{:S(2)}, u32[]{:S(2)}) async-start(bf16[64,4,512]{2,1,0:T(4,128)(2,1)} %broadcast_select_fusion), calls=%async_computation | async-start | bytes 524288 | tf_op jit(solution)/shard_map/all_to_all | solution.py:119
  362.8 3.9 copy-start.29
  363.0 18.2 %copy-start.9 = (f32[128,128]{0,1:T(8,128)}, f32[128,128]{0,1:T(8,128)S(1)}, u32[]{:S(2)}) copy-start(f32[128,128]{0,1:T(8,128)S(1)} %get-tuple-element.36) | copy-start | bytes 196612
  363.1 3.6 copy-start.33
  363.9 17.3 %copy-start.11 = (f32[128,128]{0,1:T(8,128)}, f32[128,128]{0,1:T(8,128)S(1)}, u32[]{:S(2)}) copy-start(f32[128,128]{0,1:T(8,128)S(1)} %get-tuple-element.38) | copy-start | bytes 196612
  365.2 1.5 copy-start.13
  365.2 1.5 copy-start.39
  390.2 1.3 copy-start.19
  397.3 19.2 %all-to-all-start.1 = ((bf16[64,4,4]{1,2,0:T(4,128)(2,1)}), bf16[64,4,4]{1,2,0:T(4,128)(2,1)S(1)}, u32[]{:S(2)}, u32[]{:S(2)}) async-start(bf16[64,4,4]{1,2,0:T(4,128)(2,1)} %copy.125), calls=%async_computation.1 | async-start | bytes 131072 | tf_op jit(solution)/shard_map/all_to_all | solution.py:136
  406.5 15.6 %copy-start.10 = (f32[128,128]{0,1:T(8,128)S(1)}, f32[128,128]{0,1:T(8,128)}, u32[]{:S(2)}) copy-start(f32[128,128]{0,1:T(8,128)} %copy-done.9) | copy-start | bytes 196612
  406.5 15.6 %copy-start.32 = (f32[128]{0:T(128)S(1)}, f32[128]{0:T(128)}, u32[]{:S(2)}) copy-start(f32[128]{0:T(128)} %copy-done.31) | copy-start | bytes 1540
  406.5 15.6 %copy-start.37 = (f32[128]{0:T(128)S(1)}, f32[128]{0:T(128)}, u32[]{:S(2)}) copy-start(f32[128]{0:T(128)} %fusion.33) | copy-start | bytes 1540
  406.5 15.8 %copy-start.12 = (f32[128,128]{0,1:T(8,128)S(1)}, f32[128,128]{0,1:T(8,128)}, u32[]{:S(2)}) copy-start(f32[128,128]{0,1:T(8,128)} %copy-done.11) | copy-start | bytes 196612
  406.5 15.8 %copy-start.36 = (f32[128]{0:T(128)S(1)}, f32[128]{0:T(128)}, u32[]{:S(2)}) copy-start(f32[128]{0:T(128)} %copy-done.35) | copy-start | bytes 1540
  406.5 15.8 %copy-start.38 = (f32[128]{0:T(128)S(1)}, f32[128]{0:T(128)}, u32[]{:S(2)}) copy-start(f32[128]{0:T(128)} %fusion.32) | copy-start | bytes 1540
  406.6 16.0 %copy-start.14 = (f32[128,128]{0,1:T(8,128)S(1)}, f32[128,128]{0,1:T(8,128)}, u32[]{:S(2)}) copy-start(f32[128,128]{0,1:T(8,128)} %copy-done.13) | copy-start | bytes 196612
  406.6 16.0 %copy-start.40 = (f32[128]{0:T(128)S(1)}, f32[128]{0:T(128)}, u32[]{:S(2)}) copy-start(f32[128]{0:T(128)} %copy-done.39) | copy-start | bytes 1540
  406.6 16.0 %copy-start.41 = (f32[128]{0:T(128)S(1)}, f32[128]{0:T(128)}, u32[]{:S(2)}) copy-start(f32[128]{0:T(128)} %fusion.31) | copy-start | bytes 1540
  406.6 16.2 %copy-start.30 = (f32[128]{0:T(128)S(1)}, f32[128]{0:T(128)}, u32[]{:S(2)}) copy-start(f32[128]{0:T(128)} %copy-done.29) | copy-start | bytes 1540
  406.6 16.2 %copy-start.34 = (f32[128]{0:T(128)S(1)}, f32[128]{0:T(128)}, u32[]{:S(2)}) copy-start(f32[128]{0:T(128)} %copy-done.33) | copy-start | bytes 1540
  406.7 34.0 %copy-start.15 = (f32[128,1,128]{0,2,1:T(8,128)S(1)}, f32[128,1,128]{0,2,1:T(8,128)}, u32[]{:S(2)}) copy-start(f32[128,1,128]{0,2,1:T(8,128)} %convolution_bitcast_fusion) | copy-start | bytes 196612
  416.6 23.0 %all-to-all-start.2 = ((bf16[64,4,512]{2,1,0:T(4,128)(2,1)}), bf16[64,4,512]{2,1,0:T(4,128)(2,1)S(1)}, u32[]{:S(2)}, u32[]{:S(2)}) async-start(bf16[64,4,512]{2,1,0:T(4,128)(2,1)} %convert_element_type.83), calls=%async_computation.2 | async-start | bytes 524288 | tf_op jit(solution)/shard_map/all_to_all | solution.py:135
  422.0 111.9 %reduce-scatter.2.cloned.1.call-start = ((), (), s32[]{:S(2)}) async-start(), calls=%async_computation.8 | async-start | bytes 1179648 | tf_op jit(solution)/shard_map/reduce_scatter | solution.py:174
  (19 other events, 19.1 us)
Sparse Core Ops, SparseCore 0:
  10.1 36.9 all-gather.4
  50.0 137.8 all-gather.6
  190.8 151.9 all-gather.8
  345.6 142.6 all-gather.10
  493.1 40.7 reduce-scatter.1
where the time goes:
time: 542 us; the launch traced here: 540 us
  waiting for transfers between devices  446 us (82%)
  local copies, waits for them, and re-layouts  25.9 us (5%)
  matrix products  21.8 us (4%)
  starting transfers between devices  19.4 us (4%)
  between operations  14.5 us (3%)
  other arithmetic  13 us (2%)
    all_gather x1, waiting for transfers between devices, shards(): lax.all_gather(key_value_weight, 'seq', axis=0, tiled=True)  149 us
    all_gather x1, waiting for transfers between devices, shards(): query_vectors = contract(lax.all_gather(w_query, 'seq', axis=0, tiled=True))  139 us
    all_gather x1, waiting for transfers between devices, shards(): lax.all_gather(w_out, 'seq', axis=1, tiled=True)  47.6 us
    reduce_scatter x1, waiting for transfers between devices, shards(): lax.psum_scatter(partial_out.astype(jnp.bfloat16), 'tensor', scatter_dime...  40 us
    all_gather x1, waiting for transfers between devices, shards(): whole = lax.all_gather(hidden, 'tensor', axis=1, tiled=True)  29.7 us
    all_to_all x1, waiting for transfers between devices, shards(): lax.all_to_all(out_block, 'seq', split_axis=0, concat_axis=0, tiled=True)  15.6 us
    all_to_all x1, waiting for transfers between devices, shards(): lax.all_to_all(outgoing, 'seq', split_axis=0, concat_axis=0, tiled=True)  13.3 us
    unnamed x90, local copies, waits for them, and re-layouts  10.9 us
  transfers between devices with their start and end apart: 8, of which 8 were waited for; matrix products, arithmetic and copies ran while one was open for 9% of the time, Pallas kernels for 0%

commit v1 on v0

--- a/solution.py
+++ b/solution.py
@@ -76,12 +76,22 @@
     full_width = key_value_weight.shape[1]
     heads_dev = width_query // head_size
     kv_heads = full_width // (2 * head_size)
+    group_full = heads_dev * tensor_count // kv_heads
+    kv_local = max(1, heads_dev // group_full)
+    kv_start = tensor_index * heads_dev // group_full
+    kv_width = kv_local * 2 * head_size
+    kv_piece = lax.dynamic_slice_in_dim(key_value_weight, kv_start * 2 * head_size, kv_width, 1)
+    packed = jnp.concatenate([w_query, kv_piece, w_out.T], axis=1)
+    gathered = lax.all_gather(packed, "seq", axis=0, tiled=True)
+    wq_full = gathered[:, :width_query]
+    kv_full = gathered[:, width_query : width_query + kv_width]
+    wo_cols = gathered[:, width_query + kv_width :]
 
     def contract(piece):
         return jnp.dot(normalized_input, piece, preferred_element_type=jnp.float32)
 
-    query_vectors = contract(lax.all_gather(w_query, "seq", axis=0, tiled=True))
-    key_value_pair = contract(lax.all_gather(key_value_weight, "seq", axis=0, tiled=True))
+    query_vectors = contract(wq_full)
+    key_value_pair = contract(kv_full)
     counts = token_counts[0]
     num_groups = counts.shape[0]
     starts, prefix_group, offset = layout(counts, length)
@@ -89,16 +99,14 @@
     query_vectors = rotate(query_vectors.reshape(length, heads_dev, head_size), positions).astype(
         jnp.bfloat16
     )
-    pair_blocks = key_value_pair.reshape(length, kv_heads, 2, head_size)
+    pair_blocks = key_value_pair.reshape(length, kv_local, 2, head_size)
     rotated_keys = rotate(pair_blocks[:, :, 0], positions)
-    pair_all = jnp.stack([rotated_keys, pair_blocks[:, :, 1]], axis=2).astype(jnp.bfloat16)
-    suffix_full = pair_all.reshape(length, full_width)
+    suffix_mine = jnp.stack([rotated_keys, pair_blocks[:, :, 1]], axis=2).astype(jnp.bfloat16)
     share = full_width // tensor_count
-    suffix_part = lax.dynamic_slice_in_dim(suffix_full, tensor_index * share, share, 1)
-    group_full = heads_dev * tensor_count // kv_heads
-    kv_local = max(1, heads_dev // group_full)
-    kv_start = tensor_index * heads_dev // group_full
-    suffix_mine = lax.dynamic_slice_in_dim(pair_all, kv_start, kv_local, 1)
+    suffix_flat = suffix_mine.reshape(length, kv_width)
+    suffix_part = lax.dynamic_slice_in_dim(
+        suffix_flat, tensor_index * share - kv_start * 2 * head_size, share, 1
+    )
     suffix_keys = suffix_mine[:, :, 0]
     suffix_values = suffix_mine[:, :, 1]
     cache_all = prefix_key_cache[0].reshape(-1, kv_heads, 2, head_size)
@@ -166,10 +174,8 @@
         (left * prefix_rows.astype(jnp.float32) + right * suffix_attn) / (left + right)
     ).astype(jnp.bfloat16)
     context = context.reshape(length, width_query)
-    partial_out = jnp.dot(
-        context,
-        lax.all_gather(w_out, "seq", axis=1, tiled=True),
-        preferred_element_type=jnp.float32,
+    partial_out = lax.dot_general(
+        context, wo_cols, (((1,), (1,)), ((), ())), preferred_element_type=jnp.float32
     )
     attn_out = lax.psum_scatter(
         partial_out.astype(jnp.bfloat16), "tensor", scatter_dimension=1, tiled=True

time: 542 us -> 345 us (0.64)
  waiting for transfers between devices: 446 us -> 270 us
  local copies, waits for them, and re-layouts: 25.9 us -> 13.2 us
  matrix products: 21.8 us -> 16 us
    all_gather x3 -> x1, waiting for transfers between devices: 336 us -> 159 us  [shards(): gathered = lax.all_gather(packed, 'seq', axis=0, tiled=True)]
    unnamed x90 -> x20, local copies, waits for them, and re-layouts: 10.9 us -> 4.05 us
  transfers between devices with their start and end apart: 8 -> 6, of which waited for: 8 -> 6; matrix products, arithmetic and copies ran while one was open for 9% -> 4% of each run, Pallas kernels for 0% -> 0%
where the time goes in v1:
time: 345 us; the launch traced here: 343 us
  waiting for transfers between devices  270 us (78%)
  starting transfers between devices  18.2 us (5%)
  matrix products  16 us (5%)
  between operations  14.2 us (4%)
  local copies, waits for them, and re-layouts  13.2 us (4%)
  other arithmetic  11.4 us (3%)
    all_gather x1, waiting for transfers between devices, shards(): gathered = lax.all_gather(packed, 'seq', axis=0, tiled=True)  159 us
    reduce_scatter x1, waiting for transfers between devices, shards(): lax.psum_scatter(partial_out.astype(jnp.bfloat16), 'tensor', scatter_dime...  35.9 us
    all_gather x1, waiting for transfers between devices, shards(): whole = lax.all_gather(hidden, 'tensor', axis=1, tiled=True)  29.6 us
    all_to_all x1, waiting for transfers between devices, shards(): lax.all_to_all(outgoing, 'seq', split_axis=0, concat_axis=0, tiled=True)  16.4 us
    all_to_all x1, waiting for transfers between devices, shards(): lax.all_to_all(out_block, 'seq', split_axis=0, concat_axis=0, tiled=True)  16.1 us
    all_to_all x1, waiting for transfers between devices, shards(): lax.all_to_all(log_block.astype(jnp.bfloat16), 'seq', split_axis=0, conca...  13 us
    all_to_all x1, starting transfers between devices, shards(): lax.all_to_all(outgoing, 'seq', split_axis=0, concat_axis=0, tiled=True)  8.88 us
  transfers between devices with their start and end apart: 6, of which 6 were waited for; matrix products, arithmetic and copies ran while one was open for 4% of the time, Pallas kernels for 0%

profile of v1, /device:TPU:1, one launch (start us, length us, event | category | flops | bytes accessed | tf_op | source)
XLA Modules:
  0.0 343.2 jit_solution(9256899727202618528)
XLA Ops:
  7.2 0.7 all-gather.3.cloned.1.call-update
  8.1 1.5 pad_maximum_fusion.1
  9.6 0.7 convert_element_type.81
  10.4 0.8 copy.118
  11.3 0.7 fusion.64
  12.0 0.8 select_reduce_fusion.4
  13.0 2.9 copy.121
  16.6 1.0 multiply_cosine_fusion.1
  17.5 29.6 %all-gather.3.cloned.1.call-done = bf16[128,4096]{1,0:T(8,128)(2,1)} async-done(((bf16[128,512]{1,0:T(8,128)(2,1)}), bf16[128,4096]{1,0:T(8,128)(2,1)}) %all-gather.3.cloned.1.call-update) | async-done | bytes 1048592 | tf_op jit(solution)/shard_map/all_gather | solution.py:68
  47.1 1.5 fusion.3
  48.6 158.5 %all-gather.5.cloned.1.call-done = bf16[4096,1280]{1,0:T(8,128)(2,1)} async-done(((bf16[64,1280]{1,0:T(8,128)(2,1)}), bf16[4096,1280]{1,0:T(8,128)(2,1)}) %all-gather.5.cloned.1.call-update) | async-done | bytes 10485776 | tf_op jit(solution)/shard_map/all_gather | solution.py:85
  207.2 4.0 %fusion.1 = f32[128,512]{1,0:T(8,128)} fusion(bf16[4096,1280]{1,0:T(8,128)(2,1)} %all-gather.5.cloned.1.call-done, bf16[128,4096]{1,0:T(8,128)(2,1)} %all-gather.3.cloned.1.call-done, f32[4096]{0:T(1024)S(1)} %convert_element_type.81, f32[128]{0:T(128)S(1)} %add_rsqrt_fusion), kind=kOutput, calls=%fused_computation.5 | convolution fusion | flops 538968064 | bytes 5521920 | tf_op jit(solution)/shard_map/dot_general | solution.py:91
  211.2 1.0 reshape.627
  212.2 2.8 fusion.6
  215.0 1.0 reshape.633
  216.1 1.0 fusion.29
  217.3 0.9 multiply_subtract_fusion
  218.6 1.2 gather_fusion
  219.9 0.9 broadcast_select_fusion
  220.8 8.9 %all-to-all-start = ((bf16[64,4,512]{2,1,0:T(4,128)(2,1)}), bf16[64,4,512]{2,1,0:T(4,128)(2,1)S(1)}, u32[]{:S(2)}, u32[]{:S(2)}) async-start(bf16[64,4,512]{2,1,0:T(4,128)(2,1)} %broadcast_select_fusion), calls=%async_computation | async-start | bytes 524288 | tf_op jit(solution)/shard_map/all_to_all | solution.py:127
  230.7 16.4 %all-to-all-done = bf16[64,4,512]{2,1,0:T(4,128)(2,1)S(1)} async-done(((bf16[64,4,512]{2,1,0:T(4,128)(2,1)}), bf16[64,4,512]{2,1,0:T(4,128)(2,1)S(1)}, u32[]{:S(2)}, u32[]{:S(2)}) %all-to-all-start) | async-done | bytes 262176 | tf_op jit(solution)/shard_map/all_to_all | solution.py:127
  252.5 0.7 copy.123
  253.1 4.6 %all-to-all-start.1 = ((bf16[64,4,4]{1,2,0:T(4,128)(2,1)}), bf16[64,4,4]{1,2,0:T(4,128)(2,1)S(1)}, u32[]{:S(2)}, u32[]{:S(2)}) async-start(bf16[64,4,4]{1,2,0:T(4,128)(2,1)} %copy.123), calls=%async_computation.1 | async-start | bytes 131072 | tf_op jit(solution)/shard_map/all_to_all | solution.py:144
  258.0 0.8 convert_element_type.91
  258.8 13.0 %all-to-all-done.1 = bf16[64,4,4]{1,2,0:T(4,128)(2,1)S(1)} async-done(((bf16[64,4,4]{1,2,0:T(4,128)(2,1)}), bf16[64,4,4]{1,2,0:T(4,128)(2,1)S(1)}, u32[]{:S(2)}, u32[]{:S(2)}) %all-to-all-start.1) | async-done | bytes 2080 | tf_op jit(solution)/shard_map/all_to_all | solution.py:144
  271.8 4.6 %all-to-all-start.2 = ((bf16[64,4,512]{2,1,0:T(4,128)(2,1)}), bf16[64,4,512]{2,1,0:T(4,128)(2,1)S(1)}, u32[]{:S(2)}, u32[]{:S(2)}) async-start(bf16[64,4,512]{2,1,0:T(4,128)(2,1)} %convert_element_type.91), calls=%async_computation.2 | async-start | bytes 524288 | tf_op jit(solution)/shard_map/all_to_all | solution.py:143
  277.3 0.6 gather_fusion.1
  278.0 16.1 %all-to-all-done.2 = bf16[64,4,512]{2,1,0:T(4,128)(2,1)S(1)} async-done(((bf16[64,4,512]{2,1,0:T(4,128)(2,1)}), bf16[64,4,512]{2,1,0:T(4,128)(2,1)S(1)}, u32[]{:S(2)}, u32[]{:S(2)}) %all-to-all-start.2) | async-done | bytes 262176 | tf_op jit(solution)/shard_map/all_to_all | solution.py:143
  294.2 0.7 gather_fusion.2
  295.1 4.7 %convolution_convert_fusion = bf16[128,4096]{1,0:T(8,128)(2,1)} fusion(bf16[128,512]{0,1:T(8,128)(2,1)S(1)} %bitcast.161, bf16[4096,1280]{1,0:T(8,128)(2,1)} %all-gather.5.cloned.1.call-done), kind=kOutput, calls=%fused_computation.3 | convolution fusion | flops 537395200 | bytes 5373952 | tf_op jit(solution)/shard_map/dot_general | solution.py:177
  300.0 0.7 copy.135
  300.7 35.9 %reduce-scatter.2.cloned.1.call-done = bf16[128,512]{1,0:T(8,128)(2,1)} async-done(((bf16[128,4096]{1,0:T(8,128)(2,1)}), bf16[128,512]{1,0:T(8,128)(2,1)}) %reduce-scatter.2.cloned.1.call-update) | async-done | bytes 131088 | tf_op jit(solution)/shard_map/reduce_scatter | solution.py:180
  (92 shorter events, 9.9 us)
Async XLA Ops:
  7.2 0.9 copy-start
  7.2 39.9 %all-gather.3.cloned.1.call-start = ((), (), s32[]{:S(2)}) async-start(), calls=%async_computation.4 | async-start | bytes 1179648 | tf_op jit(solution)/shard_map/all_gather | solution.py:68
  7.9 199.2 %all-gather.5.cloned.1.call-start = ((), (), s32[]{:S(2)}) async-start(), calls=%async_computation.5 | async-start | bytes 10649600 | tf_op jit(solution)/shard_map/all_gather | solution.py:85
  10.3 196.8 %copy-start.2 = (f32[4096]{0:T(1024)}, f32[4096]{0:T(1024)S(1)}, u32[]{:S(2)}) copy-start(f32[4096]{0:T(1024)S(1)} %convert_element_type.81) | copy-start | bytes 49156
  13.0 3.0 copy-start.5
  15.9 191.3 %copy-start.3 = (f32[64]{0:T(128)}, f32[64]{0:T(128)S(1)}, u32[]{:S(2)}) copy-start(f32[64]{0:T(128)S(1)} %multiply_power_fusion) | copy-start | bytes 772
  16.0 0.6 copy-start.6
  16.1 191.0 %copy-start.4 = (f32[128]{0:T(128)}, f32[128]{0:T(128)S(1)}, u32[]{:S(2)}) copy-start(f32[128]{0:T(128)S(1)} %add_convert_fusion.4) | copy-start | bytes 1540
  48.6 158.5 %copy-start.8 = (f32[128]{0:T(128)}, f32[128]{0:T(128)S(1)}, u32[]{:S(2)}) copy-start(f32[128]{0:T(128)S(1)} %add_rsqrt_fusion) | copy-start | bytes 1540
  48.6 163.6 %copy-start.1 = (bf16[128,4096]{1,0:T(8,128)(2,1)S(1)}, bf16[128,4096]{1,0:T(8,128)(2,1)}, u32[]{:S(2)}) copy-start(bf16[128,4096]{1,0:T(8,128)(2,1)} %all-gather.3.cloned.1.call-done) | copy-start | bytes 3145732
  215.0 3.5 %copy-start.7 = (s32[128]{0:T(128)S(1)}, s32[128]{0:T(128)}, u32[]{:S(2)}) copy-start(s32[128]{0:T(128)} %copy-done.6) | copy-start | bytes 1540
  220.8 26.4 %all-to-all-start = ((bf16[64,4,512]{2,1,0:T(4,128)(2,1)}), bf16[64,4,512]{2,1,0:T(4,128)(2,1)S(1)}, u32[]{:S(2)}, u32[]{:S(2)}) async-start(bf16[64,4,512]{2,1,0:T(4,128)(2,1)} %broadcast_select_fusion), calls=%async_computation | async-start | bytes 524288 | tf_op jit(solution)/shard_map/all_to_all | solution.py:127
  253.1 18.7 %all-to-all-start.1 = ((bf16[64,4,4]{1,2,0:T(4,128)(2,1)}), bf16[64,4,4]{1,2,0:T(4,128)(2,1)S(1)}, u32[]{:S(2)}, u32[]{:S(2)}) async-start(bf16[64,4,4]{1,2,0:T(4,128)(2,1)} %copy.123), calls=%async_computation.1 | async-start | bytes 131072 | tf_op jit(solution)/shard_map/all_to_all | solution.py:144
  271.8 22.3 %all-to-all-start.2 = ((bf16[64,4,512]{2,1,0:T(4,128)(2,1)}), bf16[64,4,512]{2,1,0:T(4,128)(2,1)S(1)}, u32[]{:S(2)}, u32[]{:S(2)}) async-start(bf16[64,4,512]{2,1,0:T(4,128)(2,1)} %convert_element_type.91), calls=%async_computation.2 | async-start | bytes 524288 | tf_op jit(solution)/shard_map/all_to_all | solution.py:143
  276.4 60.2 %reduce-scatter.2.cloned.1.call-start = ((), (), s32[]{:S(2)}) async-start(), calls=%async_computation.6 | async-start | bytes 1179648 | tf_op jit(solution)/shard_map/reduce_scatter | solution.py:180
Sparse Core Ops, SparseCore 0:
  10.1 36.9 all-gather.2
  50.0 157.0 all-gather.4
  299.9 36.6 reduce-scatter.1

commit v2 on v1

--- a/solution.py
+++ b/solution.py
@@ -65,7 +65,9 @@
     seq_count = lax.axis_size("seq")
     length = hidden.shape[0]
     head_size = HEAD_DIM
-    whole = lax.all_gather(hidden, "tensor", axis=1, tiled=True)
+    tiles = jnp.broadcast_to(hidden[None], (tensor_count,) + hidden.shape)
+    tiles = lax.all_to_all(tiles, "tensor", split_axis=0, concat_axis=0, tiled=True)
+    whole = jnp.moveaxis(tiles, 0, 1).reshape(length, tensor_count * hidden.shape[1])
     wide = whole.astype(jnp.float32)
     normalized_input = (
         wide
@@ -140,10 +142,13 @@
         logs.append(serve_logsum)
     out_block = jnp.stack(outs, axis=1).astype(jnp.bfloat16).reshape(seq_count, items, width_query)
     log_block = jnp.stack(logs, axis=1).reshape(seq_count, items, heads_dev)
-    prefix_out = lax.all_to_all(out_block, "seq", split_axis=0, concat_axis=0, tiled=True)
-    prefix_log = lax.all_to_all(
-        log_block.astype(jnp.bfloat16), "seq", split_axis=0, concat_axis=0, tiled=True
-    ).astype(log_block.dtype)
+    log_row = log_block.astype(jnp.bfloat16).reshape(seq_count, 1, items * heads_dev)
+    log_row = jnp.pad(log_row, ((0, 0), (0, 0), (0, width_query - items * heads_dev)))
+    back = lax.all_to_all(
+        jnp.concatenate([out_block, log_row], axis=1), "seq", split_axis=0, concat_axis=0, tiled=True
+    )
+    prefix_out = back[:, :items]
+    prefix_log = back[:, items, : items * heads_dev].astype(jnp.float32)
     owner_of_token = jnp.sum(
         jnp.where(prefix_group[:, None] == labels[None, :], prefix_owner[None, :], 0), axis=1
     )
@@ -177,9 +182,12 @@
     partial_out = lax.dot_general(
         context, wo_cols, (((1,), (1,)), ((), ())), preferred_element_type=jnp.float32
     )
-    attn_out = lax.psum_scatter(
-        partial_out.astype(jnp.bfloat16), "tensor", scatter_dimension=1, tiled=True
-    )
+    out_width = partial_out.shape[1] // tensor_count
+    pieces = partial_out.astype(jnp.bfloat16).reshape(length, tensor_count, out_width)
+    pieces = lax.all_to_all(
+        jnp.moveaxis(pieces, 1, 0), "tensor", split_axis=0, concat_axis=0, tiled=True
+    )
+    attn_out = jnp.sum(pieces.astype(jnp.float32), axis=0).astype(jnp.bfloat16)
     return (attn_out, suffix_part)
 
 

time: 345 us -> 304 us (0.88)
  waiting for transfers between devices: 270 us -> 200 us
  starting transfers between devices: 18.2 us -> 38.3 us
  local copies, waits for them, and re-layouts: 13.2 us -> 29.9 us
  matrix products: 16 us -> 12.3 us
    reduce_scatter x1 -> x0, waiting for transfers between devices: 35.9 us -> none  [shards(): lax.psum_scatter(partial_out.astype(jnp.bfloat16), 'tensor', scatter_dime...]
    all_gather x1 -> x0, waiting for transfers between devices: 29.6 us -> none  [shards(): whole = lax.all_gather(hidden, 'tensor', axis=1, tiled=True)]
    all_gather x1, waiting for transfers between devices: 159 us -> 135 us  [shards(): gathered = lax.all_gather(packed, 'seq', axis=0, tiled=True)]
    all_to_all x2 -> x3, starting transfers between devices: 9.22 us -> 29.2 us  [the longest x1 14.3 us: shards(): lax.all_to_all(jnp.moveaxis(pieces, 1, 0), 'tensor', split_axis=0, concat...]
    all_to_all x2 -> x3, waiting for transfers between devices: 29 us -> 48.5 us  [the longest x1 22.8 us: shards(): lax.all_to_all(jnp.concatenate([out_block, log_row], axis=1), 'seq', spli...]
    dot_general x0 -> x4, local copies, waits for them, and re-layouts: none -> 16.8 us  [contract(): return jnp.dot(normalized_input, piece, preferred_element_type=jnp.float32)]
  transfers between devices with their start and end apart: 6 -> 5, of which waited for: 6 -> 5; matrix products, arithmetic and copies ran while one was open for 4% -> 3% of each run, Pallas kernels for 0% -> 0%
where the time goes in v2:
time: 304 us
  waiting for transfers between devices  200 us (66%)
  starting transfers between devices  38.3 us (13%)
  local copies, waits for them, and re-layouts  29.9 us (10%)
  between operations  14.5 us (5%)
  matrix products  12.3 us (4%)
  other arithmetic  8.42 us (3%)
    all_gather x1, waiting for transfers between devices, shards(): gathered = lax.all_gather(packed, 'seq', axis=0, tiled=True)  135 us
    all_to_all x1, waiting for transfers between devices, shards(): lax.all_to_all(jnp.concatenate([out_block, log_row], axis=1), 'seq', spli...  22.8 us
    dot_general x4, local copies, waits for them, and re-layouts, contract(): return jnp.dot(normalized_input, piece, preferred_element_type=jnp.float32)  16.8 us
    all_to_all x1, waiting for transfers between devices, shards(): lax.all_to_all(outgoing, 'seq', split_axis=0, concat_axis=0, tiled=True)  16.5 us
    all_to_all x1, waiting for transfers between devices, shards(): lax.all_to_all(jnp.moveaxis(pieces, 1, 0), 'tensor', split_axis=0, concat...  14.4 us
    all_to_all x1, starting transfers between devices, shards(): lax.all_to_all(jnp.moveaxis(pieces, 1, 0), 'tensor', split_axis=0, concat...  14.3 us
    all_to_all x1, waiting for transfers between devices, shards(): lax.all_to_all(tiles, 'tensor', split_axis=0, concat_axis=0, tiled=True)  11.3 us
    all_to_all x1, starting transfers between devices, shards(): lax.all_to_all(tiles, 'tensor', split_axis=0, concat_axis=0, tiled=True)  10.3 us
  transfers between devices with their start and end apart: 5, of which 5 were waited for; matrix products, arithmetic and copies ran while one was open for 3% of the time, Pallas kernels for 0%

profile of v2, /device:TPU:1, one launch (start us, length us, event | category | flops | bytes accessed | tf_op | source)
XLA Modules:
  0.0 303.5 jit_solution(5404006053670662164)
XLA Ops:
  7.3 0.8 copy-done
  8.1 1.5 pad_maximum_fusion.1
  9.6 2.0 broadcast_in_dim.72
  11.6 10.3 %all-to-all-start = ((bf16[8,128,512]{2,1,0:T(8,128)(2,1)}), bf16[8,128,512]{2,1,0:T(8,128)(2,1)S(1)}, u32[]{:S(2)}, u32[]{:S(2)}) async-start(bf16[8,128,512]{2,1,0:T(8,128)(2,1)} %broadcast_in_dim.72), calls=%async_computation | async-start | bytes 2097152 | tf_op jit(solution)/shard_map/all_to_all | solution.py:69
  22.9 2.6 copy.131
  25.8 11.3 %all-to-all-done = bf16[8,128,512]{2,1,0:T(8,128)(2,1)S(1)} async-done(((bf16[8,128,512]{2,1,0:T(8,128)(2,1)}), bf16[8,128,512]{2,1,0:T(8,128)(2,1)S(1)}, u32[]{:S(2)}, u32[]{:S(2)}) %all-to-all-start) | async-done | bytes 1048608 | tf_op jit(solution)/shard_map/all_to_all | solution.py:69
  37.1 0.7 copy.126
  37.7 0.6 fusion.1
  38.3 0.7 fusion.3
  39.0 135.0 %all-gather.2.cloned.1.call-done = bf16[4096,1280]{1,0:T(8,128)(2,1)} async-done(((bf16[64,1280]{1,0:T(8,128)(2,1)}), bf16[4096,1280]{1,0:T(8,128)(2,1)}) %all-gather.2.cloned.1.call-update) | async-done | bytes 10485776 | tf_op jit(solution)/shard_map/all_gather | solution.py:87
  174.1 4.5 %slice_bitcast_fusion = bf16[512,4096]{0,1:T(8,128)(2,1)} fusion(bf16[4096,1280]{1,0:T(8,128)(2,1)} %all-gather.2.cloned.1.call-done), kind=kLoop, calls=%fused_computation.5 | loop fusion | bytes 8388608 | tf_op jit(solution)/shard_map/dot_general | solution.py:93
  178.5 6.4 %copy.127 = bf16[512,4096]{1,0:T(8,128)(2,1)} copy(bf16[512,4096]{0,1:T(8,128)(2,1)} %slice_bitcast_fusion) | data formatting | bytes 8388608 | tf_op jit(solution)/shard_map/dot_general | solution.py:93
  184.9 3.1 %slice_bitcast_fusion.1 = bf16[256,4096]{0,1:T(8,128)(2,1)} fusion(bf16[4096,1280]{1,0:T(8,128)(2,1)} %all-gather.2.cloned.1.call-done), kind=kLoop, calls=%fused_computation.11 | loop fusion | bytes 4194304 | tf_op jit(solution)/shard_map/dot_general | solution.py:93
  188.0 2.9 copy.140
  190.9 3.4 %fusion.75 = f32[128,4,128]{0,2,1:T(8,128)S(1)} fusion(bf16[128,4096,1]{0,1,2:T(8,128)(2,1)S(1)} %bitcast.169, bf16[4,128,4096]{2,1,0:T(8,128)(2,1)} %bitcast.168), kind=kOutput, calls=%fused_computation.174 | convolution fusion | flops 536870912 | bytes 5505024 | tf_op jit(solution)/shard_map/dot_general | solution.py:93
  194.3 0.7 convolution_bitcast_fusion
  195.5 1.2 gather_fusion
  196.7 0.9 broadcast_select_fusion
  197.6 9.1 %all-to-all-start.1 = ((bf16[64,4,512]{2,1,0:T(4,128)(2,1)}), bf16[64,4,512]{2,1,0:T(4,128)(2,1)S(1)}, u32[]{:S(2)}, u32[]{:S(2)}) async-start(bf16[64,4,512]{2,1,0:T(4,128)(2,1)} %broadcast_select_fusion), calls=%async_computation.1 | async-start | bytes 524288 | tf_op jit(solution)/shard_map/all_to_all | solution.py:129
  207.5 16.5 %all-to-all-done.1 = bf16[64,4,512]{2,1,0:T(4,128)(2,1)S(1)} async-done(((bf16[64,4,512]{2,1,0:T(4,128)(2,1)}), bf16[64,4,512]{2,1,0:T(4,128)(2,1)S(1)}, u32[]{:S(2)}, u32[]{:S(2)}) %all-to-all-start.1) | async-done | bytes 262176 | tf_op jit(solution)/shard_map/all_to_all | solution.py:129
  224.1 0.4 fusion.66
  230.2 1.0 fusion.17
  231.2 4.6 %all-to-all-start.2 = ((bf16[64,5,512]{2,1,0:T(8,128)(2,1)}), bf16[64,5,512]{2,1,0:T(8,128)(2,1)S(1)}, u32[]{:S(2)}, u32[]{:S(2)}) async-start(bf16[64,5,512]{2,1,0:T(8,128)(2,1)} %fusion.17), calls=%async_computation.2 | async-start | bytes 1048576 | tf_op jit(solution)/shard_map/all_to_all | solution.py:147
  236.8 22.8 %all-to-all-done.2 = bf16[64,5,512]{2,1,0:T(8,128)(2,1)S(1)} async-done(((bf16[64,5,512]{2,1,0:T(8,128)(2,1)}), bf16[64,5,512]{2,1,0:T(8,128)(2,1)S(1)}, u32[]{:S(2)}, u32[]{:S(2)}) %all-to-all-start.2) | async-done | bytes 327712 | tf_op jit(solution)/shard_map/all_to_all | solution.py:147
  259.8 0.7 gather_fusion.1
  260.7 0.7 gather_fusion.2
  261.7 3.7 %convolution_convert_fusion = bf16[128,4096]{1,0:T(8,128)(2,1)S(1)} fusion(bf16[128,512]{0,1:T(8,128)(2,1)S(1)} %bitcast.183, bf16[4096,1280]{1,0:T(8,128)(2,1)} %all-gather.2.cloned.1.call-done), kind=kOutput, calls=%fused_computation.3 | convolution fusion | flops 537395200 | bytes 5373952 | tf_op jit(solution)/shard_map/dot_general | solution.py:182
  265.4 1.1 copy.182
  266.5 14.3 %all-to-all-start.3 = ((bf16[8,128,512]{2,1,0:T(8,128)(2,1)}), bf16[8,128,512]{2,1,0:T(8,128)(2,1)S(1)}, u32[]{:S(2)}, u32[]{:S(2)}) async-start(bf16[8,128,512]{2,1,0:T(8,128)(2,1)} %bitcast.167), calls=%async_computation.3 | async-start | bytes 2097152 | tf_op jit(solution)/shard_map/all_to_all | solution.py:187
  280.8 0.7 copy.155
  281.5 14.4 %all-to-all-done.3 = bf16[8,128,512]{2,1,0:T(8,128)(2,1)S(1)} async-done(((bf16[8,128,512]{2,1,0:T(8,128)(2,1)}), bf16[8,128,512]{2,1,0:T(8,128)(2,1)S(1)}, u32[]{:S(2)}, u32[]{:S(2)}) %all-to-all-start.3) | async-done | bytes 1048608 | tf_op jit(solution)/shard_map/all_to_all | solution.py:187
  295.8 0.8 reduce_sum.155
  (94 shorter events, 9.8 us)
Async XLA Ops:
  7.2 0.9 copy-start
  7.2 14.8 %copy-start.4 = (s32[1,64]{1,0:T(1,128)S(1)}, s32[1,64]{1,0:T(1,128)}, u32[]{:S(2)}) copy-start(s32[1,64]{1,0:T(1,128)} %param.15) | copy-start | bytes 772
  7.2 15.1 %copy-start.5 = (s32[64]{0:T(128)S(1)}, s32[64]{0:T(128)}, u32[]{:S(2)}) copy-start(s32[64]{0:T(128)} %param.14) | copy-start | bytes 772
  7.2 15.5 %copy-start.3 = (bf16[4096]{0:T(1024)(128)(2,1)S(1)}, bf16[4096]{0:T(1024)(128)(2,1)}, u32[]{:S(2)}) copy-start(bf16[4096]{0:T(1024)(128)(2,1)} %param.9) | copy-start | bytes 24580
  7.2 15.6 %copy-start.2 = (bf16[1,1024,1024]{2,1,0:T(8,128)(2,1)S(1)}, bf16[1,1024,1024]{2,1,0:T(8,128)(2,1)}, u32[]{:S(2)}) copy-start(bf16[1,1024,1024]{2,1,0:T(8,128)(2,1)} %param.13) | copy-start | bytes 6291460
  7.2 166.8 %all-gather.2.cloned.1.call-start = ((), (), s32[]{:S(2)}) async-start(), calls=%async_computation.4 | async-start | bytes 10649600 | tf_op jit(solution)/shard_map/all_gather | solution.py:87
  11.6 25.5 %all-to-all-start = ((bf16[8,128,512]{2,1,0:T(8,128)(2,1)}), bf16[8,128,512]{2,1,0:T(8,128)(2,1)S(1)}, u32[]{:S(2)}, u32[]{:S(2)}) async-start(bf16[8,128,512]{2,1,0:T(8,128)(2,1)} %broadcast_in_dim.72), calls=%async_computation | async-start | bytes 2097152 | tf_op jit(solution)/shard_map/all_to_all | solution.py:69
  196.6 27.9 %copy-start.1 = (bf16[1,1024,1024]{1,2,0:T(8,128)(2,1)S(1)}, bf16[1,1024,1024]{1,2,0:T(8,128)(2,1)}, u32[]{:S(2)}) copy-start(bf16[1,1024,1024]{1,2,0:T(8,128)(2,1)} %copy.131) | copy-start | bytes 6291460
  197.6 26.4 %all-to-all-start.1 = ((bf16[64,4,512]{2,1,0:T(4,128)(2,1)}), bf16[64,4,512]{2,1,0:T(4,128)(2,1)S(1)}, u32[]{:S(2)}, u32[]{:S(2)}) async-start(bf16[64,4,512]{2,1,0:T(4,128)(2,1)} %broadcast_select_fusion), calls=%async_computation.1 | async-start | bytes 524288 | tf_op jit(solution)/shard_map/all_to_all | solution.py:129
  231.2 28.4 %all-to-all-start.2 = ((bf16[64,5,512]{2,1,0:T(8,128)(2,1)}), bf16[64,5,512]{2,1,0:T(8,128)(2,1)S(1)}, u32[]{:S(2)}, u32[]{:S(2)}) async-start(bf16[64,5,512]{2,1,0:T(8,128)(2,1)} %fusion.17), calls=%async_computation.2 | async-start | bytes 1048576 | tf_op jit(solution)/shard_map/all_to_all | solution.py:147
  266.5 29.4 %all-to-all-start.3 = ((bf16[8,128,512]{2,1,0:T(8,128)(2,1)}), bf16[8,128,512]{2,1,0:T(8,128)(2,1)S(1)}, u32[]{:S(2)}, u32[]{:S(2)}) async-start(bf16[8,128,512]{2,1,0:T(8,128)(2,1)} %bitcast.167), calls=%async_computation.3 | async-start | bytes 2097152 | tf_op jit(solution)/shard_map/all_to_all | solution.py:187
Sparse Core Ops, SparseCore 0:
  11.0 163.0 all-gather.1

commit v3 on v2

--- a/solution.py
+++ b/solution.py
@@ -48,6 +48,39 @@
     weights = (expo / total).astype(jnp.bfloat16)
     result = jnp.dot(weights, values, preferred_element_type=jnp.float32)
     return (result, top[:, 0] + jnp.log(total[:, 0]))
+
+
+Y_CHIPS = 4
+
+
+def ring(value, count, step):
+    rel = [None] * count
+    rel[0] = value
+    ahead = value
+    behind = value
+    for k in range(1, count // 2 + 1):
+        behind = step(behind, 1)
+        rel[(-k) % count] = behind
+        if k < count - k:
+            ahead = step(ahead, -1)
+            rel[k] = ahead
+    return rel
+
+
+def ring_gather(block, axis_name, seq_count):
+    z_count = seq_count // Y_CHIPS
+    here = lax.axis_index(axis_name)
+
+    def shift(value, dz, dy):
+        pairs = []
+        for i in range(seq_count):
+            z, y = divmod(i, Y_CHIPS)
+            pairs.append((i, ((z + dz) % z_count) * Y_CHIPS + (y + dy) % Y_CHIPS))
+        return lax.ppermute(value, axis_name, pairs)
+
+    along_y = jnp.stack(ring(block, Y_CHIPS, lambda v, d: shift(v, 0, d)), axis=1)
+    along_z = jnp.stack(ring(along_y, z_count, lambda v, d: shift(v, d, 0)), axis=1)
+    return along_z.reshape(block.shape[0], -1), here // Y_CHIPS, here % Y_CHIPS
 
 
 def shards(
@@ -83,17 +116,22 @@
     kv_start = tensor_index * heads_dev // group_full
     kv_width = kv_local * 2 * head_size
     kv_piece = lax.dynamic_slice_in_dim(key_value_weight, kv_start * 2 * head_size, kv_width, 1)
-    packed = jnp.concatenate([w_query, kv_piece, w_out.T], axis=1)
-    gathered = lax.all_gather(packed, "seq", axis=0, tiled=True)
-    wq_full = gathered[:, :width_query]
-    kv_full = gathered[:, width_query : width_query + kv_width]
-    wo_cols = gathered[:, width_query + kv_width :]
-
-    def contract(piece):
-        return jnp.dot(normalized_input, piece, preferred_element_type=jnp.float32)
-
-    query_vectors = contract(wq_full)
-    key_value_pair = contract(kv_full)
+    packed = jnp.concatenate([w_query.T, kv_piece.T, w_out], axis=0)
+    gathered, z_at, y_at = ring_gather(packed, "seq", seq_count)
+    wq_rows = gathered[:width_query]
+    kv_rows = gathered[width_query : width_query + kv_width]
+    wo_rel = gathered[width_query + kv_width :]
+    z_count = seq_count // Y_CHIPS
+    rel_input = normalized_input.reshape(length, z_count, Y_CHIPS, -1)
+    rel_input = jnp.roll(jnp.roll(rel_input, -z_at, axis=1), -y_at, axis=2).reshape(length, -1)
+
+    def contract(rows):
+        return lax.dot_general(
+            rel_input, rows, (((1,), (1,)), ((), ())), preferred_element_type=jnp.float32
+        )
+
+    query_vectors = contract(wq_rows)
+    key_value_pair = contract(kv_rows)
     counts = token_counts[0]
     num_groups = counts.shape[0]
     starts, prefix_group, offset = layout(counts, length)
@@ -179,9 +217,9 @@
         (left * prefix_rows.astype(jnp.float32) + right * suffix_attn) / (left + right)
     ).astype(jnp.bfloat16)
     context = context.reshape(length, width_query)
-    partial_out = lax.dot_general(
-        context, wo_cols, (((1,), (1,)), ((), ())), preferred_element_type=jnp.float32
-    )
+    partial_out = jnp.dot(context, wo_rel, preferred_element_type=jnp.float32)
+    partial_out = partial_out.reshape(length, z_count, Y_CHIPS, -1)
+    partial_out = jnp.roll(jnp.roll(partial_out, z_at, axis=1), y_at, axis=2).reshape(length, -1)
     out_width = partial_out.shape[1] // tensor_count
     pieces = partial_out.astype(jnp.bfloat16).reshape(length, tensor_count, out_width)
     pieces = lax.all_to_all(

time: 304 us -> 290 us (0.954)
  waiting for transfers between devices: 200 us -> 125 us
  starting transfers between devices: 38.3 us -> 97.5 us
  between operations: 14.5 us -> 1.64 us
  other arithmetic: 8.42 us -> 16 us
  local copies, waits for them, and re-layouts: 29.9 us -> 35.4 us
    all_gather x1 -> x0, waiting for transfers between devices: 135 us -> none  [shards(): gathered = lax.all_gather(packed, 'seq', axis=0, tiled=True)]
    ppermute x0 -> x18, waiting for transfers between devices: none -> 73 us  [shift(): return lax.ppermute(value, axis_name, pairs)]
    ppermute x0 -> x18, starting transfers between devices: none -> 59.4 us  [shift(): return lax.ppermute(value, axis_name, pairs)]
    all_to_all x1, waiting for transfers between devices: 11.3 us -> 0.01 us  [shards(): lax.all_to_all(tiles, 'tensor', split_axis=0, concat_axis=0, tiled=True)]
    unnamed x14 -> x46, local copies, waits for them, and re-layouts: 4.16 us -> 15.4 us
    dot_general x4 -> x1, local copies, waits for them, and re-layouts: 16.8 us -> 6.92 us  [contract(): lax.dot_general(rel_input, rows, (((1,), (1,)), ((), ())), preferred_elem...]
    another operation x7 -> x8, other arithmetic: 0.29 us -> 3.69 us  [the longest x2 3.46 us: ring_gather(): jnp.stack(ring(block, Y_CHIPS, lambda v, d: shift(v, 0, d)), axis=1)]
    another operation x0 -> x2, local copies, waits for them, and re-layouts: none -> 3.2 us
  transfers between devices with their start and end apart: 5 -> 22, of which waited for: 5 -> 13; matrix products, arithmetic and copies ran while one was open for 3% -> 7% of each run, Pallas kernels for 0% -> 0%
where the time goes in v3:
time: 290 us; the launch traced here: 289 us
  waiting for transfers between devices  125 us (43%)
  starting transfers between devices  97.5 us (34%)
  local copies, waits for them, and re-layouts  35.4 us (12%)
  other arithmetic  16 us (6%)
  matrix products  12.9 us (4%)
    ppermute x18, waiting for transfers between devices, shift(): return lax.ppermute(value, axis_name, pairs)  73 us
    ppermute x18, starting transfers between devices, shift(): return lax.ppermute(value, axis_name, pairs)  59.4 us
    all_to_all x1, waiting for transfers between devices, shards(): lax.all_to_all(jnp.concatenate([out_block, log_row], axis=1), 'seq', spli...  21.3 us
    all_to_all x1, waiting for transfers between devices, shards(): lax.all_to_all(outgoing, 'seq', split_axis=0, concat_axis=0, tiled=True)  16.5 us
    all_to_all x1, starting transfers between devices, shards(): lax.all_to_all(jnp.moveaxis(pieces, 1, 0), 'tensor', split_axis=0, concat...  15.6 us
    unnamed x46, local copies, waits for them, and re-layouts  15.4 us
    all_to_all x1, waiting for transfers between devices, shards(): lax.all_to_all(jnp.moveaxis(pieces, 1, 0), 'tensor', split_axis=0, concat...  14.4 us
    all_to_all x1, starting transfers between devices, shards(): lax.all_to_all(tiles, 'tensor', split_axis=0, concat_axis=0, tiled=True)  10 us
  transfers between devices with their start and end apart: 22, of which 13 were waited for; matrix products, arithmetic and copies ran while one was open for 7% of the time, Pallas kernels for 0%

profile of v3, /device:TPU:1, one launch (start us, length us, event | category | flops | bytes accessed | tf_op | source)
XLA Modules:
  0.0 288.6 jit_solution(3394955140373566381)
XLA Ops:
  3.1 4.0 %collective-permute-start.1 = (bf16[1280,64]{0,1:T(8,128)(2,1)}, bf16[1280,64]{0,1:T(8,128)(2,1)}, u32[]{:S(2)}, u32[]{:S(2)}) collective-permute-start(bf16[1280,64]{0,1:T(8,128)(2,1)} %get-tuple-element.22), channel_id=1, source_target_pairs={{0,8},{8,16},{16,24},{24,0},{32,40},{40,48},{48,56},{56,32},{64,72... | collective-permute-start | bytes 491528 | tf_op jit(solution)/shard_map/ppermute | solution.py:79
  7.1 3.4 %collective-permute-start = (bf16[1280,64]{0,1:T(8,128)(2,1)}, bf16[1280,64]{0,1:T(8,128)(2,1)}, u32[]{:S(2)}, u32[]{:S(2)}) collective-permute-start(bf16[1280,64]{0,1:T(8,128)(2,1)} %get-tuple-element.22), channel_id=1, source_target_pairs={{0,24},{8,0},{16,8},{24,16},{32,56},{40,32},{48,40},{56,48},{64,88... | collective-permute-start | bytes 491528 | tf_op jit(solution)/shard_map/ppermute | solution.py:79
  12.6 10.0 %all-to-all-start = ((bf16[8,128,512]{1,2,0:T(8,128)(2,1)}), bf16[8,128,512]{1,2,0:T(8,128)(2,1)S(1)}, u32[]{:S(2)}, u32[]{:S(2)}) async-start(bf16[8,128,512]{1,2,0:T(8,128)(2,1)} %broadcast_in_dim.72), calls=%async_computation | async-start | bytes 2097152 | tf_op jit(solution)/shard_map/all_to_all | solution.py:102
  25.6 7.1 %collective-permute-done.2 = bf16[1280,64]{0,1:T(8,128)(2,1)S(1)} collective-permute-done((bf16[1280,64]{0,1:T(8,128)(2,1)}, bf16[1280,64]{0,1:T(8,128)(2,1)S(1)}, u32[]{:S(2)}, u32[]{:S(2)}) %collective-permute-start.2) | collective-permute-done | bytes 163872 | tf_op jit(solution)/shard_map/ppermute | solution.py:79
  37.3 6.6 %collective-permute-start.3 = (bf16[1280,4,64]{0,2,1:T(8,128)(2,1)}, bf16[1280,4,64]{0,2,1:T(8,128)(2,1)}, u32[]{:S(2)}, u32[]{:S(2)}) collective-permute-start(bf16[1280,4,64]{0,2,1:T(8,128)(2,1)} %pad_maximum_fusion), channel_id=1, source_target_pairs={{0,480},{8,488},{16,496},{24,504},{32,0},{40,8},{48,16},{56,24},{6... | collective-permute-start | bytes 1966088 | tf_op jit(solution)/shard_map/ppermute | solution.py:79
  44.4 12.1 %collective-permute-done.10 = bf16[1280,4,64]{0,2,1:T(8,128)(2,1)} collective-permute-done((bf16[1280,4,64]{0,2,1:T(8,128)(2,1)}, bf16[1280,4,64]{0,2,1:T(8,128)(2,1)}, u32[]{:S(2)}, u32[]{:S(2)}) %collective-permute-start.10) | collective-permute-done | bytes 655392 | tf_op jit(solution)/shard_map/ppermute | solution.py:79
  58.5 4.6 %collective-permute-start.4 = (bf16[1280,4,64]{0,2,1:T(8,128)(2,1)}, bf16[1280,4,64]{0,2,1:T(8,128)(2,1)}, u32[]{:S(2)}, u32[]{:S(2)}) collective-permute-start(bf16[1280,4,64]{0,2,1:T(8,128)(2,1)} %collective-permute-done.3), channel_id=1, source_target_pairs={{0,480},{8,488},{16,496},{24,504},{32,0},{40,8},{48,16},{56,24},{6... | collective-permute-start | bytes 1966088 | tf_op jit(solution)/shard_map/ppermute | solution.py:79
  63.7 11.1 %collective-permute-done.11 = bf16[1280,4,64]{0,2,1:T(8,128)(2,1)} collective-permute-done((bf16[1280,4,64]{0,2,1:T(8,128)(2,1)}, bf16[1280,4,64]{0,2,1:T(8,128)(2,1)}, u32[]{:S(2)}, u32[]{:S(2)}) %collective-permute-start.11) | collective-permute-done | bytes 655392 | tf_op jit(solution)/shard_map/ppermute | solution.py:79
  77.3 4.6 %collective-permute-start.5 = (bf16[1280,4,64]{0,2,1:T(8,128)(2,1)}, bf16[1280,4,64]{0,2,1:T(8,128)(2,1)}, u32[]{:S(2)}, u32[]{:S(2)}) collective-permute-start(bf16[1280,4,64]{0,2,1:T(8,128)(2,1)} %collective-permute-done.4), channel_id=1, source_target_pairs={{0,480},{8,488},{16,496},{24,504},{32,0},{40,8},{48,16},{56,24},{6... | collective-permute-start | bytes 1966088 | tf_op jit(solution)/shard_map/ppermute | solution.py:79
  82.0 2.6 copy.121
  87.4 4.7 %collective-permute-done.12 = bf16[1280,4,64]{0,2,1:T(8,128)(2,1)} collective-permute-done((bf16[1280,4,64]{0,2,1:T(8,128)(2,1)}, bf16[1280,4,64]{0,2,1:T(8,128)(2,1)}, u32[]{:S(2)}, u32[]{:S(2)}) %collective-permute-start.12) | collective-permute-done | bytes 655392 | tf_op jit(solution)/shard_map/ppermute | solution.py:79
  94.7 4.6 %collective-permute-start.6 = (bf16[1280,4,64]{0,2,1:T(8,128)(2,1)}, bf16[1280,4,64]{0,2,1:T(8,128)(2,1)S(1)}, u32[]{:S(2)}, u32[]{:S(2)}) collective-permute-start(bf16[1280,4,64]{0,2,1:T(8,128)(2,1)} %collective-permute-done.5), channel_id=1, source_target_pairs={{0,480},{8,488},{16,496},{24,504},{32,0},{40,8},{48,16},{56,24},{6... | collective-permute-start | bytes 1966088 | tf_op jit(solution)/shard_map/ppermute | solution.py:79
  100.1 8.4 %collective-permute-done.13 = bf16[1280,4,64]{0,2,1:T(8,128)(2,1)S(1)} collective-permute-done((bf16[1280,4,64]{0,2,1:T(8,128)(2,1)}, bf16[1280,4,64]{0,2,1:T(8,128)(2,1)S(1)}, u32[]{:S(2)}, u32[]{:S(2)}) %collective-permute-start.13) | collective-permute-done | bytes 655392 | tf_op jit(solution)/shard_map/ppermute | solution.py:79
  111.2 4.6 %collective-permute-start.7 = (bf16[1280,4,64]{0,2,1:T(8,128)(2,1)S(1)}, bf16[1280,4,64]{0,2,1:T(8,128)(2,1)S(1)}, u32[]{:S(2)}, u32[]{:S(2)}) collective-permute-start(bf16[1280,4,64]{0,2,1:T(8,128)(2,1)S(1)} %collective-permute-done.6), channel_id=1, source_target_pairs={{0,480},{8,488},{16,496},{24,504},{32,0},{40,8},{48,16},{56,24},{6... | collective-permute-start | bytes 1966088 | tf_op jit(solution)/shard_map/ppermute | solution.py:79
  117.0 6.7 %collective-permute-done.14 = bf16[1280,4,64]{0,2,1:T(8,128)(2,1)S(1)} collective-permute-done((bf16[1280,4,64]{0,2,1:T(8,128)(2,1)S(1)}, bf16[1280,4,64]{0,2,1:T(8,128)(2,1)S(1)}, u32[]{:S(2)}, u32[]{:S(2)}) %collective-permute-start.14) | collective-permute-done | bytes 655392 | tf_op jit(solution)/shard_map/ppermute | solution.py:79
  126.8 4.6 %collective-permute-start.8 = (bf16[1280,4,64]{0,2,1:T(8,128)(2,1)S(1)}, bf16[1280,4,64]{0,2,1:T(8,128)(2,1)S(1)}, u32[]{:S(2)}, u32[]{:S(2)}) collective-permute-start(bf16[1280,4,64]{0,2,1:T(8,128)(2,1)S(1)} %collective-permute-done.7), channel_id=1, source_target_pairs={{0,480},{8,488},{16,496},{24,504},{32,0},{40,8},{48,16},{56,24},{6... | collective-permute-start | bytes 1966088 | tf_op jit(solution)/shard_map/ppermute | solution.py:79
  132.5 5.5 %collective-permute-done.15 = bf16[1280,4,64]{0,2,1:T(8,128)(2,1)S(1)} collective-permute-done((bf16[1280,4,64]{0,2,1:T(8,128)(2,1)S(1)}, bf16[1280,4,64]{0,2,1:T(8,128)(2,1)S(1)}, u32[]{:S(2)}, u32[]{:S(2)}) %collective-permute-start.15) | collective-permute-done | bytes 655392 | tf_op jit(solution)/shard_map/ppermute | solution.py:79
  140.0 5.3 %collective-permute-start.9 = (bf16[1280,4,64]{0,2,1:T(8,128)(2,1)S(1)}, bf16[1280,4,64]{0,2,1:T(8,128)(2,1)S(1)}, u32[]{:S(2)}, u32[]{:S(2)}) collective-permute-start(bf16[1280,4,64]{0,2,1:T(8,128)(2,1)S(1)} %collective-permute-done.8), channel_id=1, source_target_pairs={{0,480},{8,488},{16,496},{24,504},{32,0},{40,8},{48,16},{56,24},{6... | collective-permute-start | bytes 1966088 | tf_op jit(solution)/shard_map/ppermute | solution.py:79
  145.4 5.9 %collective-permute-done.16 = bf16[1280,4,64]{0,2,1:T(8,128)(2,1)S(1)} collective-permute-done((bf16[1280,4,64]{0,2,1:T(8,128)(2,1)S(1)}, bf16[1280,4,64]{0,2,1:T(8,128)(2,1)S(1)}, u32[]{:S(2)}, u32[]{:S(2)}) %collective-permute-start.16) | collective-permute-done | bytes 655392 | tf_op jit(solution)/shard_map/ppermute | solution.py:79
  153.4 11.2 %collective-permute-done.17 = bf16[1280,4,64]{0,2,1:T(8,128)(2,1)S(1)} collective-permute-done((bf16[1280,4,64]{0,2,1:T(8,128)(2,1)S(1)}, bf16[1280,4,64]{0,2,1:T(8,128)(2,1)S(1)}, u32[]{:S(2)}, u32[]{:S(2)}) %collective-permute-start.17) | collective-permute-done | bytes 655392 | tf_op jit(solution)/shard_map/ppermute | solution.py:79
  168.2 2.6 slice.104
  170.8 2.6 copy-done.3
  173.7 6.9 %dot_general.65 = bf16[4,128,4096]{1,0,2:T(4,128)(2,1)} reshape(bf16[512,16,4,64]{0,3,2,1:T(8,128)(2,1)} %slice.104) | data formatting | bytes 8388608 | tf_op jit(solution)/shard_map/dot_general | solution.py:129
  180.6 2.1 reshape.689
  182.7 4.1 %fusion.1 = f32[128,4,128]{0,2,1:T(8,128)S(1)} fusion(bf16[128,4096,1]{0,1,2:T(8,128)(2,1)S(1)} %bitcast.222, bf16[4,128,4096]{1,0,2:T(4,128)(2,1)} %dot_general.65), kind=kOutput, calls=%fused_computation.9 | convolution fusion | flops 536870912 | bytes 5505024 | tf_op jit(solution)/shard_map/dot_general | solution.py:129
  190.3 7.8 %all-to-all-start.1 = ((bf16[64,4,512]{2,1,0:T(4,128)(2,1)}), bf16[64,4,512]{2,1,0:T(4,128)(2,1)S(1)}, u32[]{:S(2)}, u32[]{:S(2)}) async-start(bf16[64,4,512]{2,1,0:T(4,128)(2,1)} %broadcast_select_fusion), calls=%async_computation.1 | async-start | bytes 524288 | tf_op jit(solution)/shard_map/all_to_all | solution.py:167
  199.0 16.5 %all-to-all-done.1 = bf16[64,4,512]{2,1,0:T(4,128)(2,1)S(1)} async-done(((bf16[64,4,512]{2,1,0:T(4,128)(2,1)}), bf16[64,4,512]{2,1,0:T(4,128)(2,1)S(1)}, u32[]{:S(2)}, u32[]{:S(2)}) %all-to-all-start.1) | async-done | bytes 262176 | tf_op jit(solution)/shard_map/all_to_all | solution.py:167
  222.7 4.6 %all-to-all-start.2 = ((bf16[64,5,512]{2,1,0:T(8,128)(2,1)}), bf16[64,5,512]{2,1,0:T(8,128)(2,1)S(1)}, u32[]{:S(2)}, u32[]{:S(2)}) async-start(bf16[64,5,512]{2,1,0:T(8,128)(2,1)} %fusion.26), calls=%async_computation.2 | async-start | bytes 1048576 | tf_op jit(solution)/shard_map/all_to_all | solution.py:185
  228.3 21.3 %all-to-all-done.2 = bf16[64,5,512]{2,1,0:T(8,128)(2,1)S(1)} async-done(((bf16[64,5,512]{2,1,0:T(8,128)(2,1)}), bf16[64,5,512]{2,1,0:T(8,128)(2,1)S(1)}, u32[]{:S(2)}, u32[]{:S(2)}) %all-to-all-start.2) | async-done | bytes 327712 | tf_op jit(solution)/shard_map/all_to_all | solution.py:185
  251.7 3.4 %fusion = bf16[128,16,4,64]{0,3,2,1:T(8,128)(2,1)S(1)} fusion(bf16[128,512,1,1]{0,1,3,2:T(8,128)(2,1)S(1)} %bitcast.228, bf16[1280,16,4,64]{0,3,2,1:T(8,128)(2,1)} %copy-done.3), kind=kOutput, calls=%fused_computation.4 | convolution fusion | flops 536870912 | bytes 5373952 | tf_op jit(solution)/shard_map/dot_general | solution.py:220
  256.9 15.6 %all-to-all-start.3 = ((bf16[8,128,512]{1,2,0:T(8,128)(2,1)}), bf16[8,128,512]{1,2,0:T(8,128)(2,1)S(1)}, u32[]{:S(2)}, u32[]{:S(2)}) async-start(bf16[8,128,512]{1,2,0:T(8,128)(2,1)} %bitcast.65), calls=%async_computation.3 | async-start | bytes 2097152 | tf_op jit(solution)/shard_map/all_to_all | solution.py:225
  273.3 14.4 %all-to-all-done.3 = bf16[8,128,512]{1,2,0:T(8,128)(2,1)S(1)} async-done(((bf16[8,128,512]{1,2,0:T(8,128)(2,1)}), bf16[8,128,512]{1,2,0:T(8,128)(2,1)S(1)}, u32[]{:S(2)}, u32[]{:S(2)}) %all-to-all-start.3) | async-done | bytes 1048608 | tf_op jit(solution)/shard_map/all_to_all | solution.py:225
  (165 shorter events, 57.3 us)
Async XLA Ops:
  0.6 24.9 %copy-start.10 = (s32[1,64]{1,0:T(1,128)S(1)}, s32[1,64]{1,0:T(1,128)}, u32[]{:S(2)}) copy-start(s32[1,64]{1,0:T(1,128)} %param.15) | copy-start | bytes 772
  0.7 36.5 %copy-start.11 = (s32[64]{0:T(128)S(1)}, s32[64]{0:T(128)}, u32[]{:S(2)}) copy-start(s32[64]{0:T(128)} %param.14) | copy-start | bytes 772
  0.7 81.2 %copy-start.7 = (bf16[4096]{0:T(1024)(128)(2,1)S(1)}, bf16[4096]{0:T(1024)(128)(2,1)}, u32[]{:S(2)}) copy-start(bf16[4096]{0:T(1024)(128)(2,1)} %param.9) | copy-start | bytes 24580
  0.7 81.3 %copy-start.4 = (bf16[1,1024,1024]{2,1,0:T(8,128)(2,1)S(1)}, bf16[1,1024,1024]{2,1,0:T(8,128)(2,1)}, u32[]{:S(2)}) copy-start(bf16[1,1024,1024]{2,1,0:T(8,128)(2,1)} %param.13) | copy-start | bytes 6291460
  3.1 20.5 %collective-permute-start.1 = (bf16[1280,64]{0,1:T(8,128)(2,1)}, bf16[1280,64]{0,1:T(8,128)(2,1)}, u32[]{:S(2)}, u32[]{:S(2)}) collective-permute-start(bf16[1280,64]{0,1:T(8,128)(2,1)} %get-tuple-element.22), channel_id=1, source_target_pairs={{0,8},{8,16},{16,24},{24,0},{32,40},{40,48},{48,56},{56,32},{64,72... | collective-permute-start | bytes 491528 | tf_op jit(solution)/shard_map/ppermute | solution.py:79
  7.1 18.4 %collective-permute-start = (bf16[1280,64]{0,1:T(8,128)(2,1)}, bf16[1280,64]{0,1:T(8,128)(2,1)}, u32[]{:S(2)}, u32[]{:S(2)}) collective-permute-start(bf16[1280,64]{0,1:T(8,128)(2,1)} %get-tuple-element.22), channel_id=1, source_target_pairs={{0,24},{8,0},{16,8},{24,16},{32,56},{40,32},{48,40},{56,48},{64,88... | collective-permute-start | bytes 491528 | tf_op jit(solution)/shard_map/ppermute | solution.py:79
  12.6 81.5 %all-to-all-start = ((bf16[8,128,512]{1,2,0:T(8,128)(2,1)}), bf16[8,128,512]{1,2,0:T(8,128)(2,1)S(1)}, u32[]{:S(2)}, u32[]{:S(2)}) async-start(bf16[8,128,512]{1,2,0:T(8,128)(2,1)} %broadcast_in_dim.72), calls=%async_computation | async-start | bytes 2097152 | tf_op jit(solution)/shard_map/all_to_all | solution.py:102
  23.6 9.1 %collective-permute-start.2 = (bf16[1280,64]{0,1:T(8,128)(2,1)}, bf16[1280,64]{0,1:T(8,128)(2,1)S(1)}, u32[]{:S(2)}, u32[]{:S(2)}) collective-permute-start(bf16[1280,64]{0,1:T(8,128)(2,1)} %collective-permute-done.1), channel_id=1, source_target_pairs={{0,8},{8,16},{16,24},{24,0},{32,40},{40,48},{48,56},{56,32},{64,72... | collective-permute-start | bytes 491528 | tf_op jit(solution)/shard_map/ppermute | solution.py:79
  35.3 21.3 %collective-permute-start.10 = (bf16[1280,4,64]{0,2,1:T(8,128)(2,1)}, bf16[1280,4,64]{0,2,1:T(8,128)(2,1)}, u32[]{:S(2)}, u32[]{:S(2)}) collective-permute-start(bf16[1280,4,64]{0,2,1:T(8,128)(2,1)} %pad_maximum_fusion), channel_id=1, source_target_pairs={{0,32},{8,40},{16,48},{24,56},{32,64},{40,72},{48,80},{56,88},{64,... | collective-permute-start | bytes 1966088 | tf_op jit(solution)/shard_map/ppermute | solution.py:79
  37.3 21.2 %collective-permute-start.3 = (bf16[1280,4,64]{0,2,1:T(8,128)(2,1)}, bf16[1280,4,64]{0,2,1:T(8,128)(2,1)}, u32[]{:S(2)}, u32[]{:S(2)}) collective-permute-start(bf16[1280,4,64]{0,2,1:T(8,128)(2,1)} %pad_maximum_fusion), channel_id=1, source_target_pairs={{0,480},{8,488},{16,496},{24,504},{32,0},{40,8},{48,16},{56,24},{6... | collective-permute-start | bytes 1966088 | tf_op jit(solution)/shard_map/ppermute | solution.py:79
  44.3 14.1 %copy-start.12 = (s32[128]{0:T(128)}, s32[128]{0:T(128)S(1)}, u32[]{:S(2)}) copy-start(s32[128]{0:T(128)S(1)} %get-tuple-element.8) | copy-start | bytes 1540
  56.5 18.3 %collective-permute-start.11 = (bf16[1280,4,64]{0,2,1:T(8,128)(2,1)}, bf16[1280,4,64]{0,2,1:T(8,128)(2,1)}, u32[]{:S(2)}, u32[]{:S(2)}) collective-permute-start(bf16[1280,4,64]{0,2,1:T(8,128)(2,1)} %collective-permute-done.10), channel_id=1, source_target_pairs={{0,32},{8,40},{16,48},{24,56},{32,64},{40,72},{48,80},{56,88},{64,... | collective-permute-start | bytes 1966088 | tf_op jit(solution)/shard_map/ppermute | solution.py:79
  58.5 18.8 %collective-permute-start.4 = (bf16[1280,4,64]{0,2,1:T(8,128)(2,1)}, bf16[1280,4,64]{0,2,1:T(8,128)(2,1)}, u32[]{:S(2)}, u32[]{:S(2)}) collective-permute-start(bf16[1280,4,64]{0,2,1:T(8,128)(2,1)} %collective-permute-done.3), channel_id=1, source_target_pairs={{0,480},{8,488},{16,496},{24,504},{32,0},{40,8},{48,16},{56,24},{6... | collective-permute-start | bytes 1966088 | tf_op jit(solution)/shard_map/ppermute | solution.py:79
  74.8 17.4 %collective-permute-start.12 = (bf16[1280,4,64]{0,2,1:T(8,128)(2,1)}, bf16[1280,4,64]{0,2,1:T(8,128)(2,1)}, u32[]{:S(2)}, u32[]{:S(2)}) collective-permute-start(bf16[1280,4,64]{0,2,1:T(8,128)(2,1)} %collective-permute-done.11), channel_id=1, source_target_pairs={{0,32},{8,40},{16,48},{24,56},{32,64},{40,72},{48,80},{56,88},{64,... | collective-permute-start | bytes 1966088 | tf_op jit(solution)/shard_map/ppermute | solution.py:79
  77.3 17.4 %collective-permute-start.5 = (bf16[1280,4,64]{0,2,1:T(8,128)(2,1)}, bf16[1280,4,64]{0,2,1:T(8,128)(2,1)}, u32[]{:S(2)}, u32[]{:S(2)}) collective-permute-start(bf16[1280,4,64]{0,2,1:T(8,128)(2,1)} %collective-permute-done.4), channel_id=1, source_target_pairs={{0,480},{8,488},{16,496},{24,504},{32,0},{40,8},{48,16},{56,24},{6... | collective-permute-start | bytes 1966088 | tf_op jit(solution)/shard_map/ppermute | solution.py:79
  92.2 16.3 %collective-permute-start.13 = (bf16[1280,4,64]{0,2,1:T(8,128)(2,1)}, bf16[1280,4,64]{0,2,1:T(8,128)(2,1)S(1)}, u32[]{:S(2)}, u32[]{:S(2)}) collective-permute-start(bf16[1280,4,64]{0,2,1:T(8,128)(2,1)} %collective-permute-done.12), channel_id=1, source_target_pairs={{0,32},{8,40},{16,48},{24,56},{32,64},{40,72},{48,80},{56,88},{64,... | collective-permute-start | bytes 1966088 | tf_op jit(solution)/shard_map/ppermute | solution.py:79
  94.7 16.6 %collective-permute-start.6 = (bf16[1280,4,64]{0,2,1:T(8,128)(2,1)}, bf16[1280,4,64]{0,2,1:T(8,128)(2,1)S(1)}, u32[]{:S(2)}, u32[]{:S(2)}) collective-permute-start(bf16[1280,4,64]{0,2,1:T(8,128)(2,1)} %collective-permute-done.5), channel_id=1, source_target_pairs={{0,480},{8,488},{16,496},{24,504},{32,0},{40,8},{48,16},{56,24},{6... | collective-permute-start | bytes 1966088 | tf_op jit(solution)/shard_map/ppermute | solution.py:79
  99.3 16.6 %copy-start.2 = (bf16[1280,16,4,64]{0,3,2,1:T(8,128)(2,1)S(1)}, bf16[1280,16,4,64]{0,3,2,1:T(8,128)(2,1)}, u32[]{:S(2)}) copy-start(bf16[1280,16,4,64]{0,3,2,1:T(8,128)(2,1)} %bitcast_dynamic-update-slice_fusion.15) | copy-start | bytes 31457284
  108.5 15.2 %collective-permute-start.14 = (bf16[1280,4,64]{0,2,1:T(8,128)(2,1)S(1)}, bf16[1280,4,64]{0,2,1:T(8,128)(2,1)S(1)}, u32[]{:S(2)}, u32[]{:S(2)}) collective-permute-start(bf16[1280,4,64]{0,2,1:T(8,128)(2,1)S(1)} %collective-permute-done.13), channel_id=1, source_target_pairs={{0,32},{8,40},{16,48},{24,56},{32,64},{40,72},{48,80},{56,88},{64,... | collective-permute-start | bytes 1966088 | tf_op jit(solution)/shard_map/ppermute | solution.py:79
  111.2 15.5 %collective-permute-start.7 = (bf16[1280,4,64]{0,2,1:T(8,128)(2,1)S(1)}, bf16[1280,4,64]{0,2,1:T(8,128)(2,1)S(1)}, u32[]{:S(2)}, u32[]{:S(2)}) collective-permute-start(bf16[1280,4,64]{0,2,1:T(8,128)(2,1)S(1)} %collective-permute-done.6), channel_id=1, source_target_pairs={{0,480},{8,488},{16,496},{24,504},{32,0},{40,8},{48,16},{56,24},{6... | collective-permute-start | bytes 1966088 | tf_op jit(solution)/shard_map/ppermute | solution.py:79
  123.7 14.3 %collective-permute-start.15 = (bf16[1280,4,64]{0,2,1:T(8,128)(2,1)S(1)}, bf16[1280,4,64]{0,2,1:T(8,128)(2,1)S(1)}, u32[]{:S(2)}, u32[]{:S(2)}) collective-permute-start(bf16[1280,4,64]{0,2,1:T(8,128)(2,1)S(1)} %collective-permute-done.14), channel_id=1, source_target_pairs={{0,32},{8,40},{16,48},{24,56},{32,64},{40,72},{48,80},{56,88},{64,... | collective-permute-start | bytes 1966088 | tf_op jit(solution)/shard_map/ppermute | solution.py:79
  126.8 13.3 %collective-permute-start.8 = (bf16[1280,4,64]{0,2,1:T(8,128)(2,1)S(1)}, bf16[1280,4,64]{0,2,1:T(8,128)(2,1)S(1)}, u32[]{:S(2)}, u32[]{:S(2)}) collective-permute-start(bf16[1280,4,64]{0,2,1:T(8,128)(2,1)S(1)} %collective-permute-done.7), channel_id=1, source_target_pairs={{0,480},{8,488},{16,496},{24,504},{32,0},{40,8},{48,16},{56,24},{6... | collective-permute-start | bytes 1966088 | tf_op jit(solution)/shard_map/ppermute | solution.py:79
  138.0 13.4 %collective-permute-start.16 = (bf16[1280,4,64]{0,2,1:T(8,128)(2,1)S(1)}, bf16[1280,4,64]{0,2,1:T(8,128)(2,1)S(1)}, u32[]{:S(2)}, u32[]{:S(2)}) collective-permute-start(bf16[1280,4,64]{0,2,1:T(8,128)(2,1)S(1)} %collective-permute-done.15), channel_id=1, source_target_pairs={{0,32},{8,40},{16,48},{24,56},{32,64},{40,72},{48,80},{56,88},{64,... | collective-permute-start | bytes 1966088 | tf_op jit(solution)/shard_map/ppermute | solution.py:79
  140.0 13.3 %collective-permute-start.9 = (bf16[1280,4,64]{0,2,1:T(8,128)(2,1)S(1)}, bf16[1280,4,64]{0,2,1:T(8,128)(2,1)S(1)}, u32[]{:S(2)}, u32[]{:S(2)}) collective-permute-start(bf16[1280,4,64]{0,2,1:T(8,128)(2,1)S(1)} %collective-permute-done.8), channel_id=1, source_target_pairs={{0,480},{8,488},{16,496},{24,504},{32,0},{40,8},{48,16},{56,24},{6... | collective-permute-start | bytes 1966088 | tf_op jit(solution)/shard_map/ppermute | solution.py:79
  151.3 13.2 %collective-permute-start.17 = (bf16[1280,4,64]{0,2,1:T(8,128)(2,1)S(1)}, bf16[1280,4,64]{0,2,1:T(8,128)(2,1)S(1)}, u32[]{:S(2)}, u32[]{:S(2)}) collective-permute-start(bf16[1280,4,64]{0,2,1:T(8,128)(2,1)S(1)} %collective-permute-done.16), channel_id=1, source_target_pairs={{0,32},{8,40},{16,48},{24,56},{32,64},{40,72},{48,80},{56,88},{64,... | collective-permute-start | bytes 1966088 | tf_op jit(solution)/shard_map/ppermute | solution.py:79
  168.2 5.2 %copy-start.3 = (bf16[1280,16,4,64]{0,3,2,1:T(8,128)(2,1)}, bf16[1280,16,4,64]{0,3,2,1:T(8,128)(2,1)S(1)}, u32[]{:S(2)}) copy-start(bf16[1280,16,4,64]{0,3,2,1:T(8,128)(2,1)S(1)} %bitcast_dynamic-update-slice_fusion) | copy-start | bytes 31457284
  182.7 5.1 %copy-start.9 = (f32[128]{0:T(128)S(1)}, f32[128]{0:T(128)}, u32[]{:S(2)}) copy-start(f32[128]{0:T(128)} %add_convert_fusion.4) | copy-start | bytes 1540
  186.8 11.4 %copy-start.13 = (s32[128]{0:T(128)S(1)}, s32[128]{0:T(128)}, u32[]{:S(2)}) copy-start(s32[128]{0:T(128)} %copy-done.12) | copy-start | bytes 1540
  187.8 28.3 %copy-start.1 = (bf16[1,1024,1024]{1,2,0:T(8,128)(2,1)S(1)}, bf16[1,1024,1024]{1,2,0:T(8,128)(2,1)}, u32[]{:S(2)}) copy-start(bf16[1,1024,1024]{1,2,0:T(8,128)(2,1)} %copy.121) | copy-start | bytes 6291460
  190.3 25.2 %all-to-all-start.1 = ((bf16[64,4,512]{2,1,0:T(4,128)(2,1)}), bf16[64,4,512]{2,1,0:T(4,128)(2,1)S(1)}, u32[]{:S(2)}, u32[]{:S(2)}) async-start(bf16[64,4,512]{2,1,0:T(4,128)(2,1)} %broadcast_select_fusion), calls=%async_computation.1 | async-start | bytes 524288 | tf_op jit(solution)/shard_map/all_to_all | solution.py:167
  222.7 26.8 %all-to-all-start.2 = ((bf16[64,5,512]{2,1,0:T(8,128)(2,1)}), bf16[64,5,512]{2,1,0:T(8,128)(2,1)S(1)}, u32[]{:S(2)}, u32[]{:S(2)}) async-start(bf16[64,5,512]{2,1,0:T(8,128)(2,1)} %fusion.26), calls=%async_computation.2 | async-start | bytes 1048576 | tf_op jit(solution)/shard_map/all_to_all | solution.py:185
  256.9 30.7 %all-to-all-start.3 = ((bf16[8,128,512]{1,2,0:T(8,128)(2,1)}), bf16[8,128,512]{1,2,0:T(8,128)(2,1)S(1)}, u32[]{:S(2)}, u32[]{:S(2)}) async-start(bf16[8,128,512]{1,2,0:T(8,128)(2,1)} %bitcast.65), calls=%async_computation.3 | async-start | bytes 2097152 | tf_op jit(solution)/shard_map/all_to_all | solution.py:225
  (4 other events, 10.7 us)

commit v4 on v3

--- a/solution.py
+++ b/solution.py
@@ -59,15 +59,18 @@
     ahead = value
     behind = value
     for k in range(1, count // 2 + 1):
-        behind = step(behind, 1)
-        rel[(-k) % count] = behind
         if k < count - k:
+            behind = step(behind, 1)
+            rel[(-k) % count] = behind
             ahead = step(ahead, -1)
             rel[k] = ahead
+        else:
+            half = value.shape[0] // 2
+            rel[k] = jnp.concatenate([step(behind[:half], 1), step(ahead[half:], -1)], axis=0)
     return rel
 
 
-def ring_gather(block, axis_name, seq_count):
+def ring_gather(y_first, z_first, axis_name, seq_count):
     z_count = seq_count // Y_CHIPS
     here = lax.axis_index(axis_name)
 
@@ -78,9 +81,17 @@
             pairs.append((i, ((z + dz) % z_count) * Y_CHIPS + (y + dy) % Y_CHIPS))
         return lax.ppermute(value, axis_name, pairs)
 
-    along_y = jnp.stack(ring(block, Y_CHIPS, lambda v, d: shift(v, 0, d)), axis=1)
-    along_z = jnp.stack(ring(along_y, z_count, lambda v, d: shift(v, d, 0)), axis=1)
-    return along_z.reshape(block.shape[0], -1), here // Y_CHIPS, here % Y_CHIPS
+    def on_y(v, d):
+        return shift(v, 0, d)
+
+    def on_z(v, d):
+        return shift(v, d, 0)
+
+    part_a = jnp.stack(ring(jnp.stack(ring(y_first, Y_CHIPS, on_y), axis=1), z_count, on_z), axis=1)
+    part_b = jnp.stack(ring(jnp.stack(ring(z_first, z_count, on_z), axis=1), Y_CHIPS, on_y), axis=2)
+    rows_a = part_a.reshape(y_first.shape[0], -1)
+    rows_b = part_b.reshape(z_first.shape[0], -1)
+    return rows_a, rows_b, here // Y_CHIPS, here % Y_CHIPS
 
 
 def shards(
@@ -116,11 +127,10 @@
     kv_start = tensor_index * heads_dev // group_full
     kv_width = kv_local * 2 * head_size
     kv_piece = lax.dynamic_slice_in_dim(key_value_weight, kv_start * 2 * head_size, kv_width, 1)
-    packed = jnp.concatenate([w_query.T, kv_piece.T, w_out], axis=0)
-    gathered, z_at, y_at = ring_gather(packed, "seq", seq_count)
-    wq_rows = gathered[:width_query]
-    kv_rows = gathered[width_query : width_query + kv_width]
-    wo_rel = gathered[width_query + kv_width :]
+    packed = jnp.concatenate([kv_piece.T, w_out], axis=0)
+    wq_rows, rest, z_at, y_at = ring_gather(w_query.T, packed, "seq", seq_count)
+    kv_rows = rest[:kv_width]
+    wo_rel = rest[kv_width:]
     z_count = seq_count // Y_CHIPS
     rel_input = normalized_input.reshape(length, z_count, Y_CHIPS, -1)
     rel_input = jnp.roll(jnp.roll(rel_input, -z_at, axis=1), -y_at, axis=2).reshape(length, -1)

time: 290 us -> 330 us (1.14)
  starting transfers between devices: 97.5 us -> 181 us
  waiting for transfers between devices: 125 us -> 47 us
  local copies, waits for them, and re-layouts: 35.4 us -> 55.4 us
  matrix products: 12.9 us -> 20.5 us
  other arithmetic: 16 us -> 21.2 us
    ppermute x18 -> x40, starting transfers between devices: 59.4 us -> 139 us  [shift(): return lax.ppermute(value, axis_name, pairs)]
    ppermute x18 -> x40, waiting for transfers between devices: 73 us -> 12.6 us  [shift(): return lax.ppermute(value, axis_name, pairs)]
    unnamed x46 -> x90, local copies, waits for them, and re-layouts: 15.4 us -> 29.8 us
    all_to_all x1, waiting for transfers between devices: 16.5 us -> 7.33 us  [shards(): lax.all_to_all(outgoing, 'seq', split_axis=0, concat_axis=0, tiled=True)]
    all_to_all x1, waiting for transfers between devices: 21.3 us -> 12.8 us  [shards(): lax.all_to_all(jnp.concatenate([out_block, log_row], axis=1), 'seq', spli...]
    dot_general x8, matrix products: 2.07 us -> 8.04 us  [attend(): result = jnp.dot(weights, values, preferred_element_type=jnp.float32)]
    all_to_all x1, starting transfers between devices: 15.6 us -> 19.9 us  [shards(): lax.all_to_all(jnp.moveaxis(pieces, 1, 0), 'tensor', split_axis=0, concat...]
    all_to_all x1, starting transfers between devices: 10 us -> 5.74 us  [shards(): lax.all_to_all(tiles, 'tensor', split_axis=0, concat_axis=0, tiled=True)]
  transfers between devices with their start and end apart: 22 -> 44, of which waited for: 13 -> 9; matrix products, arithmetic and copies ran while one was open for 7% -> 23% of each run, Pallas kernels for 0% -> 0%
where the time goes in v4:
time: 330 us; the launch traced here: 327 us
  starting transfers between devices  181 us (55%)
  local copies, waits for them, and re-layouts  55.4 us (17%)
  waiting for transfers between devices  47 us (14%)
  other arithmetic  21.2 us (6%)
  matrix products  20.5 us (6%)
    ppermute x40, starting transfers between devices, shift(): return lax.ppermute(value, axis_name, pairs)  139 us
    unnamed x90, local copies, waits for them, and re-layouts  29.8 us
    all_to_all x1, starting transfers between devices, shards(): lax.all_to_all(jnp.moveaxis(pieces, 1, 0), 'tensor', split_axis=0, concat...  19.9 us
    all_to_all x1, waiting for transfers between devices, shards(): lax.all_to_all(jnp.moveaxis(pieces, 1, 0), 'tensor', split_axis=0, concat...  14.4 us
    all_to_all x1, waiting for transfers between devices, shards(): lax.all_to_all(jnp.concatenate([out_block, log_row], axis=1), 'seq', spli...  12.8 us
    ppermute x40, waiting for transfers between devices, shift(): return lax.ppermute(value, axis_name, pairs)  12.6 us
    all_to_all x1, starting transfers between devices, shards(): lax.all_to_all(outgoing, 'seq', split_axis=0, concat_axis=0, tiled=True)  8.53 us
    dot_general x8, matrix products, attend(): result = jnp.dot(weights, values, preferred_element_type=jnp.float32)  8.04 us
  transfers between devices with their start and end apart: 44, of which 9 were waited for; matrix products, arithmetic and copies ran while one was open for 23% of the time, Pallas kernels for 0%

profile of v4, /device:TPU:1, one launch (start us, length us, event | category | flops | bytes accessed | tf_op | source)
XLA Modules:
  0.0 327.0 jit_solution(17627084467421607261)
XLA Ops:
  0.7 4.2 %collective-permute-start.1 = (bf16[512,64]{0,1:T(8,128)(2,1)}, bf16[512,64]{0,1:T(8,128)(2,1)S(1)}, u32[]{:S(2)}, u32[]{:S(2)}) collective-permute-start(bf16[512,64]{0,1:T(8,128)(2,1)} %bitcast.281), channel_id=1, source_target_pairs={{0,8},{8,16},{16,24},{24,0},{32,40},{40,48},{48,56},{56,32},{64,72... | collective-permute-start | bytes 196616 | tf_op jit(solution)/shard_map/ppermute | solution.py:82
  4.9 3.4 %collective-permute-start = (bf16[512,64]{0,1:T(8,128)(2,1)}, bf16[512,64]{0,1:T(8,128)(2,1)S(1)}, u32[]{:S(2)}, u32[]{:S(2)}) collective-permute-start(bf16[512,64]{0,1:T(8,128)(2,1)} %bitcast.282), channel_id=1, source_target_pairs={{0,24},{8,0},{16,8},{24,16},{32,56},{40,32},{48,40},{56,48},{64,88... | collective-permute-start | bytes 196616 | tf_op jit(solution)/shard_map/ppermute | solution.py:82
  9.8 11.1 %collective-permute-start.20 = (bf16[768,64]{0,1:T(8,128)(2,1)}, bf16[768,64]{0,1:T(8,128)(2,1)}, u32[]{:S(2)}, u32[]{:S(2)}) collective-permute-start(bf16[768,64]{0,1:T(8,128)(2,1)} %pad_maximum_fusion.8), channel_id=1, source_target_pairs={{0,480},{8,488},{16,496},{24,504},{32,0},{40,8},{48,16},{56,24},{6... | collective-permute-start | bytes 294920 | tf_op jit(solution)/shard_map/ppermute | solution.py:82
  25.0 5.7 %all-to-all-start = ((bf16[8,128,512]{1,2,0:T(8,128)(2,1)}), bf16[8,128,512]{1,2,0:T(8,128)(2,1)S(1)}, u32[]{:S(2)}, u32[]{:S(2)}) async-start(bf16[8,128,512]{1,2,0:T(8,128)(2,1)} %broadcast_in_dim.72), calls=%async_computation | async-start | bytes 2097152 | tf_op jit(solution)/shard_map/all_to_all | solution.py:113
  36.4 4.5 %collective-permute-start.3 = (bf16[256,64]{0,1:T(8,128)(2,1)}, bf16[256,64]{0,1:T(8,128)(2,1)}, u32[]{:S(2)}, u32[]{:S(2)}) collective-permute-start(bf16[256,64]{0,1:T(8,128)(2,1)} %slice.132), channel_id=1, source_target_pairs={{0,24},{8,0},{16,8},{24,16},{32,56},{40,32},{48,40},{56,48},{64,88... | collective-permute-start | bytes 98312 | tf_op jit(solution)/shard_map/ppermute | solution.py:82
  45.4 4.9 %collective-permute-start.4 = (bf16[512,4,64]{0,2,1:T(8,128)(2,1)S(1)}, bf16[512,4,64]{0,2,1:T(8,128)(2,1)S(1)}, u32[]{:S(2)}, u32[]{:S(2)}) collective-permute-start(bf16[512,4,64]{0,2,1:T(8,128)(2,1)S(1)} %pad_maximum_fusion.6), channel_id=1, source_target_pairs={{0,480},{8,488},{16,496},{24,504},{32,0},{40,8},{48,16},{56,24},{6... | collective-permute-start | bytes 786440 | tf_op jit(solution)/shard_map/ppermute | solution.py:82
  52.9 4.6 %collective-permute-start.21 = (bf16[768,64]{0,1:T(8,128)(2,1)}, bf16[768,64]{0,1:T(8,128)(2,1)S(1)}, u32[]{:S(2)}, u32[]{:S(2)}) collective-permute-start(bf16[768,64]{0,1:T(8,128)(2,1)} %collective-permute-done.20), channel_id=1, source_target_pairs={{0,480},{8,488},{16,496},{24,504},{32,0},{40,8},{48,16},{56,24},{6... | collective-permute-start | bytes 294920 | tf_op jit(solution)/shard_map/ppermute | solution.py:82
  60.9 4.6 %collective-permute-start.22 = (bf16[768,64]{0,1:T(8,128)(2,1)S(1)}, bf16[768,64]{0,1:T(8,128)(2,1)S(1)}, u32[]{:S(2)}, u32[]{:S(2)}) collective-permute-start(bf16[768,64]{0,1:T(8,128)(2,1)S(1)} %collective-permute-done.21), channel_id=1, source_target_pairs={{0,480},{8,488},{16,496},{24,504},{32,0},{40,8},{48,16},{56,24},{6... | collective-permute-start | bytes 294920 | tf_op jit(solution)/shard_map/ppermute | solution.py:82
  68.1 4.6 %collective-permute-start.23 = (bf16[768,64]{0,1:T(8,128)(2,1)S(1)}, bf16[768,64]{0,1:T(8,128)(2,1)S(1)}, u32[]{:S(2)}, u32[]{:S(2)}) collective-permute-start(bf16[768,64]{0,1:T(8,128)(2,1)S(1)} %collective-permute-done.22), channel_id=1, source_target_pairs={{0,480},{8,488},{16,496},{24,504},{32,0},{40,8},{48,16},{56,24},{6... | collective-permute-start | bytes 294920 | tf_op jit(solution)/shard_map/ppermute | solution.py:82
  75.2 4.6 %collective-permute-start.5 = (bf16[512,4,64]{0,2,1:T(8,128)(2,1)S(1)}, bf16[512,4,64]{0,2,1:T(8,128)(2,1)S(1)}, u32[]{:S(2)}, u32[]{:S(2)}) collective-permute-start(bf16[512,4,64]{0,2,1:T(8,128)(2,1)S(1)} %collective-permute-done.4), channel_id=1, source_target_pairs={{0,480},{8,488},{16,496},{24,504},{32,0},{40,8},{48,16},{56,24},{6... | collective-permute-start | bytes 786440 | tf_op jit(solution)/shard_map/ppermute | solution.py:82
  82.4 4.6 %collective-permute-start.24 = (bf16[768,64]{0,1:T(8,128)(2,1)S(1)}, bf16[768,64]{0,1:T(8,128)(2,1)S(1)}, u32[]{:S(2)}, u32[]{:S(2)}) collective-permute-start(bf16[768,64]{0,1:T(8,128)(2,1)S(1)} %collective-permute-done.23), channel_id=1, source_target_pairs={{0,480},{8,488},{16,496},{24,504},{32,0},{40,8},{48,16},{56,24},{6... | collective-permute-start | bytes 294920 | tf_op jit(solution)/shard_map/ppermute | solution.py:82
  89.6 4.6 %collective-permute-start.25 = (bf16[768,64]{0,1:T(8,128)(2,1)S(1)}, bf16[768,64]{0,1:T(8,128)(2,1)S(1)}, u32[]{:S(2)}, u32[]{:S(2)}) collective-permute-start(bf16[768,64]{0,1:T(8,128)(2,1)S(1)} %collective-permute-done.24), channel_id=1, source_target_pairs={{0,480},{8,488},{16,496},{24,504},{32,0},{40,8},{48,16},{56,24},{6... | collective-permute-start | bytes 294920 | tf_op jit(solution)/shard_map/ppermute | solution.py:82
  96.7 4.6 %collective-permute-start.26 = (bf16[768,64]{0,1:T(8,128)(2,1)S(1)}, bf16[768,64]{0,1:T(8,128)(2,1)S(1)}, u32[]{:S(2)}, u32[]{:S(2)}) collective-permute-start(bf16[768,64]{0,1:T(8,128)(2,1)S(1)} %collective-permute-done.25), channel_id=1, source_target_pairs={{0,480},{8,488},{16,496},{24,504},{32,0},{40,8},{48,16},{56,24},{6... | collective-permute-start | bytes 294920 | tf_op jit(solution)/shard_map/ppermute | solution.py:82
  103.9 4.6 %collective-permute-start.6 = (bf16[512,4,64]{0,2,1:T(8,128)(2,1)S(1)}, bf16[512,4,64]{0,2,1:T(8,128)(2,1)}, u32[]{:S(2)}, u32[]{:S(2)}) collective-permute-start(bf16[512,4,64]{0,2,1:T(8,128)(2,1)S(1)} %collective-permute-done.5), channel_id=1, source_target_pairs={{0,480},{8,488},{16,496},{24,504},{32,0},{40,8},{48,16},{56,24},{6... | collective-permute-start | bytes 786440 | tf_op jit(solution)/shard_map/ppermute | solution.py:82
  113.1 4.6 %collective-permute-start.35 = (bf16[384,64]{0,1:T(8,128)(2,1)S(1)}, bf16[384,64]{0,1:T(8,128)(2,1)S(1)}, u32[]{:S(2)}, u32[]{:S(2)}) collective-permute-start(bf16[384,64]{0,1:T(8,128)(2,1)S(1)} %slice.144), channel_id=1, source_target_pairs={{0,480},{8,488},{16,496},{24,504},{32,0},{40,8},{48,16},{56,24},{6... | collective-permute-start | bytes 147464 | tf_op jit(solution)/shard_map/ppermute | solution.py:82
  126.8 4.6 %collective-permute-start.36 = (bf16[768,16,64]{0,2,1:T(8,128)(2,1)}, bf16[768,16,64]{0,2,1:T(8,128)(2,1)}, u32[]{:S(2)}, u32[]{:S(2)}) collective-permute-start(bf16[768,16,64]{0,2,1:T(8,128)(2,1)} %bitcast_dynamic-update-slice_fusion.15), channel_id=1, source_target_pairs={{0,24},{8,0},{16,8},{24,16},{32,56},{40,32},{48,40},{56,48},{64,88... | collective-permute-start | bytes 4718600 | tf_op jit(solution)/shard_map/ppermute | solution.py:82
  131.4 4.9 %collective-permute-start.7 = (bf16[512,4,64]{0,2,1:T(8,128)(2,1)}, bf16[512,4,64]{0,2,1:T(8,128)(2,1)}, u32[]{:S(2)}, u32[]{:S(2)}) collective-permute-start(bf16[512,4,64]{0,2,1:T(8,128)(2,1)} %collective-permute-done.6), channel_id=1, source_target_pairs={{0,480},{8,488},{16,496},{24,504},{32,0},{40,8},{48,16},{56,24},{6... | collective-permute-start | bytes 786440 | tf_op jit(solution)/shard_map/ppermute | solution.py:82
  140.6 4.6 %collective-permute-start.8 = (bf16[512,4,64]{0,2,1:T(8,128)(2,1)}, bf16[512,4,64]{0,2,1:T(8,128)(2,1)S(1)}, u32[]{:S(2)}, u32[]{:S(2)}) collective-permute-start(bf16[512,4,64]{0,2,1:T(8,128)(2,1)} %collective-permute-done.7), channel_id=1, source_target_pairs={{0,480},{8,488},{16,496},{24,504},{32,0},{40,8},{48,16},{56,24},{6... | collective-permute-start | bytes 786440 | tf_op jit(solution)/shard_map/ppermute | solution.py:82
  150.7 5.2 %collective-permute-start.9 = (bf16[512,4,64]{0,2,1:T(8,128)(2,1)S(1)}, bf16[512,4,64]{0,2,1:T(8,128)(2,1)S(1)}, u32[]{:S(2)}, u32[]{:S(2)}) collective-permute-start(bf16[512,4,64]{0,2,1:T(8,128)(2,1)S(1)} %collective-permute-done.8), channel_id=1, source_target_pairs={{0,480},{8,488},{16,496},{24,504},{32,0},{40,8},{48,16},{56,24},{6... | collective-permute-start | bytes 786440 | tf_op jit(solution)/shard_map/ppermute | solution.py:82
  161.8 5.3 %collective-permute-start.10 = (bf16[512,4,64]{0,2,1:T(8,128)(2,1)S(1)}, bf16[512,4,64]{0,2,1:T(8,128)(2,1)S(1)}, u32[]{:S(2)}, u32[]{:S(2)}) collective-permute-start(bf16[512,4,64]{0,2,1:T(8,128)(2,1)S(1)} %collective-permute-done.9), channel_id=1, source_target_pairs={{0,480},{8,488},{16,496},{24,504},{32,0},{40,8},{48,16},{56,24},{6... | collective-permute-start | bytes 786440 | tf_op jit(solution)/shard_map/ppermute | solution.py:82
  170.5 6.7 %collective-permute-done.17 = bf16[512,4,64]{0,2,1:T(8,128)(2,1)S(1)} collective-permute-done((bf16[512,4,64]{0,2,1:T(8,128)(2,1)S(1)}, bf16[512,4,64]{0,2,1:T(8,128)(2,1)S(1)}, u32[]{:S(2)}, u32[]{:S(2)}) %collective-permute-start.17) | collective-permute-done | bytes 262176 | tf_op jit(solution)/shard_map/ppermute | solution.py:82
  179.1 4.6 %collective-permute-start.19 = (bf16[256,4,64]{0,2,1:T(8,128)(2,1)S(1)}, bf16[256,4,64]{0,2,1:T(8,128)(2,1)S(1)}, u32[]{:S(2)}, u32[]{:S(2)}) collective-permute-start(bf16[256,4,64]{0,2,1:T(8,128)(2,1)S(1)} %slice.134), channel_id=1, source_target_pairs={{0,480},{8,488},{16,496},{24,504},{32,0},{40,8},{48,16},{56,24},{6... | collective-permute-start | bytes 393224 | tf_op jit(solution)/shard_map/ppermute | solution.py:82
  193.3 7.0 %dot_general.65 = bf16[4,128,4096]{1,0,2:T(4,128)(2,1)} reshape(bf16[512,16,4,64]{0,3,2,1:T(8,128)(2,1)} %bitcast_dynamic-update-slice_fusion) | data formatting | bytes 8388608 | tf_op jit(solution)/shard_map/dot_general | solution.py:139
  205.4 4.6 %collective-permute-start.39 = (bf16[384,16,64]{0,2,1:T(8,128)(2,1)}, bf16[384,16,64]{0,2,1:T(8,128)(2,1)}, u32[]{:S(2)}, u32[]{:S(2)}) collective-permute-start(bf16[384,16,64]{0,2,1:T(8,128)(2,1)} %slice.146), channel_id=1, source_target_pairs={{0,24},{8,0},{16,8},{24,16},{32,56},{40,32},{48,40},{56,48},{64,88... | collective-permute-start | bytes 2359304 | tf_op jit(solution)/shard_map/ppermute | solution.py:82
  210.0 3.9 %fusion.4 = f32[128,4,128]{0,2,1:T(8,128)S(1)} fusion(bf16[128,4096,1]{0,1,2:T(8,128)(2,1)S(1)} %bitcast.274, bf16[4,128,4096]{1,0,2:T(4,128)(2,1)} %dot_general.65), kind=kOutput, calls=%fused_computation.13 | convolution fusion | flops 536870912 | bytes 5505024 | tf_op jit(solution)/shard_map/dot_general | solution.py:139
  217.0 8.5 %all-to-all-start.1 = ((bf16[64,4,512]{2,1,0:T(4,128)(2,1)}), bf16[64,4,512]{2,1,0:T(4,128)(2,1)S(1)}, u32[]{:S(2)}, u32[]{:S(2)}) async-start(bf16[64,4,512]{2,1,0:T(4,128)(2,1)} %broadcast_select_fusion), calls=%async_computation.1 | async-start | bytes 524288 | tf_op jit(solution)/shard_map/all_to_all | solution.py:177
  235.5 7.3 %all-to-all-done.1 = bf16[64,4,512]{2,1,0:T(4,128)(2,1)S(1)} async-done(((bf16[64,4,512]{2,1,0:T(4,128)(2,1)}), bf16[64,4,512]{2,1,0:T(4,128)(2,1)S(1)}, u32[]{:S(2)}, u32[]{:S(2)}) %all-to-all-start.1) | async-done | bytes 262176 | tf_op jit(solution)/shard_map/all_to_all | solution.py:177
  250.0 7.4 %all-to-all-start.2 = ((bf16[64,5,512]{2,1,0:T(8,128)(2,1)}), bf16[64,5,512]{2,1,0:T(8,128)(2,1)}, u32[]{:S(2)}, u32[]{:S(2)}) async-start(bf16[64,5,512]{2,1,0:T(8,128)(2,1)} %fusion.29), calls=%async_computation.2 | async-start | bytes 1048576 | tf_op jit(solution)/shard_map/all_to_all | solution.py:195
  266.3 12.8 %all-to-all-done.2 = bf16[64,5,512]{2,1,0:T(8,128)(2,1)} async-done(((bf16[64,5,512]{2,1,0:T(8,128)(2,1)}), bf16[64,5,512]{2,1,0:T(8,128)(2,1)}, u32[]{:S(2)}, u32[]{:S(2)}) %all-to-all-start.2) | async-done | bytes 327712 | tf_op jit(solution)/shard_map/all_to_all | solution.py:195
  286.4 2.8 fusion.1
  291.0 19.9 %all-to-all-start.3 = ((bf16[8,128,512]{1,2,0:T(8,128)(2,1)}), bf16[8,128,512]{1,2,0:T(8,128)(2,1)S(1)}, u32[]{:S(2)}, u32[]{:S(2)}) async-start(bf16[8,128,512]{1,2,0:T(8,128)(2,1)} %bitcast.88), calls=%async_computation.3 | async-start | bytes 2097152 | tf_op jit(solution)/shard_map/all_to_all | solution.py:235
  311.7 14.4 %all-to-all-done.3 = bf16[8,128,512]{1,2,0:T(8,128)(2,1)S(1)} async-done(((bf16[8,128,512]{1,2,0:T(8,128)(2,1)}), bf16[8,128,512]{1,2,0:T(8,128)(2,1)S(1)}, u32[]{:S(2)}, u32[]{:S(2)}) %all-to-all-start.3) | async-done | bytes 1048608 | tf_op jit(solution)/shard_map/all_to_all | solution.py:235
  (266 shorter events, 125.7 us)
Async XLA Ops:
  0.7 32.5 %collective-permute-start.1 = (bf16[512,64]{0,1:T(8,128)(2,1)}, bf16[512,64]{0,1:T(8,128)(2,1)S(1)}, u32[]{:S(2)}, u32[]{:S(2)}) collective-permute-start(bf16[512,64]{0,1:T(8,128)(2,1)} %bitcast.281), channel_id=1, source_target_pairs={{0,8},{8,16},{16,24},{24,0},{32,40},{40,48},{48,56},{56,32},{64,72... | collective-permute-start | bytes 196616 | tf_op jit(solution)/shard_map/ppermute | solution.py:82
  4.9 30.9 %collective-permute-start = (bf16[512,64]{0,1:T(8,128)(2,1)}, bf16[512,64]{0,1:T(8,128)(2,1)S(1)}, u32[]{:S(2)}, u32[]{:S(2)}) collective-permute-start(bf16[512,64]{0,1:T(8,128)(2,1)} %bitcast.282), channel_id=1, source_target_pairs={{0,24},{8,0},{16,8},{24,16},{32,56},{40,32},{48,40},{56,48},{64,88... | collective-permute-start | bytes 196616 | tf_op jit(solution)/shard_map/ppermute | solution.py:82
  9.8 43.1 %collective-permute-start.20 = (bf16[768,64]{0,1:T(8,128)(2,1)}, bf16[768,64]{0,1:T(8,128)(2,1)}, u32[]{:S(2)}, u32[]{:S(2)}) collective-permute-start(bf16[768,64]{0,1:T(8,128)(2,1)} %pad_maximum_fusion.8), channel_id=1, source_target_pairs={{0,480},{8,488},{16,496},{24,504},{32,0},{40,8},{48,16},{56,24},{6... | collective-permute-start | bytes 294920 | tf_op jit(solution)/shard_map/ppermute | solution.py:82
  20.9 38.1 %collective-permute-start.27 = (bf16[768,64]{0,1:T(8,128)(2,1)}, bf16[768,64]{0,1:T(8,128)(2,1)}, u32[]{:S(2)}, u32[]{:S(2)}) collective-permute-start(bf16[768,64]{0,1:T(8,128)(2,1)} %pad_maximum_fusion.8), channel_id=1, source_target_pairs={{0,32},{8,40},{16,48},{24,56},{32,64},{40,72},{48,80},{56,88},{64,... | collective-permute-start | bytes 294920 | tf_op jit(solution)/shard_map/ppermute | solution.py:82
  25.0 114.9 %all-to-all-start = ((bf16[8,128,512]{1,2,0:T(8,128)(2,1)}), bf16[8,128,512]{1,2,0:T(8,128)(2,1)S(1)}, u32[]{:S(2)}, u32[]{:S(2)}) async-start(bf16[8,128,512]{1,2,0:T(8,128)(2,1)} %broadcast_in_dim.72), calls=%async_computation | async-start | bytes 2097152 | tf_op jit(solution)/shard_map/all_to_all | solution.py:113
  33.8 10.7 %collective-permute-start.2 = (bf16[256,64]{0,1:T(8,128)(2,1)}, bf16[256,64]{0,1:T(8,128)(2,1)}, u32[]{:S(2)}, u32[]{:S(2)}) collective-permute-start(bf16[256,64]{0,1:T(8,128)(2,1)} %slice.131), channel_id=1, source_target_pairs={{0,8},{8,16},{16,24},{24,0},{32,40},{40,48},{48,56},{56,32},{64,72... | collective-permute-start | bytes 98312 | tf_op jit(solution)/shard_map/ppermute | solution.py:82
  36.4 8.1 %collective-permute-start.3 = (bf16[256,64]{0,1:T(8,128)(2,1)}, bf16[256,64]{0,1:T(8,128)(2,1)}, u32[]{:S(2)}, u32[]{:S(2)}) collective-permute-start(bf16[256,64]{0,1:T(8,128)(2,1)} %slice.132), channel_id=1, source_target_pairs={{0,24},{8,0},{16,8},{24,16},{32,56},{40,32},{48,40},{56,48},{64,88... | collective-permute-start | bytes 98312 | tf_op jit(solution)/shard_map/ppermute | solution.py:82
  45.4 29.9 %collective-permute-start.4 = (bf16[512,4,64]{0,2,1:T(8,128)(2,1)S(1)}, bf16[512,4,64]{0,2,1:T(8,128)(2,1)S(1)}, u32[]{:S(2)}, u32[]{:S(2)}) collective-permute-start(bf16[512,4,64]{0,2,1:T(8,128)(2,1)S(1)} %pad_maximum_fusion.6), channel_id=1, source_target_pairs={{0,480},{8,488},{16,496},{24,504},{32,0},{40,8},{48,16},{56,24},{6... | collective-permute-start | bytes 786440 | tf_op jit(solution)/shard_map/ppermute | solution.py:82
  50.2 30.3 %collective-permute-start.11 = (bf16[512,4,64]{0,2,1:T(8,128)(2,1)S(1)}, bf16[512,4,64]{0,2,1:T(8,128)(2,1)S(1)}, u32[]{:S(2)}, u32[]{:S(2)}) collective-permute-start(bf16[512,4,64]{0,2,1:T(8,128)(2,1)S(1)} %pad_maximum_fusion.6), channel_id=1, source_target_pairs={{0,32},{8,40},{16,48},{24,56},{32,64},{40,72},{48,80},{56,88},{64,... | collective-permute-start | bytes 786440 | tf_op jit(solution)/shard_map/ppermute | solution.py:82
  68.1 14.4 %collective-permute-start.23 = (bf16[768,64]{0,1:T(8,128)(2,1)S(1)}, bf16[768,64]{0,1:T(8,128)(2,1)S(1)}, u32[]{:S(2)}, u32[]{:S(2)}) collective-permute-start(bf16[768,64]{0,1:T(8,128)(2,1)S(1)} %collective-permute-done.22), channel_id=1, source_target_pairs={{0,480},{8,488},{16,496},{24,504},{32,0},{40,8},{48,16},{56,24},{6... | collective-permute-start | bytes 294920 | tf_op jit(solution)/shard_map/ppermute | solution.py:82
  73.3 14.4 %collective-permute-start.30 = (bf16[768,64]{0,1:T(8,128)(2,1)S(1)}, bf16[768,64]{0,1:T(8,128)(2,1)S(1)}, u32[]{:S(2)}, u32[]{:S(2)}) collective-permute-start(bf16[768,64]{0,1:T(8,128)(2,1)S(1)} %collective-permute-done.29), channel_id=1, source_target_pairs={{0,32},{8,40},{16,48},{24,56},{32,64},{40,72},{48,80},{56,88},{64,... | collective-permute-start | bytes 294920 | tf_op jit(solution)/shard_map/ppermute | solution.py:82
  75.2 28.7 %collective-permute-start.5 = (bf16[512,4,64]{0,2,1:T(8,128)(2,1)S(1)}, bf16[512,4,64]{0,2,1:T(8,128)(2,1)S(1)}, u32[]{:S(2)}, u32[]{:S(2)}) collective-permute-start(bf16[512,4,64]{0,2,1:T(8,128)(2,1)S(1)} %collective-permute-done.4), channel_id=1, source_target_pairs={{0,480},{8,488},{16,496},{24,504},{32,0},{40,8},{48,16},{56,24},{6... | collective-permute-start | bytes 786440 | tf_op jit(solution)/shard_map/ppermute | solution.py:82
  80.5 28.7 %collective-permute-start.12 = (bf16[512,4,64]{0,2,1:T(8,128)(2,1)S(1)}, bf16[512,4,64]{0,2,1:T(8,128)(2,1)S(1)}, u32[]{:S(2)}, u32[]{:S(2)}) collective-permute-start(bf16[512,4,64]{0,2,1:T(8,128)(2,1)S(1)} %collective-permute-done.11), channel_id=1, source_target_pairs={{0,32},{8,40},{16,48},{24,56},{32,64},{40,72},{48,80},{56,88},{64,... | collective-permute-start | bytes 786440 | tf_op jit(solution)/shard_map/ppermute | solution.py:82
  96.7 16.3 %collective-permute-start.26 = (bf16[768,64]{0,1:T(8,128)(2,1)S(1)}, bf16[768,64]{0,1:T(8,128)(2,1)S(1)}, u32[]{:S(2)}, u32[]{:S(2)}) collective-permute-start(bf16[768,64]{0,1:T(8,128)(2,1)S(1)} %collective-permute-done.25), channel_id=1, source_target_pairs={{0,480},{8,488},{16,496},{24,504},{32,0},{40,8},{48,16},{56,24},{6... | collective-permute-start | bytes 294920 | tf_op jit(solution)/shard_map/ppermute | solution.py:82
  102.0 9.2 %collective-permute-start.33 = (bf16[768,64]{0,1:T(8,128)(2,1)S(1)}, bf16[768,64]{0,1:T(8,128)(2,1)S(1)}, u32[]{:S(2)}, u32[]{:S(2)}) collective-permute-start(bf16[768,64]{0,1:T(8,128)(2,1)S(1)} %collective-permute-done.32), channel_id=1, source_target_pairs={{0,32},{8,40},{16,48},{24,56},{32,64},{40,72},{48,80},{56,88},{64,... | collective-permute-start | bytes 294920 | tf_op jit(solution)/shard_map/ppermute | solution.py:82
  103.9 27.5 %collective-permute-start.6 = (bf16[512,4,64]{0,2,1:T(8,128)(2,1)S(1)}, bf16[512,4,64]{0,2,1:T(8,128)(2,1)}, u32[]{:S(2)}, u32[]{:S(2)}) collective-permute-start(bf16[512,4,64]{0,2,1:T(8,128)(2,1)S(1)} %collective-permute-done.5), channel_id=1, source_target_pairs={{0,480},{8,488},{16,496},{24,504},{32,0},{40,8},{48,16},{56,24},{6... | collective-permute-start | bytes 786440 | tf_op jit(solution)/shard_map/ppermute | solution.py:82
  109.2 27.1 %collective-permute-start.13 = (bf16[512,4,64]{0,2,1:T(8,128)(2,1)S(1)}, bf16[512,4,64]{0,2,1:T(8,128)(2,1)}, u32[]{:S(2)}, u32[]{:S(2)}) collective-permute-start(bf16[512,4,64]{0,2,1:T(8,128)(2,1)S(1)} %collective-permute-done.12), channel_id=1, source_target_pairs={{0,32},{8,40},{16,48},{24,56},{32,64},{40,72},{48,80},{56,88},{64,... | collective-permute-start | bytes 786440 | tf_op jit(solution)/shard_map/ppermute | solution.py:82
  124.9 75.4 %collective-permute-start.37 = (bf16[768,16,64]{0,2,1:T(8,128)(2,1)}, bf16[768,16,64]{0,2,1:T(8,128)(2,1)S(1)}, u32[]{:S(2)}, u32[]{:S(2)}) collective-permute-start(bf16[768,16,64]{0,2,1:T(8,128)(2,1)} %bitcast_dynamic-update-slice_fusion.15), channel_id=1, source_target_pairs={{0,8},{8,16},{16,24},{24,0},{32,40},{40,48},{48,56},{56,32},{64,72... | collective-permute-start | bytes 4718600 | tf_op jit(solution)/shard_map/ppermute | solution.py:82
  126.8 76.5 %collective-permute-start.36 = (bf16[768,16,64]{0,2,1:T(8,128)(2,1)}, bf16[768,16,64]{0,2,1:T(8,128)(2,1)}, u32[]{:S(2)}, u32[]{:S(2)}) collective-permute-start(bf16[768,16,64]{0,2,1:T(8,128)(2,1)} %bitcast_dynamic-update-slice_fusion.15), channel_id=1, source_target_pairs={{0,24},{8,0},{16,8},{24,16},{32,56},{40,32},{48,40},{56,48},{64,88... | collective-permute-start | bytes 4718600 | tf_op jit(solution)/shard_map/ppermute | solution.py:82
  131.4 9.2 %collective-permute-start.7 = (bf16[512,4,64]{0,2,1:T(8,128)(2,1)}, bf16[512,4,64]{0,2,1:T(8,128)(2,1)}, u32[]{:S(2)}, u32[]{:S(2)}) collective-permute-start(bf16[512,4,64]{0,2,1:T(8,128)(2,1)} %collective-permute-done.6), channel_id=1, source_target_pairs={{0,480},{8,488},{16,496},{24,504},{32,0},{40,8},{48,16},{56,24},{6... | collective-permute-start | bytes 786440 | tf_op jit(solution)/shard_map/ppermute | solution.py:82
  136.3 8.9 %collective-permute-start.14 = (bf16[512,4,64]{0,2,1:T(8,128)(2,1)}, bf16[512,4,64]{0,2,1:T(8,128)(2,1)}, u32[]{:S(2)}, u32[]{:S(2)}) collective-permute-start(bf16[512,4,64]{0,2,1:T(8,128)(2,1)} %collective-permute-done.13), channel_id=1, source_target_pairs={{0,32},{8,40},{16,48},{24,56},{32,64},{40,72},{48,80},{56,88},{64,... | collective-permute-start | bytes 786440 | tf_op jit(solution)/shard_map/ppermute | solution.py:82
  140.6 10.1 %collective-permute-start.8 = (bf16[512,4,64]{0,2,1:T(8,128)(2,1)}, bf16[512,4,64]{0,2,1:T(8,128)(2,1)S(1)}, u32[]{:S(2)}, u32[]{:S(2)}) collective-permute-start(bf16[512,4,64]{0,2,1:T(8,128)(2,1)} %collective-permute-done.7), channel_id=1, source_target_pairs={{0,480},{8,488},{16,496},{24,504},{32,0},{40,8},{48,16},{56,24},{6... | collective-permute-start | bytes 786440 | tf_op jit(solution)/shard_map/ppermute | solution.py:82
  145.2 11.0 %collective-permute-start.15 = (bf16[512,4,64]{0,2,1:T(8,128)(2,1)}, bf16[512,4,64]{0,2,1:T(8,128)(2,1)S(1)}, u32[]{:S(2)}, u32[]{:S(2)}) collective-permute-start(bf16[512,4,64]{0,2,1:T(8,128)(2,1)} %collective-permute-done.14), channel_id=1, source_target_pairs={{0,32},{8,40},{16,48},{24,56},{32,64},{40,72},{48,80},{56,88},{64,... | collective-permute-start | bytes 786440 | tf_op jit(solution)/shard_map/ppermute | solution.py:82
  150.7 11.1 %collective-permute-start.9 = (bf16[512,4,64]{0,2,1:T(8,128)(2,1)S(1)}, bf16[512,4,64]{0,2,1:T(8,128)(2,1)S(1)}, u32[]{:S(2)}, u32[]{:S(2)}) collective-permute-start(bf16[512,4,64]{0,2,1:T(8,128)(2,1)S(1)} %collective-permute-done.8), channel_id=1, source_target_pairs={{0,480},{8,488},{16,496},{24,504},{32,0},{40,8},{48,16},{56,24},{6... | collective-permute-start | bytes 786440 | tf_op jit(solution)/shard_map/ppermute | solution.py:82
  156.2 10.9 %collective-permute-start.16 = (bf16[512,4,64]{0,2,1:T(8,128)(2,1)S(1)}, bf16[512,4,64]{0,2,1:T(8,128)(2,1)S(1)}, u32[]{:S(2)}, u32[]{:S(2)}) collective-permute-start(bf16[512,4,64]{0,2,1:T(8,128)(2,1)S(1)} %collective-permute-done.15), channel_id=1, source_target_pairs={{0,32},{8,40},{16,48},{24,56},{32,64},{40,72},{48,80},{56,88},{64,... | collective-permute-start | bytes 786440 | tf_op jit(solution)/shard_map/ppermute | solution.py:82
  161.8 17.3 %collective-permute-start.10 = (bf16[512,4,64]{0,2,1:T(8,128)(2,1)S(1)}, bf16[512,4,64]{0,2,1:T(8,128)(2,1)S(1)}, u32[]{:S(2)}, u32[]{:S(2)}) collective-permute-start(bf16[512,4,64]{0,2,1:T(8,128)(2,1)S(1)} %collective-permute-done.9), channel_id=1, source_target_pairs={{0,480},{8,488},{16,496},{24,504},{32,0},{40,8},{48,16},{56,24},{6... | collective-permute-start | bytes 786440 | tf_op jit(solution)/shard_map/ppermute | solution.py:82
  167.1 10.0 %collective-permute-start.17 = (bf16[512,4,64]{0,2,1:T(8,128)(2,1)S(1)}, bf16[512,4,64]{0,2,1:T(8,128)(2,1)S(1)}, u32[]{:S(2)}, u32[]{:S(2)}) collective-permute-start(bf16[512,4,64]{0,2,1:T(8,128)(2,1)S(1)} %collective-permute-done.16), channel_id=1, source_target_pairs={{0,32},{8,40},{16,48},{24,56},{32,64},{40,72},{48,80},{56,88},{64,... | collective-permute-start | bytes 786440 | tf_op jit(solution)/shard_map/ppermute | solution.py:82
  201.4 24.1 %collective-permute-start.38 = (bf16[384,16,64]{0,2,1:T(8,128)(2,1)}, bf16[384,16,64]{0,2,1:T(8,128)(2,1)}, u32[]{:S(2)}, u32[]{:S(2)}) collective-permute-start(bf16[384,16,64]{0,2,1:T(8,128)(2,1)} %slice.145), channel_id=1, source_target_pairs={{0,8},{8,16},{16,24},{24,0},{32,40},{40,48},{48,56},{56,32},{64,72... | collective-permute-start | bytes 2359304 | tf_op jit(solution)/shard_map/ppermute | solution.py:82
  205.4 20.1 %collective-permute-start.39 = (bf16[384,16,64]{0,2,1:T(8,128)(2,1)}, bf16[384,16,64]{0,2,1:T(8,128)(2,1)}, u32[]{:S(2)}, u32[]{:S(2)}) collective-permute-start(bf16[384,16,64]{0,2,1:T(8,128)(2,1)} %slice.146), channel_id=1, source_target_pairs={{0,24},{8,0},{16,8},{24,16},{32,56},{40,32},{48,40},{56,48},{64,88... | collective-permute-start | bytes 2359304 | tf_op jit(solution)/shard_map/ppermute | solution.py:82
  217.0 25.8 %all-to-all-start.1 = ((bf16[64,4,512]{2,1,0:T(4,128)(2,1)}), bf16[64,4,512]{2,1,0:T(4,128)(2,1)S(1)}, u32[]{:S(2)}, u32[]{:S(2)}) async-start(bf16[64,4,512]{2,1,0:T(4,128)(2,1)} %broadcast_select_fusion), calls=%async_computation.1 | async-start | bytes 524288 | tf_op jit(solution)/shard_map/all_to_all | solution.py:177
  250.0 29.1 %all-to-all-start.2 = ((bf16[64,5,512]{2,1,0:T(8,128)(2,1)}), bf16[64,5,512]{2,1,0:T(8,128)(2,1)}, u32[]{:S(2)}, u32[]{:S(2)}) async-start(bf16[64,5,512]{2,1,0:T(8,128)(2,1)} %fusion.29), calls=%async_computation.2 | async-start | bytes 1048576 | tf_op jit(solution)/shard_map/all_to_all | solution.py:195
  291.0 35.0 %all-to-all-start.3 = ((bf16[8,128,512]{1,2,0:T(8,128)(2,1)}), bf16[8,128,512]{1,2,0:T(8,128)(2,1)S(1)}, u32[]{:S(2)}, u32[]{:S(2)}) async-start(bf16[8,128,512]{1,2,0:T(8,128)(2,1)} %bitcast.88), calls=%async_computation.3 | async-start | bytes 2097152 | tf_op jit(solution)/shard_map/all_to_all | solution.py:235
  (42 other events, 533.8 us)

commit v5 on v3

--- a/solution.py
+++ b/solution.py
@@ -116,11 +116,10 @@
     kv_start = tensor_index * heads_dev // group_full
     kv_width = kv_local * 2 * head_size
     kv_piece = lax.dynamic_slice_in_dim(key_value_weight, kv_start * 2 * head_size, kv_width, 1)
-    packed = jnp.concatenate([w_query.T, kv_piece.T, w_out], axis=0)
+    packed = jnp.concatenate([w_query.T, kv_piece.T], axis=0)
     gathered, z_at, y_at = ring_gather(packed, "seq", seq_count)
     wq_rows = gathered[:width_query]
-    kv_rows = gathered[width_query : width_query + kv_width]
-    wo_rel = gathered[width_query + kv_width :]
+    kv_rows = gathered[width_query:]
     z_count = seq_count // Y_CHIPS
     rel_input = normalized_input.reshape(length, z_count, Y_CHIPS, -1)
     rel_input = jnp.roll(jnp.roll(rel_input, -z_at, axis=1), -y_at, axis=2).reshape(length, -1)
@@ -164,6 +163,8 @@
     source_rows = jnp.where(valid, owner_start[:, None] + slots[None, :], 0)
     flat_query = query_vectors.reshape(length, width_query)
     outgoing = jnp.where(valid[:, :, None], flat_query[source_rows], jnp.zeros((), jnp.bfloat16))
+    outgoing, wo_block = lax.optimization_barrier((outgoing, w_out))
+    wo_rel, _, _ = ring_gather(wo_block, "seq", seq_count)
     arrived = lax.all_to_all(outgoing, "seq", split_axis=0, concat_axis=0, tiled=True)
     items = arrived.shape[1]
     rows_in = arrived.reshape(seq_count * items, heads_dev, head_size)

time: 290 us -> 341 us (1.18)
  starting transfers between devices: 97.5 us -> 167 us
  waiting for transfers between devices: 125 us -> 81.8 us
  local copies, waits for them, and re-layouts: 35.4 us -> 50.8 us
  matrix products: 12.9 us -> 19.1 us
    ppermute x18 -> x36, starting transfers between devices: 59.4 us -> 118 us  [shift(): return lax.ppermute(value, axis_name, pairs)]
    all_to_all x1, waiting for transfers between devices: 21.3 us -> 0.01 us  [shards(): lax.all_to_all(jnp.concatenate([out_block, log_row], axis=1), 'seq', spli...]
    all_to_all x1, waiting for transfers between devices: 16.5 us -> 0.01 us  [shards(): lax.all_to_all(outgoing, 'seq', split_axis=0, concat_axis=0, tiled=True)]
    unnamed x46 -> x82, local copies, waits for them, and re-layouts: 15.4 us -> 27.4 us
    all_to_all x1, starting transfers between devices: 4.63 us -> 15.2 us  [shards(): lax.all_to_all(jnp.concatenate([out_block, log_row], axis=1), 'seq', spli...]
    ppermute x18 -> x36, waiting for transfers between devices: 73 us -> 67.4 us  [shift(): return lax.ppermute(value, axis_name, pairs)]
    dot_general x8, matrix products: 2.07 us -> 6.28 us  [attend(): result = jnp.dot(weights, values, preferred_element_type=jnp.float32)]
  transfers between devices with their start and end apart: 22 -> 40, of which waited for: 13 -> 24; matrix products, arithmetic and copies ran while one was open for 7% -> 14% of each run, Pallas kernels for 0% -> 0%
where the time goes in v5:
time: 341 us; the launch traced here: 339 us
  starting transfers between devices  167 us (49%)
  waiting for transfers between devices  81.8 us (24%)
  local copies, waits for them, and re-layouts  50.8 us (15%)
  matrix products  19.1 us (6%)
  other arithmetic  18.2 us (5%)
    ppermute x36, starting transfers between devices, shift(): return lax.ppermute(value, axis_name, pairs)  118 us
    ppermute x36, waiting for transfers between devices, shift(): return lax.ppermute(value, axis_name, pairs)  67.4 us
    unnamed x82, local copies, waits for them, and re-layouts  27.4 us
    all_to_all x1, starting transfers between devices, shards(): lax.all_to_all(jnp.concatenate([out_block, log_row], axis=1), 'seq', spli...  15.2 us
    all_to_all x1, waiting for transfers between devices, shards(): lax.all_to_all(jnp.moveaxis(pieces, 1, 0), 'tensor', split_axis=0, concat...  14.4 us
    all_to_all x1, starting transfers between devices, shards(): lax.all_to_all(jnp.moveaxis(pieces, 1, 0), 'tensor', split_axis=0, concat...  14.4 us
    all_to_all x1, starting transfers between devices, shards(): lax.all_to_all(tiles, 'tensor', split_axis=0, concat_axis=0, tiled=True)  10 us
    all_to_all x1, starting transfers between devices, shards(): lax.all_to_all(outgoing, 'seq', split_axis=0, concat_axis=0, tiled=True)  8.74 us
  transfers between devices with their start and end apart: 40, of which 24 were waited for; matrix products, arithmetic and copies ran while one was open for 14% of the time, Pallas kernels for 0%

profile of v5, /device:TPU:1, one launch (start us, length us, event | category | flops | bytes accessed | tf_op | source)
XLA Modules:
  0.0 338.5 jit_solution(8935151727402957613)
XLA Ops:
  3.0 4.0 %collective-permute-start.1 = (bf16[768,64]{0,1:T(8,128)(2,1)}, bf16[768,64]{0,1:T(8,128)(2,1)S(1)}, u32[]{:S(2)}, u32[]{:S(2)}) collective-permute-start(bf16[768,64]{0,1:T(8,128)(2,1)} %get-tuple-element.26), channel_id=1, source_target_pairs={{0,8},{8,16},{16,24},{24,0},{32,40},{40,48},{48,56},{56,32},{64,72... | collective-permute-start | bytes 294920 | tf_op jit(solution)/shard_map/ppermute | solution.py:79
  12.6 10.0 %all-to-all-start = ((bf16[8,128,512]{1,2,0:T(8,128)(2,1)}), bf16[8,128,512]{1,2,0:T(8,128)(2,1)S(1)}, u32[]{:S(2)}, u32[]{:S(2)}) async-start(bf16[8,128,512]{1,2,0:T(8,128)(2,1)} %broadcast_in_dim.72), calls=%async_computation | async-start | bytes 2097152 | tf_op jit(solution)/shard_map/all_to_all | solution.py:102
  27.2 5.4 %collective-permute-done.2 = bf16[768,64]{0,1:T(8,128)(2,1)S(1)} collective-permute-done((bf16[768,64]{0,1:T(8,128)(2,1)S(1)}, bf16[768,64]{0,1:T(8,128)(2,1)S(1)}, u32[]{:S(2)}, u32[]{:S(2)}) %collective-permute-start.2) | collective-permute-done | bytes 98336 | tf_op jit(solution)/shard_map/ppermute | solution.py:79
  36.2 6.6 %collective-permute-start.3 = (bf16[768,4,64]{0,2,1:T(8,128)(2,1)S(1)}, bf16[768,4,64]{0,2,1:T(8,128)(2,1)}, u32[]{:S(2)}, u32[]{:S(2)}) collective-permute-start(bf16[768,4,64]{0,2,1:T(8,128)(2,1)S(1)} %pad_maximum_fusion), channel_id=1, source_target_pairs={{0,480},{8,488},{16,496},{24,504},{32,0},{40,8},{48,16},{56,24},{6... | collective-permute-start | bytes 1179656 | tf_op jit(solution)/shard_map/ppermute | solution.py:79
  43.7 6.0 %collective-permute-done.10 = bf16[768,4,64]{0,2,1:T(8,128)(2,1)} collective-permute-done((bf16[768,4,64]{0,2,1:T(8,128)(2,1)S(1)}, bf16[768,4,64]{0,2,1:T(8,128)(2,1)}, u32[]{:S(2)}, u32[]{:S(2)}) %collective-permute-start.10) | collective-permute-done | bytes 393248 | tf_op jit(solution)/shard_map/ppermute | solution.py:79
  51.7 4.6 %collective-permute-start.4 = (bf16[768,4,64]{0,2,1:T(8,128)(2,1)}, bf16[768,4,64]{0,2,1:T(8,128)(2,1)}, u32[]{:S(2)}, u32[]{:S(2)}) collective-permute-start(bf16[768,4,64]{0,2,1:T(8,128)(2,1)} %collective-permute-done.3), channel_id=1, source_target_pairs={{0,480},{8,488},{16,496},{24,504},{32,0},{40,8},{48,16},{56,24},{6... | collective-permute-start | bytes 1179656 | tf_op jit(solution)/shard_map/ppermute | solution.py:79
  56.4 5.9 %collective-permute-done.11 = bf16[768,4,64]{0,2,1:T(8,128)(2,1)} collective-permute-done((bf16[768,4,64]{0,2,1:T(8,128)(2,1)}, bf16[768,4,64]{0,2,1:T(8,128)(2,1)}, u32[]{:S(2)}, u32[]{:S(2)}) %collective-permute-start.11) | collective-permute-done | bytes 393248 | tf_op jit(solution)/shard_map/ppermute | solution.py:79
  69.5 4.6 %collective-permute-start.5 = (bf16[768,4,64]{0,2,1:T(8,128)(2,1)}, bf16[768,4,64]{0,2,1:T(8,128)(2,1)S(1)}, u32[]{:S(2)}, u32[]{:S(2)}) collective-permute-start(bf16[768,4,64]{0,2,1:T(8,128)(2,1)} %collective-permute-done.4), channel_id=1, source_target_pairs={{0,480},{8,488},{16,496},{24,504},{32,0},{40,8},{48,16},{56,24},{6... | collective-permute-start | bytes 1179656 | tf_op jit(solution)/shard_map/ppermute | solution.py:79
  80.2 5.2 %collective-permute-start.6 = (bf16[768,4,64]{0,2,1:T(8,128)(2,1)S(1)}, bf16[768,4,64]{0,2,1:T(8,128)(2,1)S(1)}, u32[]{:S(2)}, u32[]{:S(2)}) collective-permute-start(bf16[768,4,64]{0,2,1:T(8,128)(2,1)S(1)} %collective-permute-done.5), channel_id=1, source_target_pairs={{0,480},{8,488},{16,496},{24,504},{32,0},{40,8},{48,16},{56,24},{6... | collective-permute-start | bytes 1179656 | tf_op jit(solution)/shard_map/ppermute | solution.py:79
  90.1 5.5 %collective-permute-start.7 = (bf16[768,4,64]{0,2,1:T(8,128)(2,1)S(1)}, bf16[768,4,64]{0,2,1:T(8,128)(2,1)S(1)}, u32[]{:S(2)}, u32[]{:S(2)}) collective-permute-start(bf16[768,4,64]{0,2,1:T(8,128)(2,1)S(1)} %collective-permute-done.6), channel_id=1, source_target_pairs={{0,480},{8,488},{16,496},{24,504},{32,0},{40,8},{48,16},{56,24},{6... | collective-permute-start | bytes 1179656 | tf_op jit(solution)/shard_map/ppermute | solution.py:79
  100.3 5.0 %collective-permute-start.8 = (bf16[768,4,64]{0,2,1:T(8,128)(2,1)S(1)}, bf16[768,4,64]{0,2,1:T(8,128)(2,1)S(1)}, u32[]{:S(2)}, u32[]{:S(2)}) collective-permute-start(bf16[768,4,64]{0,2,1:T(8,128)(2,1)S(1)} %collective-permute-done.7), channel_id=1, source_target_pairs={{0,480},{8,488},{16,496},{24,504},{32,0},{40,8},{48,16},{56,24},{6... | collective-permute-start | bytes 1179656 | tf_op jit(solution)/shard_map/ppermute | solution.py:79
  110.0 5.0 %collective-permute-start.9 = (bf16[768,4,64]{0,2,1:T(8,128)(2,1)S(1)}, bf16[768,4,64]{0,2,1:T(8,128)(2,1)S(1)}, u32[]{:S(2)}, u32[]{:S(2)}) collective-permute-start(bf16[768,4,64]{0,2,1:T(8,128)(2,1)S(1)} %collective-permute-done.8), channel_id=1, source_target_pairs={{0,480},{8,488},{16,496},{24,504},{32,0},{40,8},{48,16},{56,24},{6... | collective-permute-start | bytes 1179656 | tf_op jit(solution)/shard_map/ppermute | solution.py:79
  120.3 6.6 %collective-permute-done.17 = bf16[768,4,64]{0,2,1:T(8,128)(2,1)S(1)} collective-permute-done((bf16[768,4,64]{0,2,1:T(8,128)(2,1)S(1)}, bf16[768,4,64]{0,2,1:T(8,128)(2,1)S(1)}, u32[]{:S(2)}, u32[]{:S(2)}) %collective-permute-start.17) | collective-permute-done | bytes 393248 | tf_op jit(solution)/shard_map/ppermute | solution.py:79
  137.7 4.7 %slice.96 = bf16[512,16,4,64]{0,3,2,1:T(8,128)(2,1)} slice(bf16[768,16,4,64]{0,3,2,1:T(8,128)(2,1)} %copy-done.2), slice={[0:512], [0:16], [0:4], [0:64]} | slice | bytes 8388608 | tf_op jit(solution)/shard_map/slice | solution.py:121
  142.6 6.9 %dot_general.65 = bf16[4,128,4096]{1,0,2:T(4,128)(2,1)} reshape(bf16[512,16,4,64]{0,3,2,1:T(8,128)(2,1)} %slice.96) | data formatting | bytes 8388608 | tf_op jit(solution)/shard_map/dot_general | solution.py:128
  149.5 3.9 %fusion.2 = f32[128,4,128]{0,2,1:T(8,128)S(1)} fusion(bf16[128,4096,1]{0,1,2:T(8,128)(2,1)S(1)} %bitcast.259, bf16[4,128,4096]{1,0,2:T(4,128)(2,1)} %dot_general.65), kind=kOutput, calls=%fused_computation.9 | convolution fusion | flops 536870912 | bytes 5505024 | tf_op jit(solution)/shard_map/dot_general | solution.py:128
  159.3 4.6 %collective-permute-start.18 = (bf16[512,64]{0,1:T(8,128)(2,1)S(1)}, bf16[512,64]{0,1:T(8,128)(2,1)S(1)}, u32[]{:S(2)}, u32[]{:S(2)}) collective-permute-start(bf16[512,64]{0,1:T(8,128)(2,1)S(1)} %copy-done.6), channel_id=1, source_target_pairs={{0,24},{8,0},{16,8},{24,16},{32,56},{40,32},{48,40},{56,48},{64,88... | collective-permute-start | bytes 196616 | tf_op jit(solution)/shard_map/ppermute | solution.py:79
  164.7 8.7 %all-to-all-start.1 = ((bf16[64,4,512]{2,1,0:T(4,128)(2,1)}), bf16[64,4,512]{2,1,0:T(4,128)(2,1)S(1)}, u32[]{:S(2)}, u32[]{:S(2)}) async-start(bf16[64,4,512]{2,1,0:T(4,128)(2,1)} %broadcast_select_fusion), calls=%async_computation.1 | async-start | bytes 524288 | tf_op jit(solution)/shard_map/all_to_all | solution.py:168
  181.5 4.3 %collective-permute-start.21 = (bf16[512,4,64]{0,2,1:T(8,128)(2,1)S(1)}, bf16[512,4,64]{0,2,1:T(8,128)(2,1)S(1)}, u32[]{:S(2)}, u32[]{:S(2)}) collective-permute-start(bf16[512,4,64]{0,2,1:T(8,128)(2,1)S(1)} %pad_maximum_fusion.2), channel_id=1, source_target_pairs={{0,480},{8,488},{16,496},{24,504},{32,0},{40,8},{48,16},{56,24},{6... | collective-permute-start | bytes 786440 | tf_op jit(solution)/shard_map/ppermute | solution.py:79
  189.7 3.7 %collective-permute-done.21 = bf16[512,4,64]{0,2,1:T(8,128)(2,1)S(1)} collective-permute-done((bf16[512,4,64]{0,2,1:T(8,128)(2,1)S(1)}, bf16[512,4,64]{0,2,1:T(8,128)(2,1)S(1)}, u32[]{:S(2)}, u32[]{:S(2)}) %collective-permute-start.21) | collective-permute-done | bytes 262176 | tf_op jit(solution)/shard_map/ppermute | solution.py:79
  193.4 3.8 %collective-permute-start.22 = (bf16[512,4,64]{0,2,1:T(8,128)(2,1)S(1)}, bf16[512,4,64]{0,2,1:T(8,128)(2,1)S(1)}, u32[]{:S(2)}, u32[]{:S(2)}) collective-permute-start(bf16[512,4,64]{0,2,1:T(8,128)(2,1)S(1)} %collective-permute-done.21), channel_id=1, source_target_pairs={{0,480},{8,488},{16,496},{24,504},{32,0},{40,8},{48,16},{56,24},{6... | collective-permute-start | bytes 786440 | tf_op jit(solution)/shard_map/ppermute | solution.py:79
  203.3 5.1 %collective-permute-start.23 = (bf16[512,4,64]{0,2,1:T(8,128)(2,1)S(1)}, bf16[512,4,64]{0,2,1:T(8,128)(2,1)}, u32[]{:S(2)}, u32[]{:S(2)}) collective-permute-start(bf16[512,4,64]{0,2,1:T(8,128)(2,1)S(1)} %collective-permute-done.22), channel_id=1, source_target_pairs={{0,480},{8,488},{16,496},{24,504},{32,0},{40,8},{48,16},{56,24},{6... | collective-permute-start | bytes 786440 | tf_op jit(solution)/shard_map/ppermute | solution.py:79
  213.6 5.3 %collective-permute-start.24 = (bf16[512,4,64]{0,2,1:T(8,128)(2,1)}, bf16[512,4,64]{0,2,1:T(8,128)(2,1)}, u32[]{:S(2)}, u32[]{:S(2)}) collective-permute-start(bf16[512,4,64]{0,2,1:T(8,128)(2,1)} %collective-permute-done.23), channel_id=1, source_target_pairs={{0,480},{8,488},{16,496},{24,504},{32,0},{40,8},{48,16},{56,24},{6... | collective-permute-start | bytes 786440 | tf_op jit(solution)/shard_map/ppermute | solution.py:79
  230.3 4.6 %collective-permute-start.25 = (bf16[512,4,64]{0,2,1:T(8,128)(2,1)}, bf16[512,4,64]{0,2,1:T(8,128)(2,1)S(1)}, u32[]{:S(2)}, u32[]{:S(2)}) collective-permute-start(bf16[512,4,64]{0,2,1:T(8,128)(2,1)} %collective-permute-done.24), channel_id=1, source_target_pairs={{0,480},{8,488},{16,496},{24,504},{32,0},{40,8},{48,16},{56,24},{6... | collective-permute-start | bytes 786440 | tf_op jit(solution)/shard_map/ppermute | solution.py:79
  239.3 4.6 %collective-permute-start.26 = (bf16[512,4,64]{0,2,1:T(8,128)(2,1)S(1)}, bf16[512,4,64]{0,2,1:T(8,128)(2,1)S(1)}, u32[]{:S(2)}, u32[]{:S(2)}) collective-permute-start(bf16[512,4,64]{0,2,1:T(8,128)(2,1)S(1)} %collective-permute-done.25), channel_id=1, source_target_pairs={{0,480},{8,488},{16,496},{24,504},{32,0},{40,8},{48,16},{56,24},{6... | collective-permute-start | bytes 786440 | tf_op jit(solution)/shard_map/ppermute | solution.py:79
  244.9 15.2 %all-to-all-start.2 = ((bf16[64,5,512]{2,1,0:T(8,128)(2,1)}), bf16[64,5,512]{2,1,0:T(8,128)(2,1)S(1)}, u32[]{:S(2)}, u32[]{:S(2)}) async-start(bf16[64,5,512]{2,1,0:T(8,128)(2,1)} %fusion.27), calls=%async_computation.2 | async-start | bytes 1048576 | tf_op jit(solution)/shard_map/all_to_all | solution.py:186
  264.7 3.7 %collective-permute-start.27 = (bf16[512,4,64]{0,2,1:T(8,128)(2,1)S(1)}, bf16[512,4,64]{0,2,1:T(8,128)(2,1)S(1)}, u32[]{:S(2)}, u32[]{:S(2)}) collective-permute-start(bf16[512,4,64]{0,2,1:T(8,128)(2,1)S(1)} %collective-permute-done.26), channel_id=1, source_target_pairs={{0,480},{8,488},{16,496},{24,504},{32,0},{40,8},{48,16},{56,24},{6... | collective-permute-start | bytes 786440 | tf_op jit(solution)/shard_map/ppermute | solution.py:79
  269.2 9.1 %collective-permute-done.34 = bf16[512,4,64]{0,2,1:T(8,128)(2,1)S(1)} collective-permute-done((bf16[512,4,64]{0,2,1:T(8,128)(2,1)S(1)}, bf16[512,4,64]{0,2,1:T(8,128)(2,1)S(1)}, u32[]{:S(2)}, u32[]{:S(2)}) %collective-permute-start.34) | collective-permute-done | bytes 262176 | tf_op jit(solution)/shard_map/ppermute | solution.py:79
  285.0 9.0 %collective-permute-done.35 = bf16[512,4,64]{0,2,1:T(8,128)(2,1)S(1)} collective-permute-done((bf16[512,4,64]{0,2,1:T(8,128)(2,1)S(1)}, bf16[512,4,64]{0,2,1:T(8,128)(2,1)S(1)}, u32[]{:S(2)}, u32[]{:S(2)}) %collective-permute-start.35) | collective-permute-done | bytes 262176 | tf_op jit(solution)/shard_map/ppermute | solution.py:79
  303.0 3.4 %fusion = bf16[128,16,4,64]{0,3,2,1:T(8,128)(2,1)S(1)} fusion(bf16[128,512,1,1]{0,1,3,2:T(8,128)(2,1)S(1)} %bitcast.261, bf16[512,16,4,64]{0,3,2,1:T(8,128)(2,1)} %bitcast_dynamic-update-slice_fusion.16), kind=kOutput, calls=%fused_computation.7 | convolution fusion | flops 536870912 | bytes 5373952 | tf_op jit(solution)/shard_map/dot_general | solution.py:221
  308.2 14.4 %all-to-all-start.3 = ((bf16[8,128,512]{1,2,0:T(8,128)(2,1)}), bf16[8,128,512]{1,2,0:T(8,128)(2,1)S(1)}, u32[]{:S(2)}, u32[]{:S(2)}) async-start(bf16[8,128,512]{1,2,0:T(8,128)(2,1)} %bitcast.85), calls=%async_computation.3 | async-start | bytes 2097152 | tf_op jit(solution)/shard_map/all_to_all | solution.py:226
  323.3 14.4 %all-to-all-done.3 = bf16[8,128,512]{1,2,0:T(8,128)(2,1)S(1)} async-done(((bf16[8,128,512]{1,2,0:T(8,128)(2,1)}), bf16[8,128,512]{1,2,0:T(8,128)(2,1)S(1)}, u32[]{:S(2)}, u32[]{:S(2)}) %all-to-all-start.3) | async-done | bytes 1048608 | tf_op jit(solution)/shard_map/all_to_all | solution.py:226
  (240 shorter events, 132.7 us)
Async XLA Ops:
  3.0 22.1 %collective-permute-start.1 = (bf16[768,64]{0,1:T(8,128)(2,1)}, bf16[768,64]{0,1:T(8,128)(2,1)S(1)}, u32[]{:S(2)}, u32[]{:S(2)}) collective-permute-start(bf16[768,64]{0,1:T(8,128)(2,1)} %get-tuple-element.26), channel_id=1, source_target_pairs={{0,8},{8,16},{16,24},{24,0},{32,40},{40,48},{48,56},{56,32},{64,72... | collective-permute-start | bytes 294920 | tf_op jit(solution)/shard_map/ppermute | solution.py:79
  7.1 20.1 %collective-permute-start = (bf16[768,64]{0,1:T(8,128)(2,1)}, bf16[768,64]{0,1:T(8,128)(2,1)}, u32[]{:S(2)}, u32[]{:S(2)}) collective-permute-start(bf16[768,64]{0,1:T(8,128)(2,1)} %get-tuple-element.26), channel_id=1, source_target_pairs={{0,24},{8,0},{16,8},{24,16},{32,56},{40,32},{48,40},{56,48},{64,88... | collective-permute-start | bytes 294920 | tf_op jit(solution)/shard_map/ppermute | solution.py:79
  12.6 65.1 %all-to-all-start = ((bf16[8,128,512]{1,2,0:T(8,128)(2,1)}), bf16[8,128,512]{1,2,0:T(8,128)(2,1)S(1)}, u32[]{:S(2)}, u32[]{:S(2)}) async-start(bf16[8,128,512]{1,2,0:T(8,128)(2,1)} %broadcast_in_dim.72), calls=%async_computation | async-start | bytes 2097152 | tf_op jit(solution)/shard_map/all_to_all | solution.py:102
  34.2 15.5 %collective-permute-start.10 = (bf16[768,4,64]{0,2,1:T(8,128)(2,1)S(1)}, bf16[768,4,64]{0,2,1:T(8,128)(2,1)}, u32[]{:S(2)}, u32[]{:S(2)}) collective-permute-start(bf16[768,4,64]{0,2,1:T(8,128)(2,1)S(1)} %pad_maximum_fusion), channel_id=1, source_target_pairs={{0,32},{8,40},{16,48},{24,56},{32,64},{40,72},{48,80},{56,88},{64,... | collective-permute-start | bytes 1179656 | tf_op jit(solution)/shard_map/ppermute | solution.py:79
  36.2 15.5 %collective-permute-start.3 = (bf16[768,4,64]{0,2,1:T(8,128)(2,1)S(1)}, bf16[768,4,64]{0,2,1:T(8,128)(2,1)}, u32[]{:S(2)}, u32[]{:S(2)}) collective-permute-start(bf16[768,4,64]{0,2,1:T(8,128)(2,1)S(1)} %pad_maximum_fusion), channel_id=1, source_target_pairs={{0,480},{8,488},{16,496},{24,504},{32,0},{40,8},{48,16},{56,24},{6... | collective-permute-start | bytes 1179656 | tf_op jit(solution)/shard_map/ppermute | solution.py:79
  49.7 12.7 %collective-permute-start.11 = (bf16[768,4,64]{0,2,1:T(8,128)(2,1)}, bf16[768,4,64]{0,2,1:T(8,128)(2,1)}, u32[]{:S(2)}, u32[]{:S(2)}) collective-permute-start(bf16[768,4,64]{0,2,1:T(8,128)(2,1)} %collective-permute-done.10), channel_id=1, source_target_pairs={{0,32},{8,40},{16,48},{24,56},{32,64},{40,72},{48,80},{56,88},{64,... | collective-permute-start | bytes 1179656 | tf_op jit(solution)/shard_map/ppermute | solution.py:79
  51.7 17.7 %collective-permute-start.4 = (bf16[768,4,64]{0,2,1:T(8,128)(2,1)}, bf16[768,4,64]{0,2,1:T(8,128)(2,1)}, u32[]{:S(2)}, u32[]{:S(2)}) collective-permute-start(bf16[768,4,64]{0,2,1:T(8,128)(2,1)} %collective-permute-done.3), channel_id=1, source_target_pairs={{0,480},{8,488},{16,496},{24,504},{32,0},{40,8},{48,16},{56,24},{6... | collective-permute-start | bytes 1179656 | tf_op jit(solution)/shard_map/ppermute | solution.py:79
  62.4 13.4 %collective-permute-start.12 = (bf16[768,4,64]{0,2,1:T(8,128)(2,1)}, bf16[768,4,64]{0,2,1:T(8,128)(2,1)}, u32[]{:S(2)}, u32[]{:S(2)}) collective-permute-start(bf16[768,4,64]{0,2,1:T(8,128)(2,1)} %collective-permute-done.11), channel_id=1, source_target_pairs={{0,32},{8,40},{16,48},{24,56},{32,64},{40,72},{48,80},{56,88},{64,... | collective-permute-start | bytes 1179656 | tf_op jit(solution)/shard_map/ppermute | solution.py:79
  69.5 10.7 %collective-permute-start.5 = (bf16[768,4,64]{0,2,1:T(8,128)(2,1)}, bf16[768,4,64]{0,2,1:T(8,128)(2,1)S(1)}, u32[]{:S(2)}, u32[]{:S(2)}) collective-permute-start(bf16[768,4,64]{0,2,1:T(8,128)(2,1)} %collective-permute-done.4), channel_id=1, source_target_pairs={{0,480},{8,488},{16,496},{24,504},{32,0},{40,8},{48,16},{56,24},{6... | collective-permute-start | bytes 1179656 | tf_op jit(solution)/shard_map/ppermute | solution.py:79
  75.8 11.1 %collective-permute-start.13 = (bf16[768,4,64]{0,2,1:T(8,128)(2,1)}, bf16[768,4,64]{0,2,1:T(8,128)(2,1)S(1)}, u32[]{:S(2)}, u32[]{:S(2)}) collective-permute-start(bf16[768,4,64]{0,2,1:T(8,128)(2,1)} %collective-permute-done.12), channel_id=1, source_target_pairs={{0,32},{8,40},{16,48},{24,56},{32,64},{40,72},{48,80},{56,88},{64,... | collective-permute-start | bytes 1179656 | tf_op jit(solution)/shard_map/ppermute | solution.py:79
  80.2 9.9 %collective-permute-start.6 = (bf16[768,4,64]{0,2,1:T(8,128)(2,1)S(1)}, bf16[768,4,64]{0,2,1:T(8,128)(2,1)S(1)}, u32[]{:S(2)}, u32[]{:S(2)}) collective-permute-start(bf16[768,4,64]{0,2,1:T(8,128)(2,1)S(1)} %collective-permute-done.5), channel_id=1, source_target_pairs={{0,480},{8,488},{16,496},{24,504},{32,0},{40,8},{48,16},{56,24},{6... | collective-permute-start | bytes 1179656 | tf_op jit(solution)/shard_map/ppermute | solution.py:79
  86.9 9.9 %collective-permute-start.14 = (bf16[768,4,64]{0,2,1:T(8,128)(2,1)S(1)}, bf16[768,4,64]{0,2,1:T(8,128)(2,1)S(1)}, u32[]{:S(2)}, u32[]{:S(2)}) collective-permute-start(bf16[768,4,64]{0,2,1:T(8,128)(2,1)S(1)} %collective-permute-done.13), channel_id=1, source_target_pairs={{0,32},{8,40},{16,48},{24,56},{32,64},{40,72},{48,80},{56,88},{64,... | collective-permute-start | bytes 1179656 | tf_op jit(solution)/shard_map/ppermute | solution.py:79
  90.1 10.2 %collective-permute-start.7 = (bf16[768,4,64]{0,2,1:T(8,128)(2,1)S(1)}, bf16[768,4,64]{0,2,1:T(8,128)(2,1)S(1)}, u32[]{:S(2)}, u32[]{:S(2)}) collective-permute-start(bf16[768,4,64]{0,2,1:T(8,128)(2,1)S(1)} %collective-permute-done.6), channel_id=1, source_target_pairs={{0,480},{8,488},{16,496},{24,504},{32,0},{40,8},{48,16},{56,24},{6... | collective-permute-start | bytes 1179656 | tf_op jit(solution)/shard_map/ppermute | solution.py:79
  110.0 10.2 %collective-permute-start.9 = (bf16[768,4,64]{0,2,1:T(8,128)(2,1)S(1)}, bf16[768,4,64]{0,2,1:T(8,128)(2,1)S(1)}, u32[]{:S(2)}, u32[]{:S(2)}) collective-permute-start(bf16[768,4,64]{0,2,1:T(8,128)(2,1)S(1)} %collective-permute-done.8), channel_id=1, source_target_pairs={{0,480},{8,488},{16,496},{24,504},{32,0},{40,8},{48,16},{56,24},{6... | collective-permute-start | bytes 1179656 | tf_op jit(solution)/shard_map/ppermute | solution.py:79
  116.2 10.7 %collective-permute-start.17 = (bf16[768,4,64]{0,2,1:T(8,128)(2,1)S(1)}, bf16[768,4,64]{0,2,1:T(8,128)(2,1)S(1)}, u32[]{:S(2)}, u32[]{:S(2)}) collective-permute-start(bf16[768,4,64]{0,2,1:T(8,128)(2,1)S(1)} %collective-permute-done.16), channel_id=1, source_target_pairs={{0,32},{8,40},{16,48},{24,56},{32,64},{40,72},{48,80},{56,88},{64,... | collective-permute-start | bytes 1179656 | tf_op jit(solution)/shard_map/ppermute | solution.py:79
  157.4 17.5 %collective-permute-start.19 = (bf16[512,64]{0,1:T(8,128)(2,1)S(1)}, bf16[512,64]{0,1:T(8,128)(2,1)S(1)}, u32[]{:S(2)}, u32[]{:S(2)}) collective-permute-start(bf16[512,64]{0,1:T(8,128)(2,1)S(1)} %copy-done.6), channel_id=1, source_target_pairs={{0,8},{8,16},{16,24},{24,0},{32,40},{40,48},{48,56},{56,32},{64,72... | collective-permute-start | bytes 196616 | tf_op jit(solution)/shard_map/ppermute | solution.py:79
  159.3 18.7 %collective-permute-start.18 = (bf16[512,64]{0,1:T(8,128)(2,1)S(1)}, bf16[512,64]{0,1:T(8,128)(2,1)S(1)}, u32[]{:S(2)}, u32[]{:S(2)}) collective-permute-start(bf16[512,64]{0,1:T(8,128)(2,1)S(1)} %copy-done.6), channel_id=1, source_target_pairs={{0,24},{8,0},{16,8},{24,16},{32,56},{40,32},{48,40},{56,48},{64,88... | collective-permute-start | bytes 196616 | tf_op jit(solution)/shard_map/ppermute | solution.py:79
  164.7 57.9 %all-to-all-start.1 = ((bf16[64,4,512]{2,1,0:T(4,128)(2,1)}), bf16[64,4,512]{2,1,0:T(4,128)(2,1)S(1)}, u32[]{:S(2)}, u32[]{:S(2)}) async-start(bf16[64,4,512]{2,1,0:T(4,128)(2,1)} %broadcast_select_fusion), calls=%async_computation.1 | async-start | bytes 524288 | tf_op jit(solution)/shard_map/all_to_all | solution.py:168
  181.5 12.0 %collective-permute-start.21 = (bf16[512,4,64]{0,2,1:T(8,128)(2,1)S(1)}, bf16[512,4,64]{0,2,1:T(8,128)(2,1)S(1)}, u32[]{:S(2)}, u32[]{:S(2)}) collective-permute-start(bf16[512,4,64]{0,2,1:T(8,128)(2,1)S(1)} %pad_maximum_fusion.2), channel_id=1, source_target_pairs={{0,480},{8,488},{16,496},{24,504},{32,0},{40,8},{48,16},{56,24},{6... | collective-permute-start | bytes 786440 | tf_op jit(solution)/shard_map/ppermute | solution.py:79
  185.8 11.4 %collective-permute-start.28 = (bf16[512,4,64]{0,2,1:T(8,128)(2,1)S(1)}, bf16[512,4,64]{0,2,1:T(8,128)(2,1)S(1)}, u32[]{:S(2)}, u32[]{:S(2)}) collective-permute-start(bf16[512,4,64]{0,2,1:T(8,128)(2,1)S(1)} %pad_maximum_fusion.2), channel_id=1, source_target_pairs={{0,32},{8,40},{16,48},{24,56},{32,64},{40,72},{48,80},{56,88},{64,... | collective-permute-start | bytes 786440 | tf_op jit(solution)/shard_map/ppermute | solution.py:79
  193.4 9.8 %collective-permute-start.22 = (bf16[512,4,64]{0,2,1:T(8,128)(2,1)S(1)}, bf16[512,4,64]{0,2,1:T(8,128)(2,1)S(1)}, u32[]{:S(2)}, u32[]{:S(2)}) collective-permute-start(bf16[512,4,64]{0,2,1:T(8,128)(2,1)S(1)} %collective-permute-done.21), channel_id=1, source_target_pairs={{0,480},{8,488},{16,496},{24,504},{32,0},{40,8},{48,16},{56,24},{6... | collective-permute-start | bytes 786440 | tf_op jit(solution)/shard_map/ppermute | solution.py:79
  197.2 11.3 %collective-permute-start.29 = (bf16[512,4,64]{0,2,1:T(8,128)(2,1)S(1)}, bf16[512,4,64]{0,2,1:T(8,128)(2,1)S(1)}, u32[]{:S(2)}, u32[]{:S(2)}) collective-permute-start(bf16[512,4,64]{0,2,1:T(8,128)(2,1)S(1)} %collective-permute-done.28), channel_id=1, source_target_pairs={{0,32},{8,40},{16,48},{24,56},{32,64},{40,72},{48,80},{56,88},{64,... | collective-permute-start | bytes 786440 | tf_op jit(solution)/shard_map/ppermute | solution.py:79
  203.3 10.4 %collective-permute-start.23 = (bf16[512,4,64]{0,2,1:T(8,128)(2,1)S(1)}, bf16[512,4,64]{0,2,1:T(8,128)(2,1)}, u32[]{:S(2)}, u32[]{:S(2)}) collective-permute-start(bf16[512,4,64]{0,2,1:T(8,128)(2,1)S(1)} %collective-permute-done.22), channel_id=1, source_target_pairs={{0,480},{8,488},{16,496},{24,504},{32,0},{40,8},{48,16},{56,24},{6... | collective-permute-start | bytes 786440 | tf_op jit(solution)/shard_map/ppermute | solution.py:79
  208.5 10.4 %collective-permute-start.30 = (bf16[512,4,64]{0,2,1:T(8,128)(2,1)S(1)}, bf16[512,4,64]{0,2,1:T(8,128)(2,1)S(1)}, u32[]{:S(2)}, u32[]{:S(2)}) collective-permute-start(bf16[512,4,64]{0,2,1:T(8,128)(2,1)S(1)} %collective-permute-done.29), channel_id=1, source_target_pairs={{0,32},{8,40},{16,48},{24,56},{32,64},{40,72},{48,80},{56,88},{64,... | collective-permute-start | bytes 786440 | tf_op jit(solution)/shard_map/ppermute | solution.py:79
  213.6 16.6 %collective-permute-start.24 = (bf16[512,4,64]{0,2,1:T(8,128)(2,1)}, bf16[512,4,64]{0,2,1:T(8,128)(2,1)}, u32[]{:S(2)}, u32[]{:S(2)}) collective-permute-start(bf16[512,4,64]{0,2,1:T(8,128)(2,1)} %collective-permute-done.23), channel_id=1, source_target_pairs={{0,480},{8,488},{16,496},{24,504},{32,0},{40,8},{48,16},{56,24},{6... | collective-permute-start | bytes 786440 | tf_op jit(solution)/shard_map/ppermute | solution.py:79
  236.9 23.2 %collective-permute-start.33 = (bf16[512,4,64]{0,2,1:T(8,128)(2,1)S(1)}, bf16[512,4,64]{0,2,1:T(8,128)(2,1)S(1)}, u32[]{:S(2)}, u32[]{:S(2)}) collective-permute-start(bf16[512,4,64]{0,2,1:T(8,128)(2,1)S(1)} %collective-permute-done.32), channel_id=1, source_target_pairs={{0,32},{8,40},{16,48},{24,56},{32,64},{40,72},{48,80},{56,88},{64,... | collective-permute-start | bytes 786440 | tf_op jit(solution)/shard_map/ppermute | solution.py:79
  239.3 25.4 %collective-permute-start.26 = (bf16[512,4,64]{0,2,1:T(8,128)(2,1)S(1)}, bf16[512,4,64]{0,2,1:T(8,128)(2,1)S(1)}, u32[]{:S(2)}, u32[]{:S(2)}) collective-permute-start(bf16[512,4,64]{0,2,1:T(8,128)(2,1)S(1)} %collective-permute-done.25), channel_id=1, source_target_pairs={{0,480},{8,488},{16,496},{24,504},{32,0},{40,8},{48,16},{56,24},{6... | collective-permute-start | bytes 786440 | tf_op jit(solution)/shard_map/ppermute | solution.py:79
  244.9 55.9 %all-to-all-start.2 = ((bf16[64,5,512]{2,1,0:T(8,128)(2,1)}), bf16[64,5,512]{2,1,0:T(8,128)(2,1)S(1)}, u32[]{:S(2)}, u32[]{:S(2)}) async-start(bf16[64,5,512]{2,1,0:T(8,128)(2,1)} %fusion.27), calls=%async_computation.2 | async-start | bytes 1048576 | tf_op jit(solution)/shard_map/all_to_all | solution.py:186
  260.1 18.2 %collective-permute-start.34 = (bf16[512,4,64]{0,2,1:T(8,128)(2,1)S(1)}, bf16[512,4,64]{0,2,1:T(8,128)(2,1)S(1)}, u32[]{:S(2)}, u32[]{:S(2)}) collective-permute-start(bf16[512,4,64]{0,2,1:T(8,128)(2,1)S(1)} %collective-permute-done.33), channel_id=1, source_target_pairs={{0,32},{8,40},{16,48},{24,56},{32,64},{40,72},{48,80},{56,88},{64,... | collective-permute-start | bytes 786440 | tf_op jit(solution)/shard_map/ppermute | solution.py:79
  264.7 19.6 %collective-permute-start.27 = (bf16[512,4,64]{0,2,1:T(8,128)(2,1)S(1)}, bf16[512,4,64]{0,2,1:T(8,128)(2,1)S(1)}, u32[]{:S(2)}, u32[]{:S(2)}) collective-permute-start(bf16[512,4,64]{0,2,1:T(8,128)(2,1)S(1)} %collective-permute-done.26), channel_id=1, source_target_pairs={{0,480},{8,488},{16,496},{24,504},{32,0},{40,8},{48,16},{56,24},{6... | collective-permute-start | bytes 786440 | tf_op jit(solution)/shard_map/ppermute | solution.py:79
  278.3 15.8 %collective-permute-start.35 = (bf16[512,4,64]{0,2,1:T(8,128)(2,1)S(1)}, bf16[512,4,64]{0,2,1:T(8,128)(2,1)S(1)}, u32[]{:S(2)}, u32[]{:S(2)}) collective-permute-start(bf16[512,4,64]{0,2,1:T(8,128)(2,1)S(1)} %collective-permute-done.34), channel_id=1, source_target_pairs={{0,32},{8,40},{16,48},{24,56},{32,64},{40,72},{48,80},{56,88},{64,... | collective-permute-start | bytes 786440 | tf_op jit(solution)/shard_map/ppermute | solution.py:79
  308.2 29.5 %all-to-all-start.3 = ((bf16[8,128,512]{1,2,0:T(8,128)(2,1)}), bf16[8,128,512]{1,2,0:T(8,128)(2,1)S(1)}, u32[]{:S(2)}, u32[]{:S(2)}) async-start(bf16[8,128,512]{1,2,0:T(8,128)(2,1)} %bitcast.85), calls=%async_computation.3 | async-start | bytes 2097152 | tf_op jit(solution)/shard_map/all_to_all | solution.py:226
  (33 other events, 803.1 us)

commit v6 on v5

--- a/solution.py
+++ b/solution.py
@@ -116,6 +116,7 @@
     kv_start = tensor_index * heads_dev // group_full
     kv_width = kv_local * 2 * head_size
     kv_piece = lax.dynamic_slice_in_dim(key_value_weight, kv_start * 2 * head_size, kv_width, 1)
+    wo_full = lax.all_gather(w_out, "seq", axis=1, tiled=True)
     packed = jnp.concatenate([w_query.T, kv_piece.T], axis=0)
     gathered, z_at, y_at = ring_gather(packed, "seq", seq_count)
     wq_rows = gathered[:width_query]
@@ -163,8 +164,6 @@
     source_rows = jnp.where(valid, owner_start[:, None] + slots[None, :], 0)
     flat_query = query_vectors.reshape(length, width_query)
     outgoing = jnp.where(valid[:, :, None], flat_query[source_rows], jnp.zeros((), jnp.bfloat16))
-    outgoing, wo_block = lax.optimization_barrier((outgoing, w_out))
-    wo_rel, _, _ = ring_gather(wo_block, "seq", seq_count)
     arrived = lax.all_to_all(outgoing, "seq", split_axis=0, concat_axis=0, tiled=True)
     items = arrived.shape[1]
     rows_in = arrived.reshape(seq_count * items, heads_dev, head_size)
@@ -218,9 +217,7 @@
         (left * prefix_rows.astype(jnp.float32) + right * suffix_attn) / (left + right)
     ).astype(jnp.bfloat16)
     context = context.reshape(length, width_query)
-    partial_out = jnp.dot(context, wo_rel, preferred_element_type=jnp.float32)
-    partial_out = partial_out.reshape(length, z_count, Y_CHIPS, -1)
-    partial_out = jnp.roll(jnp.roll(partial_out, z_at, axis=1), y_at, axis=2).reshape(length, -1)
+    partial_out = jnp.dot(context, wo_full, preferred_element_type=jnp.float32)
     out_width = partial_out.shape[1] // tensor_count
     pieces = partial_out.astype(jnp.bfloat16).reshape(length, tensor_count, out_width)
     pieces = lax.all_to_all(

time: 341 us -> 279 us (0.82)
  starting transfers between devices: 167 us -> 101 us
  between operations: 1.9 us -> 14.8 us
  local copies, waits for them, and re-layouts: 50.8 us -> 40.2 us
  waiting for transfers between devices: 81.8 us -> 88.2 us
    ppermute x36 -> x18, starting transfers between devices: 118 us -> 61.2 us  [shift(): return lax.ppermute(value, axis_name, pairs)]
    ppermute x36 -> x18, waiting for transfers between devices: 67.4 us -> 40.7 us  [shift(): return lax.ppermute(value, axis_name, pairs)]
    all_to_all x1, waiting for transfers between devices: 0.01 us -> 20.9 us  [shards(): lax.all_to_all(jnp.concatenate([out_block, log_row], axis=1), 'seq', spli...]
    unnamed x82 -> x41, local copies, waits for them, and re-layouts: 27.4 us -> 13.7 us
    all_to_all x1, waiting for transfers between devices: 0.01 us -> 11.5 us  [shards(): lax.all_to_all(outgoing, 'seq', split_axis=0, concat_axis=0, tiled=True)]
    all_to_all x1, starting transfers between devices: 15.2 us -> 4.63 us  [shards(): lax.all_to_all(jnp.concatenate([out_block, log_row], axis=1), 'seq', spli...]
    dot_general x8, matrix products: 6.28 us -> 2.06 us  [attend(): result = jnp.dot(weights, values, preferred_element_type=jnp.float32)]
  transfers between devices with their start and end apart: 40 -> 23, of which waited for: 24 -> 15; matrix products, arithmetic and copies ran while one was open for 14% -> 22% of each run, Pallas kernels for 0% -> 0%
where the time goes in v6:
time: 279 us; the launch traced here: 277 us
  starting transfers between devices  101 us (36%)
  waiting for transfers between devices  88.2 us (32%)
  local copies, waits for them, and re-layouts  40.2 us (14%)
  other arithmetic  17.3 us (6%)
  matrix products  16 us (6%)
  between operations  14.8 us (5%)
    ppermute x18, starting transfers between devices, shift(): return lax.ppermute(value, axis_name, pairs)  61.2 us
    ppermute x18, waiting for transfers between devices, shift(): return lax.ppermute(value, axis_name, pairs)  40.7 us
    all_to_all x1, waiting for transfers between devices, shards(): lax.all_to_all(jnp.concatenate([out_block, log_row], axis=1), 'seq', spli...  20.9 us
    all_to_all x1, starting transfers between devices, shards(): lax.all_to_all(jnp.moveaxis(pieces, 1, 0), 'tensor', split_axis=0, concat...  15.7 us
    all_to_all x1, waiting for transfers between devices, shards(): lax.all_to_all(jnp.moveaxis(pieces, 1, 0), 'tensor', split_axis=0, concat...  14.4 us
    unnamed x41, local copies, waits for them, and re-layouts  13.7 us
    all_to_all x1, waiting for transfers between devices, shards(): lax.all_to_all(outgoing, 'seq', split_axis=0, concat_axis=0, tiled=True)  11.5 us
    all_to_all x1, starting transfers between devices, shards(): lax.all_to_all(tiles, 'tensor', split_axis=0, concat_axis=0, tiled=True)  10 us
  transfers between devices with their start and end apart: 23, of which 15 were waited for; matrix products, arithmetic and copies ran while one was open for 22% of the time, Pallas kernels for 0%

profile of v6, /device:TPU:1, one launch (start us, length us, event | category | flops | bytes accessed | tf_op | source)
XLA Modules:
  0.0 277.3 jit_solution(4133835057590042728)
XLA Ops:
  9.6 4.0 %collective-permute-start.1 = (bf16[768,64]{0,1:T(8,128)(2,1)}, bf16[768,64]{0,1:T(8,128)(2,1)S(1)}, u32[]{:S(2)}, u32[]{:S(2)}) collective-permute-start(bf16[768,64]{0,1:T(8,128)(2,1)} %get-tuple-element.16), channel_id=1, source_target_pairs={{0,8},{8,16},{16,24},{24,0},{32,40},{40,48},{48,56},{56,32},{64,72... | collective-permute-start | bytes 294920 | tf_op jit(solution)/shard_map/ppermute | solution.py:79
  13.6 3.4 %collective-permute-start = (bf16[768,64]{0,1:T(8,128)(2,1)}, bf16[768,64]{0,1:T(8,128)(2,1)}, u32[]{:S(2)}, u32[]{:S(2)}) collective-permute-start(bf16[768,64]{0,1:T(8,128)(2,1)} %get-tuple-element.16), channel_id=1, source_target_pairs={{0,24},{8,0},{16,8},{24,16},{32,56},{40,32},{48,40},{56,48},{64,88... | collective-permute-start | bytes 294920 | tf_op jit(solution)/shard_map/ppermute | solution.py:79
  19.1 10.0 %all-to-all-start = ((bf16[8,128,512]{1,2,0:T(8,128)(2,1)}), bf16[8,128,512]{1,2,0:T(8,128)(2,1)S(1)}, u32[]{:S(2)}, u32[]{:S(2)}) async-start(bf16[8,128,512]{1,2,0:T(8,128)(2,1)} %broadcast_in_dim.72), calls=%async_computation | async-start | bytes 2097152 | tf_op jit(solution)/shard_map/all_to_all | solution.py:102
  34.5 5.3 %collective-permute-done.2 = bf16[768,64]{0,1:T(8,128)(2,1)S(1)} collective-permute-done((bf16[768,64]{0,1:T(8,128)(2,1)S(1)}, bf16[768,64]{0,1:T(8,128)(2,1)S(1)}, u32[]{:S(2)}, u32[]{:S(2)}) %collective-permute-start.2) | collective-permute-done | bytes 98336 | tf_op jit(solution)/shard_map/ppermute | solution.py:79
  41.4 1.9 collective-permute-start.10
  43.3 6.7 %collective-permute-start.3 = (bf16[768,4,64]{0,2,1:T(8,128)(2,1)S(1)}, bf16[768,4,64]{0,2,1:T(8,128)(2,1)}, u32[]{:S(2)}, u32[]{:S(2)}) collective-permute-start(bf16[768,4,64]{0,2,1:T(8,128)(2,1)S(1)} %pad_maximum_fusion), channel_id=1, source_target_pairs={{0,480},{8,488},{16,496},{24,504},{32,0},{40,8},{48,16},{56,24},{6... | collective-permute-start | bytes 1179656 | tf_op jit(solution)/shard_map/ppermute | solution.py:79
  50.9 6.4 %collective-permute-done.10 = bf16[768,4,64]{0,2,1:T(8,128)(2,1)} collective-permute-done((bf16[768,4,64]{0,2,1:T(8,128)(2,1)S(1)}, bf16[768,4,64]{0,2,1:T(8,128)(2,1)}, u32[]{:S(2)}, u32[]{:S(2)}) %collective-permute-start.10) | collective-permute-done | bytes 393248 | tf_op jit(solution)/shard_map/ppermute | solution.py:79
  59.9 4.6 %collective-permute-start.4 = (bf16[768,4,64]{0,2,1:T(8,128)(2,1)}, bf16[768,4,64]{0,2,1:T(8,128)(2,1)}, u32[]{:S(2)}, u32[]{:S(2)}) collective-permute-start(bf16[768,4,64]{0,2,1:T(8,128)(2,1)} %collective-permute-done.3), channel_id=1, source_target_pairs={{0,480},{8,488},{16,496},{24,504},{32,0},{40,8},{48,16},{56,24},{6... | collective-permute-start | bytes 1179656 | tf_op jit(solution)/shard_map/ppermute | solution.py:79
  65.3 5.5 %collective-permute-done.11 = bf16[768,4,64]{0,2,1:T(8,128)(2,1)} collective-permute-done((bf16[768,4,64]{0,2,1:T(8,128)(2,1)}, bf16[768,4,64]{0,2,1:T(8,128)(2,1)}, u32[]{:S(2)}, u32[]{:S(2)}) %collective-permute-start.11) | collective-permute-done | bytes 393248 | tf_op jit(solution)/shard_map/ppermute | solution.py:79
  74.1 2.6 copy.116
  78.4 4.6 %collective-permute-start.5 = (bf16[768,4,64]{0,2,1:T(8,128)(2,1)}, bf16[768,4,64]{0,2,1:T(8,128)(2,1)S(1)}, u32[]{:S(2)}, u32[]{:S(2)}) collective-permute-start(bf16[768,4,64]{0,2,1:T(8,128)(2,1)} %collective-permute-done.4), channel_id=1, source_target_pairs={{0,480},{8,488},{16,496},{24,504},{32,0},{40,8},{48,16},{56,24},{6... | collective-permute-start | bytes 1179656 | tf_op jit(solution)/shard_map/ppermute | solution.py:79
  87.3 2.8 %collective-permute-done.5 = bf16[768,4,64]{0,2,1:T(8,128)(2,1)S(1)} collective-permute-done((bf16[768,4,64]{0,2,1:T(8,128)(2,1)}, bf16[768,4,64]{0,2,1:T(8,128)(2,1)S(1)}, u32[]{:S(2)}, u32[]{:S(2)}) %collective-permute-start.5) | collective-permute-done | bytes 393248 | tf_op jit(solution)/shard_map/ppermute | solution.py:79
  90.1 5.2 %collective-permute-start.6 = (bf16[768,4,64]{0,2,1:T(8,128)(2,1)S(1)}, bf16[768,4,64]{0,2,1:T(8,128)(2,1)S(1)}, u32[]{:S(2)}, u32[]{:S(2)}) collective-permute-start(bf16[768,4,64]{0,2,1:T(8,128)(2,1)S(1)} %collective-permute-done.5), channel_id=1, source_target_pairs={{0,480},{8,488},{16,496},{24,504},{32,0},{40,8},{48,16},{56,24},{6... | collective-permute-start | bytes 1179656 | tf_op jit(solution)/shard_map/ppermute | solution.py:79
  100.2 5.5 %collective-permute-start.7 = (bf16[768,4,64]{0,2,1:T(8,128)(2,1)S(1)}, bf16[768,4,64]{0,2,1:T(8,128)(2,1)S(1)}, u32[]{:S(2)}, u32[]{:S(2)}) collective-permute-start(bf16[768,4,64]{0,2,1:T(8,128)(2,1)S(1)} %collective-permute-done.6), channel_id=1, source_target_pairs={{0,480},{8,488},{16,496},{24,504},{32,0},{40,8},{48,16},{56,24},{6... | collective-permute-start | bytes 1179656 | tf_op jit(solution)/shard_map/ppermute | solution.py:79
  110.4 5.0 %collective-permute-start.8 = (bf16[768,4,64]{0,2,1:T(8,128)(2,1)S(1)}, bf16[768,4,64]{0,2,1:T(8,128)(2,1)S(1)}, u32[]{:S(2)}, u32[]{:S(2)}) collective-permute-start(bf16[768,4,64]{0,2,1:T(8,128)(2,1)S(1)} %collective-permute-done.7), channel_id=1, source_target_pairs={{0,480},{8,488},{16,496},{24,504},{32,0},{40,8},{48,16},{56,24},{6... | collective-permute-start | bytes 1179656 | tf_op jit(solution)/shard_map/ppermute | solution.py:79
  118.2 3.3 %collective-permute-done.8 = bf16[768,4,64]{0,2,1:T(8,128)(2,1)S(1)} collective-permute-done((bf16[768,4,64]{0,2,1:T(8,128)(2,1)S(1)}, bf16[768,4,64]{0,2,1:T(8,128)(2,1)S(1)}, u32[]{:S(2)}, u32[]{:S(2)}) %collective-permute-start.8) | collective-permute-done | bytes 393248 | tf_op jit(solution)/shard_map/ppermute | solution.py:79
  121.5 5.0 %collective-permute-start.9 = (bf16[768,4,64]{0,2,1:T(8,128)(2,1)S(1)}, bf16[768,4,64]{0,2,1:T(8,128)(2,1)S(1)}, u32[]{:S(2)}, u32[]{:S(2)}) collective-permute-start(bf16[768,4,64]{0,2,1:T(8,128)(2,1)S(1)} %collective-permute-done.8), channel_id=1, source_target_pairs={{0,480},{8,488},{16,496},{24,504},{32,0},{40,8},{48,16},{56,24},{6... | collective-permute-start | bytes 1179656 | tf_op jit(solution)/shard_map/ppermute | solution.py:79
  130.1 3.1 %collective-permute-done.9 = bf16[768,4,64]{0,2,1:T(8,128)(2,1)S(1)} collective-permute-done((bf16[768,4,64]{0,2,1:T(8,128)(2,1)S(1)}, bf16[768,4,64]{0,2,1:T(8,128)(2,1)S(1)}, u32[]{:S(2)}, u32[]{:S(2)}) %collective-permute-start.9) | collective-permute-done | bytes 393248 | tf_op jit(solution)/shard_map/ppermute | solution.py:79
  133.2 9.0 %collective-permute-done.17 = bf16[768,4,64]{0,2,1:T(8,128)(2,1)S(1)} collective-permute-done((bf16[768,4,64]{0,2,1:T(8,128)(2,1)S(1)}, bf16[768,4,64]{0,2,1:T(8,128)(2,1)S(1)}, u32[]{:S(2)}, u32[]{:S(2)}) %collective-permute-start.17) | collective-permute-done | bytes 393248 | tf_op jit(solution)/shard_map/ppermute | solution.py:79
  145.4 2.7 copy-done.2
  148.1 2.5 slice.96
  150.5 7.0 %dot_general.61 = bf16[4,128,4096]{1,0,2:T(4,128)(2,1)} reshape(bf16[512,16,4,64]{0,3,2,1:T(8,128)(2,1)} %slice.96) | data formatting | bytes 8388608 | tf_op jit(solution)/shard_map/dot_general | solution.py:129
  157.5 3.9 %fusion = f32[128,4,128]{0,2,1:T(8,128)S(1)} fusion(bf16[128,4096,1]{0,1,2:T(8,128)(2,1)S(1)} %bitcast.219, bf16[4,128,4096]{1,0,2:T(4,128)(2,1)} %dot_general.61), kind=kOutput, calls=%fused_computation.4 | convolution fusion | flops 536870912 | bytes 5505024 | tf_op jit(solution)/shard_map/dot_general | solution.py:129
  163.3 2.1 reshape.672
  170.9 9.2 %all-to-all-start.1 = ((bf16[64,4,512]{2,1,0:T(4,128)(2,1)}), bf16[64,4,512]{2,1,0:T(4,128)(2,1)}, u32[]{:S(2)}, u32[]{:S(2)}) async-start(bf16[64,4,512]{2,1,0:T(4,128)(2,1)} %broadcast_select_fusion), calls=%async_computation.1 | async-start | bytes 524288 | tf_op jit(solution)/shard_map/all_to_all | solution.py:167
  180.1 2.5 fusion.4
  185.7 11.5 %all-to-all-done.1 = bf16[64,4,512]{2,1,0:T(4,128)(2,1)} async-done(((bf16[64,4,512]{2,1,0:T(4,128)(2,1)}), bf16[64,4,512]{2,1,0:T(4,128)(2,1)}, u32[]{:S(2)}, u32[]{:S(2)}) %all-to-all-start.1) | async-done | bytes 262176 | tf_op jit(solution)/shard_map/all_to_all | solution.py:167
  205.4 4.6 %all-to-all-start.2 = ((bf16[64,5,512]{2,1,0:T(8,128)(2,1)}), bf16[64,5,512]{2,1,0:T(8,128)(2,1)S(1)}, u32[]{:S(2)}, u32[]{:S(2)}) async-start(bf16[64,5,512]{2,1,0:T(8,128)(2,1)} %fusion.22), calls=%async_computation.2 | async-start | bytes 1048576 | tf_op jit(solution)/shard_map/all_to_all | solution.py:185
  211.0 20.9 %all-to-all-done.2 = bf16[64,5,512]{2,1,0:T(8,128)(2,1)S(1)} async-done(((bf16[64,5,512]{2,1,0:T(8,128)(2,1)}), bf16[64,5,512]{2,1,0:T(8,128)(2,1)S(1)}, u32[]{:S(2)}, u32[]{:S(2)}) %all-to-all-start.2) | async-done | bytes 327712 | tf_op jit(solution)/shard_map/all_to_all | solution.py:185
  234.0 3.7 %convolution_convert_fusion = bf16[128,4096]{1,0:T(8,128)(2,1)S(1)} fusion(bf16[128,512]{0,1:T(8,128)(2,1)S(1)} %bitcast.222, bf16[512,4096]{0,1:T(8,128)(2,1)} %all-gather.2.cloned.1.call-done), kind=kOutput, calls=%fused_computation.3 | convolution fusion | flops 537395200 | bytes 5373952 | tf_op jit(solution)/shard_map/dot_general | solution.py:220
  238.8 15.7 %all-to-all-start.3 = ((bf16[8,128,512]{2,1,0:T(8,128)(2,1)}), bf16[8,128,512]{2,1,0:T(8,128)(2,1)S(1)}, u32[]{:S(2)}, u32[]{:S(2)}) async-start(bf16[8,128,512]{2,1,0:T(8,128)(2,1)} %bitcast.208), calls=%async_computation.3 | async-start | bytes 2097152 | tf_op jit(solution)/shard_map/all_to_all | solution.py:223
  255.2 14.4 %all-to-all-done.3 = bf16[8,128,512]{2,1,0:T(8,128)(2,1)S(1)} async-done(((bf16[8,128,512]{2,1,0:T(8,128)(2,1)}), bf16[8,128,512]{2,1,0:T(8,128)(2,1)S(1)}, u32[]{:S(2)}, u32[]{:S(2)}) %all-to-all-start.3) | async-done | bytes 1048608 | tf_op jit(solution)/shard_map/all_to_all | solution.py:223
  (162 shorter events, 68.1 us)
Async XLA Ops:
  7.2 66.9 %copy-start.4 = (bf16[1,1024,1024]{2,1,0:T(8,128)(2,1)S(1)}, bf16[1,1024,1024]{2,1,0:T(8,128)(2,1)}, u32[]{:S(2)}) copy-start(bf16[1,1024,1024]{2,1,0:T(8,128)(2,1)} %param.13) | copy-start | bytes 6291460
  9.6 22.8 %collective-permute-start.1 = (bf16[768,64]{0,1:T(8,128)(2,1)}, bf16[768,64]{0,1:T(8,128)(2,1)S(1)}, u32[]{:S(2)}, u32[]{:S(2)}) collective-permute-start(bf16[768,64]{0,1:T(8,128)(2,1)} %get-tuple-element.16), channel_id=1, source_target_pairs={{0,8},{8,16},{16,24},{24,0},{32,40},{40,48},{48,56},{56,32},{64,72... | collective-permute-start | bytes 294920 | tf_op jit(solution)/shard_map/ppermute | solution.py:79
  13.6 20.9 %collective-permute-start = (bf16[768,64]{0,1:T(8,128)(2,1)}, bf16[768,64]{0,1:T(8,128)(2,1)}, u32[]{:S(2)}, u32[]{:S(2)}) collective-permute-start(bf16[768,64]{0,1:T(8,128)(2,1)} %get-tuple-element.16), channel_id=1, source_target_pairs={{0,24},{8,0},{16,8},{24,16},{32,56},{40,32},{48,40},{56,48},{64,88... | collective-permute-start | bytes 294920 | tf_op jit(solution)/shard_map/ppermute | solution.py:79
  19.1 67.6 %all-to-all-start = ((bf16[8,128,512]{1,2,0:T(8,128)(2,1)}), bf16[8,128,512]{1,2,0:T(8,128)(2,1)S(1)}, u32[]{:S(2)}, u32[]{:S(2)}) async-start(bf16[8,128,512]{1,2,0:T(8,128)(2,1)} %broadcast_in_dim.72), calls=%async_computation | async-start | bytes 2097152 | tf_op jit(solution)/shard_map/all_to_all | solution.py:102
  29.1 204.9 %all-gather.2.cloned.1.call-start = ((), (), s32[]{:S(2)}) async-start(), calls=%async_computation.4 | async-start | bytes 4259840 | tf_op jit(solution)/shard_map/all_gather | solution.py:119
  32.4 7.4 %collective-permute-start.2 = (bf16[768,64]{0,1:T(8,128)(2,1)S(1)}, bf16[768,64]{0,1:T(8,128)(2,1)S(1)}, u32[]{:S(2)}, u32[]{:S(2)}) collective-permute-start(bf16[768,64]{0,1:T(8,128)(2,1)S(1)} %collective-permute-done.1), channel_id=1, source_target_pairs={{0,8},{8,16},{16,24},{24,0},{32,40},{40,48},{48,56},{56,32},{64,72... | collective-permute-start | bytes 294920 | tf_op jit(solution)/shard_map/ppermute | solution.py:79
  34.5 30.1 %copy-start.9 = (s32[128]{0:T(128)}, s32[128]{0:T(128)S(1)}, u32[]{:S(2)}) copy-start(s32[128]{0:T(128)S(1)} %get-tuple-element.2) | copy-start | bytes 1540
  41.4 15.9 %collective-permute-start.10 = (bf16[768,4,64]{0,2,1:T(8,128)(2,1)S(1)}, bf16[768,4,64]{0,2,1:T(8,128)(2,1)}, u32[]{:S(2)}, u32[]{:S(2)}) collective-permute-start(bf16[768,4,64]{0,2,1:T(8,128)(2,1)S(1)} %pad_maximum_fusion), channel_id=1, source_target_pairs={{0,32},{8,40},{16,48},{24,56},{32,64},{40,72},{48,80},{56,88},{64,... | collective-permute-start | bytes 1179656 | tf_op jit(solution)/shard_map/ppermute | solution.py:79
  43.3 21.8 %copy-start.7 = (f32[128]{0:T(128)}, f32[128]{0:T(128)S(1)}, u32[]{:S(2)}) copy-start(f32[128]{0:T(128)S(1)} %add_convert_fusion.4) | copy-start | bytes 1540
  43.3 16.6 %collective-permute-start.3 = (bf16[768,4,64]{0,2,1:T(8,128)(2,1)S(1)}, bf16[768,4,64]{0,2,1:T(8,128)(2,1)}, u32[]{:S(2)}, u32[]{:S(2)}) collective-permute-start(bf16[768,4,64]{0,2,1:T(8,128)(2,1)S(1)} %pad_maximum_fusion), channel_id=1, source_target_pairs={{0,480},{8,488},{16,496},{24,504},{32,0},{40,8},{48,16},{56,24},{6... | collective-permute-start | bytes 1179656 | tf_op jit(solution)/shard_map/ppermute | solution.py:79
  50.1 14.4 %copy-start.8 = (f32[64]{0:T(128)}, f32[64]{0:T(128)S(1)}, u32[]{:S(2)}) copy-start(f32[64]{0:T(128)S(1)} %multiply_power_fusion) | copy-start | bytes 772
  57.3 13.4 %collective-permute-start.11 = (bf16[768,4,64]{0,2,1:T(8,128)(2,1)}, bf16[768,4,64]{0,2,1:T(8,128)(2,1)}, u32[]{:S(2)}, u32[]{:S(2)}) collective-permute-start(bf16[768,4,64]{0,2,1:T(8,128)(2,1)} %collective-permute-done.10), channel_id=1, source_target_pairs={{0,32},{8,40},{16,48},{24,56},{32,64},{40,72},{48,80},{56,88},{64,... | collective-permute-start | bytes 1179656 | tf_op jit(solution)/shard_map/ppermute | solution.py:79
  59.9 18.5 %collective-permute-start.4 = (bf16[768,4,64]{0,2,1:T(8,128)(2,1)}, bf16[768,4,64]{0,2,1:T(8,128)(2,1)}, u32[]{:S(2)}, u32[]{:S(2)}) collective-permute-start(bf16[768,4,64]{0,2,1:T(8,128)(2,1)} %collective-permute-done.3), channel_id=1, source_target_pairs={{0,480},{8,488},{16,496},{24,504},{32,0},{40,8},{48,16},{56,24},{6... | collective-permute-start | bytes 1179656 | tf_op jit(solution)/shard_map/ppermute | solution.py:79
  70.7 14.1 %collective-permute-start.12 = (bf16[768,4,64]{0,2,1:T(8,128)(2,1)}, bf16[768,4,64]{0,2,1:T(8,128)(2,1)}, u32[]{:S(2)}, u32[]{:S(2)}) collective-permute-start(bf16[768,4,64]{0,2,1:T(8,128)(2,1)} %collective-permute-done.11), channel_id=1, source_target_pairs={{0,32},{8,40},{16,48},{24,56},{32,64},{40,72},{48,80},{56,88},{64,... | collective-permute-start | bytes 1179656 | tf_op jit(solution)/shard_map/ppermute | solution.py:79
  78.4 11.6 %collective-permute-start.5 = (bf16[768,4,64]{0,2,1:T(8,128)(2,1)}, bf16[768,4,64]{0,2,1:T(8,128)(2,1)S(1)}, u32[]{:S(2)}, u32[]{:S(2)}) collective-permute-start(bf16[768,4,64]{0,2,1:T(8,128)(2,1)} %collective-permute-done.4), channel_id=1, source_target_pairs={{0,480},{8,488},{16,496},{24,504},{32,0},{40,8},{48,16},{56,24},{6... | collective-permute-start | bytes 1179656 | tf_op jit(solution)/shard_map/ppermute | solution.py:79
  84.8 11.8 %collective-permute-start.13 = (bf16[768,4,64]{0,2,1:T(8,128)(2,1)}, bf16[768,4,64]{0,2,1:T(8,128)(2,1)S(1)}, u32[]{:S(2)}, u32[]{:S(2)}) collective-permute-start(bf16[768,4,64]{0,2,1:T(8,128)(2,1)} %collective-permute-done.12), channel_id=1, source_target_pairs={{0,32},{8,40},{16,48},{24,56},{32,64},{40,72},{48,80},{56,88},{64,... | collective-permute-start | bytes 1179656 | tf_op jit(solution)/shard_map/ppermute | solution.py:79
  86.7 21.7 %copy-start.1 = (bf16[768,16,4,64]{0,3,2,1:T(8,128)(2,1)S(1)}, bf16[768,16,4,64]{0,3,2,1:T(8,128)(2,1)}, u32[]{:S(2)}) copy-start(bf16[768,16,4,64]{0,3,2,1:T(8,128)(2,1)} %bitcast_dynamic-update-slice_fusion.14) | copy-start | bytes 18874372
  90.1 10.2 %collective-permute-start.6 = (bf16[768,4,64]{0,2,1:T(8,128)(2,1)S(1)}, bf16[768,4,64]{0,2,1:T(8,128)(2,1)S(1)}, u32[]{:S(2)}, u32[]{:S(2)}) collective-permute-start(bf16[768,4,64]{0,2,1:T(8,128)(2,1)S(1)} %collective-permute-done.5), channel_id=1, source_target_pairs={{0,480},{8,488},{16,496},{24,504},{32,0},{40,8},{48,16},{56,24},{6... | collective-permute-start | bytes 1179656 | tf_op jit(solution)/shard_map/ppermute | solution.py:79
  96.6 9.9 %collective-permute-start.14 = (bf16[768,4,64]{0,2,1:T(8,128)(2,1)S(1)}, bf16[768,4,64]{0,2,1:T(8,128)(2,1)S(1)}, u32[]{:S(2)}, u32[]{:S(2)}) collective-permute-start(bf16[768,4,64]{0,2,1:T(8,128)(2,1)S(1)} %collective-permute-done.13), channel_id=1, source_target_pairs={{0,32},{8,40},{16,48},{24,56},{32,64},{40,72},{48,80},{56,88},{64,... | collective-permute-start | bytes 1179656 | tf_op jit(solution)/shard_map/ppermute | solution.py:79
  100.2 10.2 %collective-permute-start.7 = (bf16[768,4,64]{0,2,1:T(8,128)(2,1)S(1)}, bf16[768,4,64]{0,2,1:T(8,128)(2,1)S(1)}, u32[]{:S(2)}, u32[]{:S(2)}) collective-permute-start(bf16[768,4,64]{0,2,1:T(8,128)(2,1)S(1)} %collective-permute-done.6), channel_id=1, source_target_pairs={{0,480},{8,488},{16,496},{24,504},{32,0},{40,8},{48,16},{56,24},{6... | collective-permute-start | bytes 1179656 | tf_op jit(solution)/shard_map/ppermute | solution.py:79
  106.5 9.7 %collective-permute-start.15 = (bf16[768,4,64]{0,2,1:T(8,128)(2,1)S(1)}, bf16[768,4,64]{0,2,1:T(8,128)(2,1)S(1)}, u32[]{:S(2)}, u32[]{:S(2)}) collective-permute-start(bf16[768,4,64]{0,2,1:T(8,128)(2,1)S(1)} %collective-permute-done.14), channel_id=1, source_target_pairs={{0,32},{8,40},{16,48},{24,56},{32,64},{40,72},{48,80},{56,88},{64,... | collective-permute-start | bytes 1179656 | tf_op jit(solution)/shard_map/ppermute | solution.py:79
  110.4 11.1 %collective-permute-start.8 = (bf16[768,4,64]{0,2,1:T(8,128)(2,1)S(1)}, bf16[768,4,64]{0,2,1:T(8,128)(2,1)S(1)}, u32[]{:S(2)}, u32[]{:S(2)}) collective-permute-start(bf16[768,4,64]{0,2,1:T(8,128)(2,1)S(1)} %collective-permute-done.7), channel_id=1, source_target_pairs={{0,480},{8,488},{16,496},{24,504},{32,0},{40,8},{48,16},{56,24},{6... | collective-permute-start | bytes 1179656 | tf_op jit(solution)/shard_map/ppermute | solution.py:79
  116.2 11.9 %collective-permute-start.16 = (bf16[768,4,64]{0,2,1:T(8,128)(2,1)S(1)}, bf16[768,4,64]{0,2,1:T(8,128)(2,1)S(1)}, u32[]{:S(2)}, u32[]{:S(2)}) collective-permute-start(bf16[768,4,64]{0,2,1:T(8,128)(2,1)S(1)} %collective-permute-done.15), channel_id=1, source_target_pairs={{0,32},{8,40},{16,48},{24,56},{32,64},{40,72},{48,80},{56,88},{64,... | collective-permute-start | bytes 1179656 | tf_op jit(solution)/shard_map/ppermute | solution.py:79
  121.5 11.6 %collective-permute-start.9 = (bf16[768,4,64]{0,2,1:T(8,128)(2,1)S(1)}, bf16[768,4,64]{0,2,1:T(8,128)(2,1)S(1)}, u32[]{:S(2)}, u32[]{:S(2)}) collective-permute-start(bf16[768,4,64]{0,2,1:T(8,128)(2,1)S(1)} %collective-permute-done.8), channel_id=1, source_target_pairs={{0,480},{8,488},{16,496},{24,504},{32,0},{40,8},{48,16},{56,24},{6... | collective-permute-start | bytes 1179656 | tf_op jit(solution)/shard_map/ppermute | solution.py:79
  128.1 14.0 %collective-permute-start.17 = (bf16[768,4,64]{0,2,1:T(8,128)(2,1)S(1)}, bf16[768,4,64]{0,2,1:T(8,128)(2,1)S(1)}, u32[]{:S(2)}, u32[]{:S(2)}) collective-permute-start(bf16[768,4,64]{0,2,1:T(8,128)(2,1)S(1)} %collective-permute-done.16), channel_id=1, source_target_pairs={{0,32},{8,40},{16,48},{24,56},{32,64},{40,72},{48,80},{56,88},{64,... | collective-permute-start | bytes 1179656 | tf_op jit(solution)/shard_map/ppermute | solution.py:79
  150.5 10.9 %copy-start.6 = (f32[128,64]{0,1:T(8,128)S(1)}, f32[128,64]{0,1:T(8,128)}, u32[]{:S(2)}) copy-start(f32[128,64]{0,1:T(8,128)} %get-tuple-element.20) | copy-start | bytes 98308
  165.4 33.4 %copy-start.3 = (bf16[1,1024,1024]{1,2,0:T(8,128)(2,1)S(1)}, bf16[1,1024,1024]{1,2,0:T(8,128)(2,1)}, u32[]{:S(2)}) copy-start(bf16[1,1024,1024]{1,2,0:T(8,128)(2,1)} %copy.116) | copy-start | bytes 6291460
  167.4 18.1 %copy-start.10 = (s32[128]{0:T(128)S(1)}, s32[128]{0:T(128)}, u32[]{:S(2)}) copy-start(s32[128]{0:T(128)} %copy-done.9) | copy-start | bytes 1540
  170.9 26.3 %all-to-all-start.1 = ((bf16[64,4,512]{2,1,0:T(4,128)(2,1)}), bf16[64,4,512]{2,1,0:T(4,128)(2,1)}, u32[]{:S(2)}, u32[]{:S(2)}) async-start(bf16[64,4,512]{2,1,0:T(4,128)(2,1)} %broadcast_select_fusion), calls=%async_computation.1 | async-start | bytes 524288 | tf_op jit(solution)/shard_map/all_to_all | solution.py:167
  202.2 7.9 %copy-start.11 = (s32[128]{0:T(128)S(1)}, s32[128]{0:T(128)}, u32[]{:S(2)}) copy-start(s32[128]{0:T(128)} %copy-done.9) | copy-start | bytes 1540
  205.4 26.5 %all-to-all-start.2 = ((bf16[64,5,512]{2,1,0:T(8,128)(2,1)}), bf16[64,5,512]{2,1,0:T(8,128)(2,1)S(1)}, u32[]{:S(2)}, u32[]{:S(2)}) async-start(bf16[64,5,512]{2,1,0:T(8,128)(2,1)} %fusion.22), calls=%async_computation.2 | async-start | bytes 1048576 | tf_op jit(solution)/shard_map/all_to_all | solution.py:185
  238.8 30.8 %all-to-all-start.3 = ((bf16[8,128,512]{2,1,0:T(8,128)(2,1)}), bf16[8,128,512]{2,1,0:T(8,128)(2,1)S(1)}, u32[]{:S(2)}, u32[]{:S(2)}) async-start(bf16[8,128,512]{2,1,0:T(8,128)(2,1)} %bitcast.208), calls=%async_computation.3 | async-start | bytes 2097152 | tf_op jit(solution)/shard_map/all_to_all | solution.py:223
  (3 other events, 4.2 us)
Sparse Core Ops, SparseCore 0:
  32.9 138.3 all-gather.1

commit v7 on v6

--- a/solution.py
+++ b/solution.py
@@ -116,11 +116,10 @@
     kv_start = tensor_index * heads_dev // group_full
     kv_width = kv_local * 2 * head_size
     kv_piece = lax.dynamic_slice_in_dim(key_value_weight, kv_start * 2 * head_size, kv_width, 1)
-    wo_full = lax.all_gather(w_out, "seq", axis=1, tiled=True)
-    packed = jnp.concatenate([w_query.T, kv_piece.T], axis=0)
-    gathered, z_at, y_at = ring_gather(packed, "seq", seq_count)
-    wq_rows = gathered[:width_query]
-    kv_rows = gathered[width_query:]
+    side = lax.all_gather(jnp.concatenate([kv_piece.T, w_out], axis=0), "seq", axis=1, tiled=True)
+    kv_rows = side[:kv_width]
+    wo_full = side[kv_width:]
+    wq_rows, z_at, y_at = ring_gather(w_query.T, "seq", seq_count)
     z_count = seq_count // Y_CHIPS
     rel_input = normalized_input.reshape(length, z_count, Y_CHIPS, -1)
     rel_input = jnp.roll(jnp.roll(rel_input, -z_at, axis=1), -y_at, axis=2).reshape(length, -1)
@@ -131,7 +130,9 @@
         )
 
     query_vectors = contract(wq_rows)
-    key_value_pair = contract(kv_rows)
+    key_value_pair = lax.dot_general(
+        normalized_input, kv_rows, (((1,), (1,)), ((), ())), preferred_element_type=jnp.float32
+    )
     counts = token_counts[0]
     num_groups = counts.shape[0]
     starts, prefix_group, offset = layout(counts, length)

time: 279 us -> 258 us (0.925)
  waiting for transfers between devices: 88.2 us -> 73.5 us
  matrix products: 16 us -> 10.6 us
  starting transfers between devices: 101 us -> 105 us
  other arithmetic: 17.3 us -> 14.3 us
    ppermute x18, waiting for transfers between devices: 40.7 us -> 23.2 us  [shift(): return lax.ppermute(value, axis_name, pairs)]
    all_to_all x1, starting transfers between devices: 15.7 us -> 21 us  [shards(): lax.all_to_all(jnp.moveaxis(pieces, 1, 0), 'tensor', split_axis=0, concat...]
    all_to_all x1, waiting for transfers between devices: 11.5 us -> 16.8 us  [shards(): lax.all_to_all(outgoing, 'seq', split_axis=0, concat_axis=0, tiled=True)]
    dot_general x2 -> x1, matrix products: 6.44 us -> 3.94 us  [contract(): lax.dot_general(rel_input, rows, (((1,), (1,)), ((), ())), preferred_elem...]
    unnamed x41 -> x45, local copies, waits for them, and re-layouts: 13.7 us -> 15.5 us
  transfers between devices with their start and end apart: 23 -> 23, of which waited for: 15 -> 13; matrix products, arithmetic and copies ran while one was open for 22% -> 20% of each run, Pallas kernels for 0% -> 0%
where the time goes in v7:
time: 258 us; the launch traced here: 257 us
  starting transfers between devices  105 us (41%)
  waiting for transfers between devices  73.5 us (28%)
  local copies, waits for them, and re-layouts  38.4 us (15%)
  between operations  14.9 us (6%)
  other arithmetic  14.3 us (6%)
  matrix products  10.6 us (4%)
    ppermute x18, starting transfers between devices, shift(): return lax.ppermute(value, axis_name, pairs)  59.8 us
    ppermute x18, waiting for transfers between devices, shift(): return lax.ppermute(value, axis_name, pairs)  23.2 us
    all_to_all x1, starting transfers between devices, shards(): lax.all_to_all(jnp.moveaxis(pieces, 1, 0), 'tensor', split_axis=0, concat...  21 us
    all_to_all x1, waiting for transfers between devices, shards(): lax.all_to_all(jnp.concatenate([out_block, log_row], axis=1), 'seq', spli...  19.1 us
    all_to_all x1, waiting for transfers between devices, shards(): lax.all_to_all(outgoing, 'seq', split_axis=0, concat_axis=0, tiled=True)  16.8 us
    unnamed x45, local copies, waits for them, and re-layouts  15.5 us
    all_to_all x1, waiting for transfers between devices, shards(): lax.all_to_all(jnp.moveaxis(pieces, 1, 0), 'tensor', split_axis=0, concat...  14.4 us
    all_to_all x1, starting transfers between devices, shards(): lax.all_to_all(tiles, 'tensor', split_axis=0, concat_axis=0, tiled=True)  10 us
  transfers between devices with their start and end apart: 23, of which 13 were waited for; matrix products, arithmetic and copies ran while one was open for 20% of the time, Pallas kernels for 0%

profile of v7, /device:TPU:1, one launch (start us, length us, event | category | flops | bytes accessed | tf_op | source)
XLA Modules:
  0.0 256.8 jit_solution(3333623075971959014)
XLA Ops:
  7.2 4.2 %collective-permute-start.1 = (bf16[512,64]{0,1:T(8,128)(2,1)}, bf16[512,64]{0,1:T(8,128)(2,1)S(1)}, u32[]{:S(2)}, u32[]{:S(2)}) collective-permute-start(bf16[512,64]{0,1:T(8,128)(2,1)} %bitcast.224), channel_id=1, source_target_pairs={{0,8},{8,16},{16,24},{24,0},{32,40},{40,48},{48,56},{56,32},{64,72... | collective-permute-start | bytes 196616 | tf_op jit(solution)/shard_map/ppermute | solution.py:79
  11.4 3.4 %collective-permute-start = (bf16[512,64]{0,1:T(8,128)(2,1)}, bf16[512,64]{0,1:T(8,128)(2,1)S(1)}, u32[]{:S(2)}, u32[]{:S(2)}) collective-permute-start(bf16[512,64]{0,1:T(8,128)(2,1)} %bitcast.225), channel_id=1, source_target_pairs={{0,24},{8,0},{16,8},{24,16},{32,56},{40,32},{48,40},{56,48},{64,88... | collective-permute-start | bytes 196616 | tf_op jit(solution)/shard_map/ppermute | solution.py:79
  16.9 10.0 %all-to-all-start = ((bf16[8,128,512]{1,2,0:T(8,128)(2,1)}), bf16[8,128,512]{1,2,0:T(8,128)(2,1)S(1)}, u32[]{:S(2)}, u32[]{:S(2)}) async-start(bf16[8,128,512]{1,2,0:T(8,128)(2,1)} %broadcast_in_dim.72), calls=%async_computation | async-start | bytes 2097152 | tf_op jit(solution)/shard_map/all_to_all | solution.py:102
  31.6 1.9 collective-permute-start.2
  33.6 4.7 %collective-permute-done.2 = bf16[512,64]{0,1:T(8,128)(2,1)S(1)} collective-permute-done((bf16[512,64]{0,1:T(8,128)(2,1)S(1)}, bf16[512,64]{0,1:T(8,128)(2,1)S(1)}, u32[]{:S(2)}, u32[]{:S(2)}) %collective-permute-start.2) | collective-permute-done | bytes 65568 | tf_op jit(solution)/shard_map/ppermute | solution.py:79
  39.1 1.9 collective-permute-start.10
  41.3 6.7 %collective-permute-start.3 = (bf16[512,4,64]{0,2,1:T(8,128)(2,1)S(1)}, bf16[512,4,64]{0,2,1:T(8,128)(2,1)S(1)}, u32[]{:S(2)}, u32[]{:S(2)}) collective-permute-start(bf16[512,4,64]{0,2,1:T(8,128)(2,1)S(1)} %pad_maximum_fusion), channel_id=1, source_target_pairs={{0,480},{8,488},{16,496},{24,504},{32,0},{40,8},{48,16},{56,24},{6... | collective-permute-start | bytes 786440 | tf_op jit(solution)/shard_map/ppermute | solution.py:79
  48.0 4.3 %collective-permute-done.10 = bf16[512,4,64]{0,2,1:T(8,128)(2,1)S(1)} collective-permute-done((bf16[512,4,64]{0,2,1:T(8,128)(2,1)S(1)}, bf16[512,4,64]{0,2,1:T(8,128)(2,1)S(1)}, u32[]{:S(2)}, u32[]{:S(2)}) %collective-permute-start.10) | collective-permute-done | bytes 262176 | tf_op jit(solution)/shard_map/ppermute | solution.py:79
  52.2 1.9 collective-permute-start.11
  54.5 4.6 %collective-permute-start.4 = (bf16[512,4,64]{0,2,1:T(8,128)(2,1)S(1)}, bf16[512,4,64]{0,2,1:T(8,128)(2,1)S(1)}, u32[]{:S(2)}, u32[]{:S(2)}) collective-permute-start(bf16[512,4,64]{0,2,1:T(8,128)(2,1)S(1)} %collective-permute-done.3), channel_id=1, source_target_pairs={{0,480},{8,488},{16,496},{24,504},{32,0},{40,8},{48,16},{56,24},{6... | collective-permute-start | bytes 786440 | tf_op jit(solution)/shard_map/ppermute | solution.py:79
  59.8 2.9 %collective-permute-done.11 = bf16[512,4,64]{0,2,1:T(8,128)(2,1)S(1)} collective-permute-done((bf16[512,4,64]{0,2,1:T(8,128)(2,1)S(1)}, bf16[512,4,64]{0,2,1:T(8,128)(2,1)S(1)}, u32[]{:S(2)}, u32[]{:S(2)}) %collective-permute-start.11) | collective-permute-done | bytes 262176 | tf_op jit(solution)/shard_map/ppermute | solution.py:79
  62.7 1.9 collective-permute-start.12
  65.4 4.6 %collective-permute-start.5 = (bf16[512,4,64]{0,2,1:T(8,128)(2,1)S(1)}, bf16[512,4,64]{0,2,1:T(8,128)(2,1)S(1)}, u32[]{:S(2)}, u32[]{:S(2)}) collective-permute-start(bf16[512,4,64]{0,2,1:T(8,128)(2,1)S(1)} %collective-permute-done.4), channel_id=1, source_target_pairs={{0,480},{8,488},{16,496},{24,504},{32,0},{40,8},{48,16},{56,24},{6... | collective-permute-start | bytes 786440 | tf_op jit(solution)/shard_map/ppermute | solution.py:79
  72.3 1.9 collective-permute-start.13
  75.0 4.6 %collective-permute-start.6 = (bf16[512,4,64]{0,2,1:T(8,128)(2,1)S(1)}, bf16[512,4,64]{0,2,1:T(8,128)(2,1)S(1)}, u32[]{:S(2)}, u32[]{:S(2)}) collective-permute-start(bf16[512,4,64]{0,2,1:T(8,128)(2,1)S(1)} %collective-permute-done.5), channel_id=1, source_target_pairs={{0,480},{8,488},{16,496},{24,504},{32,0},{40,8},{48,16},{56,24},{6... | collective-permute-start | bytes 786440 | tf_op jit(solution)/shard_map/ppermute | solution.py:79
  81.1 1.9 collective-permute-start.14
  83.7 5.0 %collective-permute-start.7 = (bf16[512,4,64]{0,2,1:T(8,128)(2,1)S(1)}, bf16[512,4,64]{0,2,1:T(8,128)(2,1)S(1)}, u32[]{:S(2)}, u32[]{:S(2)}) collective-permute-start(bf16[512,4,64]{0,2,1:T(8,128)(2,1)S(1)} %collective-permute-done.6), channel_id=1, source_target_pairs={{0,480},{8,488},{16,496},{24,504},{32,0},{40,8},{48,16},{56,24},{6... | collective-permute-start | bytes 786440 | tf_op jit(solution)/shard_map/ppermute | solution.py:79
  90.0 1.9 collective-permute-start.15
  92.6 5.0 %collective-permute-start.8 = (bf16[512,4,64]{0,2,1:T(8,128)(2,1)S(1)}, bf16[512,4,64]{0,2,1:T(8,128)(2,1)S(1)}, u32[]{:S(2)}, u32[]{:S(2)}) collective-permute-start(bf16[512,4,64]{0,2,1:T(8,128)(2,1)S(1)} %collective-permute-done.7), channel_id=1, source_target_pairs={{0,480},{8,488},{16,496},{24,504},{32,0},{40,8},{48,16},{56,24},{6... | collective-permute-start | bytes 786440 | tf_op jit(solution)/shard_map/ppermute | solution.py:79
  101.4 4.7 %collective-permute-start.9 = (bf16[512,4,64]{0,2,1:T(8,128)(2,1)S(1)}, bf16[512,4,64]{0,2,1:T(8,128)(2,1)S(1)}, u32[]{:S(2)}, u32[]{:S(2)}) collective-permute-start(bf16[512,4,64]{0,2,1:T(8,128)(2,1)S(1)} %collective-permute-done.8), channel_id=1, source_target_pairs={{0,480},{8,488},{16,496},{24,504},{32,0},{40,8},{48,16},{56,24},{6... | collective-permute-start | bytes 786440 | tf_op jit(solution)/shard_map/ppermute | solution.py:79
  110.6 6.2 %collective-permute-done.17 = bf16[512,4,64]{0,2,1:T(8,128)(2,1)S(1)} collective-permute-done((bf16[512,4,64]{0,2,1:T(8,128)(2,1)S(1)}, bf16[512,4,64]{0,2,1:T(8,128)(2,1)S(1)}, u32[]{:S(2)}, u32[]{:S(2)}) %collective-permute-start.17) | collective-permute-done | bytes 262176 | tf_op jit(solution)/shard_map/ppermute | solution.py:79
  122.7 6.9 %dot_general.61 = bf16[4,128,4096]{1,0,2:T(4,128)(2,1)} reshape(bf16[512,16,4,64]{0,3,2,1:T(8,128)(2,1)} %bitcast_dynamic-update-slice_fusion) | data formatting | bytes 8388608 | tf_op jit(solution)/shard_map/dot_general | solution.py:128
  129.6 3.9 %fusion.1 = f32[128,4,128]{0,2,1:T(8,128)S(1)} fusion(bf16[128,4096,1]{0,1,2:T(8,128)(2,1)S(1)} %bitcast.221, bf16[4,128,4096]{1,0,2:T(4,128)(2,1)} %dot_general.61), kind=kOutput, calls=%fused_computation.5 | convolution fusion | flops 536870912 | bytes 5505024 | tf_op jit(solution)/shard_map/dot_general | solution.py:128
  136.5 9.6 %all-to-all-start.1 = ((bf16[64,4,512]{2,1,0:T(4,128)(2,1)}), bf16[64,4,512]{2,1,0:T(4,128)(2,1)}, u32[]{:S(2)}, u32[]{:S(2)}) async-start(bf16[64,4,512]{2,1,0:T(4,128)(2,1)} %broadcast_select_fusion), calls=%async_computation.1 | async-start | bytes 524288 | tf_op jit(solution)/shard_map/all_to_all | solution.py:168
  146.1 2.9 %copy.116 = bf16[1,1024,1024]{1,2,0:T(8,128)(2,1)S(1)} copy(bf16[1,1024,1024]{2,1,0:T(8,128)(2,1)} %param.13) | data formatting | bytes 4194304 | tf_op args[5]
  149.0 16.8 %all-to-all-done.1 = bf16[64,4,512]{2,1,0:T(4,128)(2,1)} async-done(((bf16[64,4,512]{2,1,0:T(4,128)(2,1)}), bf16[64,4,512]{2,1,0:T(4,128)(2,1)}, u32[]{:S(2)}, u32[]{:S(2)}) %all-to-all-start.1) | async-done | bytes 262176 | tf_op jit(solution)/shard_map/all_to_all | solution.py:168
  174.0 4.6 %all-to-all-start.2 = ((bf16[64,5,512]{2,1,0:T(8,128)(2,1)}), bf16[64,5,512]{2,1,0:T(8,128)(2,1)S(1)}, u32[]{:S(2)}, u32[]{:S(2)}) async-start(bf16[64,5,512]{2,1,0:T(8,128)(2,1)} %fusion.18), calls=%async_computation.2 | async-start | bytes 1048576 | tf_op jit(solution)/shard_map/all_to_all | solution.py:186
  180.3 19.1 %all-to-all-done.2 = bf16[64,5,512]{2,1,0:T(8,128)(2,1)S(1)} async-done(((bf16[64,5,512]{2,1,0:T(8,128)(2,1)}), bf16[64,5,512]{2,1,0:T(8,128)(2,1)S(1)}, u32[]{:S(2)}, u32[]{:S(2)}) %all-to-all-start.2) | async-done | bytes 327712 | tf_op jit(solution)/shard_map/all_to_all | solution.py:186
  201.5 3.2 %slice.102 = bf16[256,4096]{0,1:T(8,128)(2,1)} slice(bf16[768,4096]{0,1:T(8,128)(2,1)} %all-gather.2.cloned.1.call-done), slice={[0:256], [0:4096]} | slice | bytes 4194304 | tf_op jit(solution)/shard_map/slice | solution.py:120
  204.6 2.9 %copy.125 = bf16[256,4096]{1,0:T(8,128)(2,1)S(1)} copy(bf16[256,4096]{0,1:T(8,128)(2,1)} %slice.102) | data formatting | bytes 4194304 | tf_op jit(solution)/shard_map/slice | solution.py:120
  213.0 21.0 %all-to-all-start.3 = ((bf16[8,128,512]{2,1,0:T(8,128)(2,1)}), bf16[8,128,512]{2,1,0:T(8,128)(2,1)S(1)}, u32[]{:S(2)}, u32[]{:S(2)}) async-start(bf16[8,128,512]{2,1,0:T(8,128)(2,1)} %bitcast.209), calls=%async_computation.3 | async-start | bytes 2097152 | tf_op jit(solution)/shard_map/all_to_all | solution.py:224
  234.7 14.4 %all-to-all-done.3 = bf16[8,128,512]{2,1,0:T(8,128)(2,1)S(1)} async-done(((bf16[8,128,512]{2,1,0:T(8,128)(2,1)}), bf16[8,128,512]{2,1,0:T(8,128)(2,1)S(1)}, u32[]{:S(2)}, u32[]{:S(2)}) %all-to-all-start.3) | async-done | bytes 1048608 | tf_op jit(solution)/shard_map/all_to_all | solution.py:224
  (167 shorter events, 52.6 us)
Async XLA Ops:
  7.2 19.7 %copy-start = (bf16[64,1024]{1,0:T(8,128)(2,1)S(1)}, bf16[64,1024]{1,0:T(8,128)(2,1)}, u32[]{:S(2)}) copy-start(bf16[64,1024]{1,0:T(8,128)(2,1)} %param.11) | copy-start | bytes 393220
  7.2 51.9 %copy-start.5 = (bf16[64,512]{1,0:T(8,128)(2,1)S(1)}, bf16[64,512]{1,0:T(8,128)(2,1)}, u32[]{:S(2)}) copy-start(bf16[64,512]{1,0:T(8,128)(2,1)} %param.10) | copy-start | bytes 196612
  7.2 47.1 %copy-start.6 = (bf16[4096]{0:T(1024)(128)(2,1)S(1)}, bf16[4096]{0:T(1024)(128)(2,1)}, u32[]{:S(2)}) copy-start(bf16[4096]{0:T(1024)(128)(2,1)} %param.9) | copy-start | bytes 24580
  7.2 24.4 %collective-permute-start.1 = (bf16[512,64]{0,1:T(8,128)(2,1)}, bf16[512,64]{0,1:T(8,128)(2,1)S(1)}, u32[]{:S(2)}, u32[]{:S(2)}) collective-permute-start(bf16[512,64]{0,1:T(8,128)(2,1)} %bitcast.224), channel_id=1, source_target_pairs={{0,8},{8,16},{16,24},{24,0},{32,40},{40,48},{48,56},{56,32},{64,72... | collective-permute-start | bytes 196616 | tf_op jit(solution)/shard_map/ppermute | solution.py:79
  11.4 22.2 %collective-permute-start = (bf16[512,64]{0,1:T(8,128)(2,1)}, bf16[512,64]{0,1:T(8,128)(2,1)S(1)}, u32[]{:S(2)}, u32[]{:S(2)}) collective-permute-start(bf16[512,64]{0,1:T(8,128)(2,1)} %bitcast.225), channel_id=1, source_target_pairs={{0,24},{8,0},{16,8},{24,16},{32,56},{40,32},{48,40},{56,48},{64,88... | collective-permute-start | bytes 196616 | tf_op jit(solution)/shard_map/ppermute | solution.py:79
  16.9 57.4 %all-to-all-start = ((bf16[8,128,512]{1,2,0:T(8,128)(2,1)}), bf16[8,128,512]{1,2,0:T(8,128)(2,1)S(1)}, u32[]{:S(2)}, u32[]{:S(2)}) async-start(bf16[8,128,512]{1,2,0:T(8,128)(2,1)} %broadcast_in_dim.72), calls=%async_computation | async-start | bytes 2097152 | tf_op jit(solution)/shard_map/all_to_all | solution.py:102
  26.9 174.6 %all-gather.2.cloned.1.call-start = ((), (), s32[]{:S(2)}) async-start(), calls=%async_computation.4 | async-start | bytes 6389760 | tf_op jit(solution)/shard_map/all_gather | solution.py:119
  31.6 22.7 %copy-start.12 = (s32[128]{0:T(128)}, s32[128]{0:T(128)S(1)}, u32[]{:S(2)}) copy-start(s32[128]{0:T(128)S(1)} %get-tuple-element.3) | copy-start | bytes 1540
  31.6 6.6 %collective-permute-start.2 = (bf16[512,64]{0,1:T(8,128)(2,1)S(1)}, bf16[512,64]{0,1:T(8,128)(2,1)S(1)}, u32[]{:S(2)}, u32[]{:S(2)}) collective-permute-start(bf16[512,64]{0,1:T(8,128)(2,1)S(1)} %collective-permute-done.1), channel_id=1, source_target_pairs={{0,8},{8,16},{16,24},{24,0},{32,40},{40,48},{48,56},{56,32},{64,72... | collective-permute-start | bytes 196616 | tf_op jit(solution)/shard_map/ppermute | solution.py:79
  39.1 13.1 %collective-permute-start.10 = (bf16[512,4,64]{0,2,1:T(8,128)(2,1)S(1)}, bf16[512,4,64]{0,2,1:T(8,128)(2,1)S(1)}, u32[]{:S(2)}, u32[]{:S(2)}) collective-permute-start(bf16[512,4,64]{0,2,1:T(8,128)(2,1)S(1)} %pad_maximum_fusion), channel_id=1, source_target_pairs={{0,32},{8,40},{16,48},{24,56},{32,64},{40,72},{48,80},{56,88},{64,... | collective-permute-start | bytes 786440 | tf_op jit(solution)/shard_map/ppermute | solution.py:79
  41.3 13.3 %collective-permute-start.3 = (bf16[512,4,64]{0,2,1:T(8,128)(2,1)S(1)}, bf16[512,4,64]{0,2,1:T(8,128)(2,1)S(1)}, u32[]{:S(2)}, u32[]{:S(2)}) collective-permute-start(bf16[512,4,64]{0,2,1:T(8,128)(2,1)S(1)} %pad_maximum_fusion), channel_id=1, source_target_pairs={{0,480},{8,488},{16,496},{24,504},{32,0},{40,8},{48,16},{56,24},{6... | collective-permute-start | bytes 786440 | tf_op jit(solution)/shard_map/ppermute | solution.py:79
  52.2 10.5 %collective-permute-start.11 = (bf16[512,4,64]{0,2,1:T(8,128)(2,1)S(1)}, bf16[512,4,64]{0,2,1:T(8,128)(2,1)S(1)}, u32[]{:S(2)}, u32[]{:S(2)}) collective-permute-start(bf16[512,4,64]{0,2,1:T(8,128)(2,1)S(1)} %collective-permute-done.10), channel_id=1, source_target_pairs={{0,32},{8,40},{16,48},{24,56},{32,64},{40,72},{48,80},{56,88},{64,... | collective-permute-start | bytes 786440 | tf_op jit(solution)/shard_map/ppermute | solution.py:79
  54.5 10.9 %collective-permute-start.4 = (bf16[512,4,64]{0,2,1:T(8,128)(2,1)S(1)}, bf16[512,4,64]{0,2,1:T(8,128)(2,1)S(1)}, u32[]{:S(2)}, u32[]{:S(2)}) collective-permute-start(bf16[512,4,64]{0,2,1:T(8,128)(2,1)S(1)} %collective-permute-done.3), channel_id=1, source_target_pairs={{0,480},{8,488},{16,496},{24,504},{32,0},{40,8},{48,16},{56,24},{6... | collective-permute-start | bytes 786440 | tf_op jit(solution)/shard_map/ppermute | solution.py:79
  62.7 9.6 %collective-permute-start.12 = (bf16[512,4,64]{0,2,1:T(8,128)(2,1)S(1)}, bf16[512,4,64]{0,2,1:T(8,128)(2,1)S(1)}, u32[]{:S(2)}, u32[]{:S(2)}) collective-permute-start(bf16[512,4,64]{0,2,1:T(8,128)(2,1)S(1)} %collective-permute-done.11), channel_id=1, source_target_pairs={{0,32},{8,40},{16,48},{24,56},{32,64},{40,72},{48,80},{56,88},{64,... | collective-permute-start | bytes 786440 | tf_op jit(solution)/shard_map/ppermute | solution.py:79
  65.4 9.6 %collective-permute-start.5 = (bf16[512,4,64]{0,2,1:T(8,128)(2,1)S(1)}, bf16[512,4,64]{0,2,1:T(8,128)(2,1)S(1)}, u32[]{:S(2)}, u32[]{:S(2)}) collective-permute-start(bf16[512,4,64]{0,2,1:T(8,128)(2,1)S(1)} %collective-permute-done.4), channel_id=1, source_target_pairs={{0,480},{8,488},{16,496},{24,504},{32,0},{40,8},{48,16},{56,24},{6... | collective-permute-start | bytes 786440 | tf_op jit(solution)/shard_map/ppermute | solution.py:79
  72.3 8.8 %collective-permute-start.13 = (bf16[512,4,64]{0,2,1:T(8,128)(2,1)S(1)}, bf16[512,4,64]{0,2,1:T(8,128)(2,1)S(1)}, u32[]{:S(2)}, u32[]{:S(2)}) collective-permute-start(bf16[512,4,64]{0,2,1:T(8,128)(2,1)S(1)} %collective-permute-done.12), channel_id=1, source_target_pairs={{0,32},{8,40},{16,48},{24,56},{32,64},{40,72},{48,80},{56,88},{64,... | collective-permute-start | bytes 786440 | tf_op jit(solution)/shard_map/ppermute | solution.py:79
  75.0 8.8 %collective-permute-start.6 = (bf16[512,4,64]{0,2,1:T(8,128)(2,1)S(1)}, bf16[512,4,64]{0,2,1:T(8,128)(2,1)S(1)}, u32[]{:S(2)}, u32[]{:S(2)}) collective-permute-start(bf16[512,4,64]{0,2,1:T(8,128)(2,1)S(1)} %collective-permute-done.5), channel_id=1, source_target_pairs={{0,480},{8,488},{16,496},{24,504},{32,0},{40,8},{48,16},{56,24},{6... | collective-permute-start | bytes 786440 | tf_op jit(solution)/shard_map/ppermute | solution.py:79
  79.6 21.9 %copy-start.7 = (f32[128]{0:T(128)}, f32[128]{0:T(128)S(1)}, u32[]{:S(2)}) copy-start(f32[128]{0:T(128)S(1)} %add_rsqrt_fusion) | copy-start | bytes 1540
  81.1 8.9 %collective-permute-start.14 = (bf16[512,4,64]{0,2,1:T(8,128)(2,1)S(1)}, bf16[512,4,64]{0,2,1:T(8,128)(2,1)S(1)}, u32[]{:S(2)}, u32[]{:S(2)}) collective-permute-start(bf16[512,4,64]{0,2,1:T(8,128)(2,1)S(1)} %collective-permute-done.13), channel_id=1, source_target_pairs={{0,32},{8,40},{16,48},{24,56},{32,64},{40,72},{48,80},{56,88},{64,... | collective-permute-start | bytes 786440 | tf_op jit(solution)/shard_map/ppermute | solution.py:79
  83.7 8.9 %collective-permute-start.7 = (bf16[512,4,64]{0,2,1:T(8,128)(2,1)S(1)}, bf16[512,4,64]{0,2,1:T(8,128)(2,1)S(1)}, u32[]{:S(2)}, u32[]{:S(2)}) collective-permute-start(bf16[512,4,64]{0,2,1:T(8,128)(2,1)S(1)} %collective-permute-done.6), channel_id=1, source_target_pairs={{0,480},{8,488},{16,496},{24,504},{32,0},{40,8},{48,16},{56,24},{6... | collective-permute-start | bytes 786440 | tf_op jit(solution)/shard_map/ppermute | solution.py:79
  90.0 8.8 %collective-permute-start.15 = (bf16[512,4,64]{0,2,1:T(8,128)(2,1)S(1)}, bf16[512,4,64]{0,2,1:T(8,128)(2,1)S(1)}, u32[]{:S(2)}, u32[]{:S(2)}) collective-permute-start(bf16[512,4,64]{0,2,1:T(8,128)(2,1)S(1)} %collective-permute-done.14), channel_id=1, source_target_pairs={{0,32},{8,40},{16,48},{24,56},{32,64},{40,72},{48,80},{56,88},{64,... | collective-permute-start | bytes 786440 | tf_op jit(solution)/shard_map/ppermute | solution.py:79
  92.6 8.8 %collective-permute-start.8 = (bf16[512,4,64]{0,2,1:T(8,128)(2,1)S(1)}, bf16[512,4,64]{0,2,1:T(8,128)(2,1)S(1)}, u32[]{:S(2)}, u32[]{:S(2)}) collective-permute-start(bf16[512,4,64]{0,2,1:T(8,128)(2,1)S(1)} %collective-permute-done.7), channel_id=1, source_target_pairs={{0,480},{8,488},{16,496},{24,504},{32,0},{40,8},{48,16},{56,24},{6... | collective-permute-start | bytes 786440 | tf_op jit(solution)/shard_map/ppermute | solution.py:79
  98.8 8.5 %collective-permute-start.16 = (bf16[512,4,64]{0,2,1:T(8,128)(2,1)S(1)}, bf16[512,4,64]{0,2,1:T(8,128)(2,1)S(1)}, u32[]{:S(2)}, u32[]{:S(2)}) collective-permute-start(bf16[512,4,64]{0,2,1:T(8,128)(2,1)S(1)} %collective-permute-done.15), channel_id=1, source_target_pairs={{0,32},{8,40},{16,48},{24,56},{32,64},{40,72},{48,80},{56,88},{64,... | collective-permute-start | bytes 786440 | tf_op jit(solution)/shard_map/ppermute | solution.py:79
  101.4 8.5 %collective-permute-start.9 = (bf16[512,4,64]{0,2,1:T(8,128)(2,1)S(1)}, bf16[512,4,64]{0,2,1:T(8,128)(2,1)S(1)}, u32[]{:S(2)}, u32[]{:S(2)}) collective-permute-start(bf16[512,4,64]{0,2,1:T(8,128)(2,1)S(1)} %collective-permute-done.8), channel_id=1, source_target_pairs={{0,480},{8,488},{16,496},{24,504},{32,0},{40,8},{48,16},{56,24},{6... | collective-permute-start | bytes 786440 | tf_op jit(solution)/shard_map/ppermute | solution.py:79
  107.3 9.6 %collective-permute-start.17 = (bf16[512,4,64]{0,2,1:T(8,128)(2,1)S(1)}, bf16[512,4,64]{0,2,1:T(8,128)(2,1)S(1)}, u32[]{:S(2)}, u32[]{:S(2)}) collective-permute-start(bf16[512,4,64]{0,2,1:T(8,128)(2,1)S(1)} %collective-permute-done.16), channel_id=1, source_target_pairs={{0,32},{8,40},{16,48},{24,56},{32,64},{40,72},{48,80},{56,88},{64,... | collective-permute-start | bytes 786440 | tf_op jit(solution)/shard_map/ppermute | solution.py:79
  136.5 29.3 %all-to-all-start.1 = ((bf16[64,4,512]{2,1,0:T(4,128)(2,1)}), bf16[64,4,512]{2,1,0:T(4,128)(2,1)}, u32[]{:S(2)}, u32[]{:S(2)}) async-start(bf16[64,4,512]{2,1,0:T(4,128)(2,1)} %broadcast_select_fusion), calls=%async_computation.1 | async-start | bytes 524288 | tf_op jit(solution)/shard_map/all_to_all | solution.py:168
  171.1 7.5 %copy-start.9 = (s32[64]{0:T(128)S(1)}, s32[64]{0:T(128)}, u32[]{:S(2)}) copy-start(s32[64]{0:T(128)} %param.14) | copy-start | bytes 772
  171.1 7.5 %copy-start.10 = (s32[128]{0:T(128)S(1)}, s32[128]{0:T(128)}, u32[]{:S(2)}) copy-start(s32[128]{0:T(128)} %get-tuple-element.2) | copy-start | bytes 1540
  171.1 7.6 %copy-start.13 = (s32[128]{0:T(128)S(1)}, s32[128]{0:T(128)}, u32[]{:S(2)}) copy-start(s32[128]{0:T(128)} %copy-done.12) | copy-start | bytes 1540
  171.1 7.6 %copy-start.8 = (f32[128]{0:T(128)S(1)}, f32[128]{0:T(128)}, u32[]{:S(2)}) copy-start(f32[128]{0:T(128)} %copy-done.7) | copy-start | bytes 1540
  174.0 25.4 %all-to-all-start.2 = ((bf16[64,5,512]{2,1,0:T(8,128)(2,1)}), bf16[64,5,512]{2,1,0:T(8,128)(2,1)S(1)}, u32[]{:S(2)}, u32[]{:S(2)}) async-start(bf16[64,5,512]{2,1,0:T(8,128)(2,1)} %fusion.18), calls=%async_computation.2 | async-start | bytes 1048576 | tf_op jit(solution)/shard_map/all_to_all | solution.py:186
  213.0 36.1 %all-to-all-start.3 = ((bf16[8,128,512]{2,1,0:T(8,128)(2,1)}), bf16[8,128,512]{2,1,0:T(8,128)(2,1)S(1)}, u32[]{:S(2)}, u32[]{:S(2)}) async-start(bf16[8,128,512]{2,1,0:T(8,128)(2,1)} %bitcast.209), calls=%async_computation.3 | async-start | bytes 2097152 | tf_op jit(solution)/shard_map/all_to_all | solution.py:224
  (5 other events, 17.6 us)
Sparse Core Ops, SparseCore 0:
  30.7 150.9 all-gather.1

commit v8 on v7

--- a/solution.py
+++ b/solution.py
@@ -58,12 +58,15 @@
     rel[0] = value
     ahead = value
     behind = value
-    for k in range(1, count // 2 + 1):
+    far = count // 2 if count % 2 == 0 else None
+    for k in range(1, (count - 1) // 2 + 1):
+        if far is not None and k == far - 1:
+            half = value.shape[0] // 2
+            rel[far] = jnp.concatenate([step(behind[:half], 2), step(ahead[half:], -2)], axis=0)
         behind = step(behind, 1)
         rel[(-k) % count] = behind
-        if k < count - k:
-            ahead = step(ahead, -1)
-            rel[k] = ahead
+        ahead = step(ahead, -1)
+        rel[k] = ahead
     return rel
 
 

time: 258 us -> 259 us (level)
  waiting for transfers between devices: 73.5 us -> 63.4 us
  starting transfers between devices: 105 us -> 115 us
    ppermute x18 -> x20, starting transfers between devices: 59.8 us -> 74 us  [shift(): return lax.ppermute(value, axis_name, pairs)]
    ppermute x18 -> x20, waiting for transfers between devices: 23.2 us -> 10.4 us  [shift(): return lax.ppermute(value, axis_name, pairs)]
    all_to_all x1, starting transfers between devices: 21 us -> 14.7 us  [shards(): lax.all_to_all(jnp.moveaxis(pieces, 1, 0), 'tensor', split_axis=0, concat...]
    all_to_all x1, waiting for transfers between devices: 19.1 us -> 23.1 us  [shards(): lax.all_to_all(jnp.concatenate([out_block, log_row], axis=1), 'seq', spli...]
    all_to_all x1, starting transfers between devices: 9.57 us -> 12.3 us  [shards(): lax.all_to_all(outgoing, 'seq', split_axis=0, concat_axis=0, tiled=True)]
    unnamed x45 -> x58, local copies, waits for them, and re-layouts: 15.5 us -> 15.1 us
  transfers between devices with their start and end apart: 23 -> 25, of which waited for: 13 -> 13; matrix products, arithmetic and copies ran while one was open for 20% -> 20% of each run, Pallas kernels for 0% -> 0%
where the time goes in v8:
time: 259 us; the launch traced here: 258 us
  starting transfers between devices  115 us (44%)
  waiting for transfers between devices  63.4 us (24%)
  local copies, waits for them, and re-layouts  39.5 us (15%)
  between operations  15 us (6%)
  other arithmetic  13.5 us (5%)
  matrix products  10.6 us (4%)
    ppermute x20, starting transfers between devices, shift(): return lax.ppermute(value, axis_name, pairs)  74 us
    all_to_all x1, waiting for transfers between devices, shards(): lax.all_to_all(jnp.concatenate([out_block, log_row], axis=1), 'seq', spli...  23.1 us
    all_to_all x1, waiting for transfers between devices, shards(): lax.all_to_all(outgoing, 'seq', split_axis=0, concat_axis=0, tiled=True)  15.5 us
    unnamed x58, local copies, waits for them, and re-layouts  15.1 us
    all_to_all x1, starting transfers between devices, shards(): lax.all_to_all(jnp.moveaxis(pieces, 1, 0), 'tensor', split_axis=0, concat...  14.7 us
    all_to_all x1, waiting for transfers between devices, shards(): lax.all_to_all(jnp.moveaxis(pieces, 1, 0), 'tensor', split_axis=0, concat...  14.4 us
    all_to_all x1, starting transfers between devices, shards(): lax.all_to_all(outgoing, 'seq', split_axis=0, concat_axis=0, tiled=True)  12.3 us
    ppermute x20, waiting for transfers between devices, shift(): return lax.ppermute(value, axis_name, pairs)  10.4 us
  transfers between devices with their start and end apart: 25, of which 13 were waited for; matrix products, arithmetic and copies ran while one was open for 20% of the time, Pallas kernels for 0%

profile of v8, /device:TPU:1, one launch (start us, length us, event | category | flops | bytes accessed | tf_op | source)
XLA Modules:
  0.0 257.5 jit_solution(14059432982178618444)
XLA Ops:
  7.2 5.6 %collective-permute-start = (bf16[512,64]{0,1:T(8,128)(2,1)}, bf16[512,64]{0,1:T(8,128)(2,1)S(1)}, u32[]{:S(2)}, u32[]{:S(2)}) collective-permute-start(bf16[512,64]{0,1:T(8,128)(2,1)} %bitcast.226), channel_id=1, source_target_pairs={{0,24},{8,0},{16,8},{24,16},{32,56},{40,32},{48,40},{56,48},{64,88... | collective-permute-start | bytes 196616 | tf_op jit(solution)/shard_map/ppermute | solution.py:82
  12.8 1.9 collective-permute-start.3
  16.9 8.8 %all-to-all-start = ((bf16[8,128,512]{1,2,0:T(8,128)(2,1)}), bf16[8,128,512]{1,2,0:T(8,128)(2,1)S(1)}, u32[]{:S(2)}, u32[]{:S(2)}) async-start(bf16[8,128,512]{1,2,0:T(8,128)(2,1)} %broadcast_in_dim.72), calls=%async_computation | async-start | bytes 2097152 | tf_op jit(solution)/shard_map/all_to_all | solution.py:105
  28.4 4.9 %collective-permute-start.2 = (bf16[256,64]{0,1:T(8,128)(2,1)S(1)}, bf16[256,64]{0,1:T(8,128)(2,1)S(1)}, u32[]{:S(2)}, u32[]{:S(2)}) collective-permute-start(bf16[256,64]{0,1:T(8,128)(2,1)S(1)} %get-tuple-element.18), channel_id=1, source_target_pairs={{0,16},{8,24},{16,0},{24,8},{32,48},{40,56},{48,32},{56,40},{64,80... | collective-permute-start | bytes 98312 | tf_op jit(solution)/shard_map/ppermute | solution.py:82
  37.1 7.6 %collective-permute-start.4 = (bf16[512,4,64]{0,2,1:T(8,128)(2,1)S(1)}, bf16[512,4,64]{0,2,1:T(8,128)(2,1)S(1)}, u32[]{:S(2)}, u32[]{:S(2)}) collective-permute-start(bf16[512,4,64]{0,2,1:T(8,128)(2,1)S(1)} %pad_maximum_fusion), channel_id=1, source_target_pairs={{0,480},{8,488},{16,496},{24,504},{32,0},{40,8},{48,16},{56,24},{6... | collective-permute-start | bytes 786440 | tf_op jit(solution)/shard_map/ppermute | solution.py:82
  44.7 1.9 collective-permute-start.11
  49.3 5.3 %collective-permute-start.5 = (bf16[512,4,64]{0,2,1:T(8,128)(2,1)S(1)}, bf16[512,4,64]{0,2,1:T(8,128)(2,1)S(1)}, u32[]{:S(2)}, u32[]{:S(2)}) collective-permute-start(bf16[512,4,64]{0,2,1:T(8,128)(2,1)S(1)} %collective-permute-done.4), channel_id=1, source_target_pairs={{0,480},{8,488},{16,496},{24,504},{32,0},{40,8},{48,16},{56,24},{6... | collective-permute-start | bytes 786440 | tf_op jit(solution)/shard_map/ppermute | solution.py:82
  54.6 1.9 collective-permute-start.12
  58.5 5.2 %collective-permute-start.6 = (bf16[512,4,64]{0,2,1:T(8,128)(2,1)S(1)}, bf16[512,4,64]{0,2,1:T(8,128)(2,1)S(1)}, u32[]{:S(2)}, u32[]{:S(2)}) collective-permute-start(bf16[512,4,64]{0,2,1:T(8,128)(2,1)S(1)} %collective-permute-done.5), channel_id=1, source_target_pairs={{0,480},{8,488},{16,496},{24,504},{32,0},{40,8},{48,16},{56,24},{6... | collective-permute-start | bytes 786440 | tf_op jit(solution)/shard_map/ppermute | solution.py:82
  64.2 1.9 collective-permute-start.13
  67.5 5.0 %collective-permute-start.7 = (bf16[512,4,64]{0,2,1:T(8,128)(2,1)S(1)}, bf16[512,4,64]{0,2,1:T(8,128)(2,1)S(1)}, u32[]{:S(2)}, u32[]{:S(2)}) collective-permute-start(bf16[512,4,64]{0,2,1:T(8,128)(2,1)S(1)} %collective-permute-done.6), channel_id=1, source_target_pairs={{0,480},{8,488},{16,496},{24,504},{32,0},{40,8},{48,16},{56,24},{6... | collective-permute-start | bytes 786440 | tf_op jit(solution)/shard_map/ppermute | solution.py:82
  72.9 1.9 collective-permute-start.14
  76.3 5.3 %collective-permute-start.8 = (bf16[512,4,64]{0,2,1:T(8,128)(2,1)S(1)}, bf16[512,4,64]{0,2,1:T(8,128)(2,1)S(1)}, u32[]{:S(2)}, u32[]{:S(2)}) collective-permute-start(bf16[512,4,64]{0,2,1:T(8,128)(2,1)S(1)} %collective-permute-done.7), channel_id=1, source_target_pairs={{0,480},{8,488},{16,496},{24,504},{32,0},{40,8},{48,16},{56,24},{6... | collective-permute-start | bytes 786440 | tf_op jit(solution)/shard_map/ppermute | solution.py:82
  82.4 1.9 collective-permute-start.15
  85.5 5.1 %collective-permute-start.9 = (bf16[512,4,64]{0,2,1:T(8,128)(2,1)S(1)}, bf16[512,4,64]{0,2,1:T(8,128)(2,1)S(1)}, u32[]{:S(2)}, u32[]{:S(2)}) collective-permute-start(bf16[512,4,64]{0,2,1:T(8,128)(2,1)S(1)} %collective-permute-done.8), channel_id=1, source_target_pairs={{0,480},{8,488},{16,496},{24,504},{32,0},{40,8},{48,16},{56,24},{6... | collective-permute-start | bytes 786440 | tf_op jit(solution)/shard_map/ppermute | solution.py:82
  91.2 1.9 collective-permute-start.16
  94.8 5.5 %collective-permute-start.10 = (bf16[512,4,64]{0,2,1:T(8,128)(2,1)S(1)}, bf16[512,4,64]{0,2,1:T(8,128)(2,1)S(1)}, u32[]{:S(2)}, u32[]{:S(2)}) collective-permute-start(bf16[512,4,64]{0,2,1:T(8,128)(2,1)S(1)} %collective-permute-done.9), channel_id=1, source_target_pairs={{0,480},{8,488},{16,496},{24,504},{32,0},{40,8},{48,16},{56,24},{6... | collective-permute-start | bytes 786440 | tf_op jit(solution)/shard_map/ppermute | solution.py:82
  101.0 1.9 collective-permute-start.17
  102.9 5.5 %collective-permute-start.18 = (bf16[256,4,64]{0,2,1:T(8,128)(2,1)S(1)}, bf16[256,4,64]{0,2,1:T(8,128)(2,1)S(1)}, u32[]{:S(2)}, u32[]{:S(2)}) collective-permute-start(bf16[256,4,64]{0,2,1:T(8,128)(2,1)S(1)} %slice.113), channel_id=1, source_target_pairs={{0,448},{8,456},{16,464},{24,472},{32,480},{40,488},{48,496},{56,5... | collective-permute-start | bytes 393224 | tf_op jit(solution)/shard_map/ppermute | solution.py:82
  108.4 1.9 collective-permute-start.19
  113.1 4.8 %collective-permute-done.19 = bf16[512,4,64]{0,2,1:T(8,128)(2,1)S(1)} collective-permute-done((bf16[512,4,64]{0,2,1:T(8,128)(2,1)S(1)}, bf16[512,4,64]{0,2,1:T(8,128)(2,1)S(1)}, u32[]{:S(2)}, u32[]{:S(2)}) %collective-permute-start.19) | collective-permute-done | bytes 262176 | tf_op jit(solution)/shard_map/ppermute | solution.py:82
  123.1 7.0 %dot_general.61 = bf16[4,128,4096]{1,0,2:T(4,128)(2,1)} reshape(bf16[512,16,4,64]{0,3,2,1:T(8,128)(2,1)} %bitcast_dynamic-update-slice_fusion) | data formatting | bytes 8388608 | tf_op jit(solution)/shard_map/dot_general | solution.py:131
  130.1 4.0 %fusion.1 = f32[128,4,128]{0,2,1:T(8,128)S(1)} fusion(bf16[128,4096,1]{0,1,2:T(8,128)(2,1)S(1)} %bitcast.224, bf16[4,128,4096]{1,0,2:T(4,128)(2,1)} %dot_general.61), kind=kOutput, calls=%fused_computation.5 | convolution fusion | flops 536870912 | bytes 5505024 | tf_op jit(solution)/shard_map/dot_general | solution.py:131
  137.1 12.3 %all-to-all-start.1 = ((bf16[64,4,512]{2,1,0:T(4,128)(2,1)}), bf16[64,4,512]{2,1,0:T(4,128)(2,1)}, u32[]{:S(2)}, u32[]{:S(2)}) async-start(bf16[64,4,512]{2,1,0:T(4,128)(2,1)} %broadcast_select_fusion), calls=%async_computation.1 | async-start | bytes 524288 | tf_op jit(solution)/shard_map/all_to_all | solution.py:171
  149.4 2.9 %copy.116 = bf16[1,1024,1024]{1,2,0:T(8,128)(2,1)S(1)} copy(bf16[1,1024,1024]{2,1,0:T(8,128)(2,1)} %param.13) | data formatting | bytes 4194304 | tf_op args[5]
  152.2 15.5 %all-to-all-done.1 = bf16[64,4,512]{2,1,0:T(4,128)(2,1)} async-done(((bf16[64,4,512]{2,1,0:T(4,128)(2,1)}), bf16[64,4,512]{2,1,0:T(4,128)(2,1)}, u32[]{:S(2)}, u32[]{:S(2)}) %all-to-all-start.1) | async-done | bytes 262176 | tf_op jit(solution)/shard_map/all_to_all | solution.py:171
  175.9 5.6 %all-to-all-start.2 = ((bf16[64,5,512]{2,1,0:T(8,128)(2,1)}), bf16[64,5,512]{2,1,0:T(8,128)(2,1)S(1)}, u32[]{:S(2)}, u32[]{:S(2)}) async-start(bf16[64,5,512]{2,1,0:T(8,128)(2,1)} %fusion.18), calls=%async_computation.2 | async-start | bytes 1048576 | tf_op jit(solution)/shard_map/all_to_all | solution.py:189
  183.2 23.1 %all-to-all-done.2 = bf16[64,5,512]{2,1,0:T(8,128)(2,1)S(1)} async-done(((bf16[64,5,512]{2,1,0:T(8,128)(2,1)}), bf16[64,5,512]{2,1,0:T(8,128)(2,1)S(1)}, u32[]{:S(2)}, u32[]{:S(2)}) %all-to-all-start.2) | async-done | bytes 327712 | tf_op jit(solution)/shard_map/all_to_all | solution.py:189
  208.4 3.2 %slice.122 = bf16[256,4096]{0,1:T(8,128)(2,1)} slice(bf16[768,4096]{0,1:T(8,128)(2,1)} %all-gather.2.cloned.1.call-done), slice={[0:256], [0:4096]} | slice | bytes 4194304 | tf_op jit(solution)/shard_map/slice | solution.py:123
  211.6 2.9 %copy.125 = bf16[256,4096]{1,0:T(8,128)(2,1)S(1)} copy(bf16[256,4096]{0,1:T(8,128)(2,1)} %slice.122) | data formatting | bytes 4194304 | tf_op jit(solution)/shard_map/slice | solution.py:123
  220.0 14.7 %all-to-all-start.3 = ((bf16[8,128,512]{2,1,0:T(8,128)(2,1)}), bf16[8,128,512]{2,1,0:T(8,128)(2,1)S(1)}, u32[]{:S(2)}, u32[]{:S(2)}) async-start(bf16[8,128,512]{2,1,0:T(8,128)(2,1)} %bitcast.212), calls=%async_computation.3 | async-start | bytes 2097152 | tf_op jit(solution)/shard_map/all_to_all | solution.py:227
  235.5 14.4 %all-to-all-done.3 = bf16[8,128,512]{2,1,0:T(8,128)(2,1)S(1)} async-done(((bf16[8,128,512]{2,1,0:T(8,128)(2,1)}), bf16[8,128,512]{2,1,0:T(8,128)(2,1)S(1)}, u32[]{:S(2)}, u32[]{:S(2)}) %all-to-all-start.3) | async-done | bytes 1048608 | tf_op jit(solution)/shard_map/all_to_all | solution.py:227
  (189 shorter events, 51.2 us)
Async XLA Ops:
  7.2 26.1 %copy-start = (bf16[64,1024]{1,0:T(8,128)(2,1)S(1)}, bf16[64,1024]{1,0:T(8,128)(2,1)}, u32[]{:S(2)}) copy-start(bf16[64,1024]{1,0:T(8,128)(2,1)} %param.11) | copy-start | bytes 393220
  7.2 29.6 %copy-start.3 = (bf16[64,512]{1,0:T(8,128)(2,1)S(1)}, bf16[64,512]{1,0:T(8,128)(2,1)}, u32[]{:S(2)}) copy-start(bf16[64,512]{1,0:T(8,128)(2,1)} %param.10) | copy-start | bytes 196612
  7.2 28.6 %copy-start.13 = (s32[1,64]{1,0:T(1,128)S(1)}, s32[1,64]{1,0:T(1,128)}, u32[]{:S(2)}) copy-start(s32[1,64]{1,0:T(1,128)} %param.15) | copy-start | bytes 772
  7.2 29.3 %copy-start.16 = (s32[64]{0:T(128)S(1)}, s32[64]{0:T(128)}, u32[]{:S(2)}) copy-start(s32[64]{0:T(128)} %param.14) | copy-start | bytes 772
  7.2 49.5 %copy-start.9 = (bf16[4096]{0:T(1024)(128)(2,1)S(1)}, bf16[4096]{0:T(1024)(128)(2,1)}, u32[]{:S(2)}) copy-start(bf16[4096]{0:T(1024)(128)(2,1)} %param.9) | copy-start | bytes 24580
  7.2 29.5 %collective-permute-start = (bf16[512,64]{0,1:T(8,128)(2,1)}, bf16[512,64]{0,1:T(8,128)(2,1)S(1)}, u32[]{:S(2)}, u32[]{:S(2)}) collective-permute-start(bf16[512,64]{0,1:T(8,128)(2,1)} %bitcast.226), channel_id=1, source_target_pairs={{0,24},{8,0},{16,8},{24,16},{32,56},{40,32},{48,40},{56,48},{64,88... | collective-permute-start | bytes 196616 | tf_op jit(solution)/shard_map/ppermute | solution.py:82
  12.8 23.9 %collective-permute-start.3 = (bf16[512,64]{0,1:T(8,128)(2,1)}, bf16[512,64]{0,1:T(8,128)(2,1)S(1)}, u32[]{:S(2)}, u32[]{:S(2)}) collective-permute-start(bf16[512,64]{0,1:T(8,128)(2,1)} %bitcast.227), channel_id=1, source_target_pairs={{0,8},{8,16},{16,24},{24,0},{32,40},{40,48},{48,56},{56,32},{64,72... | collective-permute-start | bytes 196616 | tf_op jit(solution)/shard_map/ppermute | solution.py:82
  16.9 58.6 %all-to-all-start = ((bf16[8,128,512]{1,2,0:T(8,128)(2,1)}), bf16[8,128,512]{1,2,0:T(8,128)(2,1)S(1)}, u32[]{:S(2)}, u32[]{:S(2)}) async-start(bf16[8,128,512]{1,2,0:T(8,128)(2,1)} %broadcast_in_dim.72), calls=%async_computation | async-start | bytes 2097152 | tf_op jit(solution)/shard_map/all_to_all | solution.py:105
  25.7 182.7 %all-gather.2.cloned.1.call-start = ((), (), s32[]{:S(2)}) async-start(), calls=%async_computation.4 | async-start | bytes 6389760 | tf_op jit(solution)/shard_map/all_gather | solution.py:122
  26.5 10.2 %collective-permute-start.1 = (bf16[256,64]{0,1:T(8,128)(2,1)S(1)}, bf16[256,64]{0,1:T(8,128)(2,1)S(1)}, u32[]{:S(2)}, u32[]{:S(2)}) collective-permute-start(bf16[256,64]{0,1:T(8,128)(2,1)S(1)} %get-tuple-element.17), channel_id=1, source_target_pairs={{0,16},{8,24},{16,0},{24,8},{32,48},{40,56},{48,32},{56,40},{64,80... | collective-permute-start | bytes 98312 | tf_op jit(solution)/shard_map/ppermute | solution.py:82
  28.4 8.3 %collective-permute-start.2 = (bf16[256,64]{0,1:T(8,128)(2,1)S(1)}, bf16[256,64]{0,1:T(8,128)(2,1)S(1)}, u32[]{:S(2)}, u32[]{:S(2)}) collective-permute-start(bf16[256,64]{0,1:T(8,128)(2,1)S(1)} %get-tuple-element.18), channel_id=1, source_target_pairs={{0,16},{8,24},{16,0},{24,8},{32,48},{40,56},{48,32},{56,40},{64,80... | collective-permute-start | bytes 98312 | tf_op jit(solution)/shard_map/ppermute | solution.py:82
  37.1 12.2 %collective-permute-start.4 = (bf16[512,4,64]{0,2,1:T(8,128)(2,1)S(1)}, bf16[512,4,64]{0,2,1:T(8,128)(2,1)S(1)}, u32[]{:S(2)}, u32[]{:S(2)}) collective-permute-start(bf16[512,4,64]{0,2,1:T(8,128)(2,1)S(1)} %pad_maximum_fusion), channel_id=1, source_target_pairs={{0,480},{8,488},{16,496},{24,504},{32,0},{40,8},{48,16},{56,24},{6... | collective-permute-start | bytes 786440 | tf_op jit(solution)/shard_map/ppermute | solution.py:82
  44.7 9.9 %collective-permute-start.11 = (bf16[512,4,64]{0,2,1:T(8,128)(2,1)S(1)}, bf16[512,4,64]{0,2,1:T(8,128)(2,1)S(1)}, u32[]{:S(2)}, u32[]{:S(2)}) collective-permute-start(bf16[512,4,64]{0,2,1:T(8,128)(2,1)S(1)} %pad_maximum_fusion), channel_id=1, source_target_pairs={{0,32},{8,40},{16,48},{24,56},{32,64},{40,72},{48,80},{56,88},{64,... | collective-permute-start | bytes 786440 | tf_op jit(solution)/shard_map/ppermute | solution.py:82
  46.6 10.9 %copy-start.11 = (f32[64]{0:T(128)}, f32[64]{0:T(128)S(1)}, u32[]{:S(2)}) copy-start(f32[64]{0:T(128)S(1)} %multiply_power_fusion) | copy-start | bytes 772
  49.3 9.2 %collective-permute-start.5 = (bf16[512,4,64]{0,2,1:T(8,128)(2,1)S(1)}, bf16[512,4,64]{0,2,1:T(8,128)(2,1)S(1)}, u32[]{:S(2)}, u32[]{:S(2)}) collective-permute-start(bf16[512,4,64]{0,2,1:T(8,128)(2,1)S(1)} %collective-permute-done.4), channel_id=1, source_target_pairs={{0,480},{8,488},{16,496},{24,504},{32,0},{40,8},{48,16},{56,24},{6... | collective-permute-start | bytes 786440 | tf_op jit(solution)/shard_map/ppermute | solution.py:82
  54.6 9.5 %collective-permute-start.12 = (bf16[512,4,64]{0,2,1:T(8,128)(2,1)S(1)}, bf16[512,4,64]{0,2,1:T(8,128)(2,1)S(1)}, u32[]{:S(2)}, u32[]{:S(2)}) collective-permute-start(bf16[512,4,64]{0,2,1:T(8,128)(2,1)S(1)} %collective-permute-done.11), channel_id=1, source_target_pairs={{0,32},{8,40},{16,48},{24,56},{32,64},{40,72},{48,80},{56,88},{64,... | collective-permute-start | bytes 786440 | tf_op jit(solution)/shard_map/ppermute | solution.py:82
  58.2 23.4 %copy-start.6 = (f32[16,4,64]{2,1,0:T(4,128)S(1)}, f32[16,4,64]{2,1,0:T(4,128)}, u32[]{:S(2)}) copy-start(f32[16,4,64]{2,1,0:T(4,128)} %mul.198) | copy-start | bytes 49156
  58.5 9.1 %collective-permute-start.6 = (bf16[512,4,64]{0,2,1:T(8,128)(2,1)S(1)}, bf16[512,4,64]{0,2,1:T(8,128)(2,1)S(1)}, u32[]{:S(2)}, u32[]{:S(2)}) collective-permute-start(bf16[512,4,64]{0,2,1:T(8,128)(2,1)S(1)} %collective-permute-done.5), channel_id=1, source_target_pairs={{0,480},{8,488},{16,496},{24,504},{32,0},{40,8},{48,16},{56,24},{6... | collective-permute-start | bytes 786440 | tf_op jit(solution)/shard_map/ppermute | solution.py:82
  64.2 8.7 %collective-permute-start.13 = (bf16[512,4,64]{0,2,1:T(8,128)(2,1)S(1)}, bf16[512,4,64]{0,2,1:T(8,128)(2,1)S(1)}, u32[]{:S(2)}, u32[]{:S(2)}) collective-permute-start(bf16[512,4,64]{0,2,1:T(8,128)(2,1)S(1)} %collective-permute-done.12), channel_id=1, source_target_pairs={{0,32},{8,40},{16,48},{24,56},{32,64},{40,72},{48,80},{56,88},{64,... | collective-permute-start | bytes 786440 | tf_op jit(solution)/shard_map/ppermute | solution.py:82
  67.5 8.8 %collective-permute-start.7 = (bf16[512,4,64]{0,2,1:T(8,128)(2,1)S(1)}, bf16[512,4,64]{0,2,1:T(8,128)(2,1)S(1)}, u32[]{:S(2)}, u32[]{:S(2)}) collective-permute-start(bf16[512,4,64]{0,2,1:T(8,128)(2,1)S(1)} %collective-permute-done.6), channel_id=1, source_target_pairs={{0,480},{8,488},{16,496},{24,504},{32,0},{40,8},{48,16},{56,24},{6... | collective-permute-start | bytes 786440 | tf_op jit(solution)/shard_map/ppermute | solution.py:82
  72.9 9.5 %collective-permute-start.14 = (bf16[512,4,64]{0,2,1:T(8,128)(2,1)S(1)}, bf16[512,4,64]{0,2,1:T(8,128)(2,1)S(1)}, u32[]{:S(2)}, u32[]{:S(2)}) collective-permute-start(bf16[512,4,64]{0,2,1:T(8,128)(2,1)S(1)} %collective-permute-done.13), channel_id=1, source_target_pairs={{0,32},{8,40},{16,48},{24,56},{32,64},{40,72},{48,80},{56,88},{64,... | collective-permute-start | bytes 786440 | tf_op jit(solution)/shard_map/ppermute | solution.py:82
  76.3 9.1 %collective-permute-start.8 = (bf16[512,4,64]{0,2,1:T(8,128)(2,1)S(1)}, bf16[512,4,64]{0,2,1:T(8,128)(2,1)S(1)}, u32[]{:S(2)}, u32[]{:S(2)}) collective-permute-start(bf16[512,4,64]{0,2,1:T(8,128)(2,1)S(1)} %collective-permute-done.7), channel_id=1, source_target_pairs={{0,480},{8,488},{16,496},{24,504},{32,0},{40,8},{48,16},{56,24},{6... | collective-permute-start | bytes 786440 | tf_op jit(solution)/shard_map/ppermute | solution.py:82
  82.4 8.9 %collective-permute-start.15 = (bf16[512,4,64]{0,2,1:T(8,128)(2,1)S(1)}, bf16[512,4,64]{0,2,1:T(8,128)(2,1)S(1)}, u32[]{:S(2)}, u32[]{:S(2)}) collective-permute-start(bf16[512,4,64]{0,2,1:T(8,128)(2,1)S(1)} %collective-permute-done.14), channel_id=1, source_target_pairs={{0,32},{8,40},{16,48},{24,56},{32,64},{40,72},{48,80},{56,88},{64,... | collective-permute-start | bytes 786440 | tf_op jit(solution)/shard_map/ppermute | solution.py:82
  85.5 9.3 %collective-permute-start.9 = (bf16[512,4,64]{0,2,1:T(8,128)(2,1)S(1)}, bf16[512,4,64]{0,2,1:T(8,128)(2,1)S(1)}, u32[]{:S(2)}, u32[]{:S(2)}) collective-permute-start(bf16[512,4,64]{0,2,1:T(8,128)(2,1)S(1)} %collective-permute-done.8), channel_id=1, source_target_pairs={{0,480},{8,488},{16,496},{24,504},{32,0},{40,8},{48,16},{56,24},{6... | collective-permute-start | bytes 786440 | tf_op jit(solution)/shard_map/ppermute | solution.py:82
  91.2 9.7 %collective-permute-start.16 = (bf16[512,4,64]{0,2,1:T(8,128)(2,1)S(1)}, bf16[512,4,64]{0,2,1:T(8,128)(2,1)S(1)}, u32[]{:S(2)}, u32[]{:S(2)}) collective-permute-start(bf16[512,4,64]{0,2,1:T(8,128)(2,1)S(1)} %collective-permute-done.15), channel_id=1, source_target_pairs={{0,32},{8,40},{16,48},{24,56},{32,64},{40,72},{48,80},{56,88},{64,... | collective-permute-start | bytes 786440 | tf_op jit(solution)/shard_map/ppermute | solution.py:82
  94.8 16.3 %collective-permute-start.10 = (bf16[512,4,64]{0,2,1:T(8,128)(2,1)S(1)}, bf16[512,4,64]{0,2,1:T(8,128)(2,1)S(1)}, u32[]{:S(2)}, u32[]{:S(2)}) collective-permute-start(bf16[512,4,64]{0,2,1:T(8,128)(2,1)S(1)} %collective-permute-done.9), channel_id=1, source_target_pairs={{0,480},{8,488},{16,496},{24,504},{32,0},{40,8},{48,16},{56,24},{6... | collective-permute-start | bytes 786440 | tf_op jit(solution)/shard_map/ppermute | solution.py:82
  101.0 10.8 %collective-permute-start.17 = (bf16[256,4,64]{0,2,1:T(8,128)(2,1)S(1)}, bf16[256,4,64]{0,2,1:T(8,128)(2,1)S(1)}, u32[]{:S(2)}, u32[]{:S(2)}) collective-permute-start(bf16[256,4,64]{0,2,1:T(8,128)(2,1)S(1)} %slice.112), channel_id=1, source_target_pairs={{0,64},{8,72},{16,80},{24,88},{32,96},{40,104},{48,112},{56,120},{... | collective-permute-start | bytes 393224 | tf_op jit(solution)/shard_map/ppermute | solution.py:82
  102.9 9.5 %collective-permute-start.18 = (bf16[256,4,64]{0,2,1:T(8,128)(2,1)S(1)}, bf16[256,4,64]{0,2,1:T(8,128)(2,1)S(1)}, u32[]{:S(2)}, u32[]{:S(2)}) collective-permute-start(bf16[256,4,64]{0,2,1:T(8,128)(2,1)S(1)} %slice.113), channel_id=1, source_target_pairs={{0,448},{8,456},{16,464},{24,472},{32,480},{40,488},{48,496},{56,5... | collective-permute-start | bytes 393224 | tf_op jit(solution)/shard_map/ppermute | solution.py:82
  108.4 9.6 %collective-permute-start.19 = (bf16[512,4,64]{0,2,1:T(8,128)(2,1)S(1)}, bf16[512,4,64]{0,2,1:T(8,128)(2,1)S(1)}, u32[]{:S(2)}, u32[]{:S(2)}) collective-permute-start(bf16[512,4,64]{0,2,1:T(8,128)(2,1)S(1)} %collective-permute-done.16), channel_id=1, source_target_pairs={{0,32},{8,40},{16,48},{24,56},{32,64},{40,72},{48,80},{56,88},{64,... | collective-permute-start | bytes 786440 | tf_op jit(solution)/shard_map/ppermute | solution.py:82
  137.1 30.7 %all-to-all-start.1 = ((bf16[64,4,512]{2,1,0:T(4,128)(2,1)}), bf16[64,4,512]{2,1,0:T(4,128)(2,1)}, u32[]{:S(2)}, u32[]{:S(2)}) async-start(bf16[64,4,512]{2,1,0:T(4,128)(2,1)} %broadcast_select_fusion), calls=%async_computation.1 | async-start | bytes 524288 | tf_op jit(solution)/shard_map/all_to_all | solution.py:171
  175.9 30.5 %all-to-all-start.2 = ((bf16[64,5,512]{2,1,0:T(8,128)(2,1)}), bf16[64,5,512]{2,1,0:T(8,128)(2,1)S(1)}, u32[]{:S(2)}, u32[]{:S(2)}) async-start(bf16[64,5,512]{2,1,0:T(8,128)(2,1)} %fusion.18), calls=%async_computation.2 | async-start | bytes 1048576 | tf_op jit(solution)/shard_map/all_to_all | solution.py:189
  220.0 29.9 %all-to-all-start.3 = ((bf16[8,128,512]{2,1,0:T(8,128)(2,1)}), bf16[8,128,512]{2,1,0:T(8,128)(2,1)S(1)}, u32[]{:S(2)}, u32[]{:S(2)}) async-start(bf16[8,128,512]{2,1,0:T(8,128)(2,1)} %bitcast.212), calls=%async_computation.3 | async-start | bytes 2097152 | tf_op jit(solution)/shard_map/all_to_all | solution.py:227
  (14 other events, 77.9 us)
Sparse Core Ops, SparseCore 0:
  35.0 158.5 all-gather.1

commit v9 on v7

--- a/solution.py
+++ b/solution.py
@@ -117,8 +117,6 @@
     kv_width = kv_local * 2 * head_size
     kv_piece = lax.dynamic_slice_in_dim(key_value_weight, kv_start * 2 * head_size, kv_width, 1)
     side = lax.all_gather(jnp.concatenate([kv_piece.T, w_out], axis=0), "seq", axis=1, tiled=True)
-    kv_rows = side[:kv_width]
-    wo_full = side[kv_width:]
     wq_rows, z_at, y_at = ring_gather(w_query.T, "seq", seq_count)
     z_count = seq_count // Y_CHIPS
     rel_input = normalized_input.reshape(length, z_count, Y_CHIPS, -1)
@@ -130,9 +128,6 @@
         )
 
     query_vectors = contract(wq_rows)
-    key_value_pair = lax.dot_general(
-        normalized_input, kv_rows, (((1,), (1,)), ((), ())), preferred_element_type=jnp.float32
-    )
     counts = token_counts[0]
     num_groups = counts.shape[0]
     starts, prefix_group, offset = layout(counts, length)
@@ -140,16 +135,6 @@
     query_vectors = rotate(query_vectors.reshape(length, heads_dev, head_size), positions).astype(
         jnp.bfloat16
     )
-    pair_blocks = key_value_pair.reshape(length, kv_local, 2, head_size)
-    rotated_keys = rotate(pair_blocks[:, :, 0], positions)
-    suffix_mine = jnp.stack([rotated_keys, pair_blocks[:, :, 1]], axis=2).astype(jnp.bfloat16)
-    share = full_width // tensor_count
-    suffix_flat = suffix_mine.reshape(length, kv_width)
-    suffix_part = lax.dynamic_slice_in_dim(
-        suffix_flat, tensor_index * share - kv_start * 2 * head_size, share, 1
-    )
-    suffix_keys = suffix_mine[:, :, 0]
-    suffix_values = suffix_mine[:, :, 1]
     cache_all = prefix_key_cache[0].reshape(-1, kv_heads, 2, head_size)
     cache_mine = lax.dynamic_slice_in_dim(cache_all, kv_start, kv_local, 1)
     cache_keys = cache_mine[:, :, 0]
@@ -183,9 +168,24 @@
     log_block = jnp.stack(logs, axis=1).reshape(seq_count, items, heads_dev)
     log_row = log_block.astype(jnp.bfloat16).reshape(seq_count, 1, items * heads_dev)
     log_row = jnp.pad(log_row, ((0, 0), (0, 0), (0, width_query - items * heads_dev)))
-    back = lax.all_to_all(
-        jnp.concatenate([out_block, log_row], axis=1), "seq", split_axis=0, concat_axis=0, tiled=True
-    )
+    payload = jnp.concatenate([out_block, log_row], axis=1)
+    payload, side = lax.optimization_barrier((payload, side))
+    kv_rows = side[:kv_width]
+    wo_full = side[kv_width:]
+    key_value_pair = lax.dot_general(
+        normalized_input, kv_rows, (((1,), (1,)), ((), ())), preferred_element_type=jnp.float32
+    )
+    pair_blocks = key_value_pair.reshape(length, kv_local, 2, head_size)
+    rotated_keys = rotate(pair_blocks[:, :, 0], positions)
+    suffix_mine = jnp.stack([rotated_keys, pair_blocks[:, :, 1]], axis=2).astype(jnp.bfloat16)
+    share = full_width // tensor_count
+    suffix_flat = suffix_mine.reshape(length, kv_width)
+    suffix_part = lax.dynamic_slice_in_dim(
+        suffix_flat, tensor_index * share - kv_start * 2 * head_size, share, 1
+    )
+    suffix_keys = suffix_mine[:, :, 0]
+    suffix_values = suffix_mine[:, :, 1]
+    back = lax.all_to_all(payload, "seq", split_axis=0, concat_axis=0, tiled=True)
     prefix_out = back[:, :items]
     prefix_log = back[:, items, : items * heads_dev].astype(jnp.float32)
     owner_of_token = jnp.sum(

time: 258 us -> 269 us (1.043)
  waiting for transfers between devices: 73.5 us -> 81.3 us
    all_gather x1, waiting for transfers between devices: 0.02 us -> 9.8 us  [shards(): lax.all_gather(jnp.concatenate([kv_piece.T, w_out], axis=0), 'seq', axis=...]
    all_to_all x1, starting transfers between devices: 21 us -> 16 us  [shards(): lax.all_to_all(jnp.moveaxis(pieces, 1, 0), 'tensor', split_axis=0, concat...]
    all_to_all x1, starting transfers between devices: 4.63 us -> 9.53 us  [shards(): lax.all_to_all(payload, 'seq', split_axis=0, concat_axis=0, tiled=True)]
    all_to_all x1, waiting for transfers between devices: 16.8 us -> 12.1 us  [shards(): lax.all_to_all(outgoing, 'seq', split_axis=0, concat_axis=0, tiled=True)]
  transfers between devices with their start and end apart: 23 -> 23, of which waited for: 13 -> 14; matrix products, arithmetic and copies ran while one was open for 20% -> 19% of each run, Pallas kernels for 0% -> 0%
where the time goes in v9:
time: 269 us; the launch traced here: 268 us
  starting transfers between devices  104 us (39%)
  waiting for transfers between devices  81.3 us (30%)
  local copies, waits for them, and re-layouts  37.7 us (14%)
  other arithmetic  16.9 us (6%)
  between operations  14.9 us (6%)
  matrix products  12.8 us (5%)
    ppermute x18, starting transfers between devices, shift(): return lax.ppermute(value, axis_name, pairs)  59.8 us
    ppermute x18, waiting for transfers between devices, shift(): return lax.ppermute(value, axis_name, pairs)  23.2 us
    all_to_all x1, waiting for transfers between devices, shards(): lax.all_to_all(payload, 'seq', split_axis=0, concat_axis=0, tiled=True)  21.8 us
    all_to_all x1, starting transfers between devices, shards(): lax.all_to_all(jnp.moveaxis(pieces, 1, 0), 'tensor', split_axis=0, concat...  16 us
    unnamed x45, local copies, waits for them, and re-layouts  15.5 us
    all_to_all x1, waiting for transfers between devices, shards(): lax.all_to_all(jnp.moveaxis(pieces, 1, 0), 'tensor', split_axis=0, concat...  14.4 us
    all_to_all x1, waiting for transfers between devices, shards(): lax.all_to_all(outgoing, 'seq', split_axis=0, concat_axis=0, tiled=True)  12.1 us
    all_to_all x1, starting transfers between devices, shards(): lax.all_to_all(tiles, 'tensor', split_axis=0, concat_axis=0, tiled=True)  10 us
  transfers between devices with their start and end apart: 23, of which 14 were waited for; matrix products, arithmetic and copies ran while one was open for 19% of the time, Pallas kernels for 0%

profile of v9, /device:TPU:1, one launch (start us, length us, event | category | flops | bytes accessed | tf_op | source)
XLA Modules:
  0.0 268.0 jit_solution(13241928261995664182)
XLA Ops:
  7.2 4.2 %collective-permute-start.1 = (bf16[512,64]{0,1:T(8,128)(2,1)}, bf16[512,64]{0,1:T(8,128)(2,1)S(1)}, u32[]{:S(2)}, u32[]{:S(2)}) collective-permute-start(bf16[512,64]{0,1:T(8,128)(2,1)} %bitcast.224), channel_id=1, source_target_pairs={{0,8},{8,16},{16,24},{24,0},{32,40},{40,48},{48,56},{56,32},{64,72... | collective-permute-start | bytes 196616 | tf_op jit(solution)/shard_map/ppermute | solution.py:79
  11.4 3.4 %collective-permute-start = (bf16[512,64]{0,1:T(8,128)(2,1)}, bf16[512,64]{0,1:T(8,128)(2,1)S(1)}, u32[]{:S(2)}, u32[]{:S(2)}) collective-permute-start(bf16[512,64]{0,1:T(8,128)(2,1)} %bitcast.225), channel_id=1, source_target_pairs={{0,24},{8,0},{16,8},{24,16},{32,56},{40,32},{48,40},{56,48},{64,88... | collective-permute-start | bytes 196616 | tf_op jit(solution)/shard_map/ppermute | solution.py:79
  16.9 10.0 %all-to-all-start = ((bf16[8,128,512]{1,2,0:T(8,128)(2,1)}), bf16[8,128,512]{1,2,0:T(8,128)(2,1)S(1)}, u32[]{:S(2)}, u32[]{:S(2)}) async-start(bf16[8,128,512]{1,2,0:T(8,128)(2,1)} %broadcast_in_dim.72), calls=%async_computation | async-start | bytes 2097152 | tf_op jit(solution)/shard_map/all_to_all | solution.py:102
  31.6 1.9 collective-permute-start.2
  33.6 4.7 %collective-permute-done.2 = bf16[512,64]{0,1:T(8,128)(2,1)S(1)} collective-permute-done((bf16[512,64]{0,1:T(8,128)(2,1)S(1)}, bf16[512,64]{0,1:T(8,128)(2,1)S(1)}, u32[]{:S(2)}, u32[]{:S(2)}) %collective-permute-start.2) | collective-permute-done | bytes 65568 | tf_op jit(solution)/shard_map/ppermute | solution.py:79
  39.1 1.9 collective-permute-start.10
  41.3 6.7 %collective-permute-start.3 = (bf16[512,4,64]{0,2,1:T(8,128)(2,1)S(1)}, bf16[512,4,64]{0,2,1:T(8,128)(2,1)S(1)}, u32[]{:S(2)}, u32[]{:S(2)}) collective-permute-start(bf16[512,4,64]{0,2,1:T(8,128)(2,1)S(1)} %pad_maximum_fusion), channel_id=1, source_target_pairs={{0,480},{8,488},{16,496},{24,504},{32,0},{40,8},{48,16},{56,24},{6... | collective-permute-start | bytes 786440 | tf_op jit(solution)/shard_map/ppermute | solution.py:79
  48.0 4.3 %collective-permute-done.10 = bf16[512,4,64]{0,2,1:T(8,128)(2,1)S(1)} collective-permute-done((bf16[512,4,64]{0,2,1:T(8,128)(2,1)S(1)}, bf16[512,4,64]{0,2,1:T(8,128)(2,1)S(1)}, u32[]{:S(2)}, u32[]{:S(2)}) %collective-permute-start.10) | collective-permute-done | bytes 262176 | tf_op jit(solution)/shard_map/ppermute | solution.py:79
  52.2 1.9 collective-permute-start.11
  54.5 4.6 %collective-permute-start.4 = (bf16[512,4,64]{0,2,1:T(8,128)(2,1)S(1)}, bf16[512,4,64]{0,2,1:T(8,128)(2,1)S(1)}, u32[]{:S(2)}, u32[]{:S(2)}) collective-permute-start(bf16[512,4,64]{0,2,1:T(8,128)(2,1)S(1)} %collective-permute-done.3), channel_id=1, source_target_pairs={{0,480},{8,488},{16,496},{24,504},{32,0},{40,8},{48,16},{56,24},{6... | collective-permute-start | bytes 786440 | tf_op jit(solution)/shard_map/ppermute | solution.py:79
  59.9 2.9 %collective-permute-done.11 = bf16[512,4,64]{0,2,1:T(8,128)(2,1)S(1)} collective-permute-done((bf16[512,4,64]{0,2,1:T(8,128)(2,1)S(1)}, bf16[512,4,64]{0,2,1:T(8,128)(2,1)S(1)}, u32[]{:S(2)}, u32[]{:S(2)}) %collective-permute-start.11) | collective-permute-done | bytes 262176 | tf_op jit(solution)/shard_map/ppermute | solution.py:79
  65.4 4.6 %collective-permute-start.5 = (bf16[512,4,64]{0,2,1:T(8,128)(2,1)S(1)}, bf16[512,4,64]{0,2,1:T(8,128)(2,1)S(1)}, u32[]{:S(2)}, u32[]{:S(2)}) collective-permute-start(bf16[512,4,64]{0,2,1:T(8,128)(2,1)S(1)} %collective-permute-done.4), channel_id=1, source_target_pairs={{0,480},{8,488},{16,496},{24,504},{32,0},{40,8},{48,16},{56,24},{6... | collective-permute-start | bytes 786440 | tf_op jit(solution)/shard_map/ppermute | solution.py:79
  75.0 4.6 %collective-permute-start.6 = (bf16[512,4,64]{0,2,1:T(8,128)(2,1)S(1)}, bf16[512,4,64]{0,2,1:T(8,128)(2,1)S(1)}, u32[]{:S(2)}, u32[]{:S(2)}) collective-permute-start(bf16[512,4,64]{0,2,1:T(8,128)(2,1)S(1)} %collective-permute-done.5), channel_id=1, source_target_pairs={{0,480},{8,488},{16,496},{24,504},{32,0},{40,8},{48,16},{56,24},{6... | collective-permute-start | bytes 786440 | tf_op jit(solution)/shard_map/ppermute | solution.py:79
  81.1 1.9 collective-permute-start.14
  83.8 5.0 %collective-permute-start.7 = (bf16[512,4,64]{0,2,1:T(8,128)(2,1)S(1)}, bf16[512,4,64]{0,2,1:T(8,128)(2,1)S(1)}, u32[]{:S(2)}, u32[]{:S(2)}) collective-permute-start(bf16[512,4,64]{0,2,1:T(8,128)(2,1)S(1)} %collective-permute-done.6), channel_id=1, source_target_pairs={{0,480},{8,488},{16,496},{24,504},{32,0},{40,8},{48,16},{56,24},{6... | collective-permute-start | bytes 786440 | tf_op jit(solution)/shard_map/ppermute | solution.py:79
  92.6 5.0 %collective-permute-start.8 = (bf16[512,4,64]{0,2,1:T(8,128)(2,1)S(1)}, bf16[512,4,64]{0,2,1:T(8,128)(2,1)S(1)}, u32[]{:S(2)}, u32[]{:S(2)}) collective-permute-start(bf16[512,4,64]{0,2,1:T(8,128)(2,1)S(1)} %collective-permute-done.7), channel_id=1, source_target_pairs={{0,480},{8,488},{16,496},{24,504},{32,0},{40,8},{48,16},{56,24},{6... | collective-permute-start | bytes 786440 | tf_op jit(solution)/shard_map/ppermute | solution.py:79
  101.4 4.7 %collective-permute-start.9 = (bf16[512,4,64]{0,2,1:T(8,128)(2,1)S(1)}, bf16[512,4,64]{0,2,1:T(8,128)(2,1)S(1)}, u32[]{:S(2)}, u32[]{:S(2)}) collective-permute-start(bf16[512,4,64]{0,2,1:T(8,128)(2,1)S(1)} %collective-permute-done.8), channel_id=1, source_target_pairs={{0,480},{8,488},{16,496},{24,504},{32,0},{40,8},{48,16},{56,24},{6... | collective-permute-start | bytes 786440 | tf_op jit(solution)/shard_map/ppermute | solution.py:79
  110.6 6.2 %collective-permute-done.17 = bf16[512,4,64]{0,2,1:T(8,128)(2,1)S(1)} collective-permute-done((bf16[512,4,64]{0,2,1:T(8,128)(2,1)S(1)}, bf16[512,4,64]{0,2,1:T(8,128)(2,1)S(1)}, u32[]{:S(2)}, u32[]{:S(2)}) %collective-permute-start.17) | collective-permute-done | bytes 262176 | tf_op jit(solution)/shard_map/ppermute | solution.py:79
  122.7 7.0 %dot_general.61 = bf16[4,128,4096]{1,0,2:T(4,128)(2,1)} reshape(bf16[512,16,4,64]{0,3,2,1:T(8,128)(2,1)} %bitcast_dynamic-update-slice_fusion) | data formatting | bytes 8388608 | tf_op jit(solution)/shard_map/dot_general | solution.py:126
  129.6 3.9 %fusion = f32[128,4,128]{0,2,1:T(8,128)S(1)} fusion(bf16[128,4096,1]{0,1,2:T(8,128)(2,1)S(1)} %bitcast.221, bf16[4,128,4096]{1,0,2:T(4,128)(2,1)} %dot_general.61), kind=kOutput, calls=%fused_computation.4 | convolution fusion | flops 536870912 | bytes 5505024 | tf_op jit(solution)/shard_map/dot_general | solution.py:126
  136.6 9.1 %all-to-all-start.1 = ((bf16[64,4,512]{2,1,0:T(4,128)(2,1)}), bf16[64,4,512]{2,1,0:T(4,128)(2,1)S(1)}, u32[]{:S(2)}, u32[]{:S(2)}) async-start(bf16[64,4,512]{2,1,0:T(4,128)(2,1)} %broadcast_select_fusion), calls=%async_computation.1 | async-start | bytes 524288 | tf_op jit(solution)/shard_map/all_to_all | solution.py:153
  145.7 2.9 %copy.116 = bf16[1,1024,1024]{1,2,0:T(8,128)(2,1)S(1)} copy(bf16[1,1024,1024]{2,1,0:T(8,128)(2,1)} %param.13) | data formatting | bytes 4194304 | tf_op args[5]
  150.6 2.2 multiply_convert_fusion
  152.8 12.1 %all-to-all-done.1 = bf16[64,4,512]{2,1,0:T(4,128)(2,1)S(1)} async-done(((bf16[64,4,512]{2,1,0:T(4,128)(2,1)}), bf16[64,4,512]{2,1,0:T(4,128)(2,1)S(1)}, u32[]{:S(2)}, u32[]{:S(2)}) %all-to-all-start.1) | async-done | bytes 262176 | tf_op jit(solution)/shard_map/all_to_all | solution.py:153
  172.1 9.8 %all-gather.2.cloned.1.call-done = bf16[768,4096]{0,1:T(8,128)(2,1)} async-done(((bf16[768,64]{0,1:T(8,128)(2,1)}), bf16[768,4096]{0,1:T(8,128)(2,1)}) %all-gather.2.cloned.1.call-update) | async-done | bytes 6291472 | tf_op jit(solution)/shard_map/all_gather | solution.py:119
  181.9 3.1 %slice.76 = bf16[256,4096]{0,1:T(8,128)(2,1)} slice(bf16[768,4096]{0,1:T(8,128)(2,1)} %all-gather.2.cloned.1.call-done), slice={[0:256], [0:4096]} | slice | bytes 4194304 | tf_op jit(solution)/shard_map/slice | solution.py:173
  185.0 3.0 %copy.125 = bf16[256,4096]{1,0:T(8,128)(2,1)S(1)} copy(bf16[256,4096]{0,1:T(8,128)(2,1)} %slice.76) | data formatting | bytes 4194304 | tf_op jit(solution)/shard_map/slice | solution.py:173
  189.7 9.5 %all-to-all-start.2 = ((bf16[64,5,512]{2,1,0:T(8,128)(2,1)}), bf16[64,5,512]{2,1,0:T(8,128)(2,1)S(1)}, u32[]{:S(2)}, u32[]{:S(2)}) async-start(bf16[64,5,512]{2,1,0:T(8,128)(2,1)} %fusion.18), calls=%async_computation.2 | async-start | bytes 1048576 | tf_op jit(solution)/shard_map/all_to_all | solution.py:188
  200.3 21.8 %all-to-all-done.2 = bf16[64,5,512]{2,1,0:T(8,128)(2,1)S(1)} async-done(((bf16[64,5,512]{2,1,0:T(8,128)(2,1)}), bf16[64,5,512]{2,1,0:T(8,128)(2,1)S(1)}, u32[]{:S(2)}, u32[]{:S(2)}) %all-to-all-start.2) | async-done | bytes 327712 | tf_op jit(solution)/shard_map/all_to_all | solution.py:188
  224.4 3.7 %convolution_convert_fusion = bf16[128,4096]{1,0:T(8,128)(2,1)S(1)} fusion(bf16[128,512]{0,1:T(8,128)(2,1)S(1)} %bitcast.235, bf16[768,4096]{0,1:T(8,128)(2,1)} %all-gather.2.cloned.1.call-done), kind=kOutput, calls=%fused_computation.3 | convolution fusion | flops 537395200 | bytes 5373952 | tf_op jit(solution)/shard_map/dot_general | solution.py:221
  229.2 16.0 %all-to-all-start.3 = ((bf16[8,128,512]{2,1,0:T(8,128)(2,1)}), bf16[8,128,512]{2,1,0:T(8,128)(2,1)S(1)}, u32[]{:S(2)}, u32[]{:S(2)}) async-start(bf16[8,128,512]{2,1,0:T(8,128)(2,1)} %bitcast.209), calls=%async_computation.3 | async-start | bytes 2097152 | tf_op jit(solution)/shard_map/all_to_all | solution.py:224
  245.9 14.4 %all-to-all-done.3 = bf16[8,128,512]{2,1,0:T(8,128)(2,1)S(1)} async-done(((bf16[8,128,512]{2,1,0:T(8,128)(2,1)}), bf16[8,128,512]{2,1,0:T(8,128)(2,1)S(1)}, u32[]{:S(2)}, u32[]{:S(2)}) %all-to-all-start.3) | async-done | bytes 1048608 | tf_op jit(solution)/shard_map/all_to_all | solution.py:224
  (167 shorter events, 56.4 us)
Async XLA Ops:
  7.2 19.7 %copy-start = (bf16[64,1024]{1,0:T(8,128)(2,1)S(1)}, bf16[64,1024]{1,0:T(8,128)(2,1)}, u32[]{:S(2)}) copy-start(bf16[64,1024]{1,0:T(8,128)(2,1)} %param.11) | copy-start | bytes 393220
  7.2 51.9 %copy-start.4 = (bf16[64,512]{1,0:T(8,128)(2,1)S(1)}, bf16[64,512]{1,0:T(8,128)(2,1)}, u32[]{:S(2)}) copy-start(bf16[64,512]{1,0:T(8,128)(2,1)} %param.10) | copy-start | bytes 196612
  7.2 47.1 %copy-start.5 = (bf16[4096]{0:T(1024)(128)(2,1)S(1)}, bf16[4096]{0:T(1024)(128)(2,1)}, u32[]{:S(2)}) copy-start(bf16[4096]{0:T(1024)(128)(2,1)} %param.9) | copy-start | bytes 24580
  7.2 24.4 %collective-permute-start.1 = (bf16[512,64]{0,1:T(8,128)(2,1)}, bf16[512,64]{0,1:T(8,128)(2,1)S(1)}, u32[]{:S(2)}, u32[]{:S(2)}) collective-permute-start(bf16[512,64]{0,1:T(8,128)(2,1)} %bitcast.224), channel_id=1, source_target_pairs={{0,8},{8,16},{16,24},{24,0},{32,40},{40,48},{48,56},{56,32},{64,72... | collective-permute-start | bytes 196616 | tf_op jit(solution)/shard_map/ppermute | solution.py:79
  11.4 22.2 %collective-permute-start = (bf16[512,64]{0,1:T(8,128)(2,1)}, bf16[512,64]{0,1:T(8,128)(2,1)S(1)}, u32[]{:S(2)}, u32[]{:S(2)}) collective-permute-start(bf16[512,64]{0,1:T(8,128)(2,1)} %bitcast.225), channel_id=1, source_target_pairs={{0,24},{8,0},{16,8},{24,16},{32,56},{40,32},{48,40},{56,48},{64,88... | collective-permute-start | bytes 196616 | tf_op jit(solution)/shard_map/ppermute | solution.py:79
  16.9 57.4 %all-to-all-start = ((bf16[8,128,512]{1,2,0:T(8,128)(2,1)}), bf16[8,128,512]{1,2,0:T(8,128)(2,1)S(1)}, u32[]{:S(2)}, u32[]{:S(2)}) async-start(bf16[8,128,512]{1,2,0:T(8,128)(2,1)} %broadcast_in_dim.72), calls=%async_computation | async-start | bytes 2097152 | tf_op jit(solution)/shard_map/all_to_all | solution.py:102
  26.9 155.0 %all-gather.2.cloned.1.call-start = ((), (), s32[]{:S(2)}) async-start(), calls=%async_computation.4 | async-start | bytes 6389760 | tf_op jit(solution)/shard_map/all_gather | solution.py:119
  31.6 22.7 %copy-start.13 = (s32[128]{0:T(128)}, s32[128]{0:T(128)S(1)}, u32[]{:S(2)}) copy-start(s32[128]{0:T(128)S(1)} %get-tuple-element.7) | copy-start | bytes 1540
  31.6 6.6 %collective-permute-start.2 = (bf16[512,64]{0,1:T(8,128)(2,1)S(1)}, bf16[512,64]{0,1:T(8,128)(2,1)S(1)}, u32[]{:S(2)}, u32[]{:S(2)}) collective-permute-start(bf16[512,64]{0,1:T(8,128)(2,1)S(1)} %collective-permute-done.1), channel_id=1, source_target_pairs={{0,8},{8,16},{16,24},{24,0},{32,40},{40,48},{48,56},{56,32},{64,72... | collective-permute-start | bytes 196616 | tf_op jit(solution)/shard_map/ppermute | solution.py:79
  33.5 20.7 %copy-start.7 = (f32[128]{0:T(128)}, f32[128]{0:T(128)S(1)}, u32[]{:S(2)}) copy-start(f32[128]{0:T(128)S(1)} %add_convert_fusion.4) | copy-start | bytes 1540
  39.1 13.1 %collective-permute-start.10 = (bf16[512,4,64]{0,2,1:T(8,128)(2,1)S(1)}, bf16[512,4,64]{0,2,1:T(8,128)(2,1)S(1)}, u32[]{:S(2)}, u32[]{:S(2)}) collective-permute-start(bf16[512,4,64]{0,2,1:T(8,128)(2,1)S(1)} %pad_maximum_fusion), channel_id=1, source_target_pairs={{0,32},{8,40},{16,48},{24,56},{32,64},{40,72},{48,80},{56,88},{64,... | collective-permute-start | bytes 786440 | tf_op jit(solution)/shard_map/ppermute | solution.py:79
  41.1 13.2 %copy-start.9 = (f32[64]{0:T(128)}, f32[64]{0:T(128)S(1)}, u32[]{:S(2)}) copy-start(f32[64]{0:T(128)S(1)} %multiply_power_fusion) | copy-start | bytes 772
  41.3 13.3 %collective-permute-start.3 = (bf16[512,4,64]{0,2,1:T(8,128)(2,1)S(1)}, bf16[512,4,64]{0,2,1:T(8,128)(2,1)S(1)}, u32[]{:S(2)}, u32[]{:S(2)}) collective-permute-start(bf16[512,4,64]{0,2,1:T(8,128)(2,1)S(1)} %pad_maximum_fusion), channel_id=1, source_target_pairs={{0,480},{8,488},{16,496},{24,504},{32,0},{40,8},{48,16},{56,24},{6... | collective-permute-start | bytes 786440 | tf_op jit(solution)/shard_map/ppermute | solution.py:79
  52.2 10.5 %collective-permute-start.11 = (bf16[512,4,64]{0,2,1:T(8,128)(2,1)S(1)}, bf16[512,4,64]{0,2,1:T(8,128)(2,1)S(1)}, u32[]{:S(2)}, u32[]{:S(2)}) collective-permute-start(bf16[512,4,64]{0,2,1:T(8,128)(2,1)S(1)} %collective-permute-done.10), channel_id=1, source_target_pairs={{0,32},{8,40},{16,48},{24,56},{32,64},{40,72},{48,80},{56,88},{64,... | collective-permute-start | bytes 786440 | tf_op jit(solution)/shard_map/ppermute | solution.py:79
  54.5 10.8 %collective-permute-start.4 = (bf16[512,4,64]{0,2,1:T(8,128)(2,1)S(1)}, bf16[512,4,64]{0,2,1:T(8,128)(2,1)S(1)}, u32[]{:S(2)}, u32[]{:S(2)}) collective-permute-start(bf16[512,4,64]{0,2,1:T(8,128)(2,1)S(1)} %collective-permute-done.3), channel_id=1, source_target_pairs={{0,480},{8,488},{16,496},{24,504},{32,0},{40,8},{48,16},{56,24},{6... | collective-permute-start | bytes 786440 | tf_op jit(solution)/shard_map/ppermute | solution.py:79
  62.7 9.6 %collective-permute-start.12 = (bf16[512,4,64]{0,2,1:T(8,128)(2,1)S(1)}, bf16[512,4,64]{0,2,1:T(8,128)(2,1)S(1)}, u32[]{:S(2)}, u32[]{:S(2)}) collective-permute-start(bf16[512,4,64]{0,2,1:T(8,128)(2,1)S(1)} %collective-permute-done.11), channel_id=1, source_target_pairs={{0,32},{8,40},{16,48},{24,56},{32,64},{40,72},{48,80},{56,88},{64,... | collective-permute-start | bytes 786440 | tf_op jit(solution)/shard_map/ppermute | solution.py:79
  65.4 9.6 %collective-permute-start.5 = (bf16[512,4,64]{0,2,1:T(8,128)(2,1)S(1)}, bf16[512,4,64]{0,2,1:T(8,128)(2,1)S(1)}, u32[]{:S(2)}, u32[]{:S(2)}) collective-permute-start(bf16[512,4,64]{0,2,1:T(8,128)(2,1)S(1)} %collective-permute-done.4), channel_id=1, source_target_pairs={{0,480},{8,488},{16,496},{24,504},{32,0},{40,8},{48,16},{56,24},{6... | collective-permute-start | bytes 786440 | tf_op jit(solution)/shard_map/ppermute | solution.py:79
  72.3 8.8 %collective-permute-start.13 = (bf16[512,4,64]{0,2,1:T(8,128)(2,1)S(1)}, bf16[512,4,64]{0,2,1:T(8,128)(2,1)S(1)}, u32[]{:S(2)}, u32[]{:S(2)}) collective-permute-start(bf16[512,4,64]{0,2,1:T(8,128)(2,1)S(1)} %collective-permute-done.12), channel_id=1, source_target_pairs={{0,32},{8,40},{16,48},{24,56},{32,64},{40,72},{48,80},{56,88},{64,... | collective-permute-start | bytes 786440 | tf_op jit(solution)/shard_map/ppermute | solution.py:79
  75.0 8.8 %collective-permute-start.6 = (bf16[512,4,64]{0,2,1:T(8,128)(2,1)S(1)}, bf16[512,4,64]{0,2,1:T(8,128)(2,1)S(1)}, u32[]{:S(2)}, u32[]{:S(2)}) collective-permute-start(bf16[512,4,64]{0,2,1:T(8,128)(2,1)S(1)} %collective-permute-done.5), channel_id=1, source_target_pairs={{0,480},{8,488},{16,496},{24,504},{32,0},{40,8},{48,16},{56,24},{6... | collective-permute-start | bytes 786440 | tf_op jit(solution)/shard_map/ppermute | solution.py:79
  79.6 13.1 %copy-start.11 = (f32[128]{0:T(128)}, f32[128]{0:T(128)S(1)}, u32[]{:S(2)}) copy-start(f32[128]{0:T(128)S(1)} %add_rsqrt_fusion) | copy-start | bytes 1540
  81.1 8.9 %collective-permute-start.14 = (bf16[512,4,64]{0,2,1:T(8,128)(2,1)S(1)}, bf16[512,4,64]{0,2,1:T(8,128)(2,1)S(1)}, u32[]{:S(2)}, u32[]{:S(2)}) collective-permute-start(bf16[512,4,64]{0,2,1:T(8,128)(2,1)S(1)} %collective-permute-done.13), channel_id=1, source_target_pairs={{0,32},{8,40},{16,48},{24,56},{32,64},{40,72},{48,80},{56,88},{64,... | collective-permute-start | bytes 786440 | tf_op jit(solution)/shard_map/ppermute | solution.py:79
  83.8 8.9 %collective-permute-start.7 = (bf16[512,4,64]{0,2,1:T(8,128)(2,1)S(1)}, bf16[512,4,64]{0,2,1:T(8,128)(2,1)S(1)}, u32[]{:S(2)}, u32[]{:S(2)}) collective-permute-start(bf16[512,4,64]{0,2,1:T(8,128)(2,1)S(1)} %collective-permute-done.6), channel_id=1, source_target_pairs={{0,480},{8,488},{16,496},{24,504},{32,0},{40,8},{48,16},{56,24},{6... | collective-permute-start | bytes 786440 | tf_op jit(solution)/shard_map/ppermute | solution.py:79
  90.0 8.8 %collective-permute-start.15 = (bf16[512,4,64]{0,2,1:T(8,128)(2,1)S(1)}, bf16[512,4,64]{0,2,1:T(8,128)(2,1)S(1)}, u32[]{:S(2)}, u32[]{:S(2)}) collective-permute-start(bf16[512,4,64]{0,2,1:T(8,128)(2,1)S(1)} %collective-permute-done.14), channel_id=1, source_target_pairs={{0,32},{8,40},{16,48},{24,56},{32,64},{40,72},{48,80},{56,88},{64,... | collective-permute-start | bytes 786440 | tf_op jit(solution)/shard_map/ppermute | solution.py:79
  92.6 8.8 %collective-permute-start.8 = (bf16[512,4,64]{0,2,1:T(8,128)(2,1)S(1)}, bf16[512,4,64]{0,2,1:T(8,128)(2,1)S(1)}, u32[]{:S(2)}, u32[]{:S(2)}) collective-permute-start(bf16[512,4,64]{0,2,1:T(8,128)(2,1)S(1)} %collective-permute-done.7), channel_id=1, source_target_pairs={{0,480},{8,488},{16,496},{24,504},{32,0},{40,8},{48,16},{56,24},{6... | collective-permute-start | bytes 786440 | tf_op jit(solution)/shard_map/ppermute | solution.py:79
  98.8 8.5 %collective-permute-start.16 = (bf16[512,4,64]{0,2,1:T(8,128)(2,1)S(1)}, bf16[512,4,64]{0,2,1:T(8,128)(2,1)S(1)}, u32[]{:S(2)}, u32[]{:S(2)}) collective-permute-start(bf16[512,4,64]{0,2,1:T(8,128)(2,1)S(1)} %collective-permute-done.15), channel_id=1, source_target_pairs={{0,32},{8,40},{16,48},{24,56},{32,64},{40,72},{48,80},{56,88},{64,... | collective-permute-start | bytes 786440 | tf_op jit(solution)/shard_map/ppermute | solution.py:79
  101.4 8.5 %collective-permute-start.9 = (bf16[512,4,64]{0,2,1:T(8,128)(2,1)S(1)}, bf16[512,4,64]{0,2,1:T(8,128)(2,1)S(1)}, u32[]{:S(2)}, u32[]{:S(2)}) collective-permute-start(bf16[512,4,64]{0,2,1:T(8,128)(2,1)S(1)} %collective-permute-done.8), channel_id=1, source_target_pairs={{0,480},{8,488},{16,496},{24,504},{32,0},{40,8},{48,16},{56,24},{6... | collective-permute-start | bytes 786440 | tf_op jit(solution)/shard_map/ppermute | solution.py:79
  107.3 9.6 %collective-permute-start.17 = (bf16[512,4,64]{0,2,1:T(8,128)(2,1)S(1)}, bf16[512,4,64]{0,2,1:T(8,128)(2,1)S(1)}, u32[]{:S(2)}, u32[]{:S(2)}) collective-permute-start(bf16[512,4,64]{0,2,1:T(8,128)(2,1)S(1)} %collective-permute-done.16), channel_id=1, source_target_pairs={{0,32},{8,40},{16,48},{24,56},{32,64},{40,72},{48,80},{56,88},{64,... | collective-permute-start | bytes 786440 | tf_op jit(solution)/shard_map/ppermute | solution.py:79
  133.6 12.1 %copy-start.6 = (bf16[4096]{0:T(1024)(128)(2,1)S(1)}, bf16[4096]{0:T(1024)(128)(2,1)}, u32[]{:S(2)}) copy-start(bf16[4096]{0:T(1024)(128)(2,1)} %param.9) | copy-start | bytes 24580
  136.6 28.4 %all-to-all-start.1 = ((bf16[64,4,512]{2,1,0:T(4,128)(2,1)}), bf16[64,4,512]{2,1,0:T(4,128)(2,1)S(1)}, u32[]{:S(2)}, u32[]{:S(2)}) async-start(bf16[64,4,512]{2,1,0:T(4,128)(2,1)} %broadcast_select_fusion), calls=%async_computation.1 | async-start | bytes 524288 | tf_op jit(solution)/shard_map/all_to_all | solution.py:153
  172.1 15.8 %copy-start.1 = (bf16[8,128,512]{1,2,0:T(8,128)(2,1)S(1)}, bf16[8,128,512]{1,2,0:T(8,128)(2,1)}, u32[]{:S(2)}) copy-start(bf16[8,128,512]{1,2,0:T(8,128)(2,1)} %multiply_convert_fusion) | copy-start | bytes 3145732
  189.7 32.3 %all-to-all-start.2 = ((bf16[64,5,512]{2,1,0:T(8,128)(2,1)}), bf16[64,5,512]{2,1,0:T(8,128)(2,1)S(1)}, u32[]{:S(2)}, u32[]{:S(2)}) async-start(bf16[64,5,512]{2,1,0:T(8,128)(2,1)} %fusion.18), calls=%async_computation.2 | async-start | bytes 1048576 | tf_op jit(solution)/shard_map/all_to_all | solution.py:188
  229.2 31.1 %all-to-all-start.3 = ((bf16[8,128,512]{2,1,0:T(8,128)(2,1)}), bf16[8,128,512]{2,1,0:T(8,128)(2,1)S(1)}, u32[]{:S(2)}, u32[]{:S(2)}) async-start(bf16[8,128,512]{2,1,0:T(8,128)(2,1)} %bitcast.209), calls=%async_computation.3 | async-start | bytes 2097152 | tf_op jit(solution)/shard_map/all_to_all | solution.py:224
  (5 other events, 16.1 us)
Sparse Core Ops, SparseCore 0:
  30.7 151.2 all-gather.1

commit v10 on v7

--- a/solution.py
+++ b/solution.py
@@ -53,17 +53,24 @@
 Y_CHIPS = 4
 
 
-def ring(value, count, step):
+def ring(value, count, step, far_early):
     rel = [None] * count
     rel[0] = value
     ahead = value
     behind = value
+    half = value.shape[0] // 2
     for k in range(1, count // 2 + 1):
-        behind = step(behind, 1)
-        rel[(-k) % count] = behind
         if k < count - k:
+            if far_early and k == count // 2 - 1 and count % 2 == 0:
+                rel[k + 1] = jnp.concatenate(
+                    [step(behind[:half], 2), step(ahead[half:], -2)], axis=0
+                )
+            behind = step(behind, 1)
+            rel[(-k) % count] = behind
             ahead = step(ahead, -1)
             rel[k] = ahead
+        elif rel[k] is None:
+            rel[k] = jnp.concatenate([step(behind[:half], 1), step(ahead[half:], -1)], axis=0)
     return rel
 
 
@@ -78,8 +85,8 @@
             pairs.append((i, ((z + dz) % z_count) * Y_CHIPS + (y + dy) % Y_CHIPS))
         return lax.ppermute(value, axis_name, pairs)
 
-    along_y = jnp.stack(ring(block, Y_CHIPS, lambda v, d: shift(v, 0, d)), axis=1)
-    along_z = jnp.stack(ring(along_y, z_count, lambda v, d: shift(v, d, 0)), axis=1)
+    along_y = jnp.stack(ring(block, Y_CHIPS, lambda v, d: shift(v, 0, d), True), axis=1)
+    along_z = jnp.stack(ring(along_y, z_count, lambda v, d: shift(v, d, 0), False), axis=1)
     return along_z.reshape(block.shape[0], -1), here // Y_CHIPS, here % Y_CHIPS
 
 

time: 258 us -> 261 us (1.012)
  starting transfers between devices: 105 us -> 116 us
  waiting for transfers between devices: 73.5 us -> 64.5 us
    ppermute x18 -> x20, starting transfers between devices: 59.8 us -> 73.1 us  [shift(): return lax.ppermute(value, axis_name, pairs)]
    ppermute x18 -> x20, waiting for transfers between devices: 23.2 us -> 12.5 us  [shift(): return lax.ppermute(value, axis_name, pairs)]
    all_to_all x1, starting transfers between devices: 21 us -> 15.9 us  [shards(): lax.all_to_all(jnp.moveaxis(pieces, 1, 0), 'tensor', split_axis=0, concat...]
    all_to_all x1, starting transfers between devices: 9.57 us -> 13.4 us  [shards(): lax.all_to_all(outgoing, 'seq', split_axis=0, concat_axis=0, tiled=True)]
    unnamed x45 -> x58, local copies, waits for them, and re-layouts: 15.5 us -> 15.1 us
  transfers between devices with their start and end apart: 23 -> 25, of which waited for: 13 -> 15; matrix products, arithmetic and copies ran while one was open for 20% -> 19% of each run, Pallas kernels for 0% -> 0%
where the time goes in v10:
time: 261 us; the launch traced here: 259 us
  starting transfers between devices  116 us (44%)
  waiting for transfers between devices  64.5 us (25%)
  local copies, waits for them, and re-layouts  39.4 us (15%)
  between operations  15 us (6%)
  other arithmetic  13.5 us (5%)
  matrix products  10.7 us (4%)
    ppermute x20, starting transfers between devices, shift(): return lax.ppermute(value, axis_name, pairs)  73.1 us
    all_to_all x1, waiting for transfers between devices, shards(): lax.all_to_all(jnp.concatenate([out_block, log_row], axis=1), 'seq', spli...  20.9 us
    all_to_all x1, waiting for transfers between devices, shards(): lax.all_to_all(outgoing, 'seq', split_axis=0, concat_axis=0, tiled=True)  16.7 us
    all_to_all x1, starting transfers between devices, shards(): lax.all_to_all(jnp.moveaxis(pieces, 1, 0), 'tensor', split_axis=0, concat...  15.9 us
    unnamed x58, local copies, waits for them, and re-layouts  15.1 us
    all_to_all x1, waiting for transfers between devices, shards(): lax.all_to_all(jnp.moveaxis(pieces, 1, 0), 'tensor', split_axis=0, concat...  14.4 us
    all_to_all x1, starting transfers between devices, shards(): lax.all_to_all(outgoing, 'seq', split_axis=0, concat_axis=0, tiled=True)  13.4 us
    ppermute x20, waiting for transfers between devices, shift(): return lax.ppermute(value, axis_name, pairs)  12.5 us
  transfers between devices with their start and end apart: 25, of which 15 were waited for; matrix products, arithmetic and copies ran while one was open for 19% of the time, Pallas kernels for 0%

profile of v10, /device:TPU:1, one launch (start us, length us, event | category | flops | bytes accessed | tf_op | source)
XLA Modules:
  0.0 259.1 jit_solution(3222060486287778998)
XLA Ops:
  7.2 5.6 %collective-permute-start = (bf16[512,64]{0,1:T(8,128)(2,1)}, bf16[512,64]{0,1:T(8,128)(2,1)S(1)}, u32[]{:S(2)}, u32[]{:S(2)}) collective-permute-start(bf16[512,64]{0,1:T(8,128)(2,1)} %bitcast.226), channel_id=1, source_target_pairs={{0,24},{8,0},{16,8},{24,16},{32,56},{40,32},{48,40},{56,48},{64,88... | collective-permute-start | bytes 196616 | tf_op jit(solution)/shard_map/ppermute | solution.py:86
  12.8 1.9 collective-permute-start.3
  16.9 8.8 %all-to-all-start = ((bf16[8,128,512]{1,2,0:T(8,128)(2,1)}), bf16[8,128,512]{1,2,0:T(8,128)(2,1)S(1)}, u32[]{:S(2)}, u32[]{:S(2)}) async-start(bf16[8,128,512]{1,2,0:T(8,128)(2,1)} %broadcast_in_dim.72), calls=%async_computation | async-start | bytes 2097152 | tf_op jit(solution)/shard_map/all_to_all | solution.py:109
  28.4 4.9 %collective-permute-start.2 = (bf16[256,64]{0,1:T(8,128)(2,1)S(1)}, bf16[256,64]{0,1:T(8,128)(2,1)S(1)}, u32[]{:S(2)}, u32[]{:S(2)}) collective-permute-start(bf16[256,64]{0,1:T(8,128)(2,1)S(1)} %get-tuple-element.18), channel_id=1, source_target_pairs={{0,16},{8,24},{16,0},{24,8},{32,48},{40,56},{48,32},{56,40},{64,80... | collective-permute-start | bytes 98312 | tf_op jit(solution)/shard_map/ppermute | solution.py:86
  37.1 7.6 %collective-permute-start.4 = (bf16[512,4,64]{0,2,1:T(8,128)(2,1)S(1)}, bf16[512,4,64]{0,2,1:T(8,128)(2,1)S(1)}, u32[]{:S(2)}, u32[]{:S(2)}) collective-permute-start(bf16[512,4,64]{0,2,1:T(8,128)(2,1)S(1)} %pad_maximum_fusion), channel_id=1, source_target_pairs={{0,480},{8,488},{16,496},{24,504},{32,0},{40,8},{48,16},{56,24},{6... | collective-permute-start | bytes 786440 | tf_op jit(solution)/shard_map/ppermute | solution.py:86
  44.7 1.9 collective-permute-start.11
  49.3 5.3 %collective-permute-start.5 = (bf16[512,4,64]{0,2,1:T(8,128)(2,1)S(1)}, bf16[512,4,64]{0,2,1:T(8,128)(2,1)S(1)}, u32[]{:S(2)}, u32[]{:S(2)}) collective-permute-start(bf16[512,4,64]{0,2,1:T(8,128)(2,1)S(1)} %collective-permute-done.4), channel_id=1, source_target_pairs={{0,480},{8,488},{16,496},{24,504},{32,0},{40,8},{48,16},{56,24},{6... | collective-permute-start | bytes 786440 | tf_op jit(solution)/shard_map/ppermute | solution.py:86
  54.6 1.9 collective-permute-start.12
  58.5 5.2 %collective-permute-start.6 = (bf16[512,4,64]{0,2,1:T(8,128)(2,1)S(1)}, bf16[512,4,64]{0,2,1:T(8,128)(2,1)S(1)}, u32[]{:S(2)}, u32[]{:S(2)}) collective-permute-start(bf16[512,4,64]{0,2,1:T(8,128)(2,1)S(1)} %collective-permute-done.5), channel_id=1, source_target_pairs={{0,480},{8,488},{16,496},{24,504},{32,0},{40,8},{48,16},{56,24},{6... | collective-permute-start | bytes 786440 | tf_op jit(solution)/shard_map/ppermute | solution.py:86
  64.2 1.9 collective-permute-start.13
  67.5 5.0 %collective-permute-start.7 = (bf16[512,4,64]{0,2,1:T(8,128)(2,1)S(1)}, bf16[512,4,64]{0,2,1:T(8,128)(2,1)S(1)}, u32[]{:S(2)}, u32[]{:S(2)}) collective-permute-start(bf16[512,4,64]{0,2,1:T(8,128)(2,1)S(1)} %collective-permute-done.6), channel_id=1, source_target_pairs={{0,480},{8,488},{16,496},{24,504},{32,0},{40,8},{48,16},{56,24},{6... | collective-permute-start | bytes 786440 | tf_op jit(solution)/shard_map/ppermute | solution.py:86
  72.9 1.9 collective-permute-start.14
  76.3 5.3 %collective-permute-start.8 = (bf16[512,4,64]{0,2,1:T(8,128)(2,1)S(1)}, bf16[512,4,64]{0,2,1:T(8,128)(2,1)S(1)}, u32[]{:S(2)}, u32[]{:S(2)}) collective-permute-start(bf16[512,4,64]{0,2,1:T(8,128)(2,1)S(1)} %collective-permute-done.7), channel_id=1, source_target_pairs={{0,480},{8,488},{16,496},{24,504},{32,0},{40,8},{48,16},{56,24},{6... | collective-permute-start | bytes 786440 | tf_op jit(solution)/shard_map/ppermute | solution.py:86
  82.2 1.9 collective-permute-start.15
  85.5 5.1 %collective-permute-start.9 = (bf16[512,4,64]{0,2,1:T(8,128)(2,1)S(1)}, bf16[512,4,64]{0,2,1:T(8,128)(2,1)S(1)}, u32[]{:S(2)}, u32[]{:S(2)}) collective-permute-start(bf16[512,4,64]{0,2,1:T(8,128)(2,1)S(1)} %collective-permute-done.8), channel_id=1, source_target_pairs={{0,480},{8,488},{16,496},{24,504},{32,0},{40,8},{48,16},{56,24},{6... | collective-permute-start | bytes 786440 | tf_op jit(solution)/shard_map/ppermute | solution.py:86
  91.1 1.9 collective-permute-start.16
  94.8 5.5 %collective-permute-start.10 = (bf16[512,4,64]{0,2,1:T(8,128)(2,1)S(1)}, bf16[512,4,64]{0,2,1:T(8,128)(2,1)S(1)}, u32[]{:S(2)}, u32[]{:S(2)}) collective-permute-start(bf16[512,4,64]{0,2,1:T(8,128)(2,1)S(1)} %collective-permute-done.9), channel_id=1, source_target_pairs={{0,480},{8,488},{16,496},{24,504},{32,0},{40,8},{48,16},{56,24},{6... | collective-permute-start | bytes 786440 | tf_op jit(solution)/shard_map/ppermute | solution.py:86
  100.6 1.9 collective-permute-start.17
  103.9 5.8 %collective-permute-done.17 = bf16[512,4,64]{0,2,1:T(8,128)(2,1)S(1)} collective-permute-done((bf16[512,4,64]{0,2,1:T(8,128)(2,1)S(1)}, bf16[512,4,64]{0,2,1:T(8,128)(2,1)S(1)}, u32[]{:S(2)}, u32[]{:S(2)}) %collective-permute-start.17) | collective-permute-done | bytes 262176 | tf_op jit(solution)/shard_map/ppermute | solution.py:86
  109.8 1.9 collective-permute-start.18
  111.7 4.6 %collective-permute-start.19 = (bf16[256,4,64]{0,2,1:T(8,128)(2,1)S(1)}, bf16[256,4,64]{0,2,1:T(8,128)(2,1)S(1)}, u32[]{:S(2)}, u32[]{:S(2)}) collective-permute-start(bf16[256,4,64]{0,2,1:T(8,128)(2,1)S(1)} %slice.113), channel_id=1, source_target_pairs={{0,480},{8,488},{16,496},{24,504},{32,0},{40,8},{48,16},{56,24},{6... | collective-permute-start | bytes 393224 | tf_op jit(solution)/shard_map/ppermute | solution.py:86
  124.3 6.9 %dot_general.61 = bf16[4,128,4096]{1,0,2:T(4,128)(2,1)} reshape(bf16[512,16,4,64]{0,3,2,1:T(8,128)(2,1)} %bitcast_dynamic-update-slice_fusion) | data formatting | bytes 8388608 | tf_op jit(solution)/shard_map/dot_general | solution.py:135
  131.3 4.0 %fusion.1 = f32[128,4,128]{0,2,1:T(8,128)S(1)} fusion(bf16[128,4096,1]{0,1,2:T(8,128)(2,1)S(1)} %bitcast.224, bf16[4,128,4096]{1,0,2:T(4,128)(2,1)} %dot_general.61), kind=kOutput, calls=%fused_computation.5 | convolution fusion | flops 536870912 | bytes 5505024 | tf_op jit(solution)/shard_map/dot_general | solution.py:135
  138.3 13.4 %all-to-all-start.1 = ((bf16[64,4,512]{2,1,0:T(4,128)(2,1)}), bf16[64,4,512]{2,1,0:T(4,128)(2,1)}, u32[]{:S(2)}, u32[]{:S(2)}) async-start(bf16[64,4,512]{2,1,0:T(4,128)(2,1)} %broadcast_select_fusion), calls=%async_computation.1 | async-start | bytes 524288 | tf_op jit(solution)/shard_map/all_to_all | solution.py:175
  151.6 2.9 %copy.116 = bf16[1,1024,1024]{1,2,0:T(8,128)(2,1)S(1)} copy(bf16[1,1024,1024]{2,1,0:T(8,128)(2,1)} %param.13) | data formatting | bytes 4194304 | tf_op args[5]
  154.5 16.7 %all-to-all-done.1 = bf16[64,4,512]{2,1,0:T(4,128)(2,1)} async-done(((bf16[64,4,512]{2,1,0:T(4,128)(2,1)}), bf16[64,4,512]{2,1,0:T(4,128)(2,1)}, u32[]{:S(2)}, u32[]{:S(2)}) %all-to-all-start.1) | async-done | bytes 262176 | tf_op jit(solution)/shard_map/all_to_all | solution.py:175
  179.3 4.9 %all-to-all-start.2 = ((bf16[64,5,512]{2,1,0:T(8,128)(2,1)}), bf16[64,5,512]{2,1,0:T(8,128)(2,1)S(1)}, u32[]{:S(2)}, u32[]{:S(2)}) async-start(bf16[64,5,512]{2,1,0:T(8,128)(2,1)} %fusion.18), calls=%async_computation.2 | async-start | bytes 1048576 | tf_op jit(solution)/shard_map/all_to_all | solution.py:193
  186.0 20.9 %all-to-all-done.2 = bf16[64,5,512]{2,1,0:T(8,128)(2,1)S(1)} async-done(((bf16[64,5,512]{2,1,0:T(8,128)(2,1)}), bf16[64,5,512]{2,1,0:T(8,128)(2,1)S(1)}, u32[]{:S(2)}, u32[]{:S(2)}) %all-to-all-start.2) | async-done | bytes 327712 | tf_op jit(solution)/shard_map/all_to_all | solution.py:193
  208.9 3.2 %slice.122 = bf16[256,4096]{0,1:T(8,128)(2,1)} slice(bf16[768,4096]{0,1:T(8,128)(2,1)} %all-gather.2.cloned.1.call-done), slice={[0:256], [0:4096]} | slice | bytes 4194304 | tf_op jit(solution)/shard_map/slice | solution.py:127
  212.1 2.9 %copy.125 = bf16[256,4096]{1,0:T(8,128)(2,1)S(1)} copy(bf16[256,4096]{0,1:T(8,128)(2,1)} %slice.122) | data formatting | bytes 4194304 | tf_op jit(solution)/shard_map/slice | solution.py:127
  220.5 15.9 %all-to-all-start.3 = ((bf16[8,128,512]{2,1,0:T(8,128)(2,1)}), bf16[8,128,512]{2,1,0:T(8,128)(2,1)S(1)}, u32[]{:S(2)}, u32[]{:S(2)}) async-start(bf16[8,128,512]{2,1,0:T(8,128)(2,1)} %bitcast.212), calls=%async_computation.3 | async-start | bytes 2097152 | tf_op jit(solution)/shard_map/all_to_all | solution.py:231
  237.1 14.4 %all-to-all-done.3 = bf16[8,128,512]{2,1,0:T(8,128)(2,1)S(1)} async-done(((bf16[8,128,512]{2,1,0:T(8,128)(2,1)}), bf16[8,128,512]{2,1,0:T(8,128)(2,1)S(1)}, u32[]{:S(2)}, u32[]{:S(2)}) %all-to-all-start.3) | async-done | bytes 1048608 | tf_op jit(solution)/shard_map/all_to_all | solution.py:231
  (189 shorter events, 52.3 us)
Async XLA Ops:
  7.2 26.1 %copy-start = (bf16[64,1024]{1,0:T(8,128)(2,1)S(1)}, bf16[64,1024]{1,0:T(8,128)(2,1)}, u32[]{:S(2)}) copy-start(bf16[64,1024]{1,0:T(8,128)(2,1)} %param.11) | copy-start | bytes 393220
  7.2 29.6 %copy-start.3 = (bf16[64,512]{1,0:T(8,128)(2,1)S(1)}, bf16[64,512]{1,0:T(8,128)(2,1)}, u32[]{:S(2)}) copy-start(bf16[64,512]{1,0:T(8,128)(2,1)} %param.10) | copy-start | bytes 196612
  7.2 28.6 %copy-start.13 = (s32[1,64]{1,0:T(1,128)S(1)}, s32[1,64]{1,0:T(1,128)}, u32[]{:S(2)}) copy-start(s32[1,64]{1,0:T(1,128)} %param.15) | copy-start | bytes 772
  7.2 29.3 %copy-start.16 = (s32[64]{0:T(128)S(1)}, s32[64]{0:T(128)}, u32[]{:S(2)}) copy-start(s32[64]{0:T(128)} %param.14) | copy-start | bytes 772
  7.2 49.5 %copy-start.9 = (bf16[4096]{0:T(1024)(128)(2,1)S(1)}, bf16[4096]{0:T(1024)(128)(2,1)}, u32[]{:S(2)}) copy-start(bf16[4096]{0:T(1024)(128)(2,1)} %param.9) | copy-start | bytes 24580
  7.2 29.5 %collective-permute-start = (bf16[512,64]{0,1:T(8,128)(2,1)}, bf16[512,64]{0,1:T(8,128)(2,1)S(1)}, u32[]{:S(2)}, u32[]{:S(2)}) collective-permute-start(bf16[512,64]{0,1:T(8,128)(2,1)} %bitcast.226), channel_id=1, source_target_pairs={{0,24},{8,0},{16,8},{24,16},{32,56},{40,32},{48,40},{56,48},{64,88... | collective-permute-start | bytes 196616 | tf_op jit(solution)/shard_map/ppermute | solution.py:86
  12.8 23.9 %collective-permute-start.3 = (bf16[512,64]{0,1:T(8,128)(2,1)}, bf16[512,64]{0,1:T(8,128)(2,1)S(1)}, u32[]{:S(2)}, u32[]{:S(2)}) collective-permute-start(bf16[512,64]{0,1:T(8,128)(2,1)} %bitcast.227), channel_id=1, source_target_pairs={{0,8},{8,16},{16,24},{24,0},{32,40},{40,48},{48,56},{56,32},{64,72... | collective-permute-start | bytes 196616 | tf_op jit(solution)/shard_map/ppermute | solution.py:86
  16.9 58.6 %all-to-all-start = ((bf16[8,128,512]{1,2,0:T(8,128)(2,1)}), bf16[8,128,512]{1,2,0:T(8,128)(2,1)S(1)}, u32[]{:S(2)}, u32[]{:S(2)}) async-start(bf16[8,128,512]{1,2,0:T(8,128)(2,1)} %broadcast_in_dim.72), calls=%async_computation | async-start | bytes 2097152 | tf_op jit(solution)/shard_map/all_to_all | solution.py:109
  25.7 183.2 %all-gather.2.cloned.1.call-start = ((), (), s32[]{:S(2)}) async-start(), calls=%async_computation.4 | async-start | bytes 6389760 | tf_op jit(solution)/shard_map/all_gather | solution.py:126
  26.5 10.2 %collective-permute-start.1 = (bf16[256,64]{0,1:T(8,128)(2,1)S(1)}, bf16[256,64]{0,1:T(8,128)(2,1)S(1)}, u32[]{:S(2)}, u32[]{:S(2)}) collective-permute-start(bf16[256,64]{0,1:T(8,128)(2,1)S(1)} %get-tuple-element.17), channel_id=1, source_target_pairs={{0,16},{8,24},{16,0},{24,8},{32,48},{40,56},{48,32},{56,40},{64,80... | collective-permute-start | bytes 98312 | tf_op jit(solution)/shard_map/ppermute | solution.py:86
  28.4 8.3 %collective-permute-start.2 = (bf16[256,64]{0,1:T(8,128)(2,1)S(1)}, bf16[256,64]{0,1:T(8,128)(2,1)S(1)}, u32[]{:S(2)}, u32[]{:S(2)}) collective-permute-start(bf16[256,64]{0,1:T(8,128)(2,1)S(1)} %get-tuple-element.18), channel_id=1, source_target_pairs={{0,16},{8,24},{16,0},{24,8},{32,48},{40,56},{48,32},{56,40},{64,80... | collective-permute-start | bytes 98312 | tf_op jit(solution)/shard_map/ppermute | solution.py:86
  37.1 12.2 %collective-permute-start.4 = (bf16[512,4,64]{0,2,1:T(8,128)(2,1)S(1)}, bf16[512,4,64]{0,2,1:T(8,128)(2,1)S(1)}, u32[]{:S(2)}, u32[]{:S(2)}) collective-permute-start(bf16[512,4,64]{0,2,1:T(8,128)(2,1)S(1)} %pad_maximum_fusion), channel_id=1, source_target_pairs={{0,480},{8,488},{16,496},{24,504},{32,0},{40,8},{48,16},{56,24},{6... | collective-permute-start | bytes 786440 | tf_op jit(solution)/shard_map/ppermute | solution.py:86
  44.7 9.9 %collective-permute-start.11 = (bf16[512,4,64]{0,2,1:T(8,128)(2,1)S(1)}, bf16[512,4,64]{0,2,1:T(8,128)(2,1)S(1)}, u32[]{:S(2)}, u32[]{:S(2)}) collective-permute-start(bf16[512,4,64]{0,2,1:T(8,128)(2,1)S(1)} %pad_maximum_fusion), channel_id=1, source_target_pairs={{0,32},{8,40},{16,48},{24,56},{32,64},{40,72},{48,80},{56,88},{64,... | collective-permute-start | bytes 786440 | tf_op jit(solution)/shard_map/ppermute | solution.py:86
  49.3 9.2 %collective-permute-start.5 = (bf16[512,4,64]{0,2,1:T(8,128)(2,1)S(1)}, bf16[512,4,64]{0,2,1:T(8,128)(2,1)S(1)}, u32[]{:S(2)}, u32[]{:S(2)}) collective-permute-start(bf16[512,4,64]{0,2,1:T(8,128)(2,1)S(1)} %collective-permute-done.4), channel_id=1, source_target_pairs={{0,480},{8,488},{16,496},{24,504},{32,0},{40,8},{48,16},{56,24},{6... | collective-permute-start | bytes 786440 | tf_op jit(solution)/shard_map/ppermute | solution.py:86
  54.6 9.5 %collective-permute-start.12 = (bf16[512,4,64]{0,2,1:T(8,128)(2,1)S(1)}, bf16[512,4,64]{0,2,1:T(8,128)(2,1)S(1)}, u32[]{:S(2)}, u32[]{:S(2)}) collective-permute-start(bf16[512,4,64]{0,2,1:T(8,128)(2,1)S(1)} %collective-permute-done.11), channel_id=1, source_target_pairs={{0,32},{8,40},{16,48},{24,56},{32,64},{40,72},{48,80},{56,88},{64,... | collective-permute-start | bytes 786440 | tf_op jit(solution)/shard_map/ppermute | solution.py:86
  58.2 25.9 %copy-start.6 = (f32[16,4,64]{2,1,0:T(4,128)S(1)}, f32[16,4,64]{2,1,0:T(4,128)}, u32[]{:S(2)}) copy-start(f32[16,4,64]{2,1,0:T(4,128)} %mul.198) | copy-start | bytes 49156
  58.5 9.1 %collective-permute-start.6 = (bf16[512,4,64]{0,2,1:T(8,128)(2,1)S(1)}, bf16[512,4,64]{0,2,1:T(8,128)(2,1)S(1)}, u32[]{:S(2)}, u32[]{:S(2)}) collective-permute-start(bf16[512,4,64]{0,2,1:T(8,128)(2,1)S(1)} %collective-permute-done.5), channel_id=1, source_target_pairs={{0,480},{8,488},{16,496},{24,504},{32,0},{40,8},{48,16},{56,24},{6... | collective-permute-start | bytes 786440 | tf_op jit(solution)/shard_map/ppermute | solution.py:86
  64.2 8.7 %collective-permute-start.13 = (bf16[512,4,64]{0,2,1:T(8,128)(2,1)S(1)}, bf16[512,4,64]{0,2,1:T(8,128)(2,1)S(1)}, u32[]{:S(2)}, u32[]{:S(2)}) collective-permute-start(bf16[512,4,64]{0,2,1:T(8,128)(2,1)S(1)} %collective-permute-done.12), channel_id=1, source_target_pairs={{0,32},{8,40},{16,48},{24,56},{32,64},{40,72},{48,80},{56,88},{64,... | collective-permute-start | bytes 786440 | tf_op jit(solution)/shard_map/ppermute | solution.py:86
  67.5 8.8 %collective-permute-start.7 = (bf16[512,4,64]{0,2,1:T(8,128)(2,1)S(1)}, bf16[512,4,64]{0,2,1:T(8,128)(2,1)S(1)}, u32[]{:S(2)}, u32[]{:S(2)}) collective-permute-start(bf16[512,4,64]{0,2,1:T(8,128)(2,1)S(1)} %collective-permute-done.6), channel_id=1, source_target_pairs={{0,480},{8,488},{16,496},{24,504},{32,0},{40,8},{48,16},{56,24},{6... | collective-permute-start | bytes 786440 | tf_op jit(solution)/shard_map/ppermute | solution.py:86
  72.9 9.3 %collective-permute-start.14 = (bf16[512,4,64]{0,2,1:T(8,128)(2,1)S(1)}, bf16[512,4,64]{0,2,1:T(8,128)(2,1)S(1)}, u32[]{:S(2)}, u32[]{:S(2)}) collective-permute-start(bf16[512,4,64]{0,2,1:T(8,128)(2,1)S(1)} %collective-permute-done.13), channel_id=1, source_target_pairs={{0,32},{8,40},{16,48},{24,56},{32,64},{40,72},{48,80},{56,88},{64,... | collective-permute-start | bytes 786440 | tf_op jit(solution)/shard_map/ppermute | solution.py:86
  76.2 14.8 %copy-start.14 = (f32[128]{0:T(128)}, f32[128]{0:T(128)S(1)}, u32[]{:S(2)}) copy-start(f32[128]{0:T(128)S(1)} %add_rsqrt_fusion) | copy-start | bytes 1540
  76.3 9.1 %collective-permute-start.8 = (bf16[512,4,64]{0,2,1:T(8,128)(2,1)S(1)}, bf16[512,4,64]{0,2,1:T(8,128)(2,1)S(1)}, u32[]{:S(2)}, u32[]{:S(2)}) collective-permute-start(bf16[512,4,64]{0,2,1:T(8,128)(2,1)S(1)} %collective-permute-done.7), channel_id=1, source_target_pairs={{0,480},{8,488},{16,496},{24,504},{32,0},{40,8},{48,16},{56,24},{6... | collective-permute-start | bytes 786440 | tf_op jit(solution)/shard_map/ppermute | solution.py:86
  82.2 8.9 %collective-permute-start.15 = (bf16[512,4,64]{0,2,1:T(8,128)(2,1)S(1)}, bf16[512,4,64]{0,2,1:T(8,128)(2,1)S(1)}, u32[]{:S(2)}, u32[]{:S(2)}) collective-permute-start(bf16[512,4,64]{0,2,1:T(8,128)(2,1)S(1)} %collective-permute-done.14), channel_id=1, source_target_pairs={{0,32},{8,40},{16,48},{24,56},{32,64},{40,72},{48,80},{56,88},{64,... | collective-permute-start | bytes 786440 | tf_op jit(solution)/shard_map/ppermute | solution.py:86
  85.5 9.3 %collective-permute-start.9 = (bf16[512,4,64]{0,2,1:T(8,128)(2,1)S(1)}, bf16[512,4,64]{0,2,1:T(8,128)(2,1)S(1)}, u32[]{:S(2)}, u32[]{:S(2)}) collective-permute-start(bf16[512,4,64]{0,2,1:T(8,128)(2,1)S(1)} %collective-permute-done.8), channel_id=1, source_target_pairs={{0,480},{8,488},{16,496},{24,504},{32,0},{40,8},{48,16},{56,24},{6... | collective-permute-start | bytes 786440 | tf_op jit(solution)/shard_map/ppermute | solution.py:86
  91.1 9.5 %collective-permute-start.16 = (bf16[512,4,64]{0,2,1:T(8,128)(2,1)S(1)}, bf16[512,4,64]{0,2,1:T(8,128)(2,1)S(1)}, u32[]{:S(2)}, u32[]{:S(2)}) collective-permute-start(bf16[512,4,64]{0,2,1:T(8,128)(2,1)S(1)} %collective-permute-done.15), channel_id=1, source_target_pairs={{0,32},{8,40},{16,48},{24,56},{32,64},{40,72},{48,80},{56,88},{64,... | collective-permute-start | bytes 786440 | tf_op jit(solution)/shard_map/ppermute | solution.py:86
  94.8 17.0 %collective-permute-start.10 = (bf16[512,4,64]{0,2,1:T(8,128)(2,1)S(1)}, bf16[512,4,64]{0,2,1:T(8,128)(2,1)S(1)}, u32[]{:S(2)}, u32[]{:S(2)}) collective-permute-start(bf16[512,4,64]{0,2,1:T(8,128)(2,1)S(1)} %collective-permute-done.9), channel_id=1, source_target_pairs={{0,480},{8,488},{16,496},{24,504},{32,0},{40,8},{48,16},{56,24},{6... | collective-permute-start | bytes 786440 | tf_op jit(solution)/shard_map/ppermute | solution.py:86
  100.6 9.2 %collective-permute-start.17 = (bf16[512,4,64]{0,2,1:T(8,128)(2,1)S(1)}, bf16[512,4,64]{0,2,1:T(8,128)(2,1)S(1)}, u32[]{:S(2)}, u32[]{:S(2)}) collective-permute-start(bf16[512,4,64]{0,2,1:T(8,128)(2,1)S(1)} %collective-permute-done.16), channel_id=1, source_target_pairs={{0,32},{8,40},{16,48},{24,56},{32,64},{40,72},{48,80},{56,88},{64,... | collective-permute-start | bytes 786440 | tf_op jit(solution)/shard_map/ppermute | solution.py:86
  109.8 8.7 %collective-permute-start.18 = (bf16[256,4,64]{0,2,1:T(8,128)(2,1)S(1)}, bf16[256,4,64]{0,2,1:T(8,128)(2,1)S(1)}, u32[]{:S(2)}, u32[]{:S(2)}) collective-permute-start(bf16[256,4,64]{0,2,1:T(8,128)(2,1)S(1)} %slice.112), channel_id=1, source_target_pairs={{0,32},{8,40},{16,48},{24,56},{32,64},{40,72},{48,80},{56,88},{64,... | collective-permute-start | bytes 393224 | tf_op jit(solution)/shard_map/ppermute | solution.py:86
  111.7 6.7 %collective-permute-start.19 = (bf16[256,4,64]{0,2,1:T(8,128)(2,1)S(1)}, bf16[256,4,64]{0,2,1:T(8,128)(2,1)S(1)}, u32[]{:S(2)}, u32[]{:S(2)}) collective-permute-start(bf16[256,4,64]{0,2,1:T(8,128)(2,1)S(1)} %slice.113), channel_id=1, source_target_pairs={{0,480},{8,488},{16,496},{24,504},{32,0},{40,8},{48,16},{56,24},{6... | collective-permute-start | bytes 393224 | tf_op jit(solution)/shard_map/ppermute | solution.py:86
  138.3 32.9 %all-to-all-start.1 = ((bf16[64,4,512]{2,1,0:T(4,128)(2,1)}), bf16[64,4,512]{2,1,0:T(4,128)(2,1)}, u32[]{:S(2)}, u32[]{:S(2)}) async-start(bf16[64,4,512]{2,1,0:T(4,128)(2,1)} %broadcast_select_fusion), calls=%async_computation.1 | async-start | bytes 524288 | tf_op jit(solution)/shard_map/all_to_all | solution.py:175
  179.3 27.5 %all-to-all-start.2 = ((bf16[64,5,512]{2,1,0:T(8,128)(2,1)}), bf16[64,5,512]{2,1,0:T(8,128)(2,1)S(1)}, u32[]{:S(2)}, u32[]{:S(2)}) async-start(bf16[64,5,512]{2,1,0:T(8,128)(2,1)} %fusion.18), calls=%async_computation.2 | async-start | bytes 1048576 | tf_op jit(solution)/shard_map/all_to_all | solution.py:193
  220.5 31.0 %all-to-all-start.3 = ((bf16[8,128,512]{2,1,0:T(8,128)(2,1)}), bf16[8,128,512]{2,1,0:T(8,128)(2,1)S(1)}, u32[]{:S(2)}, u32[]{:S(2)}) async-start(bf16[8,128,512]{2,1,0:T(8,128)(2,1)} %bitcast.212), calls=%async_computation.3 | async-start | bytes 2097152 | tf_op jit(solution)/shard_map/all_to_all | solution.py:231
  (14 other events, 76.0 us)
Sparse Core Ops, SparseCore 0:
  35.0 154.6 all-gather.1

commit v11 on v7

--- a/solution.py
+++ b/solution.py
@@ -117,8 +117,6 @@
     kv_width = kv_local * 2 * head_size
     kv_piece = lax.dynamic_slice_in_dim(key_value_weight, kv_start * 2 * head_size, kv_width, 1)
     side = lax.all_gather(jnp.concatenate([kv_piece.T, w_out], axis=0), "seq", axis=1, tiled=True)
-    kv_rows = side[:kv_width]
-    wo_full = side[kv_width:]
     wq_rows, z_at, y_at = ring_gather(w_query.T, "seq", seq_count)
     z_count = seq_count // Y_CHIPS
     rel_input = normalized_input.reshape(length, z_count, Y_CHIPS, -1)
@@ -131,8 +129,8 @@
 
     query_vectors = contract(wq_rows)
     key_value_pair = lax.dot_general(
-        normalized_input, kv_rows, (((1,), (1,)), ((), ())), preferred_element_type=jnp.float32
-    )
+        normalized_input, side, (((1,), (1,)), ((), ())), preferred_element_type=jnp.float32
+    )[:, :kv_width]
     counts = token_counts[0]
     num_groups = counts.shape[0]
     starts, prefix_group, offset = layout(counts, length)
@@ -218,7 +216,8 @@
         (left * prefix_rows.astype(jnp.float32) + right * suffix_attn) / (left + right)
     ).astype(jnp.bfloat16)
     context = context.reshape(length, width_query)
-    partial_out = jnp.dot(context, wo_full, preferred_element_type=jnp.float32)
+    padded_context = jnp.pad(context, ((0, 0), (kv_width, 0)))
+    partial_out = jnp.dot(padded_context, side, preferred_element_type=jnp.float32)
     out_width = partial_out.shape[1] // tensor_count
     pieces = partial_out.astype(jnp.bfloat16).reshape(length, tensor_count, out_width)
     pieces = lax.all_to_all(

time: 258 us -> 257 us (level)
  local copies, waits for them, and re-layouts: 38.4 us -> 32.6 us
  matrix products: 10.6 us -> 15.5 us
    slice x3 -> x1, local copies, waits for them, and re-layouts: 6.1 us -> 0.1 us  [shards(): rotated_keys = rotate(pair_blocks[:, :, 0], positions)]
    dot_general x2, matrix products: 2.19 us -> 7.09 us  [the longest x1 4.99 us: shards(): jnp.dot(padded_context, side, preferred_element_type=jnp.float32)]
    unnamed x45 -> x39, local copies, waits for them, and re-layouts: 15.5 us -> 15.5 us
  transfers between devices with their start and end apart: 23 -> 23, of which waited for: 13 -> 12; matrix products, arithmetic and copies ran while one was open for 20% -> 19% of each run, Pallas kernels for 0% -> 0%
where the time goes in v11:
time: 257 us; the launch traced here: 256 us
  starting transfers between devices  103 us (40%)
  waiting for transfers between devices  75.8 us (29%)
  local copies, waits for them, and re-layouts  32.6 us (13%)
  matrix products  15.5 us (6%)
  between operations  14.9 us (6%)
  other arithmetic  13.6 us (5%)
    ppermute x18, starting transfers between devices, shift(): return lax.ppermute(value, axis_name, pairs)  59.1 us
    ppermute x18, waiting for transfers between devices, shift(): return lax.ppermute(value, axis_name, pairs)  23.8 us
    all_to_all x1, waiting for transfers between devices, shards(): lax.all_to_all(jnp.concatenate([out_block, log_row], axis=1), 'seq', spli...  21.3 us
    all_to_all x1, starting transfers between devices, shards(): lax.all_to_all(jnp.moveaxis(pieces, 1, 0), 'tensor', split_axis=0, concat...  19.5 us
    all_to_all x1, waiting for transfers between devices, shards(): lax.all_to_all(outgoing, 'seq', split_axis=0, concat_axis=0, tiled=True)  16.4 us
    unnamed x39, local copies, waits for them, and re-layouts  15.5 us
    all_to_all x1, waiting for transfers between devices, shards(): lax.all_to_all(jnp.moveaxis(pieces, 1, 0), 'tensor', split_axis=0, concat...  14.2 us
    all_to_all x1, starting transfers between devices, shards(): lax.all_to_all(tiles, 'tensor', split_axis=0, concat_axis=0, tiled=True)  10 us
  transfers between devices with their start and end apart: 23, of which 12 were waited for; matrix products, arithmetic and copies ran while one was open for 19% of the time, Pallas kernels for 0%

profile of v11, /device:TPU:1, one launch (start us, length us, event | category | flops | bytes accessed | tf_op | source)
XLA Modules:
  0.0 255.5 jit_solution(8426549689417496805)
XLA Ops:
  7.2 4.2 %collective-permute-start.1 = (bf16[512,64]{0,1:T(8,128)(2,1)}, bf16[512,64]{0,1:T(8,128)(2,1)S(1)}, u32[]{:S(2)}, u32[]{:S(2)}) collective-permute-start(bf16[512,64]{0,1:T(8,128)(2,1)} %bitcast.225), channel_id=1, source_target_pairs={{0,8},{8,16},{16,24},{24,0},{32,40},{40,48},{48,56},{56,32},{64,72... | collective-permute-start | bytes 196616 | tf_op jit(solution)/shard_map/ppermute | solution.py:79
  11.4 3.4 %collective-permute-start = (bf16[512,64]{0,1:T(8,128)(2,1)}, bf16[512,64]{0,1:T(8,128)(2,1)S(1)}, u32[]{:S(2)}, u32[]{:S(2)}) collective-permute-start(bf16[512,64]{0,1:T(8,128)(2,1)} %bitcast.226), channel_id=1, source_target_pairs={{0,24},{8,0},{16,8},{24,16},{32,56},{40,32},{48,40},{56,48},{64,88... | collective-permute-start | bytes 196616 | tf_op jit(solution)/shard_map/ppermute | solution.py:79
  16.9 10.0 %all-to-all-start = ((bf16[8,128,512]{1,2,0:T(8,128)(2,1)}), bf16[8,128,512]{1,2,0:T(8,128)(2,1)S(1)}, u32[]{:S(2)}, u32[]{:S(2)}) async-start(bf16[8,128,512]{1,2,0:T(8,128)(2,1)} %broadcast_in_dim.72), calls=%async_computation | async-start | bytes 2097152 | tf_op jit(solution)/shard_map/all_to_all | solution.py:102
  31.5 1.9 collective-permute-start.2
  33.5 4.7 %collective-permute-done.2 = bf16[512,64]{0,1:T(8,128)(2,1)S(1)} collective-permute-done((bf16[512,64]{0,1:T(8,128)(2,1)S(1)}, bf16[512,64]{0,1:T(8,128)(2,1)S(1)}, u32[]{:S(2)}, u32[]{:S(2)}) %collective-permute-start.2) | collective-permute-done | bytes 65568 | tf_op jit(solution)/shard_map/ppermute | solution.py:79
  39.0 1.9 collective-permute-start.10
  41.2 6.7 %collective-permute-start.3 = (bf16[512,4,64]{0,2,1:T(8,128)(2,1)S(1)}, bf16[512,4,64]{0,2,1:T(8,128)(2,1)S(1)}, u32[]{:S(2)}, u32[]{:S(2)}) collective-permute-start(bf16[512,4,64]{0,2,1:T(8,128)(2,1)S(1)} %pad_maximum_fusion), channel_id=1, source_target_pairs={{0,480},{8,488},{16,496},{24,504},{32,0},{40,8},{48,16},{56,24},{6... | collective-permute-start | bytes 786440 | tf_op jit(solution)/shard_map/ppermute | solution.py:79
  47.9 4.3 %collective-permute-done.10 = bf16[512,4,64]{0,2,1:T(8,128)(2,1)S(1)} collective-permute-done((bf16[512,4,64]{0,2,1:T(8,128)(2,1)S(1)}, bf16[512,4,64]{0,2,1:T(8,128)(2,1)S(1)}, u32[]{:S(2)}, u32[]{:S(2)}) %collective-permute-start.10) | collective-permute-done | bytes 262176 | tf_op jit(solution)/shard_map/ppermute | solution.py:79
  52.2 1.9 collective-permute-start.11
  54.5 4.6 %collective-permute-start.4 = (bf16[512,4,64]{0,2,1:T(8,128)(2,1)S(1)}, bf16[512,4,64]{0,2,1:T(8,128)(2,1)S(1)}, u32[]{:S(2)}, u32[]{:S(2)}) collective-permute-start(bf16[512,4,64]{0,2,1:T(8,128)(2,1)S(1)} %collective-permute-done.3), channel_id=1, source_target_pairs={{0,480},{8,488},{16,496},{24,504},{32,0},{40,8},{48,16},{56,24},{6... | collective-permute-start | bytes 786440 | tf_op jit(solution)/shard_map/ppermute | solution.py:79
  59.8 2.8 %collective-permute-done.11 = bf16[512,4,64]{0,2,1:T(8,128)(2,1)S(1)} collective-permute-done((bf16[512,4,64]{0,2,1:T(8,128)(2,1)S(1)}, bf16[512,4,64]{0,2,1:T(8,128)(2,1)S(1)}, u32[]{:S(2)}, u32[]{:S(2)}) %collective-permute-start.11) | collective-permute-done | bytes 262176 | tf_op jit(solution)/shard_map/ppermute | solution.py:79
  62.6 1.9 collective-permute-start.12
  65.3 4.6 %collective-permute-start.5 = (bf16[512,4,64]{0,2,1:T(8,128)(2,1)S(1)}, bf16[512,4,64]{0,2,1:T(8,128)(2,1)S(1)}, u32[]{:S(2)}, u32[]{:S(2)}) collective-permute-start(bf16[512,4,64]{0,2,1:T(8,128)(2,1)S(1)} %collective-permute-done.4), channel_id=1, source_target_pairs={{0,480},{8,488},{16,496},{24,504},{32,0},{40,8},{48,16},{56,24},{6... | collective-permute-start | bytes 786440 | tf_op jit(solution)/shard_map/ppermute | solution.py:79
  72.1 1.9 collective-permute-start.13
  74.8 4.6 %collective-permute-start.6 = (bf16[512,4,64]{0,2,1:T(8,128)(2,1)S(1)}, bf16[512,4,64]{0,2,1:T(8,128)(2,1)S(1)}, u32[]{:S(2)}, u32[]{:S(2)}) collective-permute-start(bf16[512,4,64]{0,2,1:T(8,128)(2,1)S(1)} %collective-permute-done.5), channel_id=1, source_target_pairs={{0,480},{8,488},{16,496},{24,504},{32,0},{40,8},{48,16},{56,24},{6... | collective-permute-start | bytes 786440 | tf_op jit(solution)/shard_map/ppermute | solution.py:79
  81.3 1.9 collective-permute-start.14
  83.9 4.6 %collective-permute-start.7 = (bf16[512,4,64]{0,2,1:T(8,128)(2,1)S(1)}, bf16[512,4,64]{0,2,1:T(8,128)(2,1)S(1)}, u32[]{:S(2)}, u32[]{:S(2)}) collective-permute-start(bf16[512,4,64]{0,2,1:T(8,128)(2,1)S(1)} %collective-permute-done.6), channel_id=1, source_target_pairs={{0,480},{8,488},{16,496},{24,504},{32,0},{40,8},{48,16},{56,24},{6... | collective-permute-start | bytes 786440 | tf_op jit(solution)/shard_map/ppermute | solution.py:79
  92.5 4.9 %collective-permute-start.8 = (bf16[512,4,64]{0,2,1:T(8,128)(2,1)S(1)}, bf16[512,4,64]{0,2,1:T(8,128)(2,1)S(1)}, u32[]{:S(2)}, u32[]{:S(2)}) collective-permute-start(bf16[512,4,64]{0,2,1:T(8,128)(2,1)S(1)} %collective-permute-done.7), channel_id=1, source_target_pairs={{0,480},{8,488},{16,496},{24,504},{32,0},{40,8},{48,16},{56,24},{6... | collective-permute-start | bytes 786440 | tf_op jit(solution)/shard_map/ppermute | solution.py:79
  98.8 1.9 collective-permute-start.16
  101.4 4.6 %collective-permute-start.9 = (bf16[512,4,64]{0,2,1:T(8,128)(2,1)S(1)}, bf16[512,4,64]{0,2,1:T(8,128)(2,1)S(1)}, u32[]{:S(2)}, u32[]{:S(2)}) collective-permute-start(bf16[512,4,64]{0,2,1:T(8,128)(2,1)S(1)} %collective-permute-done.8), channel_id=1, source_target_pairs={{0,480},{8,488},{16,496},{24,504},{32,0},{40,8},{48,16},{56,24},{6... | collective-permute-start | bytes 786440 | tf_op jit(solution)/shard_map/ppermute | solution.py:79
  110.6 6.1 %collective-permute-done.17 = bf16[512,4,64]{0,2,1:T(8,128)(2,1)S(1)} collective-permute-done((bf16[512,4,64]{0,2,1:T(8,128)(2,1)S(1)}, bf16[512,4,64]{0,2,1:T(8,128)(2,1)S(1)}, u32[]{:S(2)}, u32[]{:S(2)}) %collective-permute-start.17) | collective-permute-done | bytes 262176 | tf_op jit(solution)/shard_map/ppermute | solution.py:79
  122.5 6.9 %dot_general.59 = bf16[4,128,4096]{1,0,2:T(4,128)(2,1)} reshape(bf16[512,16,4,64]{0,3,2,1:T(8,128)(2,1)} %bitcast_dynamic-update-slice_fusion) | data formatting | bytes 8388608 | tf_op jit(solution)/shard_map/dot_general | solution.py:126
  129.5 3.9 %fusion = f32[128,4,128]{0,2,1:T(8,128)S(1)} fusion(bf16[128,4096,1]{0,1,2:T(8,128)(2,1)S(1)} %bitcast.220, bf16[4,128,4096]{1,0,2:T(4,128)(2,1)} %dot_general.59), kind=kOutput, calls=%fused_computation.4 | convolution fusion | flops 536870912 | bytes 5505024 | tf_op jit(solution)/shard_map/dot_general | solution.py:126
  136.4 9.9 %all-to-all-start.1 = ((bf16[64,4,512]{2,1,0:T(4,128)(2,1)}), bf16[64,4,512]{2,1,0:T(4,128)(2,1)}, u32[]{:S(2)}, u32[]{:S(2)}) async-start(bf16[64,4,512]{2,1,0:T(4,128)(2,1)} %broadcast_select_fusion), calls=%async_computation.1 | async-start | bytes 524288 | tf_op jit(solution)/shard_map/all_to_all | solution.py:166
  146.3 2.9 %copy.117 = bf16[1,1024,1024]{1,2,0:T(8,128)(2,1)S(1)} copy(bf16[1,1024,1024]{2,1,0:T(8,128)(2,1)} %param.13) | data formatting | bytes 4194304 | tf_op args[5]
  149.2 16.4 %all-to-all-done.1 = bf16[64,4,512]{2,1,0:T(4,128)(2,1)} async-done(((bf16[64,4,512]{2,1,0:T(4,128)(2,1)}), bf16[64,4,512]{2,1,0:T(4,128)(2,1)}, u32[]{:S(2)}, u32[]{:S(2)}) %all-to-all-start.1) | async-done | bytes 262176 | tf_op jit(solution)/shard_map/all_to_all | solution.py:166
  173.8 4.6 %all-to-all-start.2 = ((bf16[64,5,512]{2,1,0:T(8,128)(2,1)}), bf16[64,5,512]{2,1,0:T(8,128)(2,1)S(1)}, u32[]{:S(2)}, u32[]{:S(2)}) async-start(bf16[64,5,512]{2,1,0:T(8,128)(2,1)} %fusion.21), calls=%async_computation.2 | async-start | bytes 1048576 | tf_op jit(solution)/shard_map/all_to_all | solution.py:184
  179.3 21.3 %all-to-all-done.2 = bf16[64,5,512]{2,1,0:T(8,128)(2,1)S(1)} async-done(((bf16[64,5,512]{2,1,0:T(8,128)(2,1)}), bf16[64,5,512]{2,1,0:T(8,128)(2,1)S(1)}, u32[]{:S(2)}, u32[]{:S(2)}) %all-to-all-start.2) | async-done | bytes 327712 | tf_op jit(solution)/shard_map/all_to_all | solution.py:184
  202.7 2.1 fusion.2
  207.2 5.0 %convolution_convert_fusion = bf16[128,4096]{1,0:T(8,128)(2,1)S(1)} fusion(bf16[768,4096]{0,1:T(8,128)(2,1)} %all-gather.2.cloned.1.call-done, bf16[128,512]{0,1:T(8,128)(2,1)S(1)} %bitcast.222), kind=kOutput, calls=%fused_computation.3 | convolution fusion | flops 805830656 | bytes 7471104 | tf_op jit(solution)/shard_map/dot_general | solution.py:220
  213.3 19.5 %all-to-all-start.3 = ((bf16[8,128,512]{2,1,0:T(8,128)(2,1)}), bf16[8,128,512]{2,1,0:T(8,128)(2,1)S(1)}, u32[]{:S(2)}, u32[]{:S(2)}) async-start(bf16[8,128,512]{2,1,0:T(8,128)(2,1)} %bitcast.209), calls=%async_computation.3 | async-start | bytes 2097152 | tf_op jit(solution)/shard_map/all_to_all | solution.py:223
  233.6 14.2 %all-to-all-done.3 = bf16[8,128,512]{2,1,0:T(8,128)(2,1)S(1)} async-done(((bf16[8,128,512]{2,1,0:T(8,128)(2,1)}), bf16[8,128,512]{2,1,0:T(8,128)(2,1)S(1)}, u32[]{:S(2)}, u32[]{:S(2)}) %all-to-all-start.3) | async-done | bytes 1048608 | tf_op jit(solution)/shard_map/all_to_all | solution.py:223
  (160 shorter events, 50.6 us)
Async XLA Ops:
  7.2 19.7 %copy-start = (bf16[64,1024]{1,0:T(8,128)(2,1)S(1)}, bf16[64,1024]{1,0:T(8,128)(2,1)}, u32[]{:S(2)}) copy-start(bf16[64,1024]{1,0:T(8,128)(2,1)} %param.11) | copy-start | bytes 393220
  7.2 51.9 %copy-start.3 = (bf16[64,512]{1,0:T(8,128)(2,1)S(1)}, bf16[64,512]{1,0:T(8,128)(2,1)}, u32[]{:S(2)}) copy-start(bf16[64,512]{1,0:T(8,128)(2,1)} %param.10) | copy-start | bytes 196612
  7.2 47.2 %copy-start.4 = (bf16[4096]{0:T(1024)(128)(2,1)S(1)}, bf16[4096]{0:T(1024)(128)(2,1)}, u32[]{:S(2)}) copy-start(bf16[4096]{0:T(1024)(128)(2,1)} %param.9) | copy-start | bytes 24580
  7.2 24.3 %collective-permute-start.1 = (bf16[512,64]{0,1:T(8,128)(2,1)}, bf16[512,64]{0,1:T(8,128)(2,1)S(1)}, u32[]{:S(2)}, u32[]{:S(2)}) collective-permute-start(bf16[512,64]{0,1:T(8,128)(2,1)} %bitcast.225), channel_id=1, source_target_pairs={{0,8},{8,16},{16,24},{24,0},{32,40},{40,48},{48,56},{56,32},{64,72... | collective-permute-start | bytes 196616 | tf_op jit(solution)/shard_map/ppermute | solution.py:79
  11.4 22.1 %collective-permute-start = (bf16[512,64]{0,1:T(8,128)(2,1)}, bf16[512,64]{0,1:T(8,128)(2,1)S(1)}, u32[]{:S(2)}, u32[]{:S(2)}) collective-permute-start(bf16[512,64]{0,1:T(8,128)(2,1)} %bitcast.226), channel_id=1, source_target_pairs={{0,24},{8,0},{16,8},{24,16},{32,56},{40,32},{48,40},{56,48},{64,88... | collective-permute-start | bytes 196616 | tf_op jit(solution)/shard_map/ppermute | solution.py:79
  16.9 57.2 %all-to-all-start = ((bf16[8,128,512]{1,2,0:T(8,128)(2,1)}), bf16[8,128,512]{1,2,0:T(8,128)(2,1)S(1)}, u32[]{:S(2)}, u32[]{:S(2)}) async-start(bf16[8,128,512]{1,2,0:T(8,128)(2,1)} %broadcast_in_dim.72), calls=%async_computation | async-start | bytes 2097152 | tf_op jit(solution)/shard_map/all_to_all | solution.py:102
  26.9 175.8 %all-gather.2.cloned.1.call-start = ((), (), s32[]{:S(2)}) async-start(), calls=%async_computation.4 | async-start | bytes 6389760 | tf_op jit(solution)/shard_map/all_gather | solution.py:119
  31.5 42.5 %copy-start.9 = (s32[128]{0:T(128)}, s32[128]{0:T(128)S(1)}, u32[]{:S(2)}) copy-start(s32[128]{0:T(128)S(1)} %get-tuple-element.11) | copy-start | bytes 1540
  31.5 6.6 %collective-permute-start.2 = (bf16[512,64]{0,1:T(8,128)(2,1)S(1)}, bf16[512,64]{0,1:T(8,128)(2,1)S(1)}, u32[]{:S(2)}, u32[]{:S(2)}) collective-permute-start(bf16[512,64]{0,1:T(8,128)(2,1)S(1)} %collective-permute-done.1), channel_id=1, source_target_pairs={{0,8},{8,16},{16,24},{24,0},{32,40},{40,48},{48,56},{56,32},{64,72... | collective-permute-start | bytes 196616 | tf_op jit(solution)/shard_map/ppermute | solution.py:79
  39.0 13.1 %collective-permute-start.10 = (bf16[512,4,64]{0,2,1:T(8,128)(2,1)S(1)}, bf16[512,4,64]{0,2,1:T(8,128)(2,1)S(1)}, u32[]{:S(2)}, u32[]{:S(2)}) collective-permute-start(bf16[512,4,64]{0,2,1:T(8,128)(2,1)S(1)} %pad_maximum_fusion), channel_id=1, source_target_pairs={{0,32},{8,40},{16,48},{24,56},{32,64},{40,72},{48,80},{56,88},{64,... | collective-permute-start | bytes 786440 | tf_op jit(solution)/shard_map/ppermute | solution.py:79
  41.2 13.3 %collective-permute-start.3 = (bf16[512,4,64]{0,2,1:T(8,128)(2,1)S(1)}, bf16[512,4,64]{0,2,1:T(8,128)(2,1)S(1)}, u32[]{:S(2)}, u32[]{:S(2)}) collective-permute-start(bf16[512,4,64]{0,2,1:T(8,128)(2,1)S(1)} %pad_maximum_fusion), channel_id=1, source_target_pairs={{0,480},{8,488},{16,496},{24,504},{32,0},{40,8},{48,16},{56,24},{6... | collective-permute-start | bytes 786440 | tf_op jit(solution)/shard_map/ppermute | solution.py:79
  52.2 10.5 %collective-permute-start.11 = (bf16[512,4,64]{0,2,1:T(8,128)(2,1)S(1)}, bf16[512,4,64]{0,2,1:T(8,128)(2,1)S(1)}, u32[]{:S(2)}, u32[]{:S(2)}) collective-permute-start(bf16[512,4,64]{0,2,1:T(8,128)(2,1)S(1)} %collective-permute-done.10), channel_id=1, source_target_pairs={{0,32},{8,40},{16,48},{24,56},{32,64},{40,72},{48,80},{56,88},{64,... | collective-permute-start | bytes 786440 | tf_op jit(solution)/shard_map/ppermute | solution.py:79
  54.5 10.8 %collective-permute-start.4 = (bf16[512,4,64]{0,2,1:T(8,128)(2,1)S(1)}, bf16[512,4,64]{0,2,1:T(8,128)(2,1)S(1)}, u32[]{:S(2)}, u32[]{:S(2)}) collective-permute-start(bf16[512,4,64]{0,2,1:T(8,128)(2,1)S(1)} %collective-permute-done.3), channel_id=1, source_target_pairs={{0,480},{8,488},{16,496},{24,504},{32,0},{40,8},{48,16},{56,24},{6... | collective-permute-start | bytes 786440 | tf_op jit(solution)/shard_map/ppermute | solution.py:79
  62.6 9.5 %collective-permute-start.12 = (bf16[512,4,64]{0,2,1:T(8,128)(2,1)S(1)}, bf16[512,4,64]{0,2,1:T(8,128)(2,1)S(1)}, u32[]{:S(2)}, u32[]{:S(2)}) collective-permute-start(bf16[512,4,64]{0,2,1:T(8,128)(2,1)S(1)} %collective-permute-done.11), channel_id=1, source_target_pairs={{0,32},{8,40},{16,48},{24,56},{32,64},{40,72},{48,80},{56,88},{64,... | collective-permute-start | bytes 786440 | tf_op jit(solution)/shard_map/ppermute | solution.py:79
  65.3 9.5 %collective-permute-start.5 = (bf16[512,4,64]{0,2,1:T(8,128)(2,1)S(1)}, bf16[512,4,64]{0,2,1:T(8,128)(2,1)S(1)}, u32[]{:S(2)}, u32[]{:S(2)}) collective-permute-start(bf16[512,4,64]{0,2,1:T(8,128)(2,1)S(1)} %collective-permute-done.4), channel_id=1, source_target_pairs={{0,480},{8,488},{16,496},{24,504},{32,0},{40,8},{48,16},{56,24},{6... | collective-permute-start | bytes 786440 | tf_op jit(solution)/shard_map/ppermute | solution.py:79
  72.1 9.2 %collective-permute-start.13 = (bf16[512,4,64]{0,2,1:T(8,128)(2,1)S(1)}, bf16[512,4,64]{0,2,1:T(8,128)(2,1)S(1)}, u32[]{:S(2)}, u32[]{:S(2)}) collective-permute-start(bf16[512,4,64]{0,2,1:T(8,128)(2,1)S(1)} %collective-permute-done.12), channel_id=1, source_target_pairs={{0,32},{8,40},{16,48},{24,56},{32,64},{40,72},{48,80},{56,88},{64,... | collective-permute-start | bytes 786440 | tf_op jit(solution)/shard_map/ppermute | solution.py:79
  74.8 9.1 %collective-permute-start.6 = (bf16[512,4,64]{0,2,1:T(8,128)(2,1)S(1)}, bf16[512,4,64]{0,2,1:T(8,128)(2,1)S(1)}, u32[]{:S(2)}, u32[]{:S(2)}) collective-permute-start(bf16[512,4,64]{0,2,1:T(8,128)(2,1)S(1)} %collective-permute-done.5), channel_id=1, source_target_pairs={{0,480},{8,488},{16,496},{24,504},{32,0},{40,8},{48,16},{56,24},{6... | collective-permute-start | bytes 786440 | tf_op jit(solution)/shard_map/ppermute | solution.py:79
  79.4 22.0 %copy-start.5 = (f32[128]{0:T(128)}, f32[128]{0:T(128)S(1)}, u32[]{:S(2)}) copy-start(f32[128]{0:T(128)S(1)} %add_rsqrt_fusion) | copy-start | bytes 1540
  81.3 8.9 %collective-permute-start.14 = (bf16[512,4,64]{0,2,1:T(8,128)(2,1)S(1)}, bf16[512,4,64]{0,2,1:T(8,128)(2,1)S(1)}, u32[]{:S(2)}, u32[]{:S(2)}) collective-permute-start(bf16[512,4,64]{0,2,1:T(8,128)(2,1)S(1)} %collective-permute-done.13), channel_id=1, source_target_pairs={{0,32},{8,40},{16,48},{24,56},{32,64},{40,72},{48,80},{56,88},{64,... | collective-permute-start | bytes 786440 | tf_op jit(solution)/shard_map/ppermute | solution.py:79
  83.9 8.6 %collective-permute-start.7 = (bf16[512,4,64]{0,2,1:T(8,128)(2,1)S(1)}, bf16[512,4,64]{0,2,1:T(8,128)(2,1)S(1)}, u32[]{:S(2)}, u32[]{:S(2)}) collective-permute-start(bf16[512,4,64]{0,2,1:T(8,128)(2,1)S(1)} %collective-permute-done.6), channel_id=1, source_target_pairs={{0,480},{8,488},{16,496},{24,504},{32,0},{40,8},{48,16},{56,24},{6... | collective-permute-start | bytes 786440 | tf_op jit(solution)/shard_map/ppermute | solution.py:79
  90.2 8.6 %collective-permute-start.15 = (bf16[512,4,64]{0,2,1:T(8,128)(2,1)S(1)}, bf16[512,4,64]{0,2,1:T(8,128)(2,1)S(1)}, u32[]{:S(2)}, u32[]{:S(2)}) collective-permute-start(bf16[512,4,64]{0,2,1:T(8,128)(2,1)S(1)} %collective-permute-done.14), channel_id=1, source_target_pairs={{0,32},{8,40},{16,48},{24,56},{32,64},{40,72},{48,80},{56,88},{64,... | collective-permute-start | bytes 786440 | tf_op jit(solution)/shard_map/ppermute | solution.py:79
  92.5 8.9 %collective-permute-start.8 = (bf16[512,4,64]{0,2,1:T(8,128)(2,1)S(1)}, bf16[512,4,64]{0,2,1:T(8,128)(2,1)S(1)}, u32[]{:S(2)}, u32[]{:S(2)}) collective-permute-start(bf16[512,4,64]{0,2,1:T(8,128)(2,1)S(1)} %collective-permute-done.7), channel_id=1, source_target_pairs={{0,480},{8,488},{16,496},{24,504},{32,0},{40,8},{48,16},{56,24},{6... | collective-permute-start | bytes 786440 | tf_op jit(solution)/shard_map/ppermute | solution.py:79
  98.8 8.4 %collective-permute-start.16 = (bf16[512,4,64]{0,2,1:T(8,128)(2,1)S(1)}, bf16[512,4,64]{0,2,1:T(8,128)(2,1)S(1)}, u32[]{:S(2)}, u32[]{:S(2)}) collective-permute-start(bf16[512,4,64]{0,2,1:T(8,128)(2,1)S(1)} %collective-permute-done.15), channel_id=1, source_target_pairs={{0,32},{8,40},{16,48},{24,56},{32,64},{40,72},{48,80},{56,88},{64,... | collective-permute-start | bytes 786440 | tf_op jit(solution)/shard_map/ppermute | solution.py:79
  101.4 8.4 %collective-permute-start.9 = (bf16[512,4,64]{0,2,1:T(8,128)(2,1)S(1)}, bf16[512,4,64]{0,2,1:T(8,128)(2,1)S(1)}, u32[]{:S(2)}, u32[]{:S(2)}) collective-permute-start(bf16[512,4,64]{0,2,1:T(8,128)(2,1)S(1)} %collective-permute-done.8), channel_id=1, source_target_pairs={{0,480},{8,488},{16,496},{24,504},{32,0},{40,8},{48,16},{56,24},{6... | collective-permute-start | bytes 786440 | tf_op jit(solution)/shard_map/ppermute | solution.py:79
  107.2 9.5 %collective-permute-start.17 = (bf16[512,4,64]{0,2,1:T(8,128)(2,1)S(1)}, bf16[512,4,64]{0,2,1:T(8,128)(2,1)S(1)}, u32[]{:S(2)}, u32[]{:S(2)}) collective-permute-start(bf16[512,4,64]{0,2,1:T(8,128)(2,1)S(1)} %collective-permute-done.16), channel_id=1, source_target_pairs={{0,32},{8,40},{16,48},{24,56},{32,64},{40,72},{48,80},{56,88},{64,... | collective-permute-start | bytes 786440 | tf_op jit(solution)/shard_map/ppermute | solution.py:79
  136.4 29.2 %all-to-all-start.1 = ((bf16[64,4,512]{2,1,0:T(4,128)(2,1)}), bf16[64,4,512]{2,1,0:T(4,128)(2,1)}, u32[]{:S(2)}, u32[]{:S(2)}) async-start(bf16[64,4,512]{2,1,0:T(4,128)(2,1)} %broadcast_select_fusion), calls=%async_computation.1 | async-start | bytes 524288 | tf_op jit(solution)/shard_map/all_to_all | solution.py:166
  170.9 7.5 %copy-start.7 = (s32[64]{0:T(128)S(1)}, s32[64]{0:T(128)}, u32[]{:S(2)}) copy-start(s32[64]{0:T(128)} %param.14) | copy-start | bytes 772
  170.9 7.6 %copy-start.10 = (s32[128]{0:T(128)S(1)}, s32[128]{0:T(128)}, u32[]{:S(2)}) copy-start(s32[128]{0:T(128)} %copy-done.9) | copy-start | bytes 1540
  170.9 7.6 %copy-start.6 = (f32[128]{0:T(128)S(1)}, f32[128]{0:T(128)}, u32[]{:S(2)}) copy-start(f32[128]{0:T(128)} %copy-done.5) | copy-start | bytes 1540
  173.8 26.8 %all-to-all-start.2 = ((bf16[64,5,512]{2,1,0:T(8,128)(2,1)}), bf16[64,5,512]{2,1,0:T(8,128)(2,1)S(1)}, u32[]{:S(2)}, u32[]{:S(2)}) async-start(bf16[64,5,512]{2,1,0:T(8,128)(2,1)} %fusion.21), calls=%async_computation.2 | async-start | bytes 1048576 | tf_op jit(solution)/shard_map/all_to_all | solution.py:184
  178.6 26.8 %copy-start.2 = (bf16[128,4,128]{0,2,1:T(8,128)(2,1)S(1)}, bf16[128,4,128]{0,2,1:T(8,128)(2,1)}, u32[]{:S(2)}) copy-start(bf16[128,4,128]{0,2,1:T(8,128)(2,1)} %copy-done.1) | copy-start | bytes 393220
  213.3 34.6 %all-to-all-start.3 = ((bf16[8,128,512]{2,1,0:T(8,128)(2,1)}), bf16[8,128,512]{2,1,0:T(8,128)(2,1)S(1)}, u32[]{:S(2)}, u32[]{:S(2)}) async-start(bf16[8,128,512]{2,1,0:T(8,128)(2,1)} %bitcast.209), calls=%async_computation.3 | async-start | bytes 2097152 | tf_op jit(solution)/shard_map/all_to_all | solution.py:223
  (2 other events, 8.2 us)
Sparse Core Ops, SparseCore 0:
  30.7 150.9 all-gather.1

commit v12 on v11

--- a/solution.py
+++ b/solution.py
@@ -78,9 +78,9 @@
             pairs.append((i, ((z + dz) % z_count) * Y_CHIPS + (y + dy) % Y_CHIPS))
         return lax.ppermute(value, axis_name, pairs)
 
-    along_y = jnp.stack(ring(block, Y_CHIPS, lambda v, d: shift(v, 0, d)), axis=1)
-    along_z = jnp.stack(ring(along_y, z_count, lambda v, d: shift(v, d, 0)), axis=1)
-    return along_z.reshape(block.shape[0], -1), here // Y_CHIPS, here % Y_CHIPS
+    along_y = jnp.stack(ring(block, Y_CHIPS, lambda v, d: shift(v, 0, d)), axis=0)
+    along_z = jnp.stack(ring(along_y, z_count, lambda v, d: shift(v, d, 0)), axis=0)
+    return along_z.reshape(-1, block.shape[1]), here // Y_CHIPS, here % Y_CHIPS
 
 
 def shards(
@@ -117,17 +117,12 @@
     kv_width = kv_local * 2 * head_size
     kv_piece = lax.dynamic_slice_in_dim(key_value_weight, kv_start * 2 * head_size, kv_width, 1)
     side = lax.all_gather(jnp.concatenate([kv_piece.T, w_out], axis=0), "seq", axis=1, tiled=True)
-    wq_rows, z_at, y_at = ring_gather(w_query.T, "seq", seq_count)
+    wq_full, z_at, y_at = ring_gather(w_query, "seq", seq_count)
     z_count = seq_count // Y_CHIPS
     rel_input = normalized_input.reshape(length, z_count, Y_CHIPS, -1)
     rel_input = jnp.roll(jnp.roll(rel_input, -z_at, axis=1), -y_at, axis=2).reshape(length, -1)
 
-    def contract(rows):
-        return lax.dot_general(
-            rel_input, rows, (((1,), (1,)), ((), ())), preferred_element_type=jnp.float32
-        )
-
-    query_vectors = contract(wq_rows)
+    query_vectors = jnp.dot(rel_input, wq_full, preferred_element_type=jnp.float32)
     key_value_pair = lax.dot_general(
         normalized_input, side, (((1,), (1,)), ((), ())), preferred_element_type=jnp.float32
     )[:, :kv_width]

time: 257 us -> 256 us (level)
    dot_general x1 -> x0, local copies, waits for them, and re-layouts: 6.93 us -> none  [contract(): lax.dot_general(rel_input, rows, (((1,), (1,)), ((), ())), preferred_elem...]
    reshape x1 -> x2, local copies, waits for them, and re-layouts: 0.75 us -> 7.19 us  [the longest x1 6.44 us: ring_gather(): along_z.reshape(-1, block.shape[1])]
where the time goes in v12:
time: 256 us; the launch traced here: 255 us
  starting transfers between devices  103 us (40%)
  waiting for transfers between devices  76.1 us (30%)
  local copies, waits for them, and re-layouts  32.1 us (13%)
  matrix products  15.1 us (6%)
  between operations  14.9 us (6%)
  other arithmetic  13.6 us (5%)
    ppermute x18, starting transfers between devices, shift(): return lax.ppermute(value, axis_name, pairs)  59.1 us
    ppermute x18, waiting for transfers between devices, shift(): return lax.ppermute(value, axis_name, pairs)  23.8 us
    all_to_all x1, waiting for transfers between devices, shards(): lax.all_to_all(jnp.concatenate([out_block, log_row], axis=1), 'seq', spli...  21.7 us
    all_to_all x1, starting transfers between devices, shards(): lax.all_to_all(jnp.moveaxis(pieces, 1, 0), 'tensor', split_axis=0, concat...  19.1 us
    all_to_all x1, waiting for transfers between devices, shards(): lax.all_to_all(outgoing, 'seq', split_axis=0, concat_axis=0, tiled=True)  16.3 us
    unnamed x39, local copies, waits for them, and re-layouts  15.5 us
    all_to_all x1, waiting for transfers between devices, shards(): lax.all_to_all(jnp.moveaxis(pieces, 1, 0), 'tensor', split_axis=0, concat...  14.2 us
    all_to_all x1, starting transfers between devices, shards(): lax.all_to_all(tiles, 'tensor', split_axis=0, concat_axis=0, tiled=True)  10 us
  transfers between devices with their start and end apart: 23, of which 12 were waited for; matrix products, arithmetic and copies ran while one was open for 19% of the time, Pallas kernels for 0%

profile of v12, /device:TPU:1, one launch (start us, length us, event | category | flops | bytes accessed | tf_op | source)
XLA Modules:
  0.0 254.7 jit_solution(11174975586782958230)
XLA Ops:
  7.2 4.2 %collective-permute-start.1 = (bf16[64,512]{1,0:T(8,128)(2,1)}, bf16[64,512]{1,0:T(8,128)(2,1)S(1)}, u32[]{:S(2)}, u32[]{:S(2)}) collective-permute-start(bf16[64,512]{1,0:T(8,128)(2,1)} %param.10), channel_id=1, source_target_pairs={{0,8},{8,16},{16,24},{24,0},{32,40},{40,48},{48,56},{56,32},{64,72... | collective-permute-start | bytes 196616 | tf_op jit(solution)/shard_map/ppermute | solution.py:79
  11.4 3.4 %collective-permute-start = (bf16[64,512]{1,0:T(8,128)(2,1)}, bf16[64,512]{1,0:T(8,128)(2,1)S(1)}, u32[]{:S(2)}, u32[]{:S(2)}) collective-permute-start(bf16[64,512]{1,0:T(8,128)(2,1)} %param.10), channel_id=1, source_target_pairs={{0,24},{8,0},{16,8},{24,16},{32,56},{40,32},{48,40},{56,48},{64,88... | collective-permute-start | bytes 196616 | tf_op jit(solution)/shard_map/ppermute | solution.py:79
  16.9 10.0 %all-to-all-start = ((bf16[8,128,512]{1,2,0:T(8,128)(2,1)}), bf16[8,128,512]{1,2,0:T(8,128)(2,1)S(1)}, u32[]{:S(2)}, u32[]{:S(2)}) async-start(bf16[8,128,512]{1,2,0:T(8,128)(2,1)} %broadcast_in_dim.72), calls=%async_computation | async-start | bytes 2097152 | tf_op jit(solution)/shard_map/all_to_all | solution.py:102
  31.5 1.9 collective-permute-start.2
  33.5 4.7 %collective-permute-done.2 = bf16[64,512]{1,0:T(8,128)(2,1)S(1)} collective-permute-done((bf16[64,512]{1,0:T(8,128)(2,1)S(1)}, bf16[64,512]{1,0:T(8,128)(2,1)S(1)}, u32[]{:S(2)}, u32[]{:S(2)}) %collective-permute-start.2) | collective-permute-done | bytes 65568 | tf_op jit(solution)/shard_map/ppermute | solution.py:79
  39.0 1.9 collective-permute-start.10
  41.2 6.7 %collective-permute-start.3 = (bf16[4,64,512]{2,1,0:T(8,128)(2,1)S(1)}, bf16[4,64,512]{2,1,0:T(8,128)(2,1)S(1)}, u32[]{:S(2)}, u32[]{:S(2)}) collective-permute-start(bf16[4,64,512]{2,1,0:T(8,128)(2,1)S(1)} %pad_maximum_fusion), channel_id=1, source_target_pairs={{0,480},{8,488},{16,496},{24,504},{32,0},{40,8},{48,16},{56,24},{6... | collective-permute-start | bytes 786440 | tf_op jit(solution)/shard_map/ppermute | solution.py:79
  47.9 4.3 %collective-permute-done.10 = bf16[4,64,512]{2,1,0:T(8,128)(2,1)S(1)} collective-permute-done((bf16[4,64,512]{2,1,0:T(8,128)(2,1)S(1)}, bf16[4,64,512]{2,1,0:T(8,128)(2,1)S(1)}, u32[]{:S(2)}, u32[]{:S(2)}) %collective-permute-start.10) | collective-permute-done | bytes 262176 | tf_op jit(solution)/shard_map/ppermute | solution.py:79
  52.2 1.9 collective-permute-start.11
  54.5 4.6 %collective-permute-start.4 = (bf16[4,64,512]{2,1,0:T(8,128)(2,1)S(1)}, bf16[4,64,512]{2,1,0:T(8,128)(2,1)S(1)}, u32[]{:S(2)}, u32[]{:S(2)}) collective-permute-start(bf16[4,64,512]{2,1,0:T(8,128)(2,1)S(1)} %collective-permute-done.3), channel_id=1, source_target_pairs={{0,480},{8,488},{16,496},{24,504},{32,0},{40,8},{48,16},{56,24},{6... | collective-permute-start | bytes 786440 | tf_op jit(solution)/shard_map/ppermute | solution.py:79
  59.8 2.8 %collective-permute-done.11 = bf16[4,64,512]{2,1,0:T(8,128)(2,1)S(1)} collective-permute-done((bf16[4,64,512]{2,1,0:T(8,128)(2,1)S(1)}, bf16[4,64,512]{2,1,0:T(8,128)(2,1)S(1)}, u32[]{:S(2)}, u32[]{:S(2)}) %collective-permute-start.11) | collective-permute-done | bytes 262176 | tf_op jit(solution)/shard_map/ppermute | solution.py:79
  62.6 1.9 collective-permute-start.12
  65.3 4.6 %collective-permute-start.5 = (bf16[4,64,512]{2,1,0:T(8,128)(2,1)S(1)}, bf16[4,64,512]{2,1,0:T(8,128)(2,1)S(1)}, u32[]{:S(2)}, u32[]{:S(2)}) collective-permute-start(bf16[4,64,512]{2,1,0:T(8,128)(2,1)S(1)} %collective-permute-done.4), channel_id=1, source_target_pairs={{0,480},{8,488},{16,496},{24,504},{32,0},{40,8},{48,16},{56,24},{6... | collective-permute-start | bytes 786440 | tf_op jit(solution)/shard_map/ppermute | solution.py:79
  72.1 1.9 collective-permute-start.13
  74.8 4.6 %collective-permute-start.6 = (bf16[4,64,512]{2,1,0:T(8,128)(2,1)S(1)}, bf16[4,64,512]{2,1,0:T(8,128)(2,1)S(1)}, u32[]{:S(2)}, u32[]{:S(2)}) collective-permute-start(bf16[4,64,512]{2,1,0:T(8,128)(2,1)S(1)} %collective-permute-done.5), channel_id=1, source_target_pairs={{0,480},{8,488},{16,496},{24,504},{32,0},{40,8},{48,16},{56,24},{6... | collective-permute-start | bytes 786440 | tf_op jit(solution)/shard_map/ppermute | solution.py:79
  79.4 1.9 collective-permute-done.13
  83.9 4.6 %collective-permute-start.7 = (bf16[4,64,512]{2,1,0:T(8,128)(2,1)S(1)}, bf16[4,64,512]{2,1,0:T(8,128)(2,1)S(1)}, u32[]{:S(2)}, u32[]{:S(2)}) collective-permute-start(bf16[4,64,512]{2,1,0:T(8,128)(2,1)S(1)} %collective-permute-done.6), channel_id=1, source_target_pairs={{0,480},{8,488},{16,496},{24,504},{32,0},{40,8},{48,16},{56,24},{6... | collective-permute-start | bytes 786440 | tf_op jit(solution)/shard_map/ppermute | solution.py:79
  92.5 4.9 %collective-permute-start.8 = (bf16[4,64,512]{2,1,0:T(8,128)(2,1)S(1)}, bf16[4,64,512]{2,1,0:T(8,128)(2,1)S(1)}, u32[]{:S(2)}, u32[]{:S(2)}) collective-permute-start(bf16[4,64,512]{2,1,0:T(8,128)(2,1)S(1)} %collective-permute-done.7), channel_id=1, source_target_pairs={{0,480},{8,488},{16,496},{24,504},{32,0},{40,8},{48,16},{56,24},{6... | collective-permute-start | bytes 786440 | tf_op jit(solution)/shard_map/ppermute | solution.py:79
  98.8 1.9 collective-permute-start.16
  101.4 4.6 %collective-permute-start.9 = (bf16[4,64,512]{2,1,0:T(8,128)(2,1)S(1)}, bf16[4,64,512]{2,1,0:T(8,128)(2,1)S(1)}, u32[]{:S(2)}, u32[]{:S(2)}) collective-permute-start(bf16[4,64,512]{2,1,0:T(8,128)(2,1)S(1)} %collective-permute-done.8), channel_id=1, source_target_pairs={{0,480},{8,488},{16,496},{24,504},{32,0},{40,8},{48,16},{56,24},{6... | collective-permute-start | bytes 786440 | tf_op jit(solution)/shard_map/ppermute | solution.py:79
  110.5 6.1 %collective-permute-done.17 = bf16[4,64,512]{2,1,0:T(8,128)(2,1)S(1)} collective-permute-done((bf16[4,64,512]{2,1,0:T(8,128)(2,1)S(1)}, bf16[4,64,512]{2,1,0:T(8,128)(2,1)S(1)}, u32[]{:S(2)}, u32[]{:S(2)}) %collective-permute-start.17) | collective-permute-done | bytes 262176 | tf_op jit(solution)/shard_map/ppermute | solution.py:79
  122.5 6.4 %copy.113 = bf16[4096,512]{0,1:T(8,128)(2,1)} copy(bf16[4096,512]{1,0:T(8,128)(2,1)} %bitcast.25) | data formatting | bytes 8388608 | tf_op jit(solution)/shard_map/reshape | solution.py:83
  128.9 3.5 %fusion.80 = f32[128,4,128]{0,2,1:T(8,128)S(1)} fusion(bf16[128,4096,1]{0,1,2:T(8,128)(2,1)S(1)} %bitcast.220, bf16[4,128,4096]{2,1,0:T(8,128)(2,1)} %bitcast.209), kind=kOutput, calls=%fused_computation.197 | convolution fusion | flops 536870912 | bytes 5505024 | tf_op jit(solution)/shard_map/dot_general | solution.py:125
  135.4 9.9 %all-to-all-start.1 = ((bf16[64,4,512]{2,1,0:T(4,128)(2,1)}), bf16[64,4,512]{2,1,0:T(4,128)(2,1)}, u32[]{:S(2)}, u32[]{:S(2)}) async-start(bf16[64,4,512]{2,1,0:T(4,128)(2,1)} %broadcast_select_fusion), calls=%async_computation.1 | async-start | bytes 524288 | tf_op jit(solution)/shard_map/all_to_all | solution.py:161
  145.3 2.9 %copy.117 = bf16[1,1024,1024]{1,2,0:T(8,128)(2,1)S(1)} copy(bf16[1,1024,1024]{2,1,0:T(8,128)(2,1)} %param.13) | data formatting | bytes 4194304 | tf_op args[5]
  148.1 16.3 %all-to-all-done.1 = bf16[64,4,512]{2,1,0:T(4,128)(2,1)} async-done(((bf16[64,4,512]{2,1,0:T(4,128)(2,1)}), bf16[64,4,512]{2,1,0:T(4,128)(2,1)}, u32[]{:S(2)}, u32[]{:S(2)}) %all-to-all-start.1) | async-done | bytes 262176 | tf_op jit(solution)/shard_map/all_to_all | solution.py:161
  172.6 4.9 %all-to-all-start.2 = ((bf16[64,5,512]{2,1,0:T(8,128)(2,1)}), bf16[64,5,512]{2,1,0:T(8,128)(2,1)S(1)}, u32[]{:S(2)}, u32[]{:S(2)}) async-start(bf16[64,5,512]{2,1,0:T(8,128)(2,1)} %fusion.19), calls=%async_computation.2 | async-start | bytes 1048576 | tf_op jit(solution)/shard_map/all_to_all | solution.py:179
  178.4 21.7 %all-to-all-done.2 = bf16[64,5,512]{2,1,0:T(8,128)(2,1)S(1)} async-done(((bf16[64,5,512]{2,1,0:T(8,128)(2,1)}), bf16[64,5,512]{2,1,0:T(8,128)(2,1)S(1)}, u32[]{:S(2)}, u32[]{:S(2)}) %all-to-all-start.2) | async-done | bytes 327712 | tf_op jit(solution)/shard_map/all_to_all | solution.py:179
  202.2 2.1 fusion
  206.8 5.0 %convolution_convert_fusion = bf16[128,4096]{1,0:T(8,128)(2,1)S(1)} fusion(bf16[768,4096]{0,1:T(8,128)(2,1)} %all-gather.2.cloned.1.call-done, bf16[128,512]{0,1:T(8,128)(2,1)S(1)} %bitcast.222), kind=kOutput, calls=%fused_computation.3 | convolution fusion | flops 805830656 | bytes 7471104 | tf_op jit(solution)/shard_map/dot_general | solution.py:215
  212.8 19.1 %all-to-all-start.3 = ((bf16[8,128,512]{2,1,0:T(8,128)(2,1)}), bf16[8,128,512]{2,1,0:T(8,128)(2,1)S(1)}, u32[]{:S(2)}, u32[]{:S(2)}) async-start(bf16[8,128,512]{2,1,0:T(8,128)(2,1)} %bitcast.208), calls=%async_computation.3 | async-start | bytes 2097152 | tf_op jit(solution)/shard_map/all_to_all | solution.py:218
  232.9 14.2 %all-to-all-done.3 = bf16[8,128,512]{2,1,0:T(8,128)(2,1)S(1)} async-done(((bf16[8,128,512]{2,1,0:T(8,128)(2,1)}), bf16[8,128,512]{2,1,0:T(8,128)(2,1)S(1)}, u32[]{:S(2)}, u32[]{:S(2)}) %all-to-all-start.3) | async-done | bytes 1048608 | tf_op jit(solution)/shard_map/all_to_all | solution.py:218
  (160 shorter events, 50.6 us)
Async XLA Ops:
  7.2 19.7 %copy-start = (bf16[64,1024]{1,0:T(8,128)(2,1)S(1)}, bf16[64,1024]{1,0:T(8,128)(2,1)}, u32[]{:S(2)}) copy-start(bf16[64,1024]{1,0:T(8,128)(2,1)} %param.11) | copy-start | bytes 393220
  7.2 51.9 %copy-start.3 = (bf16[64,512]{1,0:T(8,128)(2,1)S(1)}, bf16[64,512]{1,0:T(8,128)(2,1)}, u32[]{:S(2)}) copy-start(bf16[64,512]{1,0:T(8,128)(2,1)} %param.10) | copy-start | bytes 196612
  7.2 47.0 %copy-start.4 = (bf16[4096]{0:T(1024)(128)(2,1)S(1)}, bf16[4096]{0:T(1024)(128)(2,1)}, u32[]{:S(2)}) copy-start(bf16[4096]{0:T(1024)(128)(2,1)} %param.9) | copy-start | bytes 24580
  7.2 24.3 %collective-permute-start.1 = (bf16[64,512]{1,0:T(8,128)(2,1)}, bf16[64,512]{1,0:T(8,128)(2,1)S(1)}, u32[]{:S(2)}, u32[]{:S(2)}) collective-permute-start(bf16[64,512]{1,0:T(8,128)(2,1)} %param.10), channel_id=1, source_target_pairs={{0,8},{8,16},{16,24},{24,0},{32,40},{40,48},{48,56},{56,32},{64,72... | collective-permute-start | bytes 196616 | tf_op jit(solution)/shard_map/ppermute | solution.py:79
  11.4 22.1 %collective-permute-start = (bf16[64,512]{1,0:T(8,128)(2,1)}, bf16[64,512]{1,0:T(8,128)(2,1)S(1)}, u32[]{:S(2)}, u32[]{:S(2)}) collective-permute-start(bf16[64,512]{1,0:T(8,128)(2,1)} %param.10), channel_id=1, source_target_pairs={{0,24},{8,0},{16,8},{24,16},{32,56},{40,32},{48,40},{56,48},{64,88... | collective-permute-start | bytes 196616 | tf_op jit(solution)/shard_map/ppermute | solution.py:79
  16.9 57.1 %all-to-all-start = ((bf16[8,128,512]{1,2,0:T(8,128)(2,1)}), bf16[8,128,512]{1,2,0:T(8,128)(2,1)S(1)}, u32[]{:S(2)}, u32[]{:S(2)}) async-start(bf16[8,128,512]{1,2,0:T(8,128)(2,1)} %broadcast_in_dim.72), calls=%async_computation | async-start | bytes 2097152 | tf_op jit(solution)/shard_map/all_to_all | solution.py:102
  26.9 175.3 %all-gather.2.cloned.1.call-start = ((), (), s32[]{:S(2)}) async-start(), calls=%async_computation.4 | async-start | bytes 6389760 | tf_op jit(solution)/shard_map/all_gather | solution.py:119
  31.5 22.7 %copy-start.9 = (s32[128]{0:T(128)}, s32[128]{0:T(128)S(1)}, u32[]{:S(2)}) copy-start(s32[128]{0:T(128)S(1)} %get-tuple-element.11) | copy-start | bytes 1540
  31.5 6.6 %collective-permute-start.2 = (bf16[64,512]{1,0:T(8,128)(2,1)S(1)}, bf16[64,512]{1,0:T(8,128)(2,1)S(1)}, u32[]{:S(2)}, u32[]{:S(2)}) collective-permute-start(bf16[64,512]{1,0:T(8,128)(2,1)S(1)} %collective-permute-done.1), channel_id=1, source_target_pairs={{0,8},{8,16},{16,24},{24,0},{32,40},{40,48},{48,56},{56,32},{64,72... | collective-permute-start | bytes 196616 | tf_op jit(solution)/shard_map/ppermute | solution.py:79
  39.0 13.1 %collective-permute-start.10 = (bf16[4,64,512]{2,1,0:T(8,128)(2,1)S(1)}, bf16[4,64,512]{2,1,0:T(8,128)(2,1)S(1)}, u32[]{:S(2)}, u32[]{:S(2)}) collective-permute-start(bf16[4,64,512]{2,1,0:T(8,128)(2,1)S(1)} %pad_maximum_fusion), channel_id=1, source_target_pairs={{0,32},{8,40},{16,48},{24,56},{32,64},{40,72},{48,80},{56,88},{64,... | collective-permute-start | bytes 786440 | tf_op jit(solution)/shard_map/ppermute | solution.py:79
  41.2 13.3 %collective-permute-start.3 = (bf16[4,64,512]{2,1,0:T(8,128)(2,1)S(1)}, bf16[4,64,512]{2,1,0:T(8,128)(2,1)S(1)}, u32[]{:S(2)}, u32[]{:S(2)}) collective-permute-start(bf16[4,64,512]{2,1,0:T(8,128)(2,1)S(1)} %pad_maximum_fusion), channel_id=1, source_target_pairs={{0,480},{8,488},{16,496},{24,504},{32,0},{40,8},{48,16},{56,24},{6... | collective-permute-start | bytes 786440 | tf_op jit(solution)/shard_map/ppermute | solution.py:79
  52.2 10.5 %collective-permute-start.11 = (bf16[4,64,512]{2,1,0:T(8,128)(2,1)S(1)}, bf16[4,64,512]{2,1,0:T(8,128)(2,1)S(1)}, u32[]{:S(2)}, u32[]{:S(2)}) collective-permute-start(bf16[4,64,512]{2,1,0:T(8,128)(2,1)S(1)} %collective-permute-done.10), channel_id=1, source_target_pairs={{0,32},{8,40},{16,48},{24,56},{32,64},{40,72},{48,80},{56,88},{64,... | collective-permute-start | bytes 786440 | tf_op jit(solution)/shard_map/ppermute | solution.py:79
  54.5 10.8 %collective-permute-start.4 = (bf16[4,64,512]{2,1,0:T(8,128)(2,1)S(1)}, bf16[4,64,512]{2,1,0:T(8,128)(2,1)S(1)}, u32[]{:S(2)}, u32[]{:S(2)}) collective-permute-start(bf16[4,64,512]{2,1,0:T(8,128)(2,1)S(1)} %collective-permute-done.3), channel_id=1, source_target_pairs={{0,480},{8,488},{16,496},{24,504},{32,0},{40,8},{48,16},{56,24},{6... | collective-permute-start | bytes 786440 | tf_op jit(solution)/shard_map/ppermute | solution.py:79
  62.6 9.5 %collective-permute-start.12 = (bf16[4,64,512]{2,1,0:T(8,128)(2,1)S(1)}, bf16[4,64,512]{2,1,0:T(8,128)(2,1)S(1)}, u32[]{:S(2)}, u32[]{:S(2)}) collective-permute-start(bf16[4,64,512]{2,1,0:T(8,128)(2,1)S(1)} %collective-permute-done.11), channel_id=1, source_target_pairs={{0,32},{8,40},{16,48},{24,56},{32,64},{40,72},{48,80},{56,88},{64,... | collective-permute-start | bytes 786440 | tf_op jit(solution)/shard_map/ppermute | solution.py:79
  65.3 9.5 %collective-permute-start.5 = (bf16[4,64,512]{2,1,0:T(8,128)(2,1)S(1)}, bf16[4,64,512]{2,1,0:T(8,128)(2,1)S(1)}, u32[]{:S(2)}, u32[]{:S(2)}) collective-permute-start(bf16[4,64,512]{2,1,0:T(8,128)(2,1)S(1)} %collective-permute-done.4), channel_id=1, source_target_pairs={{0,480},{8,488},{16,496},{24,504},{32,0},{40,8},{48,16},{56,24},{6... | collective-permute-start | bytes 786440 | tf_op jit(solution)/shard_map/ppermute | solution.py:79
  72.1 9.2 %collective-permute-start.13 = (bf16[4,64,512]{2,1,0:T(8,128)(2,1)S(1)}, bf16[4,64,512]{2,1,0:T(8,128)(2,1)S(1)}, u32[]{:S(2)}, u32[]{:S(2)}) collective-permute-start(bf16[4,64,512]{2,1,0:T(8,128)(2,1)S(1)} %collective-permute-done.12), channel_id=1, source_target_pairs={{0,32},{8,40},{16,48},{24,56},{32,64},{40,72},{48,80},{56,88},{64,... | collective-permute-start | bytes 786440 | tf_op jit(solution)/shard_map/ppermute | solution.py:79
  74.8 9.2 %collective-permute-start.6 = (bf16[4,64,512]{2,1,0:T(8,128)(2,1)S(1)}, bf16[4,64,512]{2,1,0:T(8,128)(2,1)S(1)}, u32[]{:S(2)}, u32[]{:S(2)}) collective-permute-start(bf16[4,64,512]{2,1,0:T(8,128)(2,1)S(1)} %collective-permute-done.5), channel_id=1, source_target_pairs={{0,480},{8,488},{16,496},{24,504},{32,0},{40,8},{48,16},{56,24},{6... | collective-permute-start | bytes 786440 | tf_op jit(solution)/shard_map/ppermute | solution.py:79
  79.3 22.1 %copy-start.5 = (f32[128]{0:T(128)}, f32[128]{0:T(128)S(1)}, u32[]{:S(2)}) copy-start(f32[128]{0:T(128)S(1)} %add_rsqrt_fusion) | copy-start | bytes 1540
  81.3 8.9 %collective-permute-start.14 = (bf16[4,64,512]{2,1,0:T(8,128)(2,1)S(1)}, bf16[4,64,512]{2,1,0:T(8,128)(2,1)S(1)}, u32[]{:S(2)}, u32[]{:S(2)}) collective-permute-start(bf16[4,64,512]{2,1,0:T(8,128)(2,1)S(1)} %collective-permute-done.13), channel_id=1, source_target_pairs={{0,32},{8,40},{16,48},{24,56},{32,64},{40,72},{48,80},{56,88},{64,... | collective-permute-start | bytes 786440 | tf_op jit(solution)/shard_map/ppermute | solution.py:79
  83.9 8.6 %collective-permute-start.7 = (bf16[4,64,512]{2,1,0:T(8,128)(2,1)S(1)}, bf16[4,64,512]{2,1,0:T(8,128)(2,1)S(1)}, u32[]{:S(2)}, u32[]{:S(2)}) collective-permute-start(bf16[4,64,512]{2,1,0:T(8,128)(2,1)S(1)} %collective-permute-done.6), channel_id=1, source_target_pairs={{0,480},{8,488},{16,496},{24,504},{32,0},{40,8},{48,16},{56,24},{6... | collective-permute-start | bytes 786440 | tf_op jit(solution)/shard_map/ppermute | solution.py:79
  90.2 8.6 %collective-permute-start.15 = (bf16[4,64,512]{2,1,0:T(8,128)(2,1)S(1)}, bf16[4,64,512]{2,1,0:T(8,128)(2,1)S(1)}, u32[]{:S(2)}, u32[]{:S(2)}) collective-permute-start(bf16[4,64,512]{2,1,0:T(8,128)(2,1)S(1)} %collective-permute-done.14), channel_id=1, source_target_pairs={{0,32},{8,40},{16,48},{24,56},{32,64},{40,72},{48,80},{56,88},{64,... | collective-permute-start | bytes 786440 | tf_op jit(solution)/shard_map/ppermute | solution.py:79
  92.5 8.9 %collective-permute-start.8 = (bf16[4,64,512]{2,1,0:T(8,128)(2,1)S(1)}, bf16[4,64,512]{2,1,0:T(8,128)(2,1)S(1)}, u32[]{:S(2)}, u32[]{:S(2)}) collective-permute-start(bf16[4,64,512]{2,1,0:T(8,128)(2,1)S(1)} %collective-permute-done.7), channel_id=1, source_target_pairs={{0,480},{8,488},{16,496},{24,504},{32,0},{40,8},{48,16},{56,24},{6... | collective-permute-start | bytes 786440 | tf_op jit(solution)/shard_map/ppermute | solution.py:79
  98.8 8.4 %collective-permute-start.16 = (bf16[4,64,512]{2,1,0:T(8,128)(2,1)S(1)}, bf16[4,64,512]{2,1,0:T(8,128)(2,1)S(1)}, u32[]{:S(2)}, u32[]{:S(2)}) collective-permute-start(bf16[4,64,512]{2,1,0:T(8,128)(2,1)S(1)} %collective-permute-done.15), channel_id=1, source_target_pairs={{0,32},{8,40},{16,48},{24,56},{32,64},{40,72},{48,80},{56,88},{64,... | collective-permute-start | bytes 786440 | tf_op jit(solution)/shard_map/ppermute | solution.py:79
  101.4 8.4 %collective-permute-start.9 = (bf16[4,64,512]{2,1,0:T(8,128)(2,1)S(1)}, bf16[4,64,512]{2,1,0:T(8,128)(2,1)S(1)}, u32[]{:S(2)}, u32[]{:S(2)}) collective-permute-start(bf16[4,64,512]{2,1,0:T(8,128)(2,1)S(1)} %collective-permute-done.8), channel_id=1, source_target_pairs={{0,480},{8,488},{16,496},{24,504},{32,0},{40,8},{48,16},{56,24},{6... | collective-permute-start | bytes 786440 | tf_op jit(solution)/shard_map/ppermute | solution.py:79
  107.2 9.5 %collective-permute-start.17 = (bf16[4,64,512]{2,1,0:T(8,128)(2,1)S(1)}, bf16[4,64,512]{2,1,0:T(8,128)(2,1)S(1)}, u32[]{:S(2)}, u32[]{:S(2)}) collective-permute-start(bf16[4,64,512]{2,1,0:T(8,128)(2,1)S(1)} %collective-permute-done.16), channel_id=1, source_target_pairs={{0,32},{8,40},{16,48},{24,56},{32,64},{40,72},{48,80},{56,88},{64,... | collective-permute-start | bytes 786440 | tf_op jit(solution)/shard_map/ppermute | solution.py:79
  135.4 29.1 %all-to-all-start.1 = ((bf16[64,4,512]{2,1,0:T(4,128)(2,1)}), bf16[64,4,512]{2,1,0:T(4,128)(2,1)}, u32[]{:S(2)}, u32[]{:S(2)}) async-start(bf16[64,4,512]{2,1,0:T(4,128)(2,1)} %broadcast_select_fusion), calls=%async_computation.1 | async-start | bytes 524288 | tf_op jit(solution)/shard_map/all_to_all | solution.py:161
  169.7 7.8 %copy-start.7 = (s32[64]{0:T(128)S(1)}, s32[64]{0:T(128)}, u32[]{:S(2)}) copy-start(s32[64]{0:T(128)} %param.14) | copy-start | bytes 772
  169.8 7.9 %copy-start.10 = (s32[128]{0:T(128)S(1)}, s32[128]{0:T(128)}, u32[]{:S(2)}) copy-start(s32[128]{0:T(128)} %copy-done.9) | copy-start | bytes 1540
  169.8 7.9 %copy-start.6 = (f32[128]{0:T(128)S(1)}, f32[128]{0:T(128)}, u32[]{:S(2)}) copy-start(f32[128]{0:T(128)} %copy-done.5) | copy-start | bytes 1540
  172.6 27.5 %all-to-all-start.2 = ((bf16[64,5,512]{2,1,0:T(8,128)(2,1)}), bf16[64,5,512]{2,1,0:T(8,128)(2,1)S(1)}, u32[]{:S(2)}, u32[]{:S(2)}) async-start(bf16[64,5,512]{2,1,0:T(8,128)(2,1)} %fusion.19), calls=%async_computation.2 | async-start | bytes 1048576 | tf_op jit(solution)/shard_map/all_to_all | solution.py:179
  177.7 27.2 %copy-start.2 = (bf16[128,4,128]{0,2,1:T(8,128)(2,1)S(1)}, bf16[128,4,128]{0,2,1:T(8,128)(2,1)}, u32[]{:S(2)}) copy-start(bf16[128,4,128]{0,2,1:T(8,128)(2,1)} %copy-done.1) | copy-start | bytes 393220
  212.8 34.2 %all-to-all-start.3 = ((bf16[8,128,512]{2,1,0:T(8,128)(2,1)}), bf16[8,128,512]{2,1,0:T(8,128)(2,1)S(1)}, u32[]{:S(2)}, u32[]{:S(2)}) async-start(bf16[8,128,512]{2,1,0:T(8,128)(2,1)} %bitcast.208), calls=%async_computation.3 | async-start | bytes 2097152 | tf_op jit(solution)/shard_map/all_to_all | solution.py:218
  (2 other events, 8.4 us)
Sparse Core Ops, SparseCore 0:
  30.7 150.6 all-gather.1

commit v13 on v12

--- a/solution.py
+++ b/solution.py
@@ -79,8 +79,8 @@
         return lax.ppermute(value, axis_name, pairs)
 
     along_y = jnp.stack(ring(block, Y_CHIPS, lambda v, d: shift(v, 0, d)), axis=0)
-    along_z = jnp.stack(ring(along_y, z_count, lambda v, d: shift(v, d, 0)), axis=0)
-    return along_z.reshape(-1, block.shape[1]), here // Y_CHIPS, here % Y_CHIPS
+    along_z = ring(along_y, z_count, lambda v, d: shift(v, d, 0))
+    return [b.reshape(-1, block.shape[1]) for b in along_z], here // Y_CHIPS, here % Y_CHIPS
 
 
 def shards(
@@ -117,12 +117,17 @@
     kv_width = kv_local * 2 * head_size
     kv_piece = lax.dynamic_slice_in_dim(key_value_weight, kv_start * 2 * head_size, kv_width, 1)
     side = lax.all_gather(jnp.concatenate([kv_piece.T, w_out], axis=0), "seq", axis=1, tiled=True)
-    wq_full, z_at, y_at = ring_gather(w_query, "seq", seq_count)
+    wq_blocks, z_at, y_at = ring_gather(w_query, "seq", seq_count)
     z_count = seq_count // Y_CHIPS
     rel_input = normalized_input.reshape(length, z_count, Y_CHIPS, -1)
     rel_input = jnp.roll(jnp.roll(rel_input, -z_at, axis=1), -y_at, axis=2).reshape(length, -1)
 
-    query_vectors = jnp.dot(rel_input, wq_full, preferred_element_type=jnp.float32)
+    rel_groups = rel_input.reshape(length, z_count, -1)
+    query_vectors = jnp.dot(rel_groups[:, 0], wq_blocks[0], preferred_element_type=jnp.float32)
+    for group in range(1, z_count):
+        query_vectors = query_vectors + jnp.dot(
+            rel_groups[:, group], wq_blocks[group], preferred_element_type=jnp.float32
+        )
     key_value_pair = lax.dot_general(
         normalized_input, side, (((1,), (1,)), ((), ())), preferred_element_type=jnp.float32
     )[:, :kv_width]

time: 256 us -> 245 us (0.957)
  local copies, waits for them, and re-layouts: 32.1 us -> 14.3 us
  waiting for transfers between devices: 76.1 us -> 93 us
  starting transfers between devices: 103 us -> 96.4 us
  other arithmetic: 13.6 us -> 10.1 us
    unnamed x39 -> x31, local copies, waits for them, and re-layouts: 15.5 us -> 5.34 us
    all_to_all x1, starting transfers between devices: 19.1 us -> 12 us  [shards(): lax.all_to_all(jnp.moveaxis(pieces, 1, 0), 'tensor', split_axis=0, concat...]
    reshape x2, local copies, waits for them, and re-layouts: 7.19 us -> 0.19 us  [the longest x1 6.44 us: ring_gather(): along_z.reshape(-1, block.shape[1])]
    all_to_all x1, waiting for transfers between devices: 21.7 us -> 28.5 us  [shards(): lax.all_to_all(jnp.concatenate([out_block, log_row], axis=1), 'seq', spli...]
    all_gather x1, waiting for transfers between devices: 0.02 us -> 5.72 us  [shards(): lax.all_gather(jnp.concatenate([kv_piece.T, w_out], axis=0), 'seq', axis=...]
    ppermute x18, waiting for transfers between devices: 23.8 us -> 27.8 us  [shift(): return lax.ppermute(value, axis_name, pairs)]
  transfers between devices with their start and end apart: 23 -> 23, of which waited for: 12 -> 15; matrix products, arithmetic and copies ran while one was open for 19% -> 11% of each run, Pallas kernels for 0% -> 0%
where the time goes in v13:
time: 245 us; the launch traced here: 244 us
  starting transfers between devices  96.4 us (39%)
  waiting for transfers between devices  93 us (38%)
  matrix products  15 us (6%)
  between operations  15 us (6%)
  local copies, waits for them, and re-layouts  14.3 us (6%)
  other arithmetic  10.1 us (4%)
    ppermute x18, starting transfers between devices, shift(): return lax.ppermute(value, axis_name, pairs)  61.6 us
    all_to_all x1, waiting for transfers between devices, shards(): lax.all_to_all(jnp.concatenate([out_block, log_row], axis=1), 'seq', spli...  28.5 us
    ppermute x18, waiting for transfers between devices, shift(): return lax.ppermute(value, axis_name, pairs)  27.8 us
    all_to_all x1, waiting for transfers between devices, shards(): lax.all_to_all(outgoing, 'seq', split_axis=0, concat_axis=0, tiled=True)  16.7 us
    all_to_all x1, waiting for transfers between devices, shards(): lax.all_to_all(jnp.moveaxis(pieces, 1, 0), 'tensor', split_axis=0, concat...  14.2 us
    all_to_all x1, starting transfers between devices, shards(): lax.all_to_all(jnp.moveaxis(pieces, 1, 0), 'tensor', split_axis=0, concat...  12 us
    all_to_all x1, starting transfers between devices, shards(): lax.all_to_all(tiles, 'tensor', split_axis=0, concat_axis=0, tiled=True)  10 us
    all_to_all x1, starting transfers between devices, shards(): lax.all_to_all(outgoing, 'seq', split_axis=0, concat_axis=0, tiled=True)  8.18 us
  transfers between devices with their start and end apart: 23, of which 15 were waited for; matrix products, arithmetic and copies ran while one was open for 11% of the time, Pallas kernels for 0%

profile of v13, /device:TPU:1, one launch (start us, length us, event | category | flops | bytes accessed | tf_op | source)
XLA Modules:
  0.0 243.8 jit_solution(8464617098719469231)
XLA Ops:
  7.2 4.2 %collective-permute-start.1 = (bf16[64,512]{1,0:T(8,128)(2,1)}, bf16[64,512]{1,0:T(8,128)(2,1)S(1)}, u32[]{:S(2)}, u32[]{:S(2)}) collective-permute-start(bf16[64,512]{1,0:T(8,128)(2,1)} %param.10), channel_id=1, source_target_pairs={{0,8},{8,16},{16,24},{24,0},{32,40},{40,48},{48,56},{56,32},{64,72... | collective-permute-start | bytes 196616 | tf_op jit(solution)/shard_map/ppermute | solution.py:79
  11.4 3.4 %collective-permute-start = (bf16[64,512]{1,0:T(8,128)(2,1)}, bf16[64,512]{1,0:T(8,128)(2,1)S(1)}, u32[]{:S(2)}, u32[]{:S(2)}) collective-permute-start(bf16[64,512]{1,0:T(8,128)(2,1)} %param.10), channel_id=1, source_target_pairs={{0,24},{8,0},{16,8},{24,16},{32,56},{40,32},{48,40},{56,48},{64,88... | collective-permute-start | bytes 196616 | tf_op jit(solution)/shard_map/ppermute | solution.py:79
  16.9 10.0 %all-to-all-start = ((bf16[8,128,512]{1,2,0:T(8,128)(2,1)}), bf16[8,128,512]{1,2,0:T(8,128)(2,1)S(1)}, u32[]{:S(2)}, u32[]{:S(2)}) async-start(bf16[8,128,512]{1,2,0:T(8,128)(2,1)} %broadcast_in_dim.72), calls=%async_computation | async-start | bytes 2097152 | tf_op jit(solution)/shard_map/all_to_all | solution.py:102
  28.8 1.9 collective-permute-start.2
  30.9 4.6 %collective-permute-done.2 = bf16[64,512]{1,0:T(8,128)(2,1)S(1)} collective-permute-done((bf16[64,512]{1,0:T(8,128)(2,1)S(1)}, bf16[64,512]{1,0:T(8,128)(2,1)S(1)}, u32[]{:S(2)}, u32[]{:S(2)}) %collective-permute-start.2) | collective-permute-done | bytes 65568 | tf_op jit(solution)/shard_map/ppermute | solution.py:79
  35.5 6.7 %collective-permute-start.3 = (bf16[4,64,512]{2,1,0:T(8,128)(2,1)S(1)}, bf16[4,64,512]{2,1,0:T(8,128)(2,1)S(1)}, u32[]{:S(2)}, u32[]{:S(2)}) collective-permute-start(bf16[4,64,512]{2,1,0:T(8,128)(2,1)S(1)} %pad_maximum_fusion), channel_id=1, source_target_pairs={{0,480},{8,488},{16,496},{24,504},{32,0},{40,8},{48,16},{56,24},{6... | collective-permute-start | bytes 786440 | tf_op jit(solution)/shard_map/ppermute | solution.py:79
  42.2 1.9 collective-permute-start.10
  44.3 3.1 %collective-permute-done.3 = bf16[4,64,512]{2,1,0:T(8,128)(2,1)S(1)} collective-permute-done((bf16[4,64,512]{2,1,0:T(8,128)(2,1)S(1)}, bf16[4,64,512]{2,1,0:T(8,128)(2,1)S(1)}, u32[]{:S(2)}, u32[]{:S(2)}) %collective-permute-start.3) | collective-permute-done | bytes 262176 | tf_op jit(solution)/shard_map/ppermute | solution.py:79
  47.3 5.2 %collective-permute-start.4 = (bf16[4,64,512]{2,1,0:T(8,128)(2,1)S(1)}, bf16[4,64,512]{2,1,0:T(8,128)(2,1)S(1)}, u32[]{:S(2)}, u32[]{:S(2)}) collective-permute-start(bf16[4,64,512]{2,1,0:T(8,128)(2,1)S(1)} %collective-permute-done.3), channel_id=1, source_target_pairs={{0,480},{8,488},{16,496},{24,504},{32,0},{40,8},{48,16},{56,24},{6... | collective-permute-start | bytes 786440 | tf_op jit(solution)/shard_map/ppermute | solution.py:79
  52.6 1.9 collective-permute-start.11
  56.7 5.3 %collective-permute-start.5 = (bf16[4,64,512]{2,1,0:T(8,128)(2,1)S(1)}, bf16[4,64,512]{2,1,0:T(8,128)(2,1)S(1)}, u32[]{:S(2)}, u32[]{:S(2)}) collective-permute-start(bf16[4,64,512]{2,1,0:T(8,128)(2,1)S(1)} %collective-permute-done.4), channel_id=1, source_target_pairs={{0,480},{8,488},{16,496},{24,504},{32,0},{40,8},{48,16},{56,24},{6... | collective-permute-start | bytes 786440 | tf_op jit(solution)/shard_map/ppermute | solution.py:79
  62.3 1.9 collective-permute-start.12
  65.9 5.4 %collective-permute-start.6 = (bf16[4,64,512]{2,1,0:T(8,128)(2,1)S(1)}, bf16[4,64,512]{2,1,0:T(8,128)(2,1)S(1)}, u32[]{:S(2)}, u32[]{:S(2)}) collective-permute-start(bf16[4,64,512]{2,1,0:T(8,128)(2,1)S(1)} %collective-permute-done.5), channel_id=1, source_target_pairs={{0,480},{8,488},{16,496},{24,504},{32,0},{40,8},{48,16},{56,24},{6... | collective-permute-start | bytes 786440 | tf_op jit(solution)/shard_map/ppermute | solution.py:79
  71.3 1.9 collective-permute-start.13
  76.3 4.6 %collective-permute-start.7 = (bf16[4,64,512]{2,1,0:T(8,128)(2,1)S(1)}, bf16[4,64,512]{2,1,0:T(8,128)(2,1)S(1)}, u32[]{:S(2)}, u32[]{:S(2)}) collective-permute-start(bf16[4,64,512]{2,1,0:T(8,128)(2,1)S(1)} %collective-permute-done.6), channel_id=1, source_target_pairs={{0,480},{8,488},{16,496},{24,504},{32,0},{40,8},{48,16},{56,24},{6... | collective-permute-start | bytes 786440 | tf_op jit(solution)/shard_map/ppermute | solution.py:79
  80.9 1.9 collective-permute-start.14
  84.7 5.0 %collective-permute-start.8 = (bf16[4,64,512]{2,1,0:T(8,128)(2,1)S(1)}, bf16[4,64,512]{2,1,0:T(8,128)(2,1)S(1)}, u32[]{:S(2)}, u32[]{:S(2)}) collective-permute-start(bf16[4,64,512]{2,1,0:T(8,128)(2,1)S(1)} %collective-permute-done.7), channel_id=1, source_target_pairs={{0,480},{8,488},{16,496},{24,504},{32,0},{40,8},{48,16},{56,24},{6... | collective-permute-start | bytes 786440 | tf_op jit(solution)/shard_map/ppermute | solution.py:79
  90.1 1.9 collective-permute-start.15
  92.4 6.6 %collective-permute-done.15 = bf16[4,64,512]{2,1,0:T(8,128)(2,1)S(1)} collective-permute-done((bf16[4,64,512]{2,1,0:T(8,128)(2,1)S(1)}, bf16[4,64,512]{2,1,0:T(8,128)(2,1)S(1)}, u32[]{:S(2)}, u32[]{:S(2)}) %collective-permute-start.15) | collective-permute-done | bytes 262176 | tf_op jit(solution)/shard_map/ppermute | solution.py:79
  101.2 4.6 %collective-permute-start.9 = (bf16[4,64,512]{2,1,0:T(8,128)(2,1)S(1)}, bf16[4,64,512]{2,1,0:T(8,128)(2,1)S(1)}, u32[]{:S(2)}, u32[]{:S(2)}) collective-permute-start(bf16[4,64,512]{2,1,0:T(8,128)(2,1)S(1)} %collective-permute-done.8), channel_id=1, source_target_pairs={{0,480},{8,488},{16,496},{24,504},{32,0},{40,8},{48,16},{56,24},{6... | collective-permute-start | bytes 786440 | tf_op jit(solution)/shard_map/ppermute | solution.py:79
  107.5 1.9 collective-permute-start.17
  109.9 7.2 %collective-permute-done.17 = bf16[4,64,512]{2,1,0:T(8,128)(2,1)S(1)} collective-permute-done((bf16[4,64,512]{2,1,0:T(8,128)(2,1)S(1)}, bf16[4,64,512]{2,1,0:T(8,128)(2,1)S(1)}, u32[]{:S(2)}, u32[]{:S(2)}) %collective-permute-start.17) | collective-permute-done | bytes 262176 | tf_op jit(solution)/shard_map/ppermute | solution.py:79
  120.6 8.2 %all-to-all-start.1 = ((bf16[64,4,512]{2,1,0:T(4,128)(2,1)}), bf16[64,4,512]{2,1,0:T(4,128)(2,1)}, u32[]{:S(2)}, u32[]{:S(2)}) async-start(bf16[64,4,512]{2,1,0:T(4,128)(2,1)} %broadcast_select_fusion), calls=%async_computation.1 | async-start | bytes 524288 | tf_op jit(solution)/shard_map/all_to_all | solution.py:166
  128.8 2.9 %copy.195 = bf16[1,1024,1024]{1,2,0:T(8,128)(2,1)S(1)} copy(bf16[1,1024,1024]{2,1,0:T(8,128)(2,1)} %param.13) | data formatting | bytes 4194304 | tf_op args[5]
  131.7 16.7 %all-to-all-done.1 = bf16[64,4,512]{2,1,0:T(4,128)(2,1)} async-done(((bf16[64,4,512]{2,1,0:T(4,128)(2,1)}), bf16[64,4,512]{2,1,0:T(4,128)(2,1)}, u32[]{:S(2)}, u32[]{:S(2)}) %all-to-all-start.1) | async-done | bytes 262176 | tf_op jit(solution)/shard_map/all_to_all | solution.py:166
  156.5 4.6 %all-to-all-start.2 = ((bf16[64,5,512]{2,1,0:T(8,128)(2,1)}), bf16[64,5,512]{2,1,0:T(8,128)(2,1)S(1)}, u32[]{:S(2)}, u32[]{:S(2)}) async-start(bf16[64,5,512]{2,1,0:T(8,128)(2,1)} %fusion.26), calls=%async_computation.2 | async-start | bytes 1048576 | tf_op jit(solution)/shard_map/all_to_all | solution.py:184
  162.1 28.5 %all-to-all-done.2 = bf16[64,5,512]{2,1,0:T(8,128)(2,1)S(1)} async-done(((bf16[64,5,512]{2,1,0:T(8,128)(2,1)}), bf16[64,5,512]{2,1,0:T(8,128)(2,1)S(1)}, u32[]{:S(2)}, u32[]{:S(2)}) %all-to-all-start.2) | async-done | bytes 327712 | tf_op jit(solution)/shard_map/all_to_all | solution.py:184
  192.6 5.7 %all-gather.2.cloned.1.call-done = bf16[768,4096]{0,1:T(8,128)(2,1)} async-done(((bf16[768,64]{0,1:T(8,128)(2,1)}), bf16[768,4096]{0,1:T(8,128)(2,1)}) %all-gather.2.cloned.1.call-update) | async-done | bytes 6291472 | tf_op jit(solution)/shard_map/all_gather | solution.py:119
  198.4 2.1 fusion
  203.0 5.0 %convolution_convert_fusion = bf16[128,4096]{1,0:T(8,128)(2,1)S(1)} fusion(bf16[768,4096]{0,1:T(8,128)(2,1)} %all-gather.2.cloned.1.call-done, bf16[128,512]{0,1:T(8,128)(2,1)S(1)} %bitcast.297), kind=kOutput, calls=%fused_computation.3 | convolution fusion | flops 805830656 | bytes 7471104 | tf_op jit(solution)/shard_map/dot_general | solution.py:220
  209.1 12.0 %all-to-all-start.3 = ((bf16[8,128,512]{2,1,0:T(8,128)(2,1)}), bf16[8,128,512]{2,1,0:T(8,128)(2,1)S(1)}, u32[]{:S(2)}, u32[]{:S(2)}) async-start(bf16[8,128,512]{2,1,0:T(8,128)(2,1)} %bitcast.268), calls=%async_computation.3 | async-start | bytes 2097152 | tf_op jit(solution)/shard_map/all_to_all | solution.py:223
  221.9 14.2 %all-to-all-done.3 = bf16[8,128,512]{2,1,0:T(8,128)(2,1)S(1)} async-done(((bf16[8,128,512]{2,1,0:T(8,128)(2,1)}), bf16[8,128,512]{2,1,0:T(8,128)(2,1)S(1)}, u32[]{:S(2)}, u32[]{:S(2)}) %all-to-all-start.3) | async-done | bytes 1048608 | tf_op jit(solution)/shard_map/all_to_all | solution.py:223
  (166 shorter events, 37.8 us)
Async XLA Ops:
  7.2 19.8 %copy-start = (bf16[64,1024]{1,0:T(8,128)(2,1)S(1)}, bf16[64,1024]{1,0:T(8,128)(2,1)}, u32[]{:S(2)}) copy-start(bf16[64,1024]{1,0:T(8,128)(2,1)} %param.11) | copy-start | bytes 393220
  7.2 28.3 %copy-start.4 = (bf16[64,512]{1,0:T(8,128)(2,1)S(1)}, bf16[64,512]{1,0:T(8,128)(2,1)}, u32[]{:S(2)}) copy-start(bf16[64,512]{1,0:T(8,128)(2,1)} %param.10) | copy-start | bytes 196612
  7.2 19.8 %copy-start.3 = (bf16[512,64]{0,1:T(8,128)(2,1)S(1)}, bf16[512,64]{0,1:T(8,128)(2,1)}, u32[]{:S(2)}) copy-start(bf16[512,64]{0,1:T(8,128)(2,1)} %param.12) | copy-start | bytes 196612
  7.2 20.5 %copy-start.6 = (s32[1,64]{1,0:T(1,128)S(1)}, s32[1,64]{1,0:T(1,128)}, u32[]{:S(2)}) copy-start(s32[1,64]{1,0:T(1,128)} %param.15) | copy-start | bytes 772
  7.2 20.8 %copy-start.9 = (s32[64]{0:T(128)S(1)}, s32[64]{0:T(128)}, u32[]{:S(2)}) copy-start(s32[64]{0:T(128)} %param.14) | copy-start | bytes 772
  7.2 21.6 %collective-permute-start.1 = (bf16[64,512]{1,0:T(8,128)(2,1)}, bf16[64,512]{1,0:T(8,128)(2,1)S(1)}, u32[]{:S(2)}, u32[]{:S(2)}) collective-permute-start(bf16[64,512]{1,0:T(8,128)(2,1)} %param.10), channel_id=1, source_target_pairs={{0,8},{8,16},{16,24},{24,0},{32,40},{40,48},{48,56},{56,32},{64,72... | collective-permute-start | bytes 196616 | tf_op jit(solution)/shard_map/ppermute | solution.py:79
  11.4 19.5 %collective-permute-start = (bf16[64,512]{1,0:T(8,128)(2,1)}, bf16[64,512]{1,0:T(8,128)(2,1)S(1)}, u32[]{:S(2)}, u32[]{:S(2)}) collective-permute-start(bf16[64,512]{1,0:T(8,128)(2,1)} %param.10), channel_id=1, source_target_pairs={{0,24},{8,0},{16,8},{24,16},{32,56},{40,32},{48,40},{56,48},{64,88... | collective-permute-start | bytes 196616 | tf_op jit(solution)/shard_map/ppermute | solution.py:79
  15.8 38.8 %copy-start.5 = (bf16[4096]{0:T(1024)(128)(2,1)S(1)}, bf16[4096]{0:T(1024)(128)(2,1)}, u32[]{:S(2)}) copy-start(bf16[4096]{0:T(1024)(128)(2,1)} %param.9) | copy-start | bytes 24580
  16.9 47.3 %all-to-all-start = ((bf16[8,128,512]{1,2,0:T(8,128)(2,1)}), bf16[8,128,512]{1,2,0:T(8,128)(2,1)S(1)}, u32[]{:S(2)}, u32[]{:S(2)}) async-start(bf16[8,128,512]{1,2,0:T(8,128)(2,1)} %broadcast_in_dim.72), calls=%async_computation | async-start | bytes 2097152 | tf_op jit(solution)/shard_map/all_to_all | solution.py:102
  26.9 171.4 %all-gather.2.cloned.1.call-start = ((), (), s32[]{:S(2)}) async-start(), calls=%async_computation.4 | async-start | bytes 6389760 | tf_op jit(solution)/shard_map/all_gather | solution.py:119
  28.8 13.4 %copy-start.12 = (s32[128]{0:T(128)}, s32[128]{0:T(128)S(1)}, u32[]{:S(2)}) copy-start(s32[128]{0:T(128)S(1)} %get-tuple-element.11) | copy-start | bytes 1540
  28.8 6.6 %collective-permute-start.2 = (bf16[64,512]{1,0:T(8,128)(2,1)S(1)}, bf16[64,512]{1,0:T(8,128)(2,1)S(1)}, u32[]{:S(2)}, u32[]{:S(2)}) collective-permute-start(bf16[64,512]{1,0:T(8,128)(2,1)S(1)} %collective-permute-done.1), channel_id=1, source_target_pairs={{0,8},{8,16},{16,24},{24,0},{32,40},{40,48},{48,56},{56,32},{64,72... | collective-permute-start | bytes 196616 | tf_op jit(solution)/shard_map/ppermute | solution.py:79
  35.5 11.8 %collective-permute-start.3 = (bf16[4,64,512]{2,1,0:T(8,128)(2,1)S(1)}, bf16[4,64,512]{2,1,0:T(8,128)(2,1)S(1)}, u32[]{:S(2)}, u32[]{:S(2)}) collective-permute-start(bf16[4,64,512]{2,1,0:T(8,128)(2,1)S(1)} %pad_maximum_fusion), channel_id=1, source_target_pairs={{0,480},{8,488},{16,496},{24,504},{32,0},{40,8},{48,16},{56,24},{6... | collective-permute-start | bytes 786440 | tf_op jit(solution)/shard_map/ppermute | solution.py:79
  42.2 10.3 %collective-permute-start.10 = (bf16[4,64,512]{2,1,0:T(8,128)(2,1)S(1)}, bf16[4,64,512]{2,1,0:T(8,128)(2,1)S(1)}, u32[]{:S(2)}, u32[]{:S(2)}) collective-permute-start(bf16[4,64,512]{2,1,0:T(8,128)(2,1)S(1)} %pad_maximum_fusion), channel_id=1, source_target_pairs={{0,32},{8,40},{16,48},{24,56},{32,64},{40,72},{48,80},{56,88},{64,... | collective-permute-start | bytes 786440 | tf_op jit(solution)/shard_map/ppermute | solution.py:79
  47.3 9.4 %collective-permute-start.4 = (bf16[4,64,512]{2,1,0:T(8,128)(2,1)S(1)}, bf16[4,64,512]{2,1,0:T(8,128)(2,1)S(1)}, u32[]{:S(2)}, u32[]{:S(2)}) collective-permute-start(bf16[4,64,512]{2,1,0:T(8,128)(2,1)S(1)} %collective-permute-done.3), channel_id=1, source_target_pairs={{0,480},{8,488},{16,496},{24,504},{32,0},{40,8},{48,16},{56,24},{6... | collective-permute-start | bytes 786440 | tf_op jit(solution)/shard_map/ppermute | solution.py:79
  52.6 9.7 %collective-permute-start.11 = (bf16[4,64,512]{2,1,0:T(8,128)(2,1)S(1)}, bf16[4,64,512]{2,1,0:T(8,128)(2,1)S(1)}, u32[]{:S(2)}, u32[]{:S(2)}) collective-permute-start(bf16[4,64,512]{2,1,0:T(8,128)(2,1)S(1)} %collective-permute-done.10), channel_id=1, source_target_pairs={{0,32},{8,40},{16,48},{24,56},{32,64},{40,72},{48,80},{56,88},{64,... | collective-permute-start | bytes 786440 | tf_op jit(solution)/shard_map/ppermute | solution.py:79
  56.7 9.1 %collective-permute-start.5 = (bf16[4,64,512]{2,1,0:T(8,128)(2,1)S(1)}, bf16[4,64,512]{2,1,0:T(8,128)(2,1)S(1)}, u32[]{:S(2)}, u32[]{:S(2)}) collective-permute-start(bf16[4,64,512]{2,1,0:T(8,128)(2,1)S(1)} %collective-permute-done.4), channel_id=1, source_target_pairs={{0,480},{8,488},{16,496},{24,504},{32,0},{40,8},{48,16},{56,24},{6... | collective-permute-start | bytes 786440 | tf_op jit(solution)/shard_map/ppermute | solution.py:79
  62.3 9.0 %collective-permute-start.12 = (bf16[4,64,512]{2,1,0:T(8,128)(2,1)S(1)}, bf16[4,64,512]{2,1,0:T(8,128)(2,1)S(1)}, u32[]{:S(2)}, u32[]{:S(2)}) collective-permute-start(bf16[4,64,512]{2,1,0:T(8,128)(2,1)S(1)} %collective-permute-done.11), channel_id=1, source_target_pairs={{0,32},{8,40},{16,48},{24,56},{32,64},{40,72},{48,80},{56,88},{64,... | collective-permute-start | bytes 786440 | tf_op jit(solution)/shard_map/ppermute | solution.py:79
  64.8 9.2 %copy-start.7 = (f32[128]{0:T(128)}, f32[128]{0:T(128)S(1)}, u32[]{:S(2)}) copy-start(f32[128]{0:T(128)S(1)} %add_rsqrt_fusion) | copy-start | bytes 1540
  65.9 10.4 %collective-permute-start.6 = (bf16[4,64,512]{2,1,0:T(8,128)(2,1)S(1)}, bf16[4,64,512]{2,1,0:T(8,128)(2,1)S(1)}, u32[]{:S(2)}, u32[]{:S(2)}) collective-permute-start(bf16[4,64,512]{2,1,0:T(8,128)(2,1)S(1)} %collective-permute-done.5), channel_id=1, source_target_pairs={{0,480},{8,488},{16,496},{24,504},{32,0},{40,8},{48,16},{56,24},{6... | collective-permute-start | bytes 786440 | tf_op jit(solution)/shard_map/ppermute | solution.py:79
  71.3 9.5 %collective-permute-start.13 = (bf16[4,64,512]{2,1,0:T(8,128)(2,1)S(1)}, bf16[4,64,512]{2,1,0:T(8,128)(2,1)S(1)}, u32[]{:S(2)}, u32[]{:S(2)}) collective-permute-start(bf16[4,64,512]{2,1,0:T(8,128)(2,1)S(1)} %collective-permute-done.12), channel_id=1, source_target_pairs={{0,32},{8,40},{16,48},{24,56},{32,64},{40,72},{48,80},{56,88},{64,... | collective-permute-start | bytes 786440 | tf_op jit(solution)/shard_map/ppermute | solution.py:79
  76.3 8.4 %collective-permute-start.7 = (bf16[4,64,512]{2,1,0:T(8,128)(2,1)S(1)}, bf16[4,64,512]{2,1,0:T(8,128)(2,1)S(1)}, u32[]{:S(2)}, u32[]{:S(2)}) collective-permute-start(bf16[4,64,512]{2,1,0:T(8,128)(2,1)S(1)} %collective-permute-done.6), channel_id=1, source_target_pairs={{0,480},{8,488},{16,496},{24,504},{32,0},{40,8},{48,16},{56,24},{6... | collective-permute-start | bytes 786440 | tf_op jit(solution)/shard_map/ppermute | solution.py:79
  80.9 9.2 %collective-permute-start.14 = (bf16[4,64,512]{2,1,0:T(8,128)(2,1)S(1)}, bf16[4,64,512]{2,1,0:T(8,128)(2,1)S(1)}, u32[]{:S(2)}, u32[]{:S(2)}) collective-permute-start(bf16[4,64,512]{2,1,0:T(8,128)(2,1)S(1)} %collective-permute-done.13), channel_id=1, source_target_pairs={{0,32},{8,40},{16,48},{24,56},{32,64},{40,72},{48,80},{56,88},{64,... | collective-permute-start | bytes 786440 | tf_op jit(solution)/shard_map/ppermute | solution.py:79
  84.7 16.3 %collective-permute-start.8 = (bf16[4,64,512]{2,1,0:T(8,128)(2,1)S(1)}, bf16[4,64,512]{2,1,0:T(8,128)(2,1)S(1)}, u32[]{:S(2)}, u32[]{:S(2)}) collective-permute-start(bf16[4,64,512]{2,1,0:T(8,128)(2,1)S(1)} %collective-permute-done.7), channel_id=1, source_target_pairs={{0,480},{8,488},{16,496},{24,504},{32,0},{40,8},{48,16},{56,24},{6... | collective-permute-start | bytes 786440 | tf_op jit(solution)/shard_map/ppermute | solution.py:79
  90.1 9.0 %collective-permute-start.15 = (bf16[4,64,512]{2,1,0:T(8,128)(2,1)S(1)}, bf16[4,64,512]{2,1,0:T(8,128)(2,1)S(1)}, u32[]{:S(2)}, u32[]{:S(2)}) collective-permute-start(bf16[4,64,512]{2,1,0:T(8,128)(2,1)S(1)} %collective-permute-done.14), channel_id=1, source_target_pairs={{0,32},{8,40},{16,48},{24,56},{32,64},{40,72},{48,80},{56,88},{64,... | collective-permute-start | bytes 786440 | tf_op jit(solution)/shard_map/ppermute | solution.py:79
  99.1 8.4 %collective-permute-start.16 = (bf16[4,64,512]{2,1,0:T(8,128)(2,1)S(1)}, bf16[4,64,512]{2,1,0:T(8,128)(2,1)S(1)}, u32[]{:S(2)}, u32[]{:S(2)}) collective-permute-start(bf16[4,64,512]{2,1,0:T(8,128)(2,1)S(1)} %collective-permute-done.15), channel_id=1, source_target_pairs={{0,32},{8,40},{16,48},{24,56},{32,64},{40,72},{48,80},{56,88},{64,... | collective-permute-start | bytes 786440 | tf_op jit(solution)/shard_map/ppermute | solution.py:79
  101.2 8.4 %collective-permute-start.9 = (bf16[4,64,512]{2,1,0:T(8,128)(2,1)S(1)}, bf16[4,64,512]{2,1,0:T(8,128)(2,1)S(1)}, u32[]{:S(2)}, u32[]{:S(2)}) collective-permute-start(bf16[4,64,512]{2,1,0:T(8,128)(2,1)S(1)} %collective-permute-done.8), channel_id=1, source_target_pairs={{0,480},{8,488},{16,496},{24,504},{32,0},{40,8},{48,16},{56,24},{6... | collective-permute-start | bytes 786440 | tf_op jit(solution)/shard_map/ppermute | solution.py:79
  107.5 9.5 %collective-permute-start.17 = (bf16[4,64,512]{2,1,0:T(8,128)(2,1)S(1)}, bf16[4,64,512]{2,1,0:T(8,128)(2,1)S(1)}, u32[]{:S(2)}, u32[]{:S(2)}) collective-permute-start(bf16[4,64,512]{2,1,0:T(8,128)(2,1)S(1)} %collective-permute-done.16), channel_id=1, source_target_pairs={{0,32},{8,40},{16,48},{24,56},{32,64},{40,72},{48,80},{56,88},{64,... | collective-permute-start | bytes 786440 | tf_op jit(solution)/shard_map/ppermute | solution.py:79
  120.6 27.8 %all-to-all-start.1 = ((bf16[64,4,512]{2,1,0:T(4,128)(2,1)}), bf16[64,4,512]{2,1,0:T(4,128)(2,1)}, u32[]{:S(2)}, u32[]{:S(2)}) async-start(bf16[64,4,512]{2,1,0:T(4,128)(2,1)} %broadcast_select_fusion), calls=%async_computation.1 | async-start | bytes 524288 | tf_op jit(solution)/shard_map/all_to_all | solution.py:166
  156.5 34.1 %all-to-all-start.2 = ((bf16[64,5,512]{2,1,0:T(8,128)(2,1)}), bf16[64,5,512]{2,1,0:T(8,128)(2,1)S(1)}, u32[]{:S(2)}, u32[]{:S(2)}) async-start(bf16[64,5,512]{2,1,0:T(8,128)(2,1)} %fusion.26), calls=%async_computation.2 | async-start | bytes 1048576 | tf_op jit(solution)/shard_map/all_to_all | solution.py:184
  192.6 8.5 %copy-start.2 = (bf16[128,4,128]{2,0,1:T(8,128)(2,1)S(1)}, bf16[128,4,128]{2,0,1:T(8,128)(2,1)}, u32[]{:S(2)}) copy-start(bf16[128,4,128]{2,0,1:T(8,128)(2,1)} %copy-done.1) | copy-start | bytes 393220
  209.1 27.1 %all-to-all-start.3 = ((bf16[8,128,512]{2,1,0:T(8,128)(2,1)}), bf16[8,128,512]{2,1,0:T(8,128)(2,1)S(1)}, u32[]{:S(2)}, u32[]{:S(2)}) async-start(bf16[8,128,512]{2,1,0:T(8,128)(2,1)} %bitcast.268), calls=%async_computation.3 | async-start | bytes 2097152 | tf_op jit(solution)/shard_map/all_to_all | solution.py:223
  (5 other events, 29.4 us)
Sparse Core Ops, SparseCore 0:
  30.7 167.6 all-gather.1

commit v14 on v13

--- a/solution.py
+++ b/solution.py
@@ -179,13 +179,12 @@
         logs.append(serve_logsum)
     out_block = jnp.stack(outs, axis=1).astype(jnp.bfloat16).reshape(seq_count, items, width_query)
     log_block = jnp.stack(logs, axis=1).reshape(seq_count, items, heads_dev)
-    log_row = log_block.astype(jnp.bfloat16).reshape(seq_count, 1, items * heads_dev)
-    log_row = jnp.pad(log_row, ((0, 0), (0, 0), (0, width_query - items * heads_dev)))
+    log_lanes = jnp.pad(log_block.astype(jnp.bfloat16), ((0, 0), (0, 0), (0, head_size - heads_dev)))
     back = lax.all_to_all(
-        jnp.concatenate([out_block, log_row], axis=1), "seq", split_axis=0, concat_axis=0, tiled=True
-    )
-    prefix_out = back[:, :items]
-    prefix_log = back[:, items, : items * heads_dev].astype(jnp.float32)
+        jnp.concatenate([out_block, log_lanes], axis=2), "seq", split_axis=0, concat_axis=0, tiled=True
+    )
+    prefix_out = back[:, :, :width_query]
+    prefix_log = back[:, :, width_query : width_query + heads_dev].astype(jnp.float32)
     owner_of_token = jnp.sum(
         jnp.where(prefix_group[:, None] == labels[None, :], prefix_owner[None, :], 0), axis=1
     )

time: 245 us -> 236 us (0.963)
  waiting for transfers between devices: 93 us -> 86.7 us
    all_to_all x1, waiting for transfers between devices: 28.5 us -> 20.6 us  [shards(): lax.all_to_all(jnp.concatenate([out_block, log_lanes], axis=2), 'seq', sp...]
  transfers between devices with their start and end apart: 23 -> 23, of which waited for: 15 -> 14; matrix products, arithmetic and copies ran while one was open for 11% -> 12% of each run, Pallas kernels for 0% -> 0%
where the time goes in v14:
time: 236 us; the launch traced here: 235 us
  starting transfers between devices  94.1 us (40%)
  waiting for transfers between devices  86.7 us (37%)
  between operations  15.1 us (6%)
  matrix products  15 us (6%)
  local copies, waits for them, and re-layouts  14.2 us (6%)
  other arithmetic  10.1 us (4%)
    ppermute x18, starting transfers between devices, shift(): return lax.ppermute(value, axis_name, pairs)  61.5 us
    ppermute x18, waiting for transfers between devices, shift(): return lax.ppermute(value, axis_name, pairs)  27.4 us
    all_to_all x1, waiting for transfers between devices, shards(): lax.all_to_all(jnp.concatenate([out_block, log_lanes], axis=2), 'seq', sp...  20.6 us
    all_to_all x1, waiting for transfers between devices, shards(): lax.all_to_all(outgoing, 'seq', split_axis=0, concat_axis=0, tiled=True)  16.5 us
    all_to_all x1, waiting for transfers between devices, shards(): lax.all_to_all(jnp.moveaxis(pieces, 1, 0), 'tensor', split_axis=0, concat...  14.2 us
    all_to_all x1, starting transfers between devices, shards(): lax.all_to_all(tiles, 'tensor', split_axis=0, concat_axis=0, tiled=True)  10 us
    all_to_all x1, starting transfers between devices, shards(): lax.all_to_all(jnp.moveaxis(pieces, 1, 0), 'tensor', split_axis=0, concat...  9.88 us
    all_gather x1, waiting for transfers between devices, shards(): lax.all_gather(jnp.concatenate([kv_piece.T, w_out], axis=0), 'seq', axis=...  7.88 us
  transfers between devices with their start and end apart: 23, of which 14 were waited for; matrix products, arithmetic and copies ran while one was open for 12% of the time, Pallas kernels for 0%

profile of v14, /device:TPU:1, one launch (start us, length us, event | category | flops | bytes accessed | tf_op | source)
XLA Modules:
  0.0 235.2 jit_solution(2061792984755258278)
XLA Ops:
  7.2 4.2 %collective-permute-start.1 = (bf16[64,512]{1,0:T(8,128)(2,1)}, bf16[64,512]{1,0:T(8,128)(2,1)S(1)}, u32[]{:S(2)}, u32[]{:S(2)}) collective-permute-start(bf16[64,512]{1,0:T(8,128)(2,1)} %param.10), channel_id=1, source_target_pairs={{0,8},{8,16},{16,24},{24,0},{32,40},{40,48},{48,56},{56,32},{64,72... | collective-permute-start | bytes 196616 | tf_op jit(solution)/shard_map/ppermute | solution.py:79
  11.4 3.4 %collective-permute-start = (bf16[64,512]{1,0:T(8,128)(2,1)}, bf16[64,512]{1,0:T(8,128)(2,1)S(1)}, u32[]{:S(2)}, u32[]{:S(2)}) collective-permute-start(bf16[64,512]{1,0:T(8,128)(2,1)} %param.10), channel_id=1, source_target_pairs={{0,24},{8,0},{16,8},{24,16},{32,56},{40,32},{48,40},{56,48},{64,88... | collective-permute-start | bytes 196616 | tf_op jit(solution)/shard_map/ppermute | solution.py:79
  16.9 10.0 %all-to-all-start = ((bf16[8,128,512]{1,2,0:T(8,128)(2,1)}), bf16[8,128,512]{1,2,0:T(8,128)(2,1)S(1)}, u32[]{:S(2)}, u32[]{:S(2)}) async-start(bf16[8,128,512]{1,2,0:T(8,128)(2,1)} %broadcast_in_dim.72), calls=%async_computation | async-start | bytes 2097152 | tf_op jit(solution)/shard_map/all_to_all | solution.py:102
  28.2 1.9 collective-permute-start.2
  30.8 4.1 %collective-permute-done.2 = bf16[64,512]{1,0:T(8,128)(2,1)S(1)} collective-permute-done((bf16[64,512]{1,0:T(8,128)(2,1)S(1)}, bf16[64,512]{1,0:T(8,128)(2,1)S(1)}, u32[]{:S(2)}, u32[]{:S(2)}) %collective-permute-start.2) | collective-permute-done | bytes 65568 | tf_op jit(solution)/shard_map/ppermute | solution.py:79
  34.9 6.7 %collective-permute-start.3 = (bf16[4,64,512]{2,1,0:T(8,128)(2,1)S(1)}, bf16[4,64,512]{2,1,0:T(8,128)(2,1)S(1)}, u32[]{:S(2)}, u32[]{:S(2)}) collective-permute-start(bf16[4,64,512]{2,1,0:T(8,128)(2,1)S(1)} %pad_maximum_fusion.1), channel_id=1, source_target_pairs={{0,480},{8,488},{16,496},{24,504},{32,0},{40,8},{48,16},{56,24},{6... | collective-permute-start | bytes 786440 | tf_op jit(solution)/shard_map/ppermute | solution.py:79
  41.6 1.9 collective-permute-start.10
  43.7 2.7 %collective-permute-done.3 = bf16[4,64,512]{2,1,0:T(8,128)(2,1)S(1)} collective-permute-done((bf16[4,64,512]{2,1,0:T(8,128)(2,1)S(1)}, bf16[4,64,512]{2,1,0:T(8,128)(2,1)S(1)}, u32[]{:S(2)}, u32[]{:S(2)}) %collective-permute-start.3) | collective-permute-done | bytes 262176 | tf_op jit(solution)/shard_map/ppermute | solution.py:79
  46.4 5.3 %collective-permute-start.4 = (bf16[4,64,512]{2,1,0:T(8,128)(2,1)S(1)}, bf16[4,64,512]{2,1,0:T(8,128)(2,1)S(1)}, u32[]{:S(2)}, u32[]{:S(2)}) collective-permute-start(bf16[4,64,512]{2,1,0:T(8,128)(2,1)S(1)} %collective-permute-done.3), channel_id=1, source_target_pairs={{0,480},{8,488},{16,496},{24,504},{32,0},{40,8},{48,16},{56,24},{6... | collective-permute-start | bytes 786440 | tf_op jit(solution)/shard_map/ppermute | solution.py:79
  51.9 1.9 collective-permute-start.11
  54.4 2.1 collective-permute-done.4
  56.5 5.3 %collective-permute-start.5 = (bf16[4,64,512]{2,1,0:T(8,128)(2,1)S(1)}, bf16[4,64,512]{2,1,0:T(8,128)(2,1)S(1)}, u32[]{:S(2)}, u32[]{:S(2)}) collective-permute-start(bf16[4,64,512]{2,1,0:T(8,128)(2,1)S(1)} %collective-permute-done.4), channel_id=1, source_target_pairs={{0,480},{8,488},{16,496},{24,504},{32,0},{40,8},{48,16},{56,24},{6... | collective-permute-start | bytes 786440 | tf_op jit(solution)/shard_map/ppermute | solution.py:79
  61.8 1.9 collective-permute-start.12
  65.6 5.3 %collective-permute-start.6 = (bf16[4,64,512]{2,1,0:T(8,128)(2,1)S(1)}, bf16[4,64,512]{2,1,0:T(8,128)(2,1)S(1)}, u32[]{:S(2)}, u32[]{:S(2)}) collective-permute-start(bf16[4,64,512]{2,1,0:T(8,128)(2,1)S(1)} %collective-permute-done.5), channel_id=1, source_target_pairs={{0,480},{8,488},{16,496},{24,504},{32,0},{40,8},{48,16},{56,24},{6... | collective-permute-start | bytes 786440 | tf_op jit(solution)/shard_map/ppermute | solution.py:79
  70.9 1.9 collective-permute-start.13
  75.9 4.6 %collective-permute-start.7 = (bf16[4,64,512]{2,1,0:T(8,128)(2,1)S(1)}, bf16[4,64,512]{2,1,0:T(8,128)(2,1)S(1)}, u32[]{:S(2)}, u32[]{:S(2)}) collective-permute-start(bf16[4,64,512]{2,1,0:T(8,128)(2,1)S(1)} %collective-permute-done.6), channel_id=1, source_target_pairs={{0,480},{8,488},{16,496},{24,504},{32,0},{40,8},{48,16},{56,24},{6... | collective-permute-start | bytes 786440 | tf_op jit(solution)/shard_map/ppermute | solution.py:79
  80.5 1.9 collective-permute-start.14
  84.3 5.0 %collective-permute-start.8 = (bf16[4,64,512]{2,1,0:T(8,128)(2,1)S(1)}, bf16[4,64,512]{2,1,0:T(8,128)(2,1)S(1)}, u32[]{:S(2)}, u32[]{:S(2)}) collective-permute-start(bf16[4,64,512]{2,1,0:T(8,128)(2,1)S(1)} %collective-permute-done.7), channel_id=1, source_target_pairs={{0,480},{8,488},{16,496},{24,504},{32,0},{40,8},{48,16},{56,24},{6... | collective-permute-start | bytes 786440 | tf_op jit(solution)/shard_map/ppermute | solution.py:79
  89.7 1.9 collective-permute-start.15
  92.0 6.3 %collective-permute-done.15 = bf16[4,64,512]{2,1,0:T(8,128)(2,1)S(1)} collective-permute-done((bf16[4,64,512]{2,1,0:T(8,128)(2,1)S(1)}, bf16[4,64,512]{2,1,0:T(8,128)(2,1)S(1)}, u32[]{:S(2)}, u32[]{:S(2)}) %collective-permute-start.15) | collective-permute-done | bytes 262176 | tf_op jit(solution)/shard_map/ppermute | solution.py:79
  100.4 4.6 %collective-permute-start.9 = (bf16[4,64,512]{2,1,0:T(8,128)(2,1)S(1)}, bf16[4,64,512]{2,1,0:T(8,128)(2,1)S(1)}, u32[]{:S(2)}, u32[]{:S(2)}) collective-permute-start(bf16[4,64,512]{2,1,0:T(8,128)(2,1)S(1)} %collective-permute-done.8), channel_id=1, source_target_pairs={{0,480},{8,488},{16,496},{24,504},{32,0},{40,8},{48,16},{56,24},{6... | collective-permute-start | bytes 786440 | tf_op jit(solution)/shard_map/ppermute | solution.py:79
  109.3 7.4 %collective-permute-done.17 = bf16[4,64,512]{2,1,0:T(8,128)(2,1)S(1)} collective-permute-done((bf16[4,64,512]{2,1,0:T(8,128)(2,1)S(1)}, bf16[4,64,512]{2,1,0:T(8,128)(2,1)S(1)}, u32[]{:S(2)}, u32[]{:S(2)}) %collective-permute-start.17) | collective-permute-done | bytes 262176 | tf_op jit(solution)/shard_map/ppermute | solution.py:79
  120.2 7.8 %all-to-all-start.1 = ((bf16[64,4,512]{2,1,0:T(4,128)(2,1)}), bf16[64,4,512]{2,1,0:T(4,128)(2,1)}, u32[]{:S(2)}, u32[]{:S(2)}) async-start(bf16[64,4,512]{2,1,0:T(4,128)(2,1)} %broadcast_select_fusion), calls=%async_computation.1 | async-start | bytes 524288 | tf_op jit(solution)/shard_map/all_to_all | solution.py:166
  128.0 2.9 %copy.198 = bf16[1,1024,1024]{1,2,0:T(8,128)(2,1)S(1)} copy(bf16[1,1024,1024]{2,1,0:T(8,128)(2,1)} %param.13) | data formatting | bytes 4194304 | tf_op args[5]
  130.9 16.5 %all-to-all-done.1 = bf16[64,4,512]{2,1,0:T(4,128)(2,1)} async-done(((bf16[64,4,512]{2,1,0:T(4,128)(2,1)}), bf16[64,4,512]{2,1,0:T(4,128)(2,1)}, u32[]{:S(2)}, u32[]{:S(2)}) %all-to-all-start.1) | async-done | bytes 262176 | tf_op jit(solution)/shard_map/all_to_all | solution.py:166
  155.7 4.9 %all-to-all-start.2 = ((bf16[64,4,640]{2,1,0:T(4,128)(2,1)}), bf16[64,4,640]{2,1,0:T(4,128)(2,1)S(1)}, u32[]{:S(2)}, u32[]{:S(2)}) async-start(bf16[64,4,640]{2,1,0:T(4,128)(2,1)} %pad_maximum_fusion), calls=%async_computation.2 | async-start | bytes 655360 | tf_op jit(solution)/shard_map/all_to_all | solution.py:183
  161.5 20.6 %all-to-all-done.2 = bf16[64,4,640]{2,1,0:T(4,128)(2,1)S(1)} async-done(((bf16[64,4,640]{2,1,0:T(4,128)(2,1)}), bf16[64,4,640]{2,1,0:T(4,128)(2,1)S(1)}, u32[]{:S(2)}, u32[]{:S(2)}) %all-to-all-start.2) | async-done | bytes 327712 | tf_op jit(solution)/shard_map/all_to_all | solution.py:183
  184.0 7.9 %all-gather.2.cloned.1.call-done = bf16[768,4096]{0,1:T(8,128)(2,1)} async-done(((bf16[768,64]{0,1:T(8,128)(2,1)}), bf16[768,4096]{0,1:T(8,128)(2,1)}) %all-gather.2.cloned.1.call-update) | async-done | bytes 6291472 | tf_op jit(solution)/shard_map/all_gather | solution.py:119
  191.8 2.1 fusion
  196.5 5.0 %convolution_convert_fusion = bf16[128,4096]{1,0:T(8,128)(2,1)S(1)} fusion(bf16[768,4096]{0,1:T(8,128)(2,1)} %all-gather.2.cloned.1.call-done, bf16[128,512]{0,1:T(8,128)(2,1)S(1)} %bitcast.298), kind=kOutput, calls=%fused_computation.3 | convolution fusion | flops 805830656 | bytes 7471104 | tf_op jit(solution)/shard_map/dot_general | solution.py:219
  202.5 9.9 %all-to-all-start.3 = ((bf16[8,128,512]{2,1,0:T(8,128)(2,1)}), bf16[8,128,512]{2,1,0:T(8,128)(2,1)S(1)}, u32[]{:S(2)}, u32[]{:S(2)}) async-start(bf16[8,128,512]{2,1,0:T(8,128)(2,1)} %bitcast.269), calls=%async_computation.3 | async-start | bytes 2097152 | tf_op jit(solution)/shard_map/all_to_all | solution.py:222
  213.3 14.2 %all-to-all-done.3 = bf16[8,128,512]{2,1,0:T(8,128)(2,1)S(1)} async-done(((bf16[8,128,512]{2,1,0:T(8,128)(2,1)}), bf16[8,128,512]{2,1,0:T(8,128)(2,1)S(1)}, u32[]{:S(2)}, u32[]{:S(2)}) %all-to-all-start.3) | async-done | bytes 1048608 | tf_op jit(solution)/shard_map/all_to_all | solution.py:222
  (161 shorter events, 38.1 us)
Async XLA Ops:
  7.2 19.8 %copy-start = (bf16[64,1024]{1,0:T(8,128)(2,1)S(1)}, bf16[64,1024]{1,0:T(8,128)(2,1)}, u32[]{:S(2)}) copy-start(bf16[64,1024]{1,0:T(8,128)(2,1)} %param.11) | copy-start | bytes 393220
  7.2 27.7 %copy-start.4 = (bf16[64,512]{1,0:T(8,128)(2,1)S(1)}, bf16[64,512]{1,0:T(8,128)(2,1)}, u32[]{:S(2)}) copy-start(bf16[64,512]{1,0:T(8,128)(2,1)} %param.10) | copy-start | bytes 196612
  7.2 19.8 %copy-start.3 = (bf16[512,64]{0,1:T(8,128)(2,1)S(1)}, bf16[512,64]{0,1:T(8,128)(2,1)}, u32[]{:S(2)}) copy-start(bf16[512,64]{0,1:T(8,128)(2,1)} %param.12) | copy-start | bytes 196612
  7.2 20.5 %copy-start.6 = (s32[1,64]{1,0:T(1,128)S(1)}, s32[1,64]{1,0:T(1,128)}, u32[]{:S(2)}) copy-start(s32[1,64]{1,0:T(1,128)} %param.15) | copy-start | bytes 772
  7.2 20.8 %copy-start.9 = (s32[64]{0:T(128)S(1)}, s32[64]{0:T(128)}, u32[]{:S(2)}) copy-start(s32[64]{0:T(128)} %param.14) | copy-start | bytes 772
  7.2 21.0 %collective-permute-start.1 = (bf16[64,512]{1,0:T(8,128)(2,1)}, bf16[64,512]{1,0:T(8,128)(2,1)S(1)}, u32[]{:S(2)}, u32[]{:S(2)}) collective-permute-start(bf16[64,512]{1,0:T(8,128)(2,1)} %param.10), channel_id=1, source_target_pairs={{0,8},{8,16},{16,24},{24,0},{32,40},{40,48},{48,56},{56,32},{64,72... | collective-permute-start | bytes 196616 | tf_op jit(solution)/shard_map/ppermute | solution.py:79
  11.4 19.4 %collective-permute-start = (bf16[64,512]{1,0:T(8,128)(2,1)}, bf16[64,512]{1,0:T(8,128)(2,1)S(1)}, u32[]{:S(2)}, u32[]{:S(2)}) collective-permute-start(bf16[64,512]{1,0:T(8,128)(2,1)} %param.10), channel_id=1, source_target_pairs={{0,24},{8,0},{16,8},{24,16},{32,56},{40,32},{48,40},{56,48},{64,88... | collective-permute-start | bytes 196616 | tf_op jit(solution)/shard_map/ppermute | solution.py:79
  15.8 38.1 %copy-start.5 = (bf16[4096]{0:T(1024)(128)(2,1)S(1)}, bf16[4096]{0:T(1024)(128)(2,1)}, u32[]{:S(2)}) copy-start(bf16[4096]{0:T(1024)(128)(2,1)} %param.9) | copy-start | bytes 24580
  16.9 46.8 %all-to-all-start = ((bf16[8,128,512]{1,2,0:T(8,128)(2,1)}), bf16[8,128,512]{1,2,0:T(8,128)(2,1)S(1)}, u32[]{:S(2)}, u32[]{:S(2)}) async-start(bf16[8,128,512]{1,2,0:T(8,128)(2,1)} %broadcast_in_dim.72), calls=%async_computation | async-start | bytes 2097152 | tf_op jit(solution)/shard_map/all_to_all | solution.py:102
  26.9 164.9 %all-gather.2.cloned.1.call-start = ((), (), s32[]{:S(2)}) async-start(), calls=%async_computation.4 | async-start | bytes 6389760 | tf_op jit(solution)/shard_map/all_gather | solution.py:119
  28.2 6.7 %collective-permute-start.2 = (bf16[64,512]{1,0:T(8,128)(2,1)S(1)}, bf16[64,512]{1,0:T(8,128)(2,1)S(1)}, u32[]{:S(2)}, u32[]{:S(2)}) collective-permute-start(bf16[64,512]{1,0:T(8,128)(2,1)S(1)} %collective-permute-done.1), channel_id=1, source_target_pairs={{0,8},{8,16},{16,24},{24,0},{32,40},{40,48},{48,56},{56,32},{64,72... | collective-permute-start | bytes 196616 | tf_op jit(solution)/shard_map/ppermute | solution.py:79
  30.8 12.8 %copy-start.12 = (s32[128]{0:T(128)}, s32[128]{0:T(128)S(1)}, u32[]{:S(2)}) copy-start(s32[128]{0:T(128)S(1)} %get-tuple-element.11) | copy-start | bytes 1540
  34.9 11.5 %collective-permute-start.3 = (bf16[4,64,512]{2,1,0:T(8,128)(2,1)S(1)}, bf16[4,64,512]{2,1,0:T(8,128)(2,1)S(1)}, u32[]{:S(2)}, u32[]{:S(2)}) collective-permute-start(bf16[4,64,512]{2,1,0:T(8,128)(2,1)S(1)} %pad_maximum_fusion.1), channel_id=1, source_target_pairs={{0,480},{8,488},{16,496},{24,504},{32,0},{40,8},{48,16},{56,24},{6... | collective-permute-start | bytes 786440 | tf_op jit(solution)/shard_map/ppermute | solution.py:79
  41.6 10.3 %collective-permute-start.10 = (bf16[4,64,512]{2,1,0:T(8,128)(2,1)S(1)}, bf16[4,64,512]{2,1,0:T(8,128)(2,1)S(1)}, u32[]{:S(2)}, u32[]{:S(2)}) collective-permute-start(bf16[4,64,512]{2,1,0:T(8,128)(2,1)S(1)} %pad_maximum_fusion.1), channel_id=1, source_target_pairs={{0,32},{8,40},{16,48},{24,56},{32,64},{40,72},{48,80},{56,88},{64,... | collective-permute-start | bytes 786440 | tf_op jit(solution)/shard_map/ppermute | solution.py:79
  46.4 10.1 %collective-permute-start.4 = (bf16[4,64,512]{2,1,0:T(8,128)(2,1)S(1)}, bf16[4,64,512]{2,1,0:T(8,128)(2,1)S(1)}, u32[]{:S(2)}, u32[]{:S(2)}) collective-permute-start(bf16[4,64,512]{2,1,0:T(8,128)(2,1)S(1)} %collective-permute-done.3), channel_id=1, source_target_pairs={{0,480},{8,488},{16,496},{24,504},{32,0},{40,8},{48,16},{56,24},{6... | collective-permute-start | bytes 786440 | tf_op jit(solution)/shard_map/ppermute | solution.py:79
  51.9 9.9 %collective-permute-start.11 = (bf16[4,64,512]{2,1,0:T(8,128)(2,1)S(1)}, bf16[4,64,512]{2,1,0:T(8,128)(2,1)S(1)}, u32[]{:S(2)}, u32[]{:S(2)}) collective-permute-start(bf16[4,64,512]{2,1,0:T(8,128)(2,1)S(1)} %collective-permute-done.10), channel_id=1, source_target_pairs={{0,32},{8,40},{16,48},{24,56},{32,64},{40,72},{48,80},{56,88},{64,... | collective-permute-start | bytes 786440 | tf_op jit(solution)/shard_map/ppermute | solution.py:79
  56.5 9.1 %collective-permute-start.5 = (bf16[4,64,512]{2,1,0:T(8,128)(2,1)S(1)}, bf16[4,64,512]{2,1,0:T(8,128)(2,1)S(1)}, u32[]{:S(2)}, u32[]{:S(2)}) collective-permute-start(bf16[4,64,512]{2,1,0:T(8,128)(2,1)S(1)} %collective-permute-done.4), channel_id=1, source_target_pairs={{0,480},{8,488},{16,496},{24,504},{32,0},{40,8},{48,16},{56,24},{6... | collective-permute-start | bytes 786440 | tf_op jit(solution)/shard_map/ppermute | solution.py:79
  61.8 9.1 %collective-permute-start.12 = (bf16[4,64,512]{2,1,0:T(8,128)(2,1)S(1)}, bf16[4,64,512]{2,1,0:T(8,128)(2,1)S(1)}, u32[]{:S(2)}, u32[]{:S(2)}) collective-permute-start(bf16[4,64,512]{2,1,0:T(8,128)(2,1)S(1)} %collective-permute-done.11), channel_id=1, source_target_pairs={{0,32},{8,40},{16,48},{24,56},{32,64},{40,72},{48,80},{56,88},{64,... | collective-permute-start | bytes 786440 | tf_op jit(solution)/shard_map/ppermute | solution.py:79
  65.6 10.3 %collective-permute-start.6 = (bf16[4,64,512]{2,1,0:T(8,128)(2,1)S(1)}, bf16[4,64,512]{2,1,0:T(8,128)(2,1)S(1)}, u32[]{:S(2)}, u32[]{:S(2)}) collective-permute-start(bf16[4,64,512]{2,1,0:T(8,128)(2,1)S(1)} %collective-permute-done.5), channel_id=1, source_target_pairs={{0,480},{8,488},{16,496},{24,504},{32,0},{40,8},{48,16},{56,24},{6... | collective-permute-start | bytes 786440 | tf_op jit(solution)/shard_map/ppermute | solution.py:79
  70.9 9.6 %collective-permute-start.13 = (bf16[4,64,512]{2,1,0:T(8,128)(2,1)S(1)}, bf16[4,64,512]{2,1,0:T(8,128)(2,1)S(1)}, u32[]{:S(2)}, u32[]{:S(2)}) collective-permute-start(bf16[4,64,512]{2,1,0:T(8,128)(2,1)S(1)} %collective-permute-done.12), channel_id=1, source_target_pairs={{0,32},{8,40},{16,48},{24,56},{32,64},{40,72},{48,80},{56,88},{64,... | collective-permute-start | bytes 786440 | tf_op jit(solution)/shard_map/ppermute | solution.py:79
  75.9 8.4 %collective-permute-start.7 = (bf16[4,64,512]{2,1,0:T(8,128)(2,1)S(1)}, bf16[4,64,512]{2,1,0:T(8,128)(2,1)S(1)}, u32[]{:S(2)}, u32[]{:S(2)}) collective-permute-start(bf16[4,64,512]{2,1,0:T(8,128)(2,1)S(1)} %collective-permute-done.6), channel_id=1, source_target_pairs={{0,480},{8,488},{16,496},{24,504},{32,0},{40,8},{48,16},{56,24},{6... | collective-permute-start | bytes 786440 | tf_op jit(solution)/shard_map/ppermute | solution.py:79
  80.5 9.2 %collective-permute-start.14 = (bf16[4,64,512]{2,1,0:T(8,128)(2,1)S(1)}, bf16[4,64,512]{2,1,0:T(8,128)(2,1)S(1)}, u32[]{:S(2)}, u32[]{:S(2)}) collective-permute-start(bf16[4,64,512]{2,1,0:T(8,128)(2,1)S(1)} %collective-permute-done.13), channel_id=1, source_target_pairs={{0,32},{8,40},{16,48},{24,56},{32,64},{40,72},{48,80},{56,88},{64,... | collective-permute-start | bytes 786440 | tf_op jit(solution)/shard_map/ppermute | solution.py:79
  84.3 15.9 %collective-permute-start.8 = (bf16[4,64,512]{2,1,0:T(8,128)(2,1)S(1)}, bf16[4,64,512]{2,1,0:T(8,128)(2,1)S(1)}, u32[]{:S(2)}, u32[]{:S(2)}) collective-permute-start(bf16[4,64,512]{2,1,0:T(8,128)(2,1)S(1)} %collective-permute-done.7), channel_id=1, source_target_pairs={{0,480},{8,488},{16,496},{24,504},{32,0},{40,8},{48,16},{56,24},{6... | collective-permute-start | bytes 786440 | tf_op jit(solution)/shard_map/ppermute | solution.py:79
  89.7 8.6 %collective-permute-start.15 = (bf16[4,64,512]{2,1,0:T(8,128)(2,1)S(1)}, bf16[4,64,512]{2,1,0:T(8,128)(2,1)S(1)}, u32[]{:S(2)}, u32[]{:S(2)}) collective-permute-start(bf16[4,64,512]{2,1,0:T(8,128)(2,1)S(1)} %collective-permute-done.14), channel_id=1, source_target_pairs={{0,32},{8,40},{16,48},{24,56},{32,64},{40,72},{48,80},{56,88},{64,... | collective-permute-start | bytes 786440 | tf_op jit(solution)/shard_map/ppermute | solution.py:79
  98.3 8.6 %collective-permute-start.16 = (bf16[4,64,512]{2,1,0:T(8,128)(2,1)S(1)}, bf16[4,64,512]{2,1,0:T(8,128)(2,1)S(1)}, u32[]{:S(2)}, u32[]{:S(2)}) collective-permute-start(bf16[4,64,512]{2,1,0:T(8,128)(2,1)S(1)} %collective-permute-done.15), channel_id=1, source_target_pairs={{0,32},{8,40},{16,48},{24,56},{32,64},{40,72},{48,80},{56,88},{64,... | collective-permute-start | bytes 786440 | tf_op jit(solution)/shard_map/ppermute | solution.py:79
  100.4 8.6 %collective-permute-start.9 = (bf16[4,64,512]{2,1,0:T(8,128)(2,1)S(1)}, bf16[4,64,512]{2,1,0:T(8,128)(2,1)S(1)}, u32[]{:S(2)}, u32[]{:S(2)}) collective-permute-start(bf16[4,64,512]{2,1,0:T(8,128)(2,1)S(1)} %collective-permute-done.8), channel_id=1, source_target_pairs={{0,480},{8,488},{16,496},{24,504},{32,0},{40,8},{48,16},{56,24},{6... | collective-permute-start | bytes 786440 | tf_op jit(solution)/shard_map/ppermute | solution.py:79
  106.9 9.7 %collective-permute-start.17 = (bf16[4,64,512]{2,1,0:T(8,128)(2,1)S(1)}, bf16[4,64,512]{2,1,0:T(8,128)(2,1)S(1)}, u32[]{:S(2)}, u32[]{:S(2)}) collective-permute-start(bf16[4,64,512]{2,1,0:T(8,128)(2,1)S(1)} %collective-permute-done.16), channel_id=1, source_target_pairs={{0,32},{8,40},{16,48},{24,56},{32,64},{40,72},{48,80},{56,88},{64,... | collective-permute-start | bytes 786440 | tf_op jit(solution)/shard_map/ppermute | solution.py:79
  120.2 27.2 %all-to-all-start.1 = ((bf16[64,4,512]{2,1,0:T(4,128)(2,1)}), bf16[64,4,512]{2,1,0:T(4,128)(2,1)}, u32[]{:S(2)}, u32[]{:S(2)}) async-start(bf16[64,4,512]{2,1,0:T(4,128)(2,1)} %broadcast_select_fusion), calls=%async_computation.1 | async-start | bytes 524288 | tf_op jit(solution)/shard_map/all_to_all | solution.py:166
  153.1 7.6 %copy-start.8 = (f32[128]{0:T(128)S(1)}, f32[128]{0:T(128)}, u32[]{:S(2)}) copy-start(f32[128]{0:T(128)} %copy-done.7) | copy-start | bytes 1540
  155.7 26.4 %all-to-all-start.2 = ((bf16[64,4,640]{2,1,0:T(4,128)(2,1)}), bf16[64,4,640]{2,1,0:T(4,128)(2,1)S(1)}, u32[]{:S(2)}, u32[]{:S(2)}) async-start(bf16[64,4,640]{2,1,0:T(4,128)(2,1)} %pad_maximum_fusion), calls=%async_computation.2 | async-start | bytes 655360 | tf_op jit(solution)/shard_map/all_to_all | solution.py:183
  184.0 10.6 %copy-start.2 = (bf16[128,4,128]{2,0,1:T(8,128)(2,1)S(1)}, bf16[128,4,128]{2,0,1:T(8,128)(2,1)}, u32[]{:S(2)}) copy-start(bf16[128,4,128]{2,0,1:T(8,128)(2,1)} %copy-done.1) | copy-start | bytes 393220
  202.5 25.0 %all-to-all-start.3 = ((bf16[8,128,512]{2,1,0:T(8,128)(2,1)}), bf16[8,128,512]{2,1,0:T(8,128)(2,1)S(1)}, u32[]{:S(2)}, u32[]{:S(2)}) async-start(bf16[8,128,512]{2,1,0:T(8,128)(2,1)} %bitcast.269), calls=%async_computation.3 | async-start | bytes 2097152 | tf_op jit(solution)/shard_map/all_to_all | solution.py:222
  (5 other events, 24.4 us)
Sparse Core Ops, SparseCore 0:
  30.7 161.0 all-gather.1

commit v15 on v14

--- a/solution.py
+++ b/solution.py
@@ -53,17 +53,24 @@
 Y_CHIPS = 4
 
 
-def ring(value, count, step):
+def ring(value, count, step, far_early):
     rel = [None] * count
     rel[0] = value
     ahead = value
     behind = value
+    half = value.shape[0] // 2
     for k in range(1, count // 2 + 1):
-        behind = step(behind, 1)
-        rel[(-k) % count] = behind
         if k < count - k:
+            if far_early and k == count // 2 - 1 and count % 2 == 0:
+                rel[k + 1] = jnp.concatenate(
+                    [step(behind[:half], 2), step(ahead[half:], -2)], axis=0
+                )
+            behind = step(behind, 1)
+            rel[(-k) % count] = behind
             ahead = step(ahead, -1)
             rel[k] = ahead
+        elif rel[k] is None:
+            rel[k] = jnp.concatenate([step(behind[:half], 1), step(ahead[half:], -1)], axis=0)
     return rel
 
 
@@ -78,8 +85,8 @@
             pairs.append((i, ((z + dz) % z_count) * Y_CHIPS + (y + dy) % Y_CHIPS))
         return lax.ppermute(value, axis_name, pairs)
 
-    along_y = jnp.stack(ring(block, Y_CHIPS, lambda v, d: shift(v, 0, d)), axis=0)
-    along_z = ring(along_y, z_count, lambda v, d: shift(v, d, 0))
+    along_y = jnp.stack(ring(block, Y_CHIPS, lambda v, d: shift(v, 0, d), True), axis=0)
+    along_z = ring(along_y, z_count, lambda v, d: shift(v, d, 0), False)
     return [b.reshape(-1, block.shape[1]) for b in along_z], here // Y_CHIPS, here % Y_CHIPS
 
 

time: 236 us -> 241 us (1.021)
  starting transfers between devices: 94.1 us -> 108 us
  waiting for transfers between devices: 86.7 us -> 76.6 us
    ppermute x18 -> x20, starting transfers between devices: 61.5 us -> 73.7 us  [shift(): return lax.ppermute(value, axis_name, pairs)]
    ppermute x18 -> x20, waiting for transfers between devices: 27.4 us -> 17.9 us  [shift(): return lax.ppermute(value, axis_name, pairs)]
    all_to_all x1, starting transfers between devices: 7.79 us -> 10.8 us  [shards(): lax.all_to_all(outgoing, 'seq', split_axis=0, concat_axis=0, tiled=True)]
  transfers between devices with their start and end apart: 23 -> 25, of which waited for: 14 -> 14; matrix products, arithmetic and copies ran while one was open for 12% -> 12% of each run, Pallas kernels for 0% -> 0%
where the time goes in v15:
time: 241 us; the launch traced here: 240 us
  starting transfers between devices  108 us (45%)
  waiting for transfers between devices  76.6 us (32%)
  matrix products  16 us (7%)
  between operations  15.1 us (6%)
  local copies, waits for them, and re-layouts  14.3 us (6%)
  other arithmetic  10.2 us (4%)
    ppermute x20, starting transfers between devices, shift(): return lax.ppermute(value, axis_name, pairs)  73.7 us
    all_to_all x1, waiting for transfers between devices, shards(): lax.all_to_all(jnp.concatenate([out_block, log_lanes], axis=2), 'seq', sp...  20.5 us
    ppermute x20, waiting for transfers between devices, shift(): return lax.ppermute(value, axis_name, pairs)  17.9 us
    all_to_all x1, waiting for transfers between devices, shards(): lax.all_to_all(outgoing, 'seq', split_axis=0, concat_axis=0, tiled=True)  16.4 us
    all_to_all x1, waiting for transfers between devices, shards(): lax.all_to_all(jnp.moveaxis(pieces, 1, 0), 'tensor', split_axis=0, concat...  14.2 us
    all_to_all x1, starting transfers between devices, shards(): lax.all_to_all(outgoing, 'seq', split_axis=0, concat_axis=0, tiled=True)  10.8 us
    all_to_all x1, starting transfers between devices, shards(): lax.all_to_all(jnp.moveaxis(pieces, 1, 0), 'tensor', split_axis=0, concat...  9.85 us
    all_to_all x1, starting transfers between devices, shards(): lax.all_to_all(tiles, 'tensor', split_axis=0, concat_axis=0, tiled=True)  8.92 us
  transfers between devices with their start and end apart: 25, of which 14 were waited for; matrix products, arithmetic and copies ran while one was open for 12% of the time, Pallas kernels for 0%

profile of v15, /device:TPU:1, one launch (start us, length us, event | category | flops | bytes accessed | tf_op | source)
XLA Modules:
  0.0 240.2 jit_solution(5844760501292921319)
XLA Ops:
  7.2 5.6 %collective-permute-start = (bf16[64,512]{1,0:T(8,128)(2,1)}, bf16[64,512]{1,0:T(8,128)(2,1)S(1)}, u32[]{:S(2)}, u32[]{:S(2)}) collective-permute-start(bf16[64,512]{1,0:T(8,128)(2,1)} %param.10), channel_id=1, source_target_pairs={{0,24},{8,0},{16,8},{24,16},{32,56},{40,32},{48,40},{56,48},{64,88... | collective-permute-start | bytes 196616 | tf_op jit(solution)/shard_map/ppermute | solution.py:86
  12.8 1.9 collective-permute-start.3
  16.9 8.9 %all-to-all-start = ((bf16[8,128,512]{1,2,0:T(8,128)(2,1)}), bf16[8,128,512]{1,2,0:T(8,128)(2,1)S(1)}, u32[]{:S(2)}, u32[]{:S(2)}) async-start(bf16[8,128,512]{1,2,0:T(8,128)(2,1)} %broadcast_in_dim.72), calls=%async_computation | async-start | bytes 2097152 | tf_op jit(solution)/shard_map/all_to_all | solution.py:109
  25.9 1.9 collective-permute-start.1
  27.8 4.9 %collective-permute-start.2 = (bf16[32,512]{1,0:T(8,128)(2,1)S(1)}, bf16[32,512]{1,0:T(8,128)(2,1)S(1)}, u32[]{:S(2)}, u32[]{:S(2)}) collective-permute-start(bf16[32,512]{1,0:T(8,128)(2,1)S(1)} %get-tuple-element.30), channel_id=1, source_target_pairs={{0,16},{8,24},{16,0},{24,8},{32,48},{40,56},{48,32},{56,40},{64,80... | collective-permute-start | bytes 98312 | tf_op jit(solution)/shard_map/ppermute | solution.py:86
  34.1 9.5 %collective-permute-start.4 = (bf16[4,64,512]{2,1,0:T(8,128)(2,1)S(1)}, bf16[4,64,512]{2,1,0:T(8,128)(2,1)S(1)}, u32[]{:S(2)}, u32[]{:S(2)}) collective-permute-start(bf16[4,64,512]{2,1,0:T(8,128)(2,1)S(1)} %pad_maximum_fusion.1), channel_id=1, source_target_pairs={{0,480},{8,488},{16,496},{24,504},{32,0},{40,8},{48,16},{56,24},{6... | collective-permute-start | bytes 786440 | tf_op jit(solution)/shard_map/ppermute | solution.py:86
  43.5 1.9 collective-permute-start.11
  47.6 5.3 %collective-permute-start.5 = (bf16[4,64,512]{2,1,0:T(8,128)(2,1)S(1)}, bf16[4,64,512]{2,1,0:T(8,128)(2,1)S(1)}, u32[]{:S(2)}, u32[]{:S(2)}) collective-permute-start(bf16[4,64,512]{2,1,0:T(8,128)(2,1)S(1)} %collective-permute-done.4), channel_id=1, source_target_pairs={{0,480},{8,488},{16,496},{24,504},{32,0},{40,8},{48,16},{56,24},{6... | collective-permute-start | bytes 786440 | tf_op jit(solution)/shard_map/ppermute | solution.py:86
  53.0 1.9 collective-permute-start.12
  56.5 5.5 %collective-permute-start.6 = (bf16[4,64,512]{2,1,0:T(8,128)(2,1)S(1)}, bf16[4,64,512]{2,1,0:T(8,128)(2,1)S(1)}, u32[]{:S(2)}, u32[]{:S(2)}) collective-permute-start(bf16[4,64,512]{2,1,0:T(8,128)(2,1)S(1)} %collective-permute-done.5), channel_id=1, source_target_pairs={{0,480},{8,488},{16,496},{24,504},{32,0},{40,8},{48,16},{56,24},{6... | collective-permute-start | bytes 786440 | tf_op jit(solution)/shard_map/ppermute | solution.py:86
  62.3 1.9 collective-permute-start.13
  65.8 5.0 %collective-permute-start.7 = (bf16[4,64,512]{2,1,0:T(8,128)(2,1)S(1)}, bf16[4,64,512]{2,1,0:T(8,128)(2,1)}, u32[]{:S(2)}, u32[]{:S(2)}) collective-permute-start(bf16[4,64,512]{2,1,0:T(8,128)(2,1)S(1)} %collective-permute-done.6), channel_id=1, source_target_pairs={{0,480},{8,488},{16,496},{24,504},{32,0},{40,8},{48,16},{56,24},{6... | collective-permute-start | bytes 786440 | tf_op jit(solution)/shard_map/ppermute | solution.py:86
  71.1 1.9 collective-permute-start.14
  76.6 4.6 %collective-permute-start.8 = (bf16[4,64,512]{2,1,0:T(8,128)(2,1)}, bf16[4,64,512]{2,1,0:T(8,128)(2,1)S(1)}, u32[]{:S(2)}, u32[]{:S(2)}) collective-permute-start(bf16[4,64,512]{2,1,0:T(8,128)(2,1)} %collective-permute-done.7), channel_id=1, source_target_pairs={{0,480},{8,488},{16,496},{24,504},{32,0},{40,8},{48,16},{56,24},{6... | collective-permute-start | bytes 786440 | tf_op jit(solution)/shard_map/ppermute | solution.py:86
  81.2 1.9 collective-permute-start.15
  85.2 5.1 %collective-permute-start.9 = (bf16[4,64,512]{2,1,0:T(8,128)(2,1)S(1)}, bf16[4,64,512]{2,1,0:T(8,128)(2,1)S(1)}, u32[]{:S(2)}, u32[]{:S(2)}) collective-permute-start(bf16[4,64,512]{2,1,0:T(8,128)(2,1)S(1)} %collective-permute-done.8), channel_id=1, source_target_pairs={{0,480},{8,488},{16,496},{24,504},{32,0},{40,8},{48,16},{56,24},{6... | collective-permute-start | bytes 786440 | tf_op jit(solution)/shard_map/ppermute | solution.py:86
  90.3 1.9 collective-permute-start.16
  92.6 6.7 %collective-permute-done.16 = bf16[4,64,512]{2,1,0:T(8,128)(2,1)S(1)} collective-permute-done((bf16[4,64,512]{2,1,0:T(8,128)(2,1)S(1)}, bf16[4,64,512]{2,1,0:T(8,128)(2,1)S(1)}, u32[]{:S(2)}, u32[]{:S(2)}) %collective-permute-start.16) | collective-permute-done | bytes 262176 | tf_op jit(solution)/shard_map/ppermute | solution.py:86
  101.3 4.6 %collective-permute-start.10 = (bf16[4,64,512]{2,1,0:T(8,128)(2,1)S(1)}, bf16[4,64,512]{2,1,0:T(8,128)(2,1)S(1)}, u32[]{:S(2)}, u32[]{:S(2)}) collective-permute-start(bf16[4,64,512]{2,1,0:T(8,128)(2,1)S(1)} %collective-permute-done.9), channel_id=1, source_target_pairs={{0,480},{8,488},{16,496},{24,504},{32,0},{40,8},{48,16},{56,24},{6... | collective-permute-start | bytes 786440 | tf_op jit(solution)/shard_map/ppermute | solution.py:86
  106.3 2.8 %collective-permute-done.17 = bf16[4,64,512]{2,1,0:T(8,128)(2,1)S(1)} collective-permute-done((bf16[4,64,512]{2,1,0:T(8,128)(2,1)S(1)}, bf16[4,64,512]{2,1,0:T(8,128)(2,1)S(1)}, u32[]{:S(2)}, u32[]{:S(2)}) %collective-permute-start.17) | collective-permute-done | bytes 262176 | tf_op jit(solution)/shard_map/ppermute | solution.py:86
  109.1 1.9 collective-permute-start.18
  111.1 4.6 %collective-permute-start.19 = (bf16[2,64,512]{2,1,0:T(8,128)(2,1)S(1)}, bf16[2,64,512]{2,1,0:T(8,128)(2,1)S(1)}, u32[]{:S(2)}, u32[]{:S(2)}) collective-permute-start(bf16[2,64,512]{2,1,0:T(8,128)(2,1)S(1)} %slice.181), channel_id=1, source_target_pairs={{0,480},{8,488},{16,496},{24,504},{32,0},{40,8},{48,16},{56,24},{6... | collective-permute-start | bytes 393224 | tf_op jit(solution)/shard_map/ppermute | solution.py:86
  122.9 10.8 %all-to-all-start.1 = ((bf16[64,4,512]{2,1,0:T(4,128)(2,1)}), bf16[64,4,512]{2,1,0:T(4,128)(2,1)}, u32[]{:S(2)}, u32[]{:S(2)}) async-start(bf16[64,4,512]{2,1,0:T(4,128)(2,1)} %broadcast_select_fusion), calls=%async_computation.1 | async-start | bytes 524288 | tf_op jit(solution)/shard_map/all_to_all | solution.py:173
  133.7 2.9 %copy.198 = bf16[1,1024,1024]{1,2,0:T(8,128)(2,1)S(1)} copy(bf16[1,1024,1024]{2,1,0:T(8,128)(2,1)} %param.13) | data formatting | bytes 4194304 | tf_op args[5]
  136.7 16.4 %all-to-all-done.1 = bf16[64,4,512]{2,1,0:T(4,128)(2,1)} async-done(((bf16[64,4,512]{2,1,0:T(4,128)(2,1)}), bf16[64,4,512]{2,1,0:T(4,128)(2,1)}, u32[]{:S(2)}, u32[]{:S(2)}) %all-to-all-start.1) | async-done | bytes 262176 | tf_op jit(solution)/shard_map/all_to_all | solution.py:173
  161.4 4.8 %all-to-all-start.2 = ((bf16[64,4,640]{2,1,0:T(4,128)(2,1)}), bf16[64,4,640]{2,1,0:T(4,128)(2,1)S(1)}, u32[]{:S(2)}, u32[]{:S(2)}) async-start(bf16[64,4,640]{2,1,0:T(4,128)(2,1)} %pad_maximum_fusion), calls=%async_computation.2 | async-start | bytes 655360 | tf_op jit(solution)/shard_map/all_to_all | solution.py:190
  167.0 20.5 %all-to-all-done.2 = bf16[64,4,640]{2,1,0:T(4,128)(2,1)S(1)} async-done(((bf16[64,4,640]{2,1,0:T(4,128)(2,1)}), bf16[64,4,640]{2,1,0:T(4,128)(2,1)S(1)}, u32[]{:S(2)}, u32[]{:S(2)}) %all-to-all-start.2) | async-done | bytes 327712 | tf_op jit(solution)/shard_map/all_to_all | solution.py:190
  189.4 7.5 %all-gather.2.cloned.1.call-done = bf16[768,4096]{0,1:T(8,128)(2,1)} async-done(((bf16[768,64]{0,1:T(8,128)(2,1)}), bf16[768,4096]{0,1:T(8,128)(2,1)}) %all-gather.2.cloned.1.call-update) | async-done | bytes 6291472 | tf_op jit(solution)/shard_map/all_gather | solution.py:126
  196.9 2.1 fusion
  201.5 5.0 %convolution_convert_fusion = bf16[128,4096]{1,0:T(8,128)(2,1)S(1)} fusion(bf16[768,4096]{0,1:T(8,128)(2,1)} %all-gather.2.cloned.1.call-done, bf16[128,512]{0,1:T(8,128)(2,1)S(1)} %bitcast.302), kind=kOutput, calls=%fused_computation.3 | convolution fusion | flops 805830656 | bytes 7471104 | tf_op jit(solution)/shard_map/dot_general | solution.py:226
  207.6 9.8 %all-to-all-start.3 = ((bf16[8,128,512]{2,1,0:T(8,128)(2,1)}), bf16[8,128,512]{2,1,0:T(8,128)(2,1)S(1)}, u32[]{:S(2)}, u32[]{:S(2)}) async-start(bf16[8,128,512]{2,1,0:T(8,128)(2,1)} %bitcast.270), calls=%async_computation.3 | async-start | bytes 2097152 | tf_op jit(solution)/shard_map/all_to_all | solution.py:229
  218.3 14.2 %all-to-all-done.3 = bf16[8,128,512]{2,1,0:T(8,128)(2,1)S(1)} async-done(((bf16[8,128,512]{2,1,0:T(8,128)(2,1)}), bf16[8,128,512]{2,1,0:T(8,128)(2,1)S(1)}, u32[]{:S(2)}, u32[]{:S(2)}) %all-to-all-start.3) | async-done | bytes 1048608 | tf_op jit(solution)/shard_map/all_to_all | solution.py:229
  (170 shorter events, 40.8 us)
Async XLA Ops:
  7.2 25.5 %copy-start = (bf16[64,1024]{1,0:T(8,128)(2,1)S(1)}, bf16[64,1024]{1,0:T(8,128)(2,1)}, u32[]{:S(2)}) copy-start(bf16[64,1024]{1,0:T(8,128)(2,1)} %param.11) | copy-start | bytes 393220
  7.2 18.7 %copy-start.3 = (bf16[64,512]{1,0:T(8,128)(2,1)S(1)}, bf16[64,512]{1,0:T(8,128)(2,1)}, u32[]{:S(2)}) copy-start(bf16[64,512]{1,0:T(8,128)(2,1)} %param.10) | copy-start | bytes 196612
  7.2 25.5 %copy-start.4 = (bf16[512,64]{0,1:T(8,128)(2,1)S(1)}, bf16[512,64]{0,1:T(8,128)(2,1)}, u32[]{:S(2)}) copy-start(bf16[512,64]{0,1:T(8,128)(2,1)} %param.12) | copy-start | bytes 196612
  7.2 26.2 %copy-start.6 = (s32[1,64]{1,0:T(1,128)S(1)}, s32[1,64]{1,0:T(1,128)}, u32[]{:S(2)}) copy-start(s32[1,64]{1,0:T(1,128)} %param.15) | copy-start | bytes 772
  7.2 26.5 %copy-start.9 = (s32[64]{0:T(128)S(1)}, s32[64]{0:T(128)}, u32[]{:S(2)}) copy-start(s32[64]{0:T(128)} %param.14) | copy-start | bytes 772
  7.2 26.8 %collective-permute-start = (bf16[64,512]{1,0:T(8,128)(2,1)}, bf16[64,512]{1,0:T(8,128)(2,1)S(1)}, u32[]{:S(2)}, u32[]{:S(2)}) collective-permute-start(bf16[64,512]{1,0:T(8,128)(2,1)} %param.10), channel_id=1, source_target_pairs={{0,24},{8,0},{16,8},{24,16},{32,56},{40,32},{48,40},{56,48},{64,88... | collective-permute-start | bytes 196616 | tf_op jit(solution)/shard_map/ppermute | solution.py:86
  12.8 21.2 %collective-permute-start.3 = (bf16[64,512]{1,0:T(8,128)(2,1)}, bf16[64,512]{1,0:T(8,128)(2,1)S(1)}, u32[]{:S(2)}, u32[]{:S(2)}) collective-permute-start(bf16[64,512]{1,0:T(8,128)(2,1)} %param.10), channel_id=1, source_target_pairs={{0,8},{8,16},{16,24},{24,0},{32,40},{40,48},{48,56},{56,32},{64,72... | collective-permute-start | bytes 196616 | tf_op jit(solution)/shard_map/ppermute | solution.py:86
  16.9 47.3 %copy-start.5 = (bf16[4096]{0:T(1024)(128)(2,1)S(1)}, bf16[4096]{0:T(1024)(128)(2,1)}, u32[]{:S(2)}) copy-start(bf16[4096]{0:T(1024)(128)(2,1)} %param.9) | copy-start | bytes 24580
  16.9 56.1 %all-to-all-start = ((bf16[8,128,512]{1,2,0:T(8,128)(2,1)}), bf16[8,128,512]{1,2,0:T(8,128)(2,1)S(1)}, u32[]{:S(2)}, u32[]{:S(2)}) async-start(bf16[8,128,512]{1,2,0:T(8,128)(2,1)} %broadcast_in_dim.72), calls=%async_computation | async-start | bytes 2097152 | tf_op jit(solution)/shard_map/all_to_all | solution.py:109
  25.9 171.0 %all-gather.2.cloned.1.call-start = ((), (), s32[]{:S(2)}) async-start(), calls=%async_computation.4 | async-start | bytes 6389760 | tf_op jit(solution)/shard_map/all_gather | solution.py:126
  25.9 8.1 %collective-permute-start.1 = (bf16[32,512]{1,0:T(8,128)(2,1)S(1)}, bf16[32,512]{1,0:T(8,128)(2,1)S(1)}, u32[]{:S(2)}, u32[]{:S(2)}) collective-permute-start(bf16[32,512]{1,0:T(8,128)(2,1)S(1)} %get-tuple-element.29), channel_id=1, source_target_pairs={{0,16},{8,24},{16,0},{24,8},{32,48},{40,56},{48,32},{56,40},{64,80... | collective-permute-start | bytes 98312 | tf_op jit(solution)/shard_map/ppermute | solution.py:86
  27.8 6.2 %collective-permute-start.2 = (bf16[32,512]{1,0:T(8,128)(2,1)S(1)}, bf16[32,512]{1,0:T(8,128)(2,1)S(1)}, u32[]{:S(2)}, u32[]{:S(2)}) collective-permute-start(bf16[32,512]{1,0:T(8,128)(2,1)S(1)} %get-tuple-element.30), channel_id=1, source_target_pairs={{0,16},{8,24},{16,0},{24,8},{32,48},{40,56},{48,32},{56,40},{64,80... | collective-permute-start | bytes 98312 | tf_op jit(solution)/shard_map/ppermute | solution.py:86
  34.1 13.6 %collective-permute-start.4 = (bf16[4,64,512]{2,1,0:T(8,128)(2,1)S(1)}, bf16[4,64,512]{2,1,0:T(8,128)(2,1)S(1)}, u32[]{:S(2)}, u32[]{:S(2)}) collective-permute-start(bf16[4,64,512]{2,1,0:T(8,128)(2,1)S(1)} %pad_maximum_fusion.1), channel_id=1, source_target_pairs={{0,480},{8,488},{16,496},{24,504},{32,0},{40,8},{48,16},{56,24},{6... | collective-permute-start | bytes 786440 | tf_op jit(solution)/shard_map/ppermute | solution.py:86
  43.5 9.4 %collective-permute-start.11 = (bf16[4,64,512]{2,1,0:T(8,128)(2,1)S(1)}, bf16[4,64,512]{2,1,0:T(8,128)(2,1)S(1)}, u32[]{:S(2)}, u32[]{:S(2)}) collective-permute-start(bf16[4,64,512]{2,1,0:T(8,128)(2,1)S(1)} %pad_maximum_fusion.1), channel_id=1, source_target_pairs={{0,32},{8,40},{16,48},{24,56},{32,64},{40,72},{48,80},{56,88},{64,... | collective-permute-start | bytes 786440 | tf_op jit(solution)/shard_map/ppermute | solution.py:86
  46.1 27.7 %copy-start.12 = (s32[128]{0:T(128)}, s32[128]{0:T(128)S(1)}, u32[]{:S(2)}) copy-start(s32[128]{0:T(128)S(1)} %get-tuple-element.11) | copy-start | bytes 1540
  47.6 8.9 %collective-permute-start.5 = (bf16[4,64,512]{2,1,0:T(8,128)(2,1)S(1)}, bf16[4,64,512]{2,1,0:T(8,128)(2,1)S(1)}, u32[]{:S(2)}, u32[]{:S(2)}) collective-permute-start(bf16[4,64,512]{2,1,0:T(8,128)(2,1)S(1)} %collective-permute-done.4), channel_id=1, source_target_pairs={{0,480},{8,488},{16,496},{24,504},{32,0},{40,8},{48,16},{56,24},{6... | collective-permute-start | bytes 786440 | tf_op jit(solution)/shard_map/ppermute | solution.py:86
  53.0 9.3 %collective-permute-start.12 = (bf16[4,64,512]{2,1,0:T(8,128)(2,1)S(1)}, bf16[4,64,512]{2,1,0:T(8,128)(2,1)S(1)}, u32[]{:S(2)}, u32[]{:S(2)}) collective-permute-start(bf16[4,64,512]{2,1,0:T(8,128)(2,1)S(1)} %collective-permute-done.11), channel_id=1, source_target_pairs={{0,32},{8,40},{16,48},{24,56},{32,64},{40,72},{48,80},{56,88},{64,... | collective-permute-start | bytes 786440 | tf_op jit(solution)/shard_map/ppermute | solution.py:86
  56.5 9.3 %collective-permute-start.6 = (bf16[4,64,512]{2,1,0:T(8,128)(2,1)S(1)}, bf16[4,64,512]{2,1,0:T(8,128)(2,1)S(1)}, u32[]{:S(2)}, u32[]{:S(2)}) collective-permute-start(bf16[4,64,512]{2,1,0:T(8,128)(2,1)S(1)} %collective-permute-done.5), channel_id=1, source_target_pairs={{0,480},{8,488},{16,496},{24,504},{32,0},{40,8},{48,16},{56,24},{6... | collective-permute-start | bytes 786440 | tf_op jit(solution)/shard_map/ppermute | solution.py:86
  62.3 8.8 %collective-permute-start.13 = (bf16[4,64,512]{2,1,0:T(8,128)(2,1)S(1)}, bf16[4,64,512]{2,1,0:T(8,128)(2,1)S(1)}, u32[]{:S(2)}, u32[]{:S(2)}) collective-permute-start(bf16[4,64,512]{2,1,0:T(8,128)(2,1)S(1)} %collective-permute-done.12), channel_id=1, source_target_pairs={{0,32},{8,40},{16,48},{24,56},{32,64},{40,72},{48,80},{56,88},{64,... | collective-permute-start | bytes 786440 | tf_op jit(solution)/shard_map/ppermute | solution.py:86
  65.8 10.8 %collective-permute-start.7 = (bf16[4,64,512]{2,1,0:T(8,128)(2,1)S(1)}, bf16[4,64,512]{2,1,0:T(8,128)(2,1)}, u32[]{:S(2)}, u32[]{:S(2)}) collective-permute-start(bf16[4,64,512]{2,1,0:T(8,128)(2,1)S(1)} %collective-permute-done.6), channel_id=1, source_target_pairs={{0,480},{8,488},{16,496},{24,504},{32,0},{40,8},{48,16},{56,24},{6... | collective-permute-start | bytes 786440 | tf_op jit(solution)/shard_map/ppermute | solution.py:86
  71.1 10.1 %collective-permute-start.14 = (bf16[4,64,512]{2,1,0:T(8,128)(2,1)S(1)}, bf16[4,64,512]{2,1,0:T(8,128)(2,1)S(1)}, u32[]{:S(2)}, u32[]{:S(2)}) collective-permute-start(bf16[4,64,512]{2,1,0:T(8,128)(2,1)S(1)} %collective-permute-done.13), channel_id=1, source_target_pairs={{0,32},{8,40},{16,48},{24,56},{32,64},{40,72},{48,80},{56,88},{64,... | collective-permute-start | bytes 786440 | tf_op jit(solution)/shard_map/ppermute | solution.py:86
  76.6 8.6 %collective-permute-start.8 = (bf16[4,64,512]{2,1,0:T(8,128)(2,1)}, bf16[4,64,512]{2,1,0:T(8,128)(2,1)S(1)}, u32[]{:S(2)}, u32[]{:S(2)}) collective-permute-start(bf16[4,64,512]{2,1,0:T(8,128)(2,1)} %collective-permute-done.7), channel_id=1, source_target_pairs={{0,480},{8,488},{16,496},{24,504},{32,0},{40,8},{48,16},{56,24},{6... | collective-permute-start | bytes 786440 | tf_op jit(solution)/shard_map/ppermute | solution.py:86
  81.2 9.1 %collective-permute-start.15 = (bf16[4,64,512]{2,1,0:T(8,128)(2,1)S(1)}, bf16[4,64,512]{2,1,0:T(8,128)(2,1)S(1)}, u32[]{:S(2)}, u32[]{:S(2)}) collective-permute-start(bf16[4,64,512]{2,1,0:T(8,128)(2,1)S(1)} %collective-permute-done.14), channel_id=1, source_target_pairs={{0,32},{8,40},{16,48},{24,56},{32,64},{40,72},{48,80},{56,88},{64,... | collective-permute-start | bytes 786440 | tf_op jit(solution)/shard_map/ppermute | solution.py:86
  85.2 16.1 %collective-permute-start.9 = (bf16[4,64,512]{2,1,0:T(8,128)(2,1)S(1)}, bf16[4,64,512]{2,1,0:T(8,128)(2,1)S(1)}, u32[]{:S(2)}, u32[]{:S(2)}) collective-permute-start(bf16[4,64,512]{2,1,0:T(8,128)(2,1)S(1)} %collective-permute-done.8), channel_id=1, source_target_pairs={{0,480},{8,488},{16,496},{24,504},{32,0},{40,8},{48,16},{56,24},{6... | collective-permute-start | bytes 786440 | tf_op jit(solution)/shard_map/ppermute | solution.py:86
  90.3 9.1 %collective-permute-start.16 = (bf16[4,64,512]{2,1,0:T(8,128)(2,1)S(1)}, bf16[4,64,512]{2,1,0:T(8,128)(2,1)S(1)}, u32[]{:S(2)}, u32[]{:S(2)}) collective-permute-start(bf16[4,64,512]{2,1,0:T(8,128)(2,1)S(1)} %collective-permute-done.15), channel_id=1, source_target_pairs={{0,32},{8,40},{16,48},{24,56},{32,64},{40,72},{48,80},{56,88},{64,... | collective-permute-start | bytes 786440 | tf_op jit(solution)/shard_map/ppermute | solution.py:86
  99.4 9.7 %collective-permute-start.17 = (bf16[4,64,512]{2,1,0:T(8,128)(2,1)S(1)}, bf16[4,64,512]{2,1,0:T(8,128)(2,1)S(1)}, u32[]{:S(2)}, u32[]{:S(2)}) collective-permute-start(bf16[4,64,512]{2,1,0:T(8,128)(2,1)S(1)} %collective-permute-done.16), channel_id=1, source_target_pairs={{0,32},{8,40},{16,48},{24,56},{32,64},{40,72},{48,80},{56,88},{64,... | collective-permute-start | bytes 786440 | tf_op jit(solution)/shard_map/ppermute | solution.py:86
  101.3 9.7 %collective-permute-start.10 = (bf16[4,64,512]{2,1,0:T(8,128)(2,1)S(1)}, bf16[4,64,512]{2,1,0:T(8,128)(2,1)S(1)}, u32[]{:S(2)}, u32[]{:S(2)}) collective-permute-start(bf16[4,64,512]{2,1,0:T(8,128)(2,1)S(1)} %collective-permute-done.9), channel_id=1, source_target_pairs={{0,480},{8,488},{16,496},{24,504},{32,0},{40,8},{48,16},{56,24},{6... | collective-permute-start | bytes 786440 | tf_op jit(solution)/shard_map/ppermute | solution.py:86
  109.1 8.6 %collective-permute-start.18 = (bf16[2,64,512]{2,1,0:T(8,128)(2,1)S(1)}, bf16[2,64,512]{2,1,0:T(8,128)(2,1)S(1)}, u32[]{:S(2)}, u32[]{:S(2)}) collective-permute-start(bf16[2,64,512]{2,1,0:T(8,128)(2,1)S(1)} %slice.180), channel_id=1, source_target_pairs={{0,32},{8,40},{16,48},{24,56},{32,64},{40,72},{48,80},{56,88},{64,... | collective-permute-start | bytes 393224 | tf_op jit(solution)/shard_map/ppermute | solution.py:86
  111.1 7.9 %collective-permute-start.19 = (bf16[2,64,512]{2,1,0:T(8,128)(2,1)S(1)}, bf16[2,64,512]{2,1,0:T(8,128)(2,1)S(1)}, u32[]{:S(2)}, u32[]{:S(2)}) collective-permute-start(bf16[2,64,512]{2,1,0:T(8,128)(2,1)S(1)} %slice.181), channel_id=1, source_target_pairs={{0,480},{8,488},{16,496},{24,504},{32,0},{40,8},{48,16},{56,24},{6... | collective-permute-start | bytes 393224 | tf_op jit(solution)/shard_map/ppermute | solution.py:86
  122.9 30.2 %all-to-all-start.1 = ((bf16[64,4,512]{2,1,0:T(4,128)(2,1)}), bf16[64,4,512]{2,1,0:T(4,128)(2,1)}, u32[]{:S(2)}, u32[]{:S(2)}) async-start(bf16[64,4,512]{2,1,0:T(4,128)(2,1)} %broadcast_select_fusion), calls=%async_computation.1 | async-start | bytes 524288 | tf_op jit(solution)/shard_map/all_to_all | solution.py:173
  161.4 26.2 %all-to-all-start.2 = ((bf16[64,4,640]{2,1,0:T(4,128)(2,1)}), bf16[64,4,640]{2,1,0:T(4,128)(2,1)S(1)}, u32[]{:S(2)}, u32[]{:S(2)}) async-start(bf16[64,4,640]{2,1,0:T(4,128)(2,1)} %pad_maximum_fusion), calls=%async_computation.2 | async-start | bytes 655360 | tf_op jit(solution)/shard_map/all_to_all | solution.py:190
  207.6 24.9 %all-to-all-start.3 = ((bf16[8,128,512]{2,1,0:T(8,128)(2,1)}), bf16[8,128,512]{2,1,0:T(8,128)(2,1)S(1)}, u32[]{:S(2)}, u32[]{:S(2)}) async-start(bf16[8,128,512]{2,1,0:T(8,128)(2,1)} %bitcast.270), calls=%async_computation.3 | async-start | bytes 2097152 | tf_op jit(solution)/shard_map/all_to_all | solution.py:229
  (7 other events, 41.4 us)
Sparse Core Ops, SparseCore 0:
  33.5 163.3 all-gather.1

commit v16 on v14

--- a/solution.py
+++ b/solution.py
@@ -216,11 +216,15 @@
     ).astype(jnp.bfloat16)
     context = context.reshape(length, width_query)
     padded_context = jnp.pad(context, ((0, 0), (kv_width, 0)))
-    partial_out = jnp.dot(padded_context, side, preferred_element_type=jnp.float32)
-    out_width = partial_out.shape[1] // tensor_count
-    pieces = partial_out.astype(jnp.bfloat16).reshape(length, tensor_count, out_width)
+    out_width = side.shape[1] // tensor_count
+    pieces = lax.dot_general(
+        side.reshape(side.shape[0], tensor_count, out_width),
+        padded_context,
+        (((0,), (1,)), ((), ())),
+        preferred_element_type=jnp.float32,
+    ).transpose(0, 2, 1)
     pieces = lax.all_to_all(
-        jnp.moveaxis(pieces, 1, 0), "tensor", split_axis=0, concat_axis=0, tiled=True
+        pieces.astype(jnp.bfloat16), "tensor", split_axis=0, concat_axis=0, tiled=True
     )
     attn_out = jnp.sum(pieces.astype(jnp.float32), axis=0).astype(jnp.bfloat16)
     return (attn_out, suffix_part)

time: 236 us -> 236 us (level)
    unnamed x31 -> x32, local copies, waits for them, and re-layouts: 5.33 us -> 6.1 us
where the time goes in v16:
time: 236 us; the launch traced here: 235 us
  starting transfers between devices  94.6 us (40%)
  waiting for transfers between devices  86.4 us (37%)
  matrix products  15.6 us (7%)
  between operations  15.1 us (6%)
  local copies, waits for them, and re-layouts  14 us (6%)
  other arithmetic  9.47 us (4%)
    ppermute x18, starting transfers between devices, shift(): return lax.ppermute(value, axis_name, pairs)  61.5 us
    ppermute x18, waiting for transfers between devices, shift(): return lax.ppermute(value, axis_name, pairs)  27.1 us
    all_to_all x1, waiting for transfers between devices, shards(): lax.all_to_all(jnp.concatenate([out_block, log_lanes], axis=2), 'seq', sp...  20.6 us
    all_to_all x1, waiting for transfers between devices, shards(): lax.all_to_all(outgoing, 'seq', split_axis=0, concat_axis=0, tiled=True)  16.5 us
    all_to_all x1, waiting for transfers between devices, shards(): lax.all_to_all(pieces.astype(jnp.bfloat16), 'tensor', split_axis=0, conca...  14.2 us
    all_to_all x1, starting transfers between devices, shards(): lax.all_to_all(pieces.astype(jnp.bfloat16), 'tensor', split_axis=0, conca...  10.1 us
    all_to_all x1, starting transfers between devices, shards(): lax.all_to_all(tiles, 'tensor', split_axis=0, concat_axis=0, tiled=True)  10 us
    all_to_all x1, starting transfers between devices, shards(): lax.all_to_all(outgoing, 'seq', split_axis=0, concat_axis=0, tiled=True)  8.06 us
  transfers between devices with their start and end apart: 23, of which 14 were waited for; matrix products, arithmetic and copies ran while one was open for 12% of the time, Pallas kernels for 0%

profile of v16, /device:TPU:1, one launch (start us, length us, event | category | flops | bytes accessed | tf_op | source)
XLA Modules:
  0.0 235.1 jit_solution(9669128222913371572)
XLA Ops:
  7.2 4.2 %collective-permute-start.1 = (bf16[64,512]{1,0:T(8,128)(2,1)}, bf16[64,512]{1,0:T(8,128)(2,1)S(1)}, u32[]{:S(2)}, u32[]{:S(2)}) collective-permute-start(bf16[64,512]{1,0:T(8,128)(2,1)} %param.10), channel_id=1, source_target_pairs={{0,8},{8,16},{16,24},{24,0},{32,40},{40,48},{48,56},{56,32},{64,72... | collective-permute-start | bytes 196616 | tf_op jit(solution)/shard_map/ppermute | solution.py:79
  11.4 3.4 %collective-permute-start = (bf16[64,512]{1,0:T(8,128)(2,1)}, bf16[64,512]{1,0:T(8,128)(2,1)S(1)}, u32[]{:S(2)}, u32[]{:S(2)}) collective-permute-start(bf16[64,512]{1,0:T(8,128)(2,1)} %param.10), channel_id=1, source_target_pairs={{0,24},{8,0},{16,8},{24,16},{32,56},{40,32},{48,40},{56,48},{64,88... | collective-permute-start | bytes 196616 | tf_op jit(solution)/shard_map/ppermute | solution.py:79
  16.9 10.0 %all-to-all-start = ((bf16[8,128,512]{1,2,0:T(8,128)(2,1)}), bf16[8,128,512]{1,2,0:T(8,128)(2,1)S(1)}, u32[]{:S(2)}, u32[]{:S(2)}) async-start(bf16[8,128,512]{1,2,0:T(8,128)(2,1)} %broadcast_in_dim.72), calls=%async_computation | async-start | bytes 2097152 | tf_op jit(solution)/shard_map/all_to_all | solution.py:102
  28.2 1.9 collective-permute-start.2
  30.8 4.1 %collective-permute-done.2 = bf16[64,512]{1,0:T(8,128)(2,1)S(1)} collective-permute-done((bf16[64,512]{1,0:T(8,128)(2,1)S(1)}, bf16[64,512]{1,0:T(8,128)(2,1)S(1)}, u32[]{:S(2)}, u32[]{:S(2)}) %collective-permute-start.2) | collective-permute-done | bytes 65568 | tf_op jit(solution)/shard_map/ppermute | solution.py:79
  34.9 6.7 %collective-permute-start.3 = (bf16[4,64,512]{2,1,0:T(8,128)(2,1)S(1)}, bf16[4,64,512]{2,1,0:T(8,128)(2,1)S(1)}, u32[]{:S(2)}, u32[]{:S(2)}) collective-permute-start(bf16[4,64,512]{2,1,0:T(8,128)(2,1)S(1)} %pad_maximum_fusion.1), channel_id=1, source_target_pairs={{0,480},{8,488},{16,496},{24,504},{32,0},{40,8},{48,16},{56,24},{6... | collective-permute-start | bytes 786440 | tf_op jit(solution)/shard_map/ppermute | solution.py:79
  41.6 1.9 collective-permute-start.10
  43.7 2.7 %collective-permute-done.3 = bf16[4,64,512]{2,1,0:T(8,128)(2,1)S(1)} collective-permute-done((bf16[4,64,512]{2,1,0:T(8,128)(2,1)S(1)}, bf16[4,64,512]{2,1,0:T(8,128)(2,1)S(1)}, u32[]{:S(2)}, u32[]{:S(2)}) %collective-permute-start.3) | collective-permute-done | bytes 262176 | tf_op jit(solution)/shard_map/ppermute | solution.py:79
  46.4 5.3 %collective-permute-start.4 = (bf16[4,64,512]{2,1,0:T(8,128)(2,1)S(1)}, bf16[4,64,512]{2,1,0:T(8,128)(2,1)S(1)}, u32[]{:S(2)}, u32[]{:S(2)}) collective-permute-start(bf16[4,64,512]{2,1,0:T(8,128)(2,1)S(1)} %collective-permute-done.3), channel_id=1, source_target_pairs={{0,480},{8,488},{16,496},{24,504},{32,0},{40,8},{48,16},{56,24},{6... | collective-permute-start | bytes 786440 | tf_op jit(solution)/shard_map/ppermute | solution.py:79
  51.9 1.9 collective-permute-start.11
  54.4 2.1 collective-permute-done.4
  56.5 5.3 %collective-permute-start.5 = (bf16[4,64,512]{2,1,0:T(8,128)(2,1)S(1)}, bf16[4,64,512]{2,1,0:T(8,128)(2,1)S(1)}, u32[]{:S(2)}, u32[]{:S(2)}) collective-permute-start(bf16[4,64,512]{2,1,0:T(8,128)(2,1)S(1)} %collective-permute-done.4), channel_id=1, source_target_pairs={{0,480},{8,488},{16,496},{24,504},{32,0},{40,8},{48,16},{56,24},{6... | collective-permute-start | bytes 786440 | tf_op jit(solution)/shard_map/ppermute | solution.py:79
  65.6 5.3 %collective-permute-start.6 = (bf16[4,64,512]{2,1,0:T(8,128)(2,1)S(1)}, bf16[4,64,512]{2,1,0:T(8,128)(2,1)S(1)}, u32[]{:S(2)}, u32[]{:S(2)}) collective-permute-start(bf16[4,64,512]{2,1,0:T(8,128)(2,1)S(1)} %collective-permute-done.5), channel_id=1, source_target_pairs={{0,480},{8,488},{16,496},{24,504},{32,0},{40,8},{48,16},{56,24},{6... | collective-permute-start | bytes 786440 | tf_op jit(solution)/shard_map/ppermute | solution.py:79
  70.9 1.9 collective-permute-start.13
  75.9 4.6 %collective-permute-start.7 = (bf16[4,64,512]{2,1,0:T(8,128)(2,1)S(1)}, bf16[4,64,512]{2,1,0:T(8,128)(2,1)S(1)}, u32[]{:S(2)}, u32[]{:S(2)}) collective-permute-start(bf16[4,64,512]{2,1,0:T(8,128)(2,1)S(1)} %collective-permute-done.6), channel_id=1, source_target_pairs={{0,480},{8,488},{16,496},{24,504},{32,0},{40,8},{48,16},{56,24},{6... | collective-permute-start | bytes 786440 | tf_op jit(solution)/shard_map/ppermute | solution.py:79
  80.5 1.9 collective-permute-start.14
  84.3 5.0 %collective-permute-start.8 = (bf16[4,64,512]{2,1,0:T(8,128)(2,1)S(1)}, bf16[4,64,512]{2,1,0:T(8,128)(2,1)S(1)}, u32[]{:S(2)}, u32[]{:S(2)}) collective-permute-start(bf16[4,64,512]{2,1,0:T(8,128)(2,1)S(1)} %collective-permute-done.7), channel_id=1, source_target_pairs={{0,480},{8,488},{16,496},{24,504},{32,0},{40,8},{48,16},{56,24},{6... | collective-permute-start | bytes 786440 | tf_op jit(solution)/shard_map/ppermute | solution.py:79
  89.8 1.9 collective-permute-start.15
  92.1 6.7 %collective-permute-done.15 = bf16[4,64,512]{2,1,0:T(8,128)(2,1)S(1)} collective-permute-done((bf16[4,64,512]{2,1,0:T(8,128)(2,1)S(1)}, bf16[4,64,512]{2,1,0:T(8,128)(2,1)S(1)}, u32[]{:S(2)}, u32[]{:S(2)}) %collective-permute-start.15) | collective-permute-done | bytes 262176 | tf_op jit(solution)/shard_map/ppermute | solution.py:79
  98.8 1.9 collective-permute-start.16
  101.0 4.6 %collective-permute-start.9 = (bf16[4,64,512]{2,1,0:T(8,128)(2,1)S(1)}, bf16[4,64,512]{2,1,0:T(8,128)(2,1)S(1)}, u32[]{:S(2)}, u32[]{:S(2)}) collective-permute-start(bf16[4,64,512]{2,1,0:T(8,128)(2,1)S(1)} %collective-permute-done.8), channel_id=1, source_target_pairs={{0,480},{8,488},{16,496},{24,504},{32,0},{40,8},{48,16},{56,24},{6... | collective-permute-start | bytes 786440 | tf_op jit(solution)/shard_map/ppermute | solution.py:79
  109.5 6.9 %collective-permute-done.17 = bf16[4,64,512]{2,1,0:T(8,128)(2,1)S(1)} collective-permute-done((bf16[4,64,512]{2,1,0:T(8,128)(2,1)S(1)}, bf16[4,64,512]{2,1,0:T(8,128)(2,1)S(1)}, u32[]{:S(2)}, u32[]{:S(2)}) %collective-permute-start.17) | collective-permute-done | bytes 262176 | tf_op jit(solution)/shard_map/ppermute | solution.py:79
  120.0 8.1 %all-to-all-start.1 = ((bf16[64,4,512]{2,1,0:T(4,128)(2,1)}), bf16[64,4,512]{2,1,0:T(4,128)(2,1)}, u32[]{:S(2)}, u32[]{:S(2)}) async-start(bf16[64,4,512]{2,1,0:T(4,128)(2,1)} %broadcast_select_fusion), calls=%async_computation.1 | async-start | bytes 524288 | tf_op jit(solution)/shard_map/all_to_all | solution.py:166
  128.1 2.9 %copy.203 = bf16[1,1024,1024]{1,2,0:T(8,128)(2,1)S(1)} copy(bf16[1,1024,1024]{2,1,0:T(8,128)(2,1)} %param.13) | data formatting | bytes 4194304 | tf_op args[5]
  130.9 16.5 %all-to-all-done.1 = bf16[64,4,512]{2,1,0:T(4,128)(2,1)} async-done(((bf16[64,4,512]{2,1,0:T(4,128)(2,1)}), bf16[64,4,512]{2,1,0:T(4,128)(2,1)}, u32[]{:S(2)}, u32[]{:S(2)}) %all-to-all-start.1) | async-done | bytes 262176 | tf_op jit(solution)/shard_map/all_to_all | solution.py:166
  155.7 4.9 %all-to-all-start.2 = ((bf16[64,4,640]{2,1,0:T(4,128)(2,1)}), bf16[64,4,640]{2,1,0:T(4,128)(2,1)S(1)}, u32[]{:S(2)}, u32[]{:S(2)}) async-start(bf16[64,4,640]{2,1,0:T(4,128)(2,1)} %pad_maximum_fusion), calls=%async_computation.2 | async-start | bytes 655360 | tf_op jit(solution)/shard_map/all_to_all | solution.py:183
  161.5 20.6 %all-to-all-done.2 = bf16[64,4,640]{2,1,0:T(4,128)(2,1)S(1)} async-done(((bf16[64,4,640]{2,1,0:T(4,128)(2,1)}), bf16[64,4,640]{2,1,0:T(4,128)(2,1)S(1)}, u32[]{:S(2)}, u32[]{:S(2)}) %all-to-all-start.2) | async-done | bytes 327712 | tf_op jit(solution)/shard_map/all_to_all | solution.py:183
  184.0 7.9 %all-gather.2.cloned.1.call-done = bf16[768,4096]{0,1:T(8,128)(2,1)} async-done(((bf16[768,64]{0,1:T(8,128)(2,1)}), bf16[768,4096]{0,1:T(8,128)(2,1)}) %all-gather.2.cloned.1.call-update) | async-done | bytes 6291472 | tf_op jit(solution)/shard_map/all_gather | solution.py:119
  191.8 2.1 fusion
  196.6 5.6 %fusion.4 = bf16[8,128,512]{1,2,0:T(8,128)(2,1)} fusion(bf16[768,8,512]{0,2,1:T(8,128)(2,1)} %bitcast.269, bf16[128,512]{1,0:T(8,128)(2,1)S(1)} %copy.216), kind=kOutput, calls=%fused_computation.15 | convolution fusion | flops 805830656 | bytes 7471104 | tf_op jit(solution)/shard_map/dot_general | solution.py:220
  202.1 10.1 %all-to-all-start.3 = ((bf16[8,128,512]{1,2,0:T(8,128)(2,1)}), bf16[8,128,512]{1,2,0:T(8,128)(2,1)S(1)}, u32[]{:S(2)}, u32[]{:S(2)}) async-start(bf16[8,128,512]{1,2,0:T(8,128)(2,1)} %fusion.4), calls=%async_computation.3 | async-start | bytes 2097152 | tf_op jit(solution)/shard_map/all_to_all | solution.py:226
  213.1 14.2 %all-to-all-done.3 = bf16[8,128,512]{1,2,0:T(8,128)(2,1)S(1)} async-done(((bf16[8,128,512]{1,2,0:T(8,128)(2,1)}), bf16[8,128,512]{1,2,0:T(8,128)(2,1)S(1)}, u32[]{:S(2)}, u32[]{:S(2)}) %all-to-all-start.3) | async-done | bytes 1048608 | tf_op jit(solution)/shard_map/all_to_all | solution.py:226
  (162 shorter events, 37.0 us)
Async XLA Ops:
  7.2 19.8 %copy-start = (bf16[64,1024]{1,0:T(8,128)(2,1)S(1)}, bf16[64,1024]{1,0:T(8,128)(2,1)}, u32[]{:S(2)}) copy-start(bf16[64,1024]{1,0:T(8,128)(2,1)} %param.11) | copy-start | bytes 393220
  7.2 27.7 %copy-start.4 = (bf16[64,512]{1,0:T(8,128)(2,1)S(1)}, bf16[64,512]{1,0:T(8,128)(2,1)}, u32[]{:S(2)}) copy-start(bf16[64,512]{1,0:T(8,128)(2,1)} %param.10) | copy-start | bytes 196612
  7.2 19.8 %copy-start.3 = (bf16[512,64]{0,1:T(8,128)(2,1)S(1)}, bf16[512,64]{0,1:T(8,128)(2,1)}, u32[]{:S(2)}) copy-start(bf16[512,64]{0,1:T(8,128)(2,1)} %param.12) | copy-start | bytes 196612
  7.2 20.5 %copy-start.6 = (s32[1,64]{1,0:T(1,128)S(1)}, s32[1,64]{1,0:T(1,128)}, u32[]{:S(2)}) copy-start(s32[1,64]{1,0:T(1,128)} %param.15) | copy-start | bytes 772
  7.2 20.8 %copy-start.9 = (s32[64]{0:T(128)S(1)}, s32[64]{0:T(128)}, u32[]{:S(2)}) copy-start(s32[64]{0:T(128)} %param.14) | copy-start | bytes 772
  7.2 21.0 %collective-permute-start.1 = (bf16[64,512]{1,0:T(8,128)(2,1)}, bf16[64,512]{1,0:T(8,128)(2,1)S(1)}, u32[]{:S(2)}, u32[]{:S(2)}) collective-permute-start(bf16[64,512]{1,0:T(8,128)(2,1)} %param.10), channel_id=1, source_target_pairs={{0,8},{8,16},{16,24},{24,0},{32,40},{40,48},{48,56},{56,32},{64,72... | collective-permute-start | bytes 196616 | tf_op jit(solution)/shard_map/ppermute | solution.py:79
  11.4 19.4 %collective-permute-start = (bf16[64,512]{1,0:T(8,128)(2,1)}, bf16[64,512]{1,0:T(8,128)(2,1)S(1)}, u32[]{:S(2)}, u32[]{:S(2)}) collective-permute-start(bf16[64,512]{1,0:T(8,128)(2,1)} %param.10), channel_id=1, source_target_pairs={{0,24},{8,0},{16,8},{24,16},{32,56},{40,32},{48,40},{56,48},{64,88... | collective-permute-start | bytes 196616 | tf_op jit(solution)/shard_map/ppermute | solution.py:79
  15.8 38.1 %copy-start.5 = (bf16[4096]{0:T(1024)(128)(2,1)S(1)}, bf16[4096]{0:T(1024)(128)(2,1)}, u32[]{:S(2)}) copy-start(bf16[4096]{0:T(1024)(128)(2,1)} %param.9) | copy-start | bytes 24580
  16.9 46.8 %all-to-all-start = ((bf16[8,128,512]{1,2,0:T(8,128)(2,1)}), bf16[8,128,512]{1,2,0:T(8,128)(2,1)S(1)}, u32[]{:S(2)}, u32[]{:S(2)}) async-start(bf16[8,128,512]{1,2,0:T(8,128)(2,1)} %broadcast_in_dim.72), calls=%async_computation | async-start | bytes 2097152 | tf_op jit(solution)/shard_map/all_to_all | solution.py:102
  26.9 164.9 %all-gather.2.cloned.1.call-start = ((), (), s32[]{:S(2)}) async-start(), calls=%async_computation.4 | async-start | bytes 6389760 | tf_op jit(solution)/shard_map/all_gather | solution.py:119
  28.2 6.7 %collective-permute-start.2 = (bf16[64,512]{1,0:T(8,128)(2,1)S(1)}, bf16[64,512]{1,0:T(8,128)(2,1)S(1)}, u32[]{:S(2)}, u32[]{:S(2)}) collective-permute-start(bf16[64,512]{1,0:T(8,128)(2,1)S(1)} %collective-permute-done.1), channel_id=1, source_target_pairs={{0,8},{8,16},{16,24},{24,0},{32,40},{40,48},{48,56},{56,32},{64,72... | collective-permute-start | bytes 196616 | tf_op jit(solution)/shard_map/ppermute | solution.py:79
  30.8 12.8 %copy-start.12 = (s32[128]{0:T(128)}, s32[128]{0:T(128)S(1)}, u32[]{:S(2)}) copy-start(s32[128]{0:T(128)S(1)} %get-tuple-element.11) | copy-start | bytes 1540
  34.9 11.5 %collective-permute-start.3 = (bf16[4,64,512]{2,1,0:T(8,128)(2,1)S(1)}, bf16[4,64,512]{2,1,0:T(8,128)(2,1)S(1)}, u32[]{:S(2)}, u32[]{:S(2)}) collective-permute-start(bf16[4,64,512]{2,1,0:T(8,128)(2,1)S(1)} %pad_maximum_fusion.1), channel_id=1, source_target_pairs={{0,480},{8,488},{16,496},{24,504},{32,0},{40,8},{48,16},{56,24},{6... | collective-permute-start | bytes 786440 | tf_op jit(solution)/shard_map/ppermute | solution.py:79
  41.6 10.3 %collective-permute-start.10 = (bf16[4,64,512]{2,1,0:T(8,128)(2,1)S(1)}, bf16[4,64,512]{2,1,0:T(8,128)(2,1)S(1)}, u32[]{:S(2)}, u32[]{:S(2)}) collective-permute-start(bf16[4,64,512]{2,1,0:T(8,128)(2,1)S(1)} %pad_maximum_fusion.1), channel_id=1, source_target_pairs={{0,32},{8,40},{16,48},{24,56},{32,64},{40,72},{48,80},{56,88},{64,... | collective-permute-start | bytes 786440 | tf_op jit(solution)/shard_map/ppermute | solution.py:79
  46.4 10.1 %collective-permute-start.4 = (bf16[4,64,512]{2,1,0:T(8,128)(2,1)S(1)}, bf16[4,64,512]{2,1,0:T(8,128)(2,1)S(1)}, u32[]{:S(2)}, u32[]{:S(2)}) collective-permute-start(bf16[4,64,512]{2,1,0:T(8,128)(2,1)S(1)} %collective-permute-done.3), channel_id=1, source_target_pairs={{0,480},{8,488},{16,496},{24,504},{32,0},{40,8},{48,16},{56,24},{6... | collective-permute-start | bytes 786440 | tf_op jit(solution)/shard_map/ppermute | solution.py:79
  51.9 9.9 %collective-permute-start.11 = (bf16[4,64,512]{2,1,0:T(8,128)(2,1)S(1)}, bf16[4,64,512]{2,1,0:T(8,128)(2,1)S(1)}, u32[]{:S(2)}, u32[]{:S(2)}) collective-permute-start(bf16[4,64,512]{2,1,0:T(8,128)(2,1)S(1)} %collective-permute-done.10), channel_id=1, source_target_pairs={{0,32},{8,40},{16,48},{24,56},{32,64},{40,72},{48,80},{56,88},{64,... | collective-permute-start | bytes 786440 | tf_op jit(solution)/shard_map/ppermute | solution.py:79
  56.5 9.1 %collective-permute-start.5 = (bf16[4,64,512]{2,1,0:T(8,128)(2,1)S(1)}, bf16[4,64,512]{2,1,0:T(8,128)(2,1)S(1)}, u32[]{:S(2)}, u32[]{:S(2)}) collective-permute-start(bf16[4,64,512]{2,1,0:T(8,128)(2,1)S(1)} %collective-permute-done.4), channel_id=1, source_target_pairs={{0,480},{8,488},{16,496},{24,504},{32,0},{40,8},{48,16},{56,24},{6... | collective-permute-start | bytes 786440 | tf_op jit(solution)/shard_map/ppermute | solution.py:79
  61.8 9.1 %collective-permute-start.12 = (bf16[4,64,512]{2,1,0:T(8,128)(2,1)S(1)}, bf16[4,64,512]{2,1,0:T(8,128)(2,1)S(1)}, u32[]{:S(2)}, u32[]{:S(2)}) collective-permute-start(bf16[4,64,512]{2,1,0:T(8,128)(2,1)S(1)} %collective-permute-done.11), channel_id=1, source_target_pairs={{0,32},{8,40},{16,48},{24,56},{32,64},{40,72},{48,80},{56,88},{64,... | collective-permute-start | bytes 786440 | tf_op jit(solution)/shard_map/ppermute | solution.py:79
  65.6 10.3 %collective-permute-start.6 = (bf16[4,64,512]{2,1,0:T(8,128)(2,1)S(1)}, bf16[4,64,512]{2,1,0:T(8,128)(2,1)S(1)}, u32[]{:S(2)}, u32[]{:S(2)}) collective-permute-start(bf16[4,64,512]{2,1,0:T(8,128)(2,1)S(1)} %collective-permute-done.5), channel_id=1, source_target_pairs={{0,480},{8,488},{16,496},{24,504},{32,0},{40,8},{48,16},{56,24},{6... | collective-permute-start | bytes 786440 | tf_op jit(solution)/shard_map/ppermute | solution.py:79
  70.9 9.6 %collective-permute-start.13 = (bf16[4,64,512]{2,1,0:T(8,128)(2,1)S(1)}, bf16[4,64,512]{2,1,0:T(8,128)(2,1)S(1)}, u32[]{:S(2)}, u32[]{:S(2)}) collective-permute-start(bf16[4,64,512]{2,1,0:T(8,128)(2,1)S(1)} %collective-permute-done.12), channel_id=1, source_target_pairs={{0,32},{8,40},{16,48},{24,56},{32,64},{40,72},{48,80},{56,88},{64,... | collective-permute-start | bytes 786440 | tf_op jit(solution)/shard_map/ppermute | solution.py:79
  75.9 8.4 %collective-permute-start.7 = (bf16[4,64,512]{2,1,0:T(8,128)(2,1)S(1)}, bf16[4,64,512]{2,1,0:T(8,128)(2,1)S(1)}, u32[]{:S(2)}, u32[]{:S(2)}) collective-permute-start(bf16[4,64,512]{2,1,0:T(8,128)(2,1)S(1)} %collective-permute-done.6), channel_id=1, source_target_pairs={{0,480},{8,488},{16,496},{24,504},{32,0},{40,8},{48,16},{56,24},{6... | collective-permute-start | bytes 786440 | tf_op jit(solution)/shard_map/ppermute | solution.py:79
  80.5 9.3 %collective-permute-start.14 = (bf16[4,64,512]{2,1,0:T(8,128)(2,1)S(1)}, bf16[4,64,512]{2,1,0:T(8,128)(2,1)S(1)}, u32[]{:S(2)}, u32[]{:S(2)}) collective-permute-start(bf16[4,64,512]{2,1,0:T(8,128)(2,1)S(1)} %collective-permute-done.13), channel_id=1, source_target_pairs={{0,32},{8,40},{16,48},{24,56},{32,64},{40,72},{48,80},{56,88},{64,... | collective-permute-start | bytes 786440 | tf_op jit(solution)/shard_map/ppermute | solution.py:79
  84.3 16.4 %collective-permute-start.8 = (bf16[4,64,512]{2,1,0:T(8,128)(2,1)S(1)}, bf16[4,64,512]{2,1,0:T(8,128)(2,1)S(1)}, u32[]{:S(2)}, u32[]{:S(2)}) collective-permute-start(bf16[4,64,512]{2,1,0:T(8,128)(2,1)S(1)} %collective-permute-done.7), channel_id=1, source_target_pairs={{0,480},{8,488},{16,496},{24,504},{32,0},{40,8},{48,16},{56,24},{6... | collective-permute-start | bytes 786440 | tf_op jit(solution)/shard_map/ppermute | solution.py:79
  89.8 9.0 %collective-permute-start.15 = (bf16[4,64,512]{2,1,0:T(8,128)(2,1)S(1)}, bf16[4,64,512]{2,1,0:T(8,128)(2,1)S(1)}, u32[]{:S(2)}, u32[]{:S(2)}) collective-permute-start(bf16[4,64,512]{2,1,0:T(8,128)(2,1)S(1)} %collective-permute-done.14), channel_id=1, source_target_pairs={{0,32},{8,40},{16,48},{24,56},{32,64},{40,72},{48,80},{56,88},{64,... | collective-permute-start | bytes 786440 | tf_op jit(solution)/shard_map/ppermute | solution.py:79
  98.8 8.3 %collective-permute-start.16 = (bf16[4,64,512]{2,1,0:T(8,128)(2,1)S(1)}, bf16[4,64,512]{2,1,0:T(8,128)(2,1)S(1)}, u32[]{:S(2)}, u32[]{:S(2)}) collective-permute-start(bf16[4,64,512]{2,1,0:T(8,128)(2,1)S(1)} %collective-permute-done.15), channel_id=1, source_target_pairs={{0,32},{8,40},{16,48},{24,56},{32,64},{40,72},{48,80},{56,88},{64,... | collective-permute-start | bytes 786440 | tf_op jit(solution)/shard_map/ppermute | solution.py:79
  101.0 8.3 %collective-permute-start.9 = (bf16[4,64,512]{2,1,0:T(8,128)(2,1)S(1)}, bf16[4,64,512]{2,1,0:T(8,128)(2,1)S(1)}, u32[]{:S(2)}, u32[]{:S(2)}) collective-permute-start(bf16[4,64,512]{2,1,0:T(8,128)(2,1)S(1)} %collective-permute-done.8), channel_id=1, source_target_pairs={{0,480},{8,488},{16,496},{24,504},{32,0},{40,8},{48,16},{56,24},{6... | collective-permute-start | bytes 786440 | tf_op jit(solution)/shard_map/ppermute | solution.py:79
  107.1 9.3 %collective-permute-start.17 = (bf16[4,64,512]{2,1,0:T(8,128)(2,1)S(1)}, bf16[4,64,512]{2,1,0:T(8,128)(2,1)S(1)}, u32[]{:S(2)}, u32[]{:S(2)}) collective-permute-start(bf16[4,64,512]{2,1,0:T(8,128)(2,1)S(1)} %collective-permute-done.16), channel_id=1, source_target_pairs={{0,32},{8,40},{16,48},{24,56},{32,64},{40,72},{48,80},{56,88},{64,... | collective-permute-start | bytes 786440 | tf_op jit(solution)/shard_map/ppermute | solution.py:79
  120.0 27.5 %all-to-all-start.1 = ((bf16[64,4,512]{2,1,0:T(4,128)(2,1)}), bf16[64,4,512]{2,1,0:T(4,128)(2,1)}, u32[]{:S(2)}, u32[]{:S(2)}) async-start(bf16[64,4,512]{2,1,0:T(4,128)(2,1)} %broadcast_select_fusion), calls=%async_computation.1 | async-start | bytes 524288 | tf_op jit(solution)/shard_map/all_to_all | solution.py:166
  153.2 7.6 %copy-start.8 = (f32[128]{0:T(128)S(1)}, f32[128]{0:T(128)}, u32[]{:S(2)}) copy-start(f32[128]{0:T(128)} %copy-done.7) | copy-start | bytes 1540
  155.7 26.4 %all-to-all-start.2 = ((bf16[64,4,640]{2,1,0:T(4,128)(2,1)}), bf16[64,4,640]{2,1,0:T(4,128)(2,1)S(1)}, u32[]{:S(2)}, u32[]{:S(2)}) async-start(bf16[64,4,640]{2,1,0:T(4,128)(2,1)} %pad_maximum_fusion), calls=%async_computation.2 | async-start | bytes 655360 | tf_op jit(solution)/shard_map/all_to_all | solution.py:183
  183.9 10.6 %copy-start.2 = (bf16[128,4,128]{2,0,1:T(8,128)(2,1)S(1)}, bf16[128,4,128]{2,0,1:T(8,128)(2,1)}, u32[]{:S(2)}) copy-start(bf16[128,4,128]{2,0,1:T(8,128)(2,1)} %copy-done.1) | copy-start | bytes 393220
  202.1 25.2 %all-to-all-start.3 = ((bf16[8,128,512]{1,2,0:T(8,128)(2,1)}), bf16[8,128,512]{1,2,0:T(8,128)(2,1)S(1)}, u32[]{:S(2)}, u32[]{:S(2)}) async-start(bf16[8,128,512]{1,2,0:T(8,128)(2,1)} %fusion.4), calls=%async_computation.3 | async-start | bytes 2097152 | tf_op jit(solution)/shard_map/all_to_all | solution.py:226
  (5 other events, 24.3 us)
Sparse Core Ops, SparseCore 0:
  30.7 161.0 all-gather.1
